TPU v7x, 32 devices: a whole 2x2x4 slice. The times are simulated.
32 devices in a mesh: rep: 2 (over x), own: 16 (over z, y, core).
Axes of the slice: x: 2, y: 2, z: 4, core: 2. Of those that a mesh axis runs over, the one named last changes fastest.
Arguments:
- gradient: bfloat16 [2, 64, 64, 1024], P('rep', 'own'), may hold values from -6 to 6
- feedback: float32 [2, 64, 64, 1024], P('rep', 'own'), may hold values from -4 to 4
- momentum: float32 [64, 64, 1024], P('own'), may hold values from -6 to 6
- tile_matrix: int32 [64], P('own'), may hold values from 0 to 8, as said below
- matrix_group: int32 [9], replicated, may hold values from 0 to 3
- group_scale: float32 [4], replicated, may hold values from 0.3 to 3
- start_basis: float32 [9, 1024, 32], replicated, may hold values from -0.1875 to 0.1875
- inverse_gram_factors: float32 [3, 9, 32, 32], replicated
- vector_grad: float32 [2, 5, 1024], P('rep'), may hold values from -6 to 6
- vector_momentum: float32 [5, 1024], replicated, may hold values from -6 to 6
Outputs:
- new_feedback: float32 [2, 64, 64, 1024], P('rep', 'own')
- new_momentum: float32 [64, 64, 1024], P('own')
- new_vector_momentum: float32 [5, 1024], replicated
Inputs may be any that keep to these rules, and one draw needn't show every extreme that they name: `tile_matrix`: matrices 4 l, 4 l + 1, 4 l + 2, 4 l + 3 are layer l's query, keys, gate and output, matrix 9 - 1 the embedding; with weights 8, 2, 2, 2 per layer and 16 for the embedding, matrix m holds 64 * weight // 44 tiles, and the embedding also takes the tiles left over; the tiles of a matrix lie at scattered positions.
All inputs are finite; a program needn't handle non-finite values.
Results may differ from a plain program's by a relative error of at most 0.0003.
Values sent between devices are 32-bit elements; how exact they have to be, the bound alone decides.
No kernel may reach another device: no remote copies, remote signals or barrier semaphores. Data moves between devices by JAX's collectives and lax.ppermute only.
A program may use at most 64 MiB of HBM per device.

v0:
```python
import jax
import jax.numpy as jnp
from jax import lax
from jax.sharding import PartitionSpec as P

TOP_PRECISION = lax.Precision.HIGHEST


def table_total(combined, ortho_rows, selector, replicas, mixing_matrix):
    tile_parts = jnp.einsum("tkd,tks->tds", combined, ortho_rows, precision=TOP_PRECISION)
    table_part = jnp.einsum("tm,tds->mds", selector, tile_parts, precision=TOP_PRECISION)
    grand_total = lax.psum(table_part, ("rep", "own")) / replicas
    if mixing_matrix is not None:
        grand_total = jnp.einsum(
            "ltj,ljw->ltw", grand_total, mixing_matrix, precision=TOP_PRECISION
        )
    return grand_total


def local(
    gradient,
    feedback,
    momentum,
    tile_matrix,
    matrix_group,
    group_scale,
    start_basis,
    inverse_gram_factors,
    vector_grad,
    vector_momentum,
):
    replicas = lax.axis_size("rep")
    matrix_count = start_basis.shape[0]
    selector = (tile_matrix[:, None] == jnp.arange(matrix_count, dtype=jnp.int32)[None, :]).astype(
        jnp.float32
    )
    combined = gradient[0].astype(jnp.float32) + feedback[0]
    q_tiles = jnp.einsum("tm,mds->tds", selector, start_basis, precision=TOP_PRECISION)
    first_local = jnp.einsum("tkd,tds->tks", combined, q_tiles, precision=TOP_PRECISION)
    vector_summed = lax.psum(vector_grad[0], "rep")
    first_summed = lax.psum(first_local, "rep")
    first_left = first_summed / replicas
    mix_first = jnp.einsum(
        "tm,mab->tab", selector, inverse_gram_factors[0], precision=TOP_PRECISION
    )
    first_ortho = jnp.einsum("tks,tsa->tka", first_left, mix_first, precision=TOP_PRECISION)
    initial_right_factor = table_total(
        combined, first_ortho, selector, replicas, inverse_gram_factors[1]
    )
    right_tiles = jnp.einsum("tm,mds->tds", selector, initial_right_factor, precision=TOP_PRECISION)
    second_local = jnp.einsum("tkd,tds->tks", combined, right_tiles, precision=TOP_PRECISION)
    second_left = lax.psum(second_local, "rep") / replicas
    mix_second = jnp.einsum(
        "tm,mab->tab", selector, inverse_gram_factors[2], precision=TOP_PRECISION
    )
    second_ortho = jnp.einsum("tks,tsa->tka", second_left, mix_second, precision=TOP_PRECISION)
    second_right = table_total(combined, second_ortho, selector, replicas, None)
    back_tiles = jnp.einsum("tm,mds->tds", selector, second_right, precision=TOP_PRECISION)
    approximation = jnp.einsum("tks,tds->tkd", second_ortho, back_tiles, precision=TOP_PRECISION)
    new_feedback = (combined - approximation)[None]
    group_select = (
        matrix_group[:, None] == jnp.arange(group_scale.shape[0], dtype=jnp.int32)[None, :]
    ).astype(jnp.float32)
    matrix_scale = jnp.dot(group_select, group_scale, precision=TOP_PRECISION)
    tile_scale = jnp.dot(selector, matrix_scale, precision=TOP_PRECISION)
    new_momentum = 0.9 * momentum + tile_scale[:, None, None] * approximation
    new_vector_momentum = 0.9 * vector_momentum + vector_summed / replicas
    return (new_feedback, new_momentum, new_vector_momentum)


def solution(mesh):
    placed = (
        P("rep", "own", None, None),
        P("rep", "own", None, None),
        P("own", None, None),
        P("own"),
        P(),
        P(),
        P(),
        P(),
        P("rep", None, None),
        P(),
    )
    return jax.shard_map(
        local,
        mesh=mesh,
        in_specs=placed,
        out_specs=(P("rep", "own", None, None), P("own", None, None), P()),
        check_vma=False,
    )
```

profile of v0, /device:TPU:0, one launch (start us, length us, event | category | flops | bytes accessed | tf_op | source)
XLA Modules:
  0.0 328.5 jit_solution(15635304952249224396)
XLA Ops:
  7.2 0.0 copy-start
  7.2 0.0 all-reduce.4.cloned.1.call-start
  7.2 1.2 fusion.52
  8.4 1.0 fusion.27
  9.4 2.1 fusion.2
  11.5 0.0 copy-start.5
  11.5 1.3 fusion.14
  12.8 10.4 %psum.35 = f32[4,64,32]{1,2,0:T(8,128)S(1)} all-reduce(f32[4,64,32]{1,2,0:T(8,128)S(1)} %fusion.14), channel_id=1, replica_groups=mesh['rep'=2,'own'=16] {'rep'}, use_global_device_ids=true, to_apply=%region_0.0 | all-reduce | flops 8192 | bytes 65536 | tf_op jit(solution)/shard_map/psum | solution.py:41
  23.2 0.3 fusion.32
  23.5 0.7 fusion.12
  24.3 0.0 copy-start.6
  24.3 2.7 fusion.23
  27.0 0.0 all-reduce.4.cloned.1.call-update
  27.0 0.0 all-reduce.6.cloned.1.call-start
  27.1 0.3 fusion.26
  27.4 134.7 %all-reduce.4.cloned.1.call-done = f32[9,1024,32]{1,0,2:T(8,128)} async-done(((f32[9,1024,32]{1,0,2:T(8,128)}), f32[9,1024,32]{1,0,2:T(8,128)}) %all-reduce.4.cloned.1.call-update) | async-done | bytes 1179664 | tf_op jit(solution)/shard_map/psum | solution.py:12
  162.0 1.8 broadcast_multiply_fusion
  163.8 2.8 fusion.6
  166.6 1.4 fusion
  168.0 1.3 fusion.10
  169.4 9.3 %all-reduce = (f32[4,64,32]{1,2,0:T(8,128)S(1)}, f32[5,1024]{1,0:T(8,128)S(1)}) all-reduce(f32[4,64,32]{1,2,0:T(8,128)S(1)} %fusion.10, f32[5,1024]{1,0:T(8,128)S(1)} %bitcast.48), channel_id=1, replica_groups=mesh['rep'=2,'own'=16] {'rep'}, use_global_device_ids=true, to_apply=%region_2.0 | all-reduce | flops 13312 | bytes 106496 | tf_op jit(solution)/shard_map/psum | solution.py:52
  178.7 0.3 fusion.30
  179.0 0.8 fusion.8
  179.7 0.0 copy-start.4
  179.7 2.7 fusion.20
  182.4 0.0 all-reduce.6.cloned.1.call-update
  182.4 0.2 convolution_bitcast_fusion.1
  182.6 0.2 convolution_bitcast_fusion
  182.8 0.6 multiply_add_fusion.1
  183.5 132.8 %all-reduce.6.cloned.1.call-done = f32[9,1024,32]{1,0,2:T(8,128)} async-done(((f32[9,1024,32]{1,0,2:T(8,128)}), f32[9,1024,32]{1,0,2:T(8,128)}) %all-reduce.6.cloned.1.call-update) | async-done | bytes 1179664 | tf_op jit(solution)/shard_map/psum | solution.py:12
  316.3 2.6 fusion.4
  318.9 2.7 multiply_add_fusion
  (15 shorter events, 0.0 us)
Async XLA Ops:
  7.2 2.2 copy-start
  7.2 4.3 %copy-start.1 = (f32[1,4,64,1024]{3,2,1,0:T(8,128)S(1)}, f32[1,4,64,1024]{3,2,1,0:T(8,128)}, u32[]{:S(2)}) copy-start(f32[1,4,64,1024]{3,2,1,0:T(8,128)} %param.11) | copy-start | bytes 3145732
  7.2 4.3 %copy-start.2 = (bf16[1,4,64,1024]{3,2,1,0:T(8,128)(2,1)S(1)}, bf16[1,4,64,1024]{3,2,1,0:T(8,128)(2,1)}, u32[]{:S(2)}) copy-start(bf16[1,4,64,1024]{3,2,1,0:T(8,128)(2,1)} %param.10) | copy-start | bytes 1572868
  7.2 154.8 %all-reduce.4.cloned.1.call-start = ((), (), s32[]{:S(2)}) async-start(), calls=%async_computation | async-start | bytes 4194304 | tf_op jit(solution)/shard_map/psum | solution.py:12
  11.5 12.8 %copy-start.5 = (s32[4]{0:T(128)S(1)}, s32[4]{0:T(128)}, u32[]{:S(2)}) copy-start(s32[4]{0:T(128)} %param.13) | copy-start | bytes 52
  24.3 2.7 copy-start.6
  27.0 289.3 %all-reduce.6.cloned.1.call-start = ((), (), s32[]{:S(2)}) async-start(), calls=%async_computation.1 | async-start | bytes 4194304 | tf_op jit(solution)/shard_map/psum | solution.py:12
  179.7 2.7 copy-start.7
  179.7 2.7 copy-start.8
  179.7 3.1 copy-start.4
  316.3 2.6 copy-start.3
Sparse Core Ops, SparseCore 0:
  27.1 134.8 all-reduce.3
  182.5 133.6 all-reduce.5
where the time goes:
time: 329 us; the launch traced here: 328 us
  waiting for transfers between devices  268 us (81%)
  matrix products  23.2 us (7%)
  blocking collectives  19.7 us (6%)
  between operations  14.3 us (4%)
    psum x2, waiting for transfers between devices, table_total(): grand_total = lax.psum(table_part, ('rep', 'own')) / replicas  267 us
    psum x1, blocking collectives, local(): first_summed = lax.psum(first_local, 'rep')  10.4 us
    psum x1, blocking collectives, local(): second_left = lax.psum(second_local, 'rep') / replicas  9.3 us
  transfers between devices with their start and end apart: 2, of which 2 were waited for; matrix products, arithmetic and copies ran while one was open for 0% of the time, Pallas kernels for 0%

commit v1 on v0

v1 whole, which is shorter than its diff:
```python
import jax
import jax.numpy as jnp
from jax import lax
from jax.sharding import PartitionSpec as P

TOP_PRECISION = lax.Precision.HIGHEST


def _bits(n):
    return (n - 1).bit_length()


def _pair_perm(n, j):
    return [(i, i ^ (1 << j)) for i in range(n)]


def swap_sum(x, axis):
    n = lax.axis_size(axis)
    for j in range(_bits(n)):
        x = x + lax.ppermute(x, axis, _pair_perm(n, j))
    return x


def _split_plan(shape, steps):
    dims = list(shape)
    plan = []
    for _ in range(steps):
        if dims[-1] > 128:
            axis = len(dims) - 1
        elif dims[-2] > 8:
            axis = len(dims) - 2
        elif dims[-1] % 2 == 0 and dims[-1] >= dims[-2]:
            axis = len(dims) - 1
        else:
            axis = len(dims) - 2
        assert dims[axis] % 2 == 0
        dims[axis] //= 2
        plan.append(axis)
    return plan


def table_sum(x, order):
    steps = []
    for name in order:
        n = lax.axis_size(name)
        for j in range(_bits(n)):
            steps.append((name, j, n))
    plan = _split_plan(x.shape, len(steps))
    bits = []
    cur = x
    for (name, j, n), axis in zip(steps, plan):
        bit = (lax.axis_index(name) >> j) & 1
        half = cur.shape[axis] // 2
        keep = lax.dynamic_slice_in_dim(cur, bit * half, half, axis)
        send = lax.dynamic_slice_in_dim(cur, (1 - bit) * half, half, axis)
        cur = keep + lax.ppermute(send, name, _pair_perm(n, j))
        bits.append(bit)
    for (name, j, n), axis, bit in reversed(list(zip(steps, plan, bits))):
        other = lax.ppermute(cur, name, _pair_perm(n, j))
        low = jnp.where(bit == 0, cur, other)
        high = jnp.where(bit == 0, other, cur)
        cur = jnp.concatenate([low, high], axis=axis)
    return cur


def local(
    gradient,
    feedback,
    momentum,
    tile_matrix,
    matrix_group,
    group_scale,
    start_basis,
    inverse_gram_factors,
    vector_grad,
    vector_momentum,
):
    replicas = lax.axis_size("rep")
    matrix_count = start_basis.shape[0]
    order = ("own", "rep")
    selector = (tile_matrix[:, None] == jnp.arange(matrix_count, dtype=jnp.int32)[None, :]).astype(
        jnp.float32
    )
    combined = gradient[0].astype(jnp.float32) + feedback[0]
    q_tiles = jnp.take(start_basis, tile_matrix, axis=0)
    first_local = jnp.einsum("tkd,tds->tks", combined, q_tiles, precision=TOP_PRECISION)
    vector_summed = swap_sum(vector_grad[0], "rep")
    first_left = swap_sum(first_local, "rep") / replicas
    mix_first = jnp.take(inverse_gram_factors[0], tile_matrix, axis=0)
    first_ortho = jnp.einsum("tks,tsa->tka", first_left, mix_first, precision=TOP_PRECISION)
    first_parts = jnp.einsum("tkd,tks->tsd", combined, first_ortho, precision=TOP_PRECISION)
    first_table = jnp.einsum("tm,tsd->msd", selector, first_parts, precision=TOP_PRECISION)
    first_table = table_sum(first_table, order) / replicas
    first_rows = jnp.take(first_table, tile_matrix, axis=0)
    mix_right = jnp.take(inverse_gram_factors[1], tile_matrix, axis=0)
    right_rows = jnp.einsum("tjw,tjd->twd", mix_right, first_rows, precision=TOP_PRECISION)
    second_local = jnp.einsum("tkd,tsd->tks", combined, right_rows, precision=TOP_PRECISION)
    second_left = swap_sum(second_local, "rep") / replicas
    mix_second = jnp.take(inverse_gram_factors[2], tile_matrix, axis=0)
    second_ortho = jnp.einsum("tks,tsa->tka", second_left, mix_second, precision=TOP_PRECISION)
    second_parts = jnp.einsum("tkd,tks->tsd", combined, second_ortho, precision=TOP_PRECISION)
    second_table = jnp.einsum("tm,tsd->msd", selector, second_parts, precision=TOP_PRECISION)
    second_table = table_sum(second_table, order) / replicas
    back_rows = jnp.take(second_table, tile_matrix, axis=0)
    approximation = jnp.einsum("tks,tsd->tkd", second_ortho, back_rows, precision=TOP_PRECISION)
    new_feedback = (combined - approximation)[None]
    group_select = (
        matrix_group[:, None] == jnp.arange(group_scale.shape[0], dtype=jnp.int32)[None, :]
    ).astype(jnp.float32)
    matrix_scale = jnp.dot(group_select, group_scale, precision=TOP_PRECISION)
    tile_scale = jnp.dot(selector, matrix_scale, precision=TOP_PRECISION)
    new_momentum = 0.9 * momentum + tile_scale[:, None, None] * approximation
    new_vector_momentum = 0.9 * vector_momentum + vector_summed / replicas
    return (new_feedback, new_momentum, new_vector_momentum)


def solution(mesh):
    placed = (
        P("rep", "own", None, None),
        P("rep", "own", None, None),
        P("own", None, None),
        P("own"),
        P(),
        P(),
        P(),
        P(),
        P("rep", None, None),
        P(),
    )
    return jax.shard_map(
        local,
        mesh=mesh,
        in_specs=placed,
        out_specs=(P("rep", "own", None, None), P("own", None, None), P()),
        check_vma=False,
    )
```

time: 329 us -> 146 us (0.44)
  waiting for transfers between devices: 268 us -> 69.8 us
  starting transfers between devices: 0.08 us -> 37.4 us
  blocking collectives: 19.7 us -> 0 us
  between operations: 14.3 us -> 1.1 us
  local copies, waits for them, and re-layouts: 1.22 us -> 13.6 us
  matrix products: 23.2 us -> 11.8 us
  other arithmetic: 2.41 us -> 12.2 us
    psum x2 -> x0, waiting for transfers between devices: 267 us -> none  [table_total(): grand_total = lax.psum(table_part, ('rep', 'own')) / replicas]
    ppermute x0 -> x23, waiting for transfers between devices: none -> 69.8 us  [the longest x10 36.7 us: table_sum(): cur = keep + lax.ppermute(send, name, _pair_perm(n, j))]
    ppermute x0 -> x23, starting transfers between devices: none -> 37.4 us  [the longest x10 15.8 us: table_sum(): cur = keep + lax.ppermute(send, name, _pair_perm(n, j))]
    psum x2 -> x0, blocking collectives: 19.7 us -> none  [the longest x1 10.4 us: local(): first_summed = lax.psum(first_local, 'rep')]
    dot_general x12 -> x7, matrix products: 21 us -> 9.63 us  [the longest x1 3.76 us: local(): jnp.einsum('tks,tsd->tkd', second_ortho, back_rows, precision=TOP_PRECISION)]
    gather x0 -> x6, local copies, waits for them, and re-layouts: none -> 7.75 us  [the longest x1 1.85 us: local(): first_rows = jnp.take(first_table, tile_matrix, axis=0)]
    add x0 -> x10, other arithmetic: none -> 4.24 us  [table_sum(): cur = keep + lax.ppermute(send, name, _pair_perm(n, j))]
  transfers between devices with their start and end apart: 2 -> 23, of which waited for: 2 -> 22; matrix products, arithmetic and copies ran while one was open for 0% -> 4% of each run, Pallas kernels for 0% -> 0%
where the time goes in v1:
time: 146 us
  waiting for transfers between devices  69.8 us (48%)
  starting transfers between devices  37.4 us (26%)
  local copies, waits for them, and re-layouts  13.6 us (9%)
  other arithmetic  12.2 us (8%)
  matrix products  11.8 us (8%)
    ppermute x10, waiting for transfers between devices, table_sum(): cur = keep + lax.ppermute(send, name, _pair_perm(n, j))  36.7 us
    ppermute x10, waiting for transfers between devices, table_sum(): other = lax.ppermute(cur, name, _pair_perm(n, j))  28.5 us
    ppermute x10, starting transfers between devices, table_sum(): cur = keep + lax.ppermute(send, name, _pair_perm(n, j))  15.8 us
    ppermute x10, starting transfers between devices, table_sum(): other = lax.ppermute(cur, name, _pair_perm(n, j))  15.8 us
    ppermute x3, starting transfers between devices, swap_sum(): x = x + lax.ppermute(x, axis, _pair_perm(n, j))  5.88 us
    ppermute x3, waiting for transfers between devices, swap_sum(): x = x + lax.ppermute(x, axis, _pair_perm(n, j))  4.55 us
    add x10, other arithmetic, table_sum(): cur = keep + lax.ppermute(send, name, _pair_perm(n, j))  4.24 us
    dot_general x1, matrix products, local(): jnp.einsum('tks,tsd->tkd', second_ortho, back_rows, precision=TOP_PRECISION)  3.76 us
  transfers between devices with their start and end apart: 23, of which 22 were waited for; matrix products, arithmetic and copies ran while one was open for 4% of the time, Pallas kernels for 0%

profile of v1, /device:TPU:0, one launch (start us, length us, event | category | flops | bytes accessed | tf_op | source)
XLA Modules:
  0.0 146.0 jit_solution(14868117258116487349)
XLA Ops:
  4.6 3.0 %collective-permute-start = (f32[4,64,32]{1,2,0:T(8,128)S(1)}, f32[4,64,32]{1,2,0:T(8,128)S(1)}, u32[]{:S(2)}, u32[]{:S(2)}) collective-permute-start(f32[4,64,32]{1,2,0:T(8,128)S(1)} %fusion.6), channel_id=1, source_target_pairs={{0,16},{16,0},{1,17},{17,1},{2,18},{18,2},{3,19},{19,3},{4,20},{20... | collective-permute-start | bytes 98312 | tf_op jit(solution)/shard_map/ppermute | solution.py:20
  13.9 2.1 %collective-permute-done.1 = f32[9,32,512]{2,1,0:T(8,128)} collective-permute-done((f32[9,32,512]{2,1,0:T(8,128)S(1)}, f32[9,32,512]{2,1,0:T(8,128)}, u32[]{:S(2)}, u32[]{:S(2)}) %collective-permute-start.1) | collective-permute-done | bytes 589856 | tf_op jit(solution)/shard_map/ppermute | solution.py:56
  16.0 1.8 %copy_add_fusion.1 = f32[9,32,512]{2,1,0:T(8,128)S(1)} fusion(f32[9,32,512]{2,1,0:T(8,128)} %collective-permute-done.1, f32[9,32,512]{2,0,1:T(8,128)} %get-tuple-element.7), kind=kLoop, calls=%fused_computation.25 | loop fusion | flops 147456 | bytes 1769472 | tf_op jit(solution)/shard_map/add | solution.py:56
  18.5 2.0 %collective-permute-start.2 = (f32[9,32,256]{2,1,0:T(8,128)}, f32[9,32,256]{2,1,0:T(8,128)}, u32[]{:S(2)}, u32[]{:S(2)}) collective-permute-start(f32[9,32,256]{2,1,0:T(8,128)} %constant_dynamic-slice_fusion.9), channel_id=1, source_target_pairs={{0,2},{1,3},{2,0},{3,1},{4,6},{5,7},{6,4},{7,5},{8,10},{9,11},{10,... | collective-permute-start | bytes 884744 | tf_op jit(solution)/shard_map/ppermute | solution.py:56
  20.6 7.6 %collective-permute-done.2 = f32[9,32,256]{2,1,0:T(8,128)} collective-permute-done((f32[9,32,256]{2,1,0:T(8,128)}, f32[9,32,256]{2,1,0:T(8,128)}, u32[]{:S(2)}, u32[]{:S(2)}) %collective-permute-start.2) | collective-permute-done | bytes 294944 | tf_op jit(solution)/shard_map/ppermute | solution.py:56
  30.0 1.9 %collective-permute-start.3 = (f32[9,32,128]{2,1,0:T(8,128)S(1)}, f32[9,32,128]{2,1,0:T(8,128)S(1)}, u32[]{:S(2)}, u32[]{:S(2)}) collective-permute-start(f32[9,32,128]{2,1,0:T(8,128)S(1)} %constant_dynamic-slice_fusion.8), channel_id=1, source_target_pairs={{0,4},{1,5},{2,6},{3,7},{4,0},{5,1},{6,2},{7,3},{8,12},{9,13},{10,... | collective-permute-start | bytes 442376 | tf_op jit(solution)/shard_map/ppermute | solution.py:56
  31.8 3.5 %collective-permute-done.3 = f32[9,32,128]{2,1,0:T(8,128)S(1)} collective-permute-done((f32[9,32,128]{2,1,0:T(8,128)S(1)}, f32[9,32,128]{2,1,0:T(8,128)S(1)}, u32[]{:S(2)}, u32[]{:S(2)}) %collective-permute-start.3) | collective-permute-done | bytes 147488 | tf_op jit(solution)/shard_map/ppermute | solution.py:56
  36.3 2.7 %collective-permute-start.4 = (f32[9,16,128]{2,1,0:T(8,128)S(1)}, f32[9,16,128]{2,1,0:T(8,128)S(1)}, u32[]{:S(2)}, u32[]{:S(2)}) collective-permute-start(f32[9,16,128]{2,1,0:T(8,128)S(1)} %constant_dynamic-slice_fusion.7), channel_id=1, source_target_pairs={{0,8},{1,9},{2,10},{3,11},{4,12},{5,13},{6,14},{7,15},{8,0},{9,1},... | collective-permute-start | bytes 221192 | tf_op jit(solution)/shard_map/ppermute | solution.py:56
  39.0 2.6 %collective-permute-done.4 = f32[9,16,128]{2,1,0:T(8,128)S(1)} collective-permute-done((f32[9,16,128]{2,1,0:T(8,128)S(1)}, f32[9,16,128]{2,1,0:T(8,128)S(1)}, u32[]{:S(2)}, u32[]{:S(2)}) %collective-permute-start.4) | collective-permute-done | bytes 73760 | tf_op jit(solution)/shard_map/ppermute | solution.py:56
  43.3 2.6 %collective-permute-done.5 = f32[9,8,128]{2,1,0:T(8,128)S(1)} collective-permute-done((f32[9,8,128]{2,1,0:T(8,128)S(1)}, f32[9,8,128]{2,1,0:T(8,128)S(1)}, u32[]{:S(2)}, u32[]{:S(2)}) %collective-permute-start.5) | collective-permute-done | bytes 36896 | tf_op jit(solution)/shard_map/ppermute | solution.py:56
  47.2 2.6 %collective-permute-done.6 = f32[9,8,128]{2,1,0:T(8,128)S(1)} collective-permute-done((f32[9,8,128]{2,1,0:T(8,128)S(1)}, f32[9,8,128]{2,1,0:T(8,128)S(1)}, u32[]{:S(2)}, u32[]{:S(2)}) %collective-permute-start.6) | collective-permute-done | bytes 36896 | tf_op jit(solution)/shard_map/ppermute | solution.py:59
  49.9 2.6 %collective-permute-start.7 = (f32[9,16,128]{2,1,0:T(8,128)S(1)}, f32[9,16,128]{2,1,0:T(8,128)S(1)}, u32[]{:S(2)}, u32[]{:S(2)}) collective-permute-start(f32[9,16,128]{2,1,0:T(8,128)S(1)} %pad_maximum_fusion.6), channel_id=1, source_target_pairs={{0,8},{1,9},{2,10},{3,11},{4,12},{5,13},{6,14},{7,15},{8,0},{9,1},... | collective-permute-start | bytes 221192 | tf_op jit(solution)/shard_map/ppermute | solution.py:59
  52.4 2.8 %collective-permute-done.7 = f32[9,16,128]{2,1,0:T(8,128)S(1)} collective-permute-done((f32[9,16,128]{2,1,0:T(8,128)S(1)}, f32[9,16,128]{2,1,0:T(8,128)S(1)}, u32[]{:S(2)}, u32[]{:S(2)}) %collective-permute-start.7) | collective-permute-done | bytes 73760 | tf_op jit(solution)/shard_map/ppermute | solution.py:59
  55.3 1.7 %collective-permute-start.8 = (f32[9,32,128]{2,1,0:T(8,128)S(1)}, f32[9,32,128]{2,1,0:T(8,128)S(1)}, u32[]{:S(2)}, u32[]{:S(2)}) collective-permute-start(f32[9,32,128]{2,1,0:T(8,128)S(1)} %pad_maximum_fusion.4), channel_id=1, source_target_pairs={{0,4},{1,5},{2,6},{3,7},{4,0},{5,1},{6,2},{7,3},{8,12},{9,13},{10,... | collective-permute-start | bytes 442376 | tf_op jit(solution)/shard_map/ppermute | solution.py:59
  57.1 3.5 %collective-permute-done.8 = f32[9,32,128]{2,1,0:T(8,128)S(1)} collective-permute-done((f32[9,32,128]{2,1,0:T(8,128)S(1)}, f32[9,32,128]{2,1,0:T(8,128)S(1)}, u32[]{:S(2)}, u32[]{:S(2)}) %collective-permute-start.8) | collective-permute-done | bytes 147488 | tf_op jit(solution)/shard_map/ppermute | solution.py:59
  62.6 5.5 %collective-permute-done.9 = f32[9,32,256]{2,1,0:T(8,128)} collective-permute-done((f32[9,32,256]{2,1,0:T(8,128)S(1)}, f32[9,32,256]{2,1,0:T(8,128)}, u32[]{:S(2)}, u32[]{:S(2)}) %collective-permute-start.9) | collective-permute-done | bytes 294944 | tf_op jit(solution)/shard_map/ppermute | solution.py:59
  74.8 1.8 %gather_fusion.3 = f32[4,32,1024]{2,1,0:T(8,128)S(1)} fusion(f32[9,32,1024]{2,1,0:T(8,128)} %maximum_multiply_fusion, s32[1024]{0:T(1024)S(1)} %pad_clamp_fusion), kind=kCustom, calls=%fused_computation.1.clone | custom fusion | bytes 1048592 | tf_op jit(solution)/shard_map/jit(_take)/gather | solution.py:94
  85.9 2.0 %collective-permute-done.12 = f32[9,32,512]{2,1,0:T(8,128)S(1)} collective-permute-done((f32[9,32,512]{2,1,0:T(8,128)S(1)}, f32[9,32,512]{2,1,0:T(8,128)S(1)}, u32[]{:S(2)}, u32[]{:S(2)}) %collective-permute-start.12) | collective-permute-done | bytes 589856 | tf_op jit(solution)/shard_map/ppermute | solution.py:56
  89.7 7.8 %collective-permute-done.13 = f32[9,32,256]{2,1,0:T(8,128)S(1)} collective-permute-done((f32[9,32,256]{2,1,0:T(8,128)S(1)}, f32[9,32,256]{2,1,0:T(8,128)S(1)}, u32[]{:S(2)}, u32[]{:S(2)}) %collective-permute-start.13) | collective-permute-done | bytes 294944 | tf_op jit(solution)/shard_map/ppermute | solution.py:56
  99.3 3.5 %collective-permute-done.14 = f32[9,32,128]{2,1,0:T(8,128)S(1)} collective-permute-done((f32[9,32,128]{2,1,0:T(8,128)S(1)}, f32[9,32,128]{2,1,0:T(8,128)S(1)}, u32[]{:S(2)}, u32[]{:S(2)}) %collective-permute-start.14) | collective-permute-done | bytes 147488 | tf_op jit(solution)/shard_map/ppermute | solution.py:56
  102.8 2.9 %collective-permute-start.15 = (f32[9,16,128]{2,1,0:T(8,128)S(1)}, f32[9,16,128]{2,1,0:T(8,128)S(1)}, u32[]{:S(2)}, u32[]{:S(2)}) collective-permute-start(f32[9,16,128]{2,1,0:T(8,128)S(1)} %constant_dynamic-slice_fusion.1), channel_id=1, source_target_pairs={{0,8},{1,9},{2,10},{3,11},{4,12},{5,13},{6,14},{7,15},{8,0},{9,1},... | collective-permute-start | bytes 221192 | tf_op jit(solution)/shard_map/ppermute | solution.py:56
  105.7 2.4 %collective-permute-done.15 = f32[9,16,128]{2,1,0:T(8,128)S(1)} collective-permute-done((f32[9,16,128]{2,1,0:T(8,128)S(1)}, f32[9,16,128]{2,1,0:T(8,128)S(1)}, u32[]{:S(2)}, u32[]{:S(2)}) %collective-permute-start.15) | collective-permute-done | bytes 73760 | tf_op jit(solution)/shard_map/ppermute | solution.py:56
  109.6 2.6 %collective-permute-done.16 = f32[9,8,128]{2,1,0:T(8,128)S(1)} collective-permute-done((f32[9,8,128]{2,1,0:T(8,128)S(1)}, f32[9,8,128]{2,1,0:T(8,128)S(1)}, u32[]{:S(2)}, u32[]{:S(2)}) %collective-permute-start.16) | collective-permute-done | bytes 36896 | tf_op jit(solution)/shard_map/ppermute | solution.py:56
  113.7 2.5 %collective-permute-done.17 = f32[9,8,128]{2,1,0:T(8,128)S(1)} collective-permute-done((f32[9,8,128]{2,1,0:T(8,128)S(1)}, f32[9,8,128]{2,1,0:T(8,128)S(1)}, u32[]{:S(2)}, u32[]{:S(2)}) %collective-permute-start.17) | collective-permute-done | bytes 36896 | tf_op jit(solution)/shard_map/ppermute | solution.py:59
  116.2 2.9 %collective-permute-start.18 = (f32[9,16,128]{2,1,0:T(8,128)S(1)}, f32[9,16,128]{2,1,0:T(8,128)S(1)}, u32[]{:S(2)}, u32[]{:S(2)}) collective-permute-start(f32[9,16,128]{2,1,0:T(8,128)S(1)} %pad_maximum_fusion.7), channel_id=1, source_target_pairs={{0,8},{1,9},{2,10},{3,11},{4,12},{5,13},{6,14},{7,15},{8,0},{9,1},... | collective-permute-start | bytes 221192 | tf_op jit(solution)/shard_map/ppermute | solution.py:59
  119.1 2.4 %collective-permute-done.18 = f32[9,16,128]{2,1,0:T(8,128)S(1)} collective-permute-done((f32[9,16,128]{2,1,0:T(8,128)S(1)}, f32[9,16,128]{2,1,0:T(8,128)S(1)}, u32[]{:S(2)}, u32[]{:S(2)}) %collective-permute-start.18) | collective-permute-done | bytes 73760 | tf_op jit(solution)/shard_map/ppermute | solution.py:59
  121.5 2.7 %collective-permute-start.19 = (f32[9,32,128]{2,1,0:T(8,128)S(1)}, f32[9,32,128]{2,1,0:T(8,128)S(1)}, u32[]{:S(2)}, u32[]{:S(2)}) collective-permute-start(f32[9,32,128]{2,1,0:T(8,128)S(1)} %pad_maximum_fusion.5), channel_id=1, source_target_pairs={{0,4},{1,5},{2,6},{3,7},{4,0},{5,1},{6,2},{7,3},{8,12},{9,13},{10,... | collective-permute-start | bytes 442376 | tf_op jit(solution)/shard_map/ppermute | solution.py:59
  124.2 3.1 %collective-permute-done.19 = f32[9,32,128]{2,1,0:T(8,128)S(1)} collective-permute-done((f32[9,32,128]{2,1,0:T(8,128)S(1)}, f32[9,32,128]{2,1,0:T(8,128)S(1)}, u32[]{:S(2)}, u32[]{:S(2)}) %collective-permute-start.19) | collective-permute-done | bytes 147488 | tf_op jit(solution)/shard_map/ppermute | solution.py:59
  129.0 5.2 %collective-permute-done.20 = f32[9,32,256]{2,1,0:T(8,128)S(1)} collective-permute-done((f32[9,32,256]{2,1,0:T(8,128)S(1)}, f32[9,32,256]{2,1,0:T(8,128)S(1)}, u32[]{:S(2)}, u32[]{:S(2)}) %collective-permute-start.20) | collective-permute-done | bytes 294944 | tf_op jit(solution)/shard_map/ppermute | solution.py:59
  136.4 2.1 %collective-permute-done.22 = f32[5,1024]{1,0:T(8,128)S(1)} collective-permute-done((f32[5,1024]{1,0:T(8,128)S(1)}, f32[5,1024]{1,0:T(8,128)S(1)}, u32[]{:S(2)}, u32[]{:S(2)}) %collective-permute-start.22) | collective-permute-done | bytes 20512 | tf_op jit(solution)/shard_map/ppermute | solution.py:20
  140.4 1.8 %gather_fusion.5 = f32[4,32,1024]{2,1,0:T(8,128)S(1)} fusion(f32[9,32,1024]{2,1,0:T(8,128)} %maximum_multiply_fusion.1, s32[1024]{0:T(1024)S(1)} %pad_clamp_fusion), kind=kCustom, calls=%fused_computation.4.clone | custom fusion | bytes 1048592 | tf_op jit(solution)/shard_map/jit(_take)/gather | solution.py:104
  142.3 3.8 %multiply_add_fusion = (f32[4,64,1024]{2,1,0:T(8,128)}, f32[1,4,64,1024]{3,2,1,0:T(8,128)}) fusion(f32[4,64,1024]{2,1,0:T(8,128)} %param.16, f32[4]{0:T(128)S(1)} %convolution_bitcast_fusion, f32[1,4,64,1024]{3,2,1,0:T(8,128)S(1)} %copy-done.1, bf16[1,4,64,1024]{3,2,1,0:T(8,128)(2,1)S(1)} %copy-done.2, f32[4,64,32]{1,2,0:T(8,128)S(1)} %fusion.24, ...), kind=kOutput, calls=%fused_computation.20 | convolution fusion | flops 102367232 | bytes 5275668 | tf_op jit(solution)/shard_map/tks,tsd->tkd/dot_general | solution.py:105
  (102 shorter events, 46.8 us)
Async XLA Ops:
  0.6 1.4 copy-start
  2.1 1.2 copy-start.1
  2.1 1.3 copy-start.2
  3.4 4.2 %copy-start.5 = (f32[3,9,32,32]{3,2,1,0:T(8,128)S(1)}, f32[3,9,32,32]{3,2,1,0:T(8,128)}, u32[]{:S(2)}) copy-start(f32[3,9,32,32]{3,2,1,0:T(8,128)} %param.21) | copy-start | bytes 331780
  4.6 5.3 %collective-permute-start = (f32[4,64,32]{1,2,0:T(8,128)S(1)}, f32[4,64,32]{1,2,0:T(8,128)S(1)}, u32[]{:S(2)}, u32[]{:S(2)}) collective-permute-start(f32[4,64,32]{1,2,0:T(8,128)S(1)} %fusion.6), channel_id=1, source_target_pairs={{0,16},{16,0},{1,17},{17,1},{2,18},{18,2},{3,19},{19,3},{4,20},{20... | collective-permute-start | bytes 98312 | tf_op jit(solution)/shard_map/ppermute | solution.py:20
  8.9 2.0 %copy-start.8 = (s32[4]{0:T(128)S(1)}, s32[4]{0:T(128)}, u32[]{:S(2)}) copy-start(s32[4]{0:T(128)} %param.17) | copy-start | bytes 52
  13.8 2.2 %collective-permute-start.1 = (f32[9,32,512]{2,1,0:T(8,128)S(1)}, f32[9,32,512]{2,1,0:T(8,128)}, u32[]{:S(2)}, u32[]{:S(2)}) collective-permute-start(f32[9,32,512]{2,1,0:T(8,128)S(1)} %copy.38), channel_id=1, source_target_pairs={{0,1},{1,0},{2,3},{3,2},{4,5},{5,4},{6,7},{7,6},{8,9},{9,8},{10,11... | collective-permute-start | bytes 1769480 | tf_op jit(solution)/shard_map/ppermute | solution.py:56
  18.5 9.7 %collective-permute-start.2 = (f32[9,32,256]{2,1,0:T(8,128)}, f32[9,32,256]{2,1,0:T(8,128)}, u32[]{:S(2)}, u32[]{:S(2)}) collective-permute-start(f32[9,32,256]{2,1,0:T(8,128)} %constant_dynamic-slice_fusion.9), channel_id=1, source_target_pairs={{0,2},{1,3},{2,0},{3,1},{4,6},{5,7},{6,4},{7,5},{8,10},{9,11},{10,... | collective-permute-start | bytes 884744 | tf_op jit(solution)/shard_map/ppermute | solution.py:56
  30.0 5.4 %collective-permute-start.3 = (f32[9,32,128]{2,1,0:T(8,128)S(1)}, f32[9,32,128]{2,1,0:T(8,128)S(1)}, u32[]{:S(2)}, u32[]{:S(2)}) collective-permute-start(f32[9,32,128]{2,1,0:T(8,128)S(1)} %constant_dynamic-slice_fusion.8), channel_id=1, source_target_pairs={{0,4},{1,5},{2,6},{3,7},{4,0},{5,1},{6,2},{7,3},{8,12},{9,13},{10,... | collective-permute-start | bytes 442376 | tf_op jit(solution)/shard_map/ppermute | solution.py:56
  36.3 5.3 %collective-permute-start.4 = (f32[9,16,128]{2,1,0:T(8,128)S(1)}, f32[9,16,128]{2,1,0:T(8,128)S(1)}, u32[]{:S(2)}, u32[]{:S(2)}) collective-permute-start(f32[9,16,128]{2,1,0:T(8,128)S(1)} %constant_dynamic-slice_fusion.7), channel_id=1, source_target_pairs={{0,8},{1,9},{2,10},{3,11},{4,12},{5,13},{6,14},{7,15},{8,0},{9,1},... | collective-permute-start | bytes 221192 | tf_op jit(solution)/shard_map/ppermute | solution.py:56
  41.6 4.2 %collective-permute-start.5 = (f32[9,8,128]{2,1,0:T(8,128)S(1)}, f32[9,8,128]{2,1,0:T(8,128)S(1)}, u32[]{:S(2)}, u32[]{:S(2)}) collective-permute-start(f32[9,8,128]{2,1,0:T(8,128)S(1)} %constant_dynamic-slice_fusion.6), channel_id=1, source_target_pairs={{0,16},{16,0},{1,17},{17,1},{2,18},{18,2},{3,19},{19,3},{4,20},{20... | collective-permute-start | bytes 110600 | tf_op jit(solution)/shard_map/ppermute | solution.py:56
  45.9 4.0 %collective-permute-start.6 = (f32[9,8,128]{2,1,0:T(8,128)S(1)}, f32[9,8,128]{2,1,0:T(8,128)S(1)}, u32[]{:S(2)}, u32[]{:S(2)}) collective-permute-start(f32[9,8,128]{2,1,0:T(8,128)S(1)} %dynamic-slice_add_fusion.7), channel_id=1, source_target_pairs={{0,16},{16,0},{1,17},{17,1},{2,18},{18,2},{3,19},{19,3},{4,20},{20... | collective-permute-start | bytes 110600 | tf_op jit(solution)/shard_map/ppermute | solution.py:59
  49.9 5.4 %collective-permute-start.7 = (f32[9,16,128]{2,1,0:T(8,128)S(1)}, f32[9,16,128]{2,1,0:T(8,128)S(1)}, u32[]{:S(2)}, u32[]{:S(2)}) collective-permute-start(f32[9,16,128]{2,1,0:T(8,128)S(1)} %pad_maximum_fusion.6), channel_id=1, source_target_pairs={{0,8},{1,9},{2,10},{3,11},{4,12},{5,13},{6,14},{7,15},{8,0},{9,1},... | collective-permute-start | bytes 221192 | tf_op jit(solution)/shard_map/ppermute | solution.py:59
  55.3 5.2 %collective-permute-start.8 = (f32[9,32,128]{2,1,0:T(8,128)S(1)}, f32[9,32,128]{2,1,0:T(8,128)S(1)}, u32[]{:S(2)}, u32[]{:S(2)}) collective-permute-start(f32[9,32,128]{2,1,0:T(8,128)S(1)} %pad_maximum_fusion.4), channel_id=1, source_target_pairs={{0,4},{1,5},{2,6},{3,7},{4,0},{5,1},{6,2},{7,3},{8,12},{9,13},{10,... | collective-permute-start | bytes 442376 | tf_op jit(solution)/shard_map/ppermute | solution.py:59
  61.2 6.9 %collective-permute-start.9 = (f32[9,32,256]{2,1,0:T(8,128)S(1)}, f32[9,32,256]{2,1,0:T(8,128)}, u32[]{:S(2)}, u32[]{:S(2)}) collective-permute-start(f32[9,32,256]{2,1,0:T(8,128)S(1)} %pad_maximum_fusion.2), channel_id=1, source_target_pairs={{0,2},{1,3},{2,0},{3,1},{4,6},{5,7},{6,4},{7,5},{8,10},{9,11},{10,... | collective-permute-start | bytes 884744 | tf_op jit(solution)/shard_map/ppermute | solution.py:59
  70.1 2.3 %collective-permute-start.10 = (f32[9,32,512]{2,1,0:T(8,128)}, f32[9,32,512]{2,1,0:T(8,128)}, u32[]{:S(2)}, u32[]{:S(2)}) collective-permute-start(f32[9,32,512]{2,1,0:T(8,128)} %pad_maximum_fusion), channel_id=1, source_target_pairs={{0,1},{1,0},{2,3},{3,2},{4,5},{5,4},{6,7},{7,6},{8,9},{9,8},{10,11... | collective-permute-start | bytes 1769480 | tf_op jit(solution)/shard_map/ppermute | solution.py:59
  78.5 4.3 %collective-permute-start.11 = (f32[4,64,32]{1,2,0:T(8,128)S(1)}, f32[4,64,32]{1,2,0:T(8,128)S(1)}, u32[]{:S(2)}, u32[]{:S(2)}) collective-permute-start(f32[4,64,32]{1,2,0:T(8,128)S(1)} %fusion.2), channel_id=1, source_target_pairs={{0,16},{16,0},{1,17},{17,1},{2,18},{18,2},{3,19},{19,3},{4,20},{20... | collective-permute-start | bytes 98312 | tf_op jit(solution)/shard_map/ppermute | solution.py:20
  85.8 2.1 %collective-permute-start.12 = (f32[9,32,512]{2,1,0:T(8,128)S(1)}, f32[9,32,512]{2,1,0:T(8,128)S(1)}, u32[]{:S(2)}, u32[]{:S(2)}) collective-permute-start(f32[9,32,512]{2,1,0:T(8,128)S(1)} %copy.43), channel_id=1, source_target_pairs={{0,1},{1,0},{2,3},{3,2},{4,5},{5,4},{6,7},{7,6},{8,9},{9,8},{10,11... | collective-permute-start | bytes 1769480 | tf_op jit(solution)/shard_map/ppermute | solution.py:56
  88.4 9.1 %collective-permute-start.13 = (f32[9,32,256]{2,1,0:T(8,128)S(1)}, f32[9,32,256]{2,1,0:T(8,128)S(1)}, u32[]{:S(2)}, u32[]{:S(2)}) collective-permute-start(f32[9,32,256]{2,1,0:T(8,128)S(1)} %constant_dynamic-slice_fusion.3), channel_id=1, source_target_pairs={{0,2},{1,3},{2,0},{3,1},{4,6},{5,7},{6,4},{7,5},{8,10},{9,11},{10,... | collective-permute-start | bytes 884744 | tf_op jit(solution)/shard_map/ppermute | solution.py:56
  97.6 5.2 %collective-permute-start.14 = (f32[9,32,128]{2,1,0:T(8,128)S(1)}, f32[9,32,128]{2,1,0:T(8,128)S(1)}, u32[]{:S(2)}, u32[]{:S(2)}) collective-permute-start(f32[9,32,128]{2,1,0:T(8,128)S(1)} %constant_dynamic-slice_fusion.2), channel_id=1, source_target_pairs={{0,4},{1,5},{2,6},{3,7},{4,0},{5,1},{6,2},{7,3},{8,12},{9,13},{10,... | collective-permute-start | bytes 442376 | tf_op jit(solution)/shard_map/ppermute | solution.py:56
  102.8 5.3 %collective-permute-start.15 = (f32[9,16,128]{2,1,0:T(8,128)S(1)}, f32[9,16,128]{2,1,0:T(8,128)S(1)}, u32[]{:S(2)}, u32[]{:S(2)}) collective-permute-start(f32[9,16,128]{2,1,0:T(8,128)S(1)} %constant_dynamic-slice_fusion.1), channel_id=1, source_target_pairs={{0,8},{1,9},{2,10},{3,11},{4,12},{5,13},{6,14},{7,15},{8,0},{9,1},... | collective-permute-start | bytes 221192 | tf_op jit(solution)/shard_map/ppermute | solution.py:56
  108.2 4.0 %collective-permute-start.16 = (f32[9,8,128]{2,1,0:T(8,128)S(1)}, f32[9,8,128]{2,1,0:T(8,128)S(1)}, u32[]{:S(2)}, u32[]{:S(2)}) collective-permute-start(f32[9,8,128]{2,1,0:T(8,128)S(1)} %constant_dynamic-slice_fusion), channel_id=1, source_target_pairs={{0,16},{16,0},{1,17},{17,1},{2,18},{18,2},{3,19},{19,3},{4,20},{20... | collective-permute-start | bytes 110600 | tf_op jit(solution)/shard_map/ppermute | solution.py:56
  112.2 4.0 %collective-permute-start.17 = (f32[9,8,128]{2,1,0:T(8,128)S(1)}, f32[9,8,128]{2,1,0:T(8,128)S(1)}, u32[]{:S(2)}, u32[]{:S(2)}) collective-permute-start(f32[9,8,128]{2,1,0:T(8,128)S(1)} %dynamic-slice_add_fusion.6), channel_id=1, source_target_pairs={{0,16},{16,0},{1,17},{17,1},{2,18},{18,2},{3,19},{19,3},{4,20},{20... | collective-permute-start | bytes 110600 | tf_op jit(solution)/shard_map/ppermute | solution.py:59
  116.2 5.3 %collective-permute-start.18 = (f32[9,16,128]{2,1,0:T(8,128)S(1)}, f32[9,16,128]{2,1,0:T(8,128)S(1)}, u32[]{:S(2)}, u32[]{:S(2)}) collective-permute-start(f32[9,16,128]{2,1,0:T(8,128)S(1)} %pad_maximum_fusion.7), channel_id=1, source_target_pairs={{0,8},{1,9},{2,10},{3,11},{4,12},{5,13},{6,14},{7,15},{8,0},{9,1},... | collective-permute-start | bytes 221192 | tf_op jit(solution)/shard_map/ppermute | solution.py:59
  121.5 5.8 %collective-permute-start.19 = (f32[9,32,128]{2,1,0:T(8,128)S(1)}, f32[9,32,128]{2,1,0:T(8,128)S(1)}, u32[]{:S(2)}, u32[]{:S(2)}) collective-permute-start(f32[9,32,128]{2,1,0:T(8,128)S(1)} %pad_maximum_fusion.5), channel_id=1, source_target_pairs={{0,4},{1,5},{2,6},{3,7},{4,0},{5,1},{6,2},{7,3},{8,12},{9,13},{10,... | collective-permute-start | bytes 442376 | tf_op jit(solution)/shard_map/ppermute | solution.py:59
  127.4 7.0 %copy-start.6 = (f32[1,5,1024]{2,0,1:T(1,128)S(1)}, f32[1,5,1024]{2,0,1:T(1,128)}, u32[]{:S(2)}) copy-start(f32[1,5,1024]{2,0,1:T(1,128)} %param.22) | copy-start | bytes 61444
  127.4 8.6 %copy-start.9 = (s32[9]{0:T(128)S(1)}, s32[9]{0:T(128)}, u32[]{:S(2)}) copy-start(s32[9]{0:T(128)} %param.18) | copy-start | bytes 112
  127.4 8.6 %copy-start.10 = (f32[4]{0:T(128)S(1)}, f32[4]{0:T(128)}, u32[]{:S(2)}) copy-start(f32[4]{0:T(128)} %param.19) | copy-start | bytes 52
  127.4 11.0 %copy-start.7 = (f32[5,1024]{1,0:T(8,128)S(1)}, f32[5,1024]{1,0:T(8,128)}, u32[]{:S(2)}) copy-start(f32[5,1024]{1,0:T(8,128)} %param.23) | copy-start | bytes 61444
  127.4 6.8 %collective-permute-start.20 = (f32[9,32,256]{2,1,0:T(8,128)S(1)}, f32[9,32,256]{2,1,0:T(8,128)S(1)}, u32[]{:S(2)}, u32[]{:S(2)}) collective-permute-start(f32[9,32,256]{2,1,0:T(8,128)S(1)} %pad_maximum_fusion.3), channel_id=1, source_target_pairs={{0,2},{1,3},{2,0},{3,1},{4,6},{5,7},{6,4},{7,5},{8,10},{9,11},{10,... | collective-permute-start | bytes 884744 | tf_op jit(solution)/shard_map/ppermute | solution.py:59
  134.4 4.7 %collective-permute-start.21 = (f32[9,32,512]{2,1,0:T(8,128)S(1)}, f32[9,32,512]{2,1,0:T(8,128)S(1)}, u32[]{:S(2)}, u32[]{:S(2)}) collective-permute-start(f32[9,32,512]{2,1,0:T(8,128)S(1)} %pad_maximum_fusion.1), channel_id=1, source_target_pairs={{0,1},{1,0},{2,3},{3,2},{4,5},{5,4},{6,7},{7,6},{8,9},{9,8},{10,11... | collective-permute-start | bytes 1769480 | tf_op jit(solution)/shard_map/ppermute | solution.py:59
  134.5 4.0 %collective-permute-start.22 = (f32[5,1024]{1,0:T(8,128)S(1)}, f32[5,1024]{1,0:T(8,128)S(1)}, u32[]{:S(2)}, u32[]{:S(2)}) collective-permute-start(f32[5,1024]{1,0:T(8,128)S(1)} %bitcast.42), channel_id=1, source_target_pairs={{0,16},{16,0},{1,17},{17,1},{2,18},{18,2},{3,19},{19,3},{4,20},{20... | collective-permute-start | bytes 61448 | tf_op jit(solution)/shard_map/ppermute | solution.py:20
  (2 other events, 1.4 us)

commit v2 on v1

--- a/solution.py
+++ b/solution.py
@@ -77,28 +77,31 @@
 ):
     replicas = lax.axis_size("rep")
     matrix_count = start_basis.shape[0]
-    order = ("own", "rep")
+    order = ("own",)
     selector = (tile_matrix[:, None] == jnp.arange(matrix_count, dtype=jnp.int32)[None, :]).astype(
         jnp.float32
     )
     combined = gradient[0].astype(jnp.float32) + feedback[0]
+    tiles, rows, width = combined.shape
+    vector_rows = vector_grad.shape[1]
+    carried = jnp.concatenate([combined.reshape(tiles * rows, width), vector_grad[0]], axis=0)
+    carried = swap_sum(carried, "rep")
+    summed = carried[: tiles * rows].reshape(tiles, rows, width)
+    vector_summed = carried[tiles * rows : tiles * rows + vector_rows]
     q_tiles = jnp.take(start_basis, tile_matrix, axis=0)
-    first_local = jnp.einsum("tkd,tds->tks", combined, q_tiles, precision=TOP_PRECISION)
-    vector_summed = swap_sum(vector_grad[0], "rep")
-    first_left = swap_sum(first_local, "rep") / replicas
+    first_left = jnp.einsum("tkd,tds->tks", summed, q_tiles, precision=TOP_PRECISION) / replicas
     mix_first = jnp.take(inverse_gram_factors[0], tile_matrix, axis=0)
     first_ortho = jnp.einsum("tks,tsa->tka", first_left, mix_first, precision=TOP_PRECISION)
-    first_parts = jnp.einsum("tkd,tks->tsd", combined, first_ortho, precision=TOP_PRECISION)
+    first_parts = jnp.einsum("tkd,tks->tsd", summed, first_ortho, precision=TOP_PRECISION)
     first_table = jnp.einsum("tm,tsd->msd", selector, first_parts, precision=TOP_PRECISION)
     first_table = table_sum(first_table, order) / replicas
     first_rows = jnp.take(first_table, tile_matrix, axis=0)
     mix_right = jnp.take(inverse_gram_factors[1], tile_matrix, axis=0)
     right_rows = jnp.einsum("tjw,tjd->twd", mix_right, first_rows, precision=TOP_PRECISION)
-    second_local = jnp.einsum("tkd,tsd->tks", combined, right_rows, precision=TOP_PRECISION)
-    second_left = swap_sum(second_local, "rep") / replicas
+    second_left = jnp.einsum("tkd,tsd->tks", summed, right_rows, precision=TOP_PRECISION) / replicas
     mix_second = jnp.take(inverse_gram_factors[2], tile_matrix, axis=0)
     second_ortho = jnp.einsum("tks,tsa->tka", second_left, mix_second, precision=TOP_PRECISION)
-    second_parts = jnp.einsum("tkd,tks->tsd", combined, second_ortho, precision=TOP_PRECISION)
+    second_parts = jnp.einsum("tkd,tks->tsd", summed, second_ortho, precision=TOP_PRECISION)
     second_table = jnp.einsum("tm,tsd->msd", selector, second_parts, precision=TOP_PRECISION)
     second_table = table_sum(second_table, order) / replicas
     back_rows = jnp.take(second_table, tile_matrix, axis=0)

time: 146 us -> 156 us (1.068)
  starting transfers between devices: 37.4 us -> 30.6 us
  local copies, waits for them, and re-layouts: 13.6 us -> 20 us
  other arithmetic: 12.2 us -> 18.3 us
  waiting for transfers between devices: 69.8 us -> 72.5 us
    ppermute x3 -> x1, waiting for transfers between devices: 4.55 us -> 19.3 us  [swap_sum(): x = x + lax.ppermute(x, axis, _pair_perm(n, j))]
    ppermute x10 -> x8, waiting for transfers between devices: 28.5 us -> 22.1 us  [table_sum(): other = lax.ppermute(cur, name, _pair_perm(n, j))]
    ppermute x10 -> x8, waiting for transfers between devices: 36.7 us -> 31.1 us  [table_sum(): cur = keep + lax.ppermute(send, name, _pair_perm(n, j))]
    unnamed x23 -> x39, local copies, waits for them, and re-layouts: 2.17 us -> 5.13 us
    ppermute x3 -> x1, starting transfers between devices: 5.88 us -> 2.97 us  [swap_sum(): x = x + lax.ppermute(x, axis, _pair_perm(n, j))]
    ppermute x10 -> x8, starting transfers between devices: 15.8 us -> 13.7 us  [table_sum(): other = lax.ppermute(cur, name, _pair_perm(n, j))]
    select_n x10 -> x8, other arithmetic: 2.59 us -> 4.57 us  [table_sum(): low = jnp.where(bit == 0, cur, other)]
    ppermute x10 -> x8, starting transfers between devices: 15.8 us -> 13.9 us  [table_sum(): cur = keep + lax.ppermute(send, name, _pair_perm(n, j))]
  transfers between devices with their start and end apart: 23 -> 17, of which waited for: 22 -> 16; matrix products, arithmetic and copies ran while one was open for 4% -> 6% of each run, Pallas kernels for 0% -> 0%
where the time goes in v2:
time: 156 us; the launch traced here: 155 us
  waiting for transfers between devices  72.5 us (46%)
  starting transfers between devices  30.6 us (20%)
  local copies, waits for them, and re-layouts  20 us (13%)
  other arithmetic  18.3 us (12%)
  matrix products  12.8 us (8%)
    ppermute x8, waiting for transfers between devices, table_sum(): cur = keep + lax.ppermute(send, name, _pair_perm(n, j))  31.1 us
    ppermute x8, waiting for transfers between devices, table_sum(): other = lax.ppermute(cur, name, _pair_perm(n, j))  22.1 us
    ppermute x1, waiting for transfers between devices, swap_sum(): x = x + lax.ppermute(x, axis, _pair_perm(n, j))  19.3 us
    ppermute x8, starting transfers between devices, table_sum(): cur = keep + lax.ppermute(send, name, _pair_perm(n, j))  13.9 us
    ppermute x8, starting transfers between devices, table_sum(): other = lax.ppermute(cur, name, _pair_perm(n, j))  13.7 us
    add x8, other arithmetic, table_sum(): cur = keep + lax.ppermute(send, name, _pair_perm(n, j))  5.26 us
    unnamed x39, local copies, waits for them, and re-layouts  5.13 us
    select_n x8, other arithmetic, table_sum(): low = jnp.where(bit == 0, cur, other)  4.57 us
  transfers between devices with their start and end apart: 17, of which 16 were waited for; matrix products, arithmetic and copies ran while one was open for 6% of the time, Pallas kernels for 0%

profile of v2, /device:TPU:0, one launch (start us, length us, event | category | flops | bytes accessed | tf_op | source)
XLA Modules:
  0.0 155.2 jit_solution(15488400725118518180)
XLA Ops:
  4.2 3.0 %collective-permute-start = (f32[261,1024]{1,0:T(8,128)}, f32[261,1024]{1,0:T(8,128)S(1)}, u32[]{:S(2)}, u32[]{:S(2)}) collective-permute-start(f32[261,1024]{1,0:T(8,128)} %pad_maximum_fusion), channel_id=1, source_target_pairs={{0,16},{16,0},{1,17},{17,1},{2,18},{18,2},{3,19},{19,3},{4,20},{20... | collective-permute-start | bytes 3207176 | tf_op jit(solution)/shard_map/ppermute | solution.py:20
  7.7 1.8 %slice_bitcast_fusion = (f32[9,32,32]{2,1,0:T(8,128)}, f32[9,32,32]{2,1,0:T(8,128)}, f32[9,32,32]{2,1,0:T(8,128)S(1)}) fusion(f32[3,9,32,32]{3,2,1,0:T(8,128)} %param.21), kind=kLoop, calls=%fused_computation.47 | loop fusion | bytes 221184 | tf_op jit(solution)/shard_map/squeeze | solution.py:102
  10.2 1.6 %gather_fusion = f32[4,1024,32]{1,2,0:T(8,128)} fusion(f32[9,1024,32]{1,2,0:T(8,128)S(1)} %copy-done, s32[1024]{0:T(1024)} %pad_clamp_fusion), kind=kCustom, calls=%fused_computation.5 | custom fusion | bytes 1048592 | tf_op jit(solution)/shard_map/jit(_take)/gather | solution.py:91
  11.9 19.3 %collective-permute-done = f32[261,1024]{1,0:T(8,128)S(1)} collective-permute-done((f32[261,1024]{1,0:T(8,128)}, f32[261,1024]{1,0:T(8,128)S(1)}, u32[]{:S(2)}, u32[]{:S(2)}) %collective-permute-start) | collective-permute-done | bytes 1069088 | tf_op jit(solution)/shard_map/ppermute | solution.py:20
  38.6 2.3 %collective-permute-done.1 = f32[9,32,512]{2,1,0:T(8,128)} collective-permute-done((f32[9,32,512]{2,1,0:T(8,128)}, f32[9,32,512]{2,1,0:T(8,128)}, u32[]{:S(2)}, u32[]{:S(2)}) %collective-permute-start.1) | collective-permute-done | bytes 589856 | tf_op jit(solution)/shard_map/ppermute | solution.py:56
  40.9 1.8 %copy_add_fusion.1 = f32[9,32,512]{2,1,0:T(8,128)S(1)} fusion(f32[9,32,512]{2,1,0:T(8,128)} %collective-permute-done.1, f32[9,32,512]{2,0,1:T(8,128)} %get-tuple-element.7), kind=kLoop, calls=%fused_computation.20 | loop fusion | flops 147456 | bytes 1769472 | tf_op jit(solution)/shard_map/add | solution.py:56
  44.3 1.8 %collective-permute-start.2 = (f32[9,32,256]{2,1,0:T(8,128)}, f32[9,32,256]{2,1,0:T(8,128)}, u32[]{:S(2)}, u32[]{:S(2)}) collective-permute-start(f32[9,32,256]{2,1,0:T(8,128)} %constant_dynamic-slice_fusion.7), channel_id=1, source_target_pairs={{0,2},{1,3},{2,0},{3,1},{4,6},{5,7},{6,4},{7,5},{8,10},{9,11},{10,... | collective-permute-start | bytes 884744 | tf_op jit(solution)/shard_map/ppermute | solution.py:56
  46.1 7.6 %collective-permute-done.2 = f32[9,32,256]{2,1,0:T(8,128)} collective-permute-done((f32[9,32,256]{2,1,0:T(8,128)}, f32[9,32,256]{2,1,0:T(8,128)}, u32[]{:S(2)}, u32[]{:S(2)}) %collective-permute-start.2) | collective-permute-done | bytes 294944 | tf_op jit(solution)/shard_map/ppermute | solution.py:56
  55.5 1.9 %collective-permute-start.3 = (f32[9,32,128]{2,1,0:T(8,128)S(1)}, f32[9,32,128]{2,1,0:T(8,128)}, u32[]{:S(2)}, u32[]{:S(2)}) collective-permute-start(f32[9,32,128]{2,1,0:T(8,128)S(1)} %constant_dynamic-slice_fusion.6), channel_id=1, source_target_pairs={{0,4},{1,5},{2,6},{3,7},{4,0},{5,1},{6,2},{7,3},{8,12},{9,13},{10,... | collective-permute-start | bytes 442376 | tf_op jit(solution)/shard_map/ppermute | solution.py:56
  57.4 3.4 %collective-permute-done.3 = f32[9,32,128]{2,1,0:T(8,128)} collective-permute-done((f32[9,32,128]{2,1,0:T(8,128)S(1)}, f32[9,32,128]{2,1,0:T(8,128)}, u32[]{:S(2)}, u32[]{:S(2)}) %collective-permute-start.3) | collective-permute-done | bytes 147488 | tf_op jit(solution)/shard_map/ppermute | solution.py:56
  61.9 2.9 %collective-permute-start.4 = (f32[9,16,128]{2,1,0:T(8,128)S(1)}, f32[9,16,128]{2,1,0:T(8,128)}, u32[]{:S(2)}, u32[]{:S(2)}) collective-permute-start(f32[9,16,128]{2,1,0:T(8,128)S(1)} %constant_dynamic-slice_fusion.5), channel_id=1, source_target_pairs={{0,8},{1,9},{2,10},{3,11},{4,12},{5,13},{6,14},{7,15},{8,0},{9,1},... | collective-permute-start | bytes 221192 | tf_op jit(solution)/shard_map/ppermute | solution.py:56
  64.7 2.5 %collective-permute-done.4 = f32[9,16,128]{2,1,0:T(8,128)} collective-permute-done((f32[9,16,128]{2,1,0:T(8,128)S(1)}, f32[9,16,128]{2,1,0:T(8,128)}, u32[]{:S(2)}, u32[]{:S(2)}) %collective-permute-start.4) | collective-permute-done | bytes 73760 | tf_op jit(solution)/shard_map/ppermute | solution.py:56
  68.2 3.0 %collective-permute-start.5 = (f32[9,16,128]{2,1,0:T(8,128)S(1)}, f32[9,16,128]{2,1,0:T(8,128)S(1)}, u32[]{:S(2)}, u32[]{:S(2)}) collective-permute-start(f32[9,16,128]{2,1,0:T(8,128)S(1)} %dynamic-slice_add_fusion.5), channel_id=1, source_target_pairs={{0,8},{1,9},{2,10},{3,11},{4,12},{5,13},{6,14},{7,15},{8,0},{9,1},... | collective-permute-start | bytes 221192 | tf_op jit(solution)/shard_map/ppermute | solution.py:59
  71.1 2.4 %collective-permute-done.5 = f32[9,16,128]{2,1,0:T(8,128)S(1)} collective-permute-done((f32[9,16,128]{2,1,0:T(8,128)S(1)}, f32[9,16,128]{2,1,0:T(8,128)S(1)}, u32[]{:S(2)}, u32[]{:S(2)}) %collective-permute-start.5) | collective-permute-done | bytes 73760 | tf_op jit(solution)/shard_map/ppermute | solution.py:59
  75.1 2.1 %collective-permute-start.6 = (f32[9,32,128]{2,1,0:T(8,128)}, f32[9,32,128]{2,1,0:T(8,128)}, u32[]{:S(2)}, u32[]{:S(2)}) collective-permute-start(f32[9,32,128]{2,1,0:T(8,128)} %pad_maximum_fusion.5), channel_id=1, source_target_pairs={{0,4},{1,5},{2,6},{3,7},{4,0},{5,1},{6,2},{7,3},{8,12},{9,13},{10,... | collective-permute-start | bytes 442376 | tf_op jit(solution)/shard_map/ppermute | solution.py:59
  77.2 3.4 %collective-permute-done.6 = f32[9,32,128]{2,1,0:T(8,128)} collective-permute-done((f32[9,32,128]{2,1,0:T(8,128)}, f32[9,32,128]{2,1,0:T(8,128)}, u32[]{:S(2)}, u32[]{:S(2)}) %collective-permute-start.6) | collective-permute-done | bytes 147488 | tf_op jit(solution)/shard_map/ppermute | solution.py:59
  84.7 5.4 %collective-permute-done.7 = f32[9,32,256]{2,1,0:T(8,128)} collective-permute-done((f32[9,32,256]{2,1,0:T(8,128)}, f32[9,32,256]{2,1,0:T(8,128)}, u32[]{:S(2)}, u32[]{:S(2)}) %collective-permute-start.7) | collective-permute-done | bytes 294944 | tf_op jit(solution)/shard_map/ppermute | solution.py:59
  98.3 2.6 %gather_fusion.3 = f32[4,32,1024]{2,1,0:T(8,128)} fusion(f32[9,32,1024]{2,1,0:T(8,128)} %maximum_multiply_fusion, s32[1024]{0:T(1024)S(1)} %copy-done.13), kind=kCustom, calls=%fused_computation.1.clone | custom fusion | bytes 1048592 | tf_op jit(solution)/shard_map/jit(_take)/gather | solution.py:98
  100.9 1.7 %fusion.7 = f32[4,32,1024]{2,1,0:T(8,128)S(1)} fusion(f32[4,32,1024]{2,1,0:T(8,128)} %gather_fusion.3, pred[4]{0:T(512)(128)(4,1)S(1)} %copy-done.12, f32[4,32,32]{2,1,0:T(8,128)S(1)} %gather_fusion.1), kind=kOutput, calls=%fused_computation.27 | convolution fusion | flops 50466816 | bytes 1064964 | tf_op jit(solution)/shard_map/tjw,tjd->twd/dot_general | solution.py:100
  107.3 1.6 %collective-permute-done.9 = f32[9,32,512]{2,1,0:T(8,128)S(1)} collective-permute-done((f32[9,32,512]{2,1,0:T(8,128)S(1)}, f32[9,32,512]{2,1,0:T(8,128)S(1)}, u32[]{:S(2)}, u32[]{:S(2)}) %collective-permute-start.9) | collective-permute-done | bytes 589856 | tf_op jit(solution)/shard_map/ppermute | solution.py:56
  109.3 1.7 %collective-permute-start.10 = (f32[9,32,256]{2,1,0:T(8,128)S(1)}, f32[9,32,256]{2,1,0:T(8,128)S(1)}, u32[]{:S(2)}, u32[]{:S(2)}) collective-permute-start(f32[9,32,256]{2,1,0:T(8,128)S(1)} %constant_dynamic-slice_fusion.2), channel_id=1, source_target_pairs={{0,2},{1,3},{2,0},{3,1},{4,6},{5,7},{6,4},{7,5},{8,10},{9,11},{10,... | collective-permute-start | bytes 884744 | tf_op jit(solution)/shard_map/ppermute | solution.py:56
  111.0 7.7 %collective-permute-done.10 = f32[9,32,256]{2,1,0:T(8,128)S(1)} collective-permute-done((f32[9,32,256]{2,1,0:T(8,128)S(1)}, f32[9,32,256]{2,1,0:T(8,128)S(1)}, u32[]{:S(2)}, u32[]{:S(2)}) %collective-permute-start.10) | collective-permute-done | bytes 294944 | tf_op jit(solution)/shard_map/ppermute | solution.py:56
  118.8 2.1 %collective-permute-start.11 = (f32[9,32,128]{2,1,0:T(8,128)S(1)}, f32[9,32,128]{2,1,0:T(8,128)S(1)}, u32[]{:S(2)}, u32[]{:S(2)}) collective-permute-start(f32[9,32,128]{2,1,0:T(8,128)S(1)} %constant_dynamic-slice_fusion.1), channel_id=1, source_target_pairs={{0,4},{1,5},{2,6},{3,7},{4,0},{5,1},{6,2},{7,3},{8,12},{9,13},{10,... | collective-permute-start | bytes 442376 | tf_op jit(solution)/shard_map/ppermute | solution.py:56
  120.9 3.5 %collective-permute-done.11 = f32[9,32,128]{2,1,0:T(8,128)S(1)} collective-permute-done((f32[9,32,128]{2,1,0:T(8,128)S(1)}, f32[9,32,128]{2,1,0:T(8,128)S(1)}, u32[]{:S(2)}, u32[]{:S(2)}) %collective-permute-start.11) | collective-permute-done | bytes 147488 | tf_op jit(solution)/shard_map/ppermute | solution.py:56
  124.4 3.1 %collective-permute-start.12 = (f32[9,16,128]{2,1,0:T(8,128)S(1)}, f32[9,16,128]{2,1,0:T(8,128)S(1)}, u32[]{:S(2)}, u32[]{:S(2)}) collective-permute-start(f32[9,16,128]{2,1,0:T(8,128)S(1)} %constant_dynamic-slice_fusion), channel_id=1, source_target_pairs={{0,8},{1,9},{2,10},{3,11},{4,12},{5,13},{6,14},{7,15},{8,0},{9,1},... | collective-permute-start | bytes 221192 | tf_op jit(solution)/shard_map/ppermute | solution.py:56
  127.5 2.3 %collective-permute-done.12 = f32[9,16,128]{2,1,0:T(8,128)S(1)} collective-permute-done((f32[9,16,128]{2,1,0:T(8,128)S(1)}, f32[9,16,128]{2,1,0:T(8,128)S(1)}, u32[]{:S(2)}, u32[]{:S(2)}) %collective-permute-start.12) | collective-permute-done | bytes 73760 | tf_op jit(solution)/shard_map/ppermute | solution.py:56
  129.8 3.0 %collective-permute-start.13 = (f32[9,16,128]{2,1,0:T(8,128)S(1)}, f32[9,16,128]{2,1,0:T(8,128)S(1)}, u32[]{:S(2)}, u32[]{:S(2)}) collective-permute-start(f32[9,16,128]{2,1,0:T(8,128)S(1)} %dynamic-slice_add_fusion.4), channel_id=1, source_target_pairs={{0,8},{1,9},{2,10},{3,11},{4,12},{5,13},{6,14},{7,15},{8,0},{9,1},... | collective-permute-start | bytes 221192 | tf_op jit(solution)/shard_map/ppermute | solution.py:59
  132.9 2.3 %collective-permute-done.13 = f32[9,16,128]{2,1,0:T(8,128)S(1)} collective-permute-done((f32[9,16,128]{2,1,0:T(8,128)S(1)}, f32[9,16,128]{2,1,0:T(8,128)S(1)}, u32[]{:S(2)}, u32[]{:S(2)}) %collective-permute-start.13) | collective-permute-done | bytes 73760 | tf_op jit(solution)/shard_map/ppermute | solution.py:59
  135.2 2.3 %collective-permute-start.14 = (f32[9,32,128]{2,1,0:T(8,128)S(1)}, f32[9,32,128]{2,1,0:T(8,128)S(1)}, u32[]{:S(2)}, u32[]{:S(2)}) collective-permute-start(f32[9,32,128]{2,1,0:T(8,128)S(1)} %pad_maximum_fusion.6), channel_id=1, source_target_pairs={{0,4},{1,5},{2,6},{3,7},{4,0},{5,1},{6,2},{7,3},{8,12},{9,13},{10,... | collective-permute-start | bytes 442376 | tf_op jit(solution)/shard_map/ppermute | solution.py:59
  137.5 3.1 %collective-permute-done.14 = f32[9,32,128]{2,1,0:T(8,128)S(1)} collective-permute-done((f32[9,32,128]{2,1,0:T(8,128)S(1)}, f32[9,32,128]{2,1,0:T(8,128)S(1)}, u32[]{:S(2)}, u32[]{:S(2)}) %collective-permute-start.14) | collective-permute-done | bytes 147488 | tf_op jit(solution)/shard_map/ppermute | solution.py:59
  142.3 5.2 %collective-permute-done.15 = f32[9,32,256]{2,1,0:T(8,128)S(1)} collective-permute-done((f32[9,32,256]{2,1,0:T(8,128)S(1)}, f32[9,32,256]{2,1,0:T(8,128)S(1)}, u32[]{:S(2)}, u32[]{:S(2)}) %collective-permute-start.15) | collective-permute-done | bytes 294944 | tf_op jit(solution)/shard_map/ppermute | solution.py:59
  151.4 3.8 %multiply_add_fusion = (f32[4,64,1024]{2,1,0:T(8,128)}, f32[1,4,64,1024]{3,2,1,0:T(8,128)}) fusion(f32[4,64,1024]{2,1,0:T(8,128)} %param.16, f32[4]{0:T(128)S(1)} %convolution_bitcast_fusion, f32[1,4,64,1024]{3,2,1,0:T(8,128)S(1)} %convert_add_fusion, f32[4,64,32]{1,2,0:T(8,128)S(1)} %fusion.16, f32[4,32,1024]{2,1,0:T(8,128)} %gather_fusion.5, ...), kind=kOutput, calls=%fused_computation.15 | convolution fusion | flops 101842944 | bytes 4751380 | tf_op jit(solution)/shard_map/tks,tsd->tkd/dot_general | solution.py:108
  (102 shorter events, 41.6 us)
Async XLA Ops:
  0.6 9.6 %copy-start = (f32[9,1024,32]{1,2,0:T(8,128)S(1)}, f32[9,1024,32]{1,2,0:T(8,128)}, u32[]{:S(2)}) copy-start(f32[9,1024,32]{1,2,0:T(8,128)} %param.20) | copy-start | bytes 3538948
  3.0 4.1 %copy-start.14 = (s32[4]{0:T(128)S(1)}, s32[4]{0:T(128)}, u32[]{:S(2)}) copy-start(s32[4]{0:T(128)} %param.17) | copy-start | bytes 52
  4.2 27.0 %collective-permute-start = (f32[261,1024]{1,0:T(8,128)}, f32[261,1024]{1,0:T(8,128)S(1)}, u32[]{:S(2)}, u32[]{:S(2)}) collective-permute-start(f32[261,1024]{1,0:T(8,128)} %pad_maximum_fusion), channel_id=1, source_target_pairs={{0,16},{16,0},{1,17},{17,1},{2,18},{18,2},{3,19},{19,3},{4,20},{20... | collective-permute-start | bytes 3207176 | tf_op jit(solution)/shard_map/ppermute | solution.py:20
  10.2 1.6 %copy-start.15 = (s32[4]{0:T(128)S(1)}, s32[4]{0:T(128)}, u32[]{:S(2)}) copy-start(s32[4]{0:T(128)} %param.17) | copy-start | bytes 52
  11.9 22.0 %copy-start.11 = (pred[4]{0:T(512)(128)(4,1)}, pred[4]{0:T(512)(128)(4,1)S(1)}, u32[]{:S(2)}) copy-start(pred[4]{0:T(512)(128)(4,1)S(1)} %compare_and_fusion) | copy-start | bytes 16
  31.3 2.5 %copy-start.2 = (f32[261,1024]{1,0:T(8,128)}, f32[261,1024]{1,0:T(8,128)S(1)}, u32[]{:S(2)}) copy-start(f32[261,1024]{1,0:T(8,128)S(1)} %fusion.41) | copy-start | bytes 3207172
  31.4 1.4 copy-start.1
  38.6 2.3 %collective-permute-start.1 = (f32[9,32,512]{2,1,0:T(8,128)}, f32[9,32,512]{2,1,0:T(8,128)}, u32[]{:S(2)}, u32[]{:S(2)}) collective-permute-start(f32[9,32,512]{2,1,0:T(8,128)} %copy.38), channel_id=1, source_target_pairs={{0,1},{1,0},{2,3},{3,2},{4,5},{5,4},{6,7},{7,6},{8,9},{9,8},{10,11... | collective-permute-start | bytes 1769480 | tf_op jit(solution)/shard_map/ppermute | solution.py:56
  44.3 9.4 %collective-permute-start.2 = (f32[9,32,256]{2,1,0:T(8,128)}, f32[9,32,256]{2,1,0:T(8,128)}, u32[]{:S(2)}, u32[]{:S(2)}) collective-permute-start(f32[9,32,256]{2,1,0:T(8,128)} %constant_dynamic-slice_fusion.7), channel_id=1, source_target_pairs={{0,2},{1,3},{2,0},{3,1},{4,6},{5,7},{6,4},{7,5},{8,10},{9,11},{10,... | collective-permute-start | bytes 884744 | tf_op jit(solution)/shard_map/ppermute | solution.py:56
  55.5 5.3 %collective-permute-start.3 = (f32[9,32,128]{2,1,0:T(8,128)S(1)}, f32[9,32,128]{2,1,0:T(8,128)}, u32[]{:S(2)}, u32[]{:S(2)}) collective-permute-start(f32[9,32,128]{2,1,0:T(8,128)S(1)} %constant_dynamic-slice_fusion.6), channel_id=1, source_target_pairs={{0,4},{1,5},{2,6},{3,7},{4,0},{5,1},{6,2},{7,3},{8,12},{9,13},{10,... | collective-permute-start | bytes 442376 | tf_op jit(solution)/shard_map/ppermute | solution.py:56
  61.9 5.4 %collective-permute-start.4 = (f32[9,16,128]{2,1,0:T(8,128)S(1)}, f32[9,16,128]{2,1,0:T(8,128)}, u32[]{:S(2)}, u32[]{:S(2)}) collective-permute-start(f32[9,16,128]{2,1,0:T(8,128)S(1)} %constant_dynamic-slice_fusion.5), channel_id=1, source_target_pairs={{0,8},{1,9},{2,10},{3,11},{4,12},{5,13},{6,14},{7,15},{8,0},{9,1},... | collective-permute-start | bytes 221192 | tf_op jit(solution)/shard_map/ppermute | solution.py:56
  68.2 3.0 %copy-start.9 = (f32[9,16,128]{2,1,0:T(8,128)}, f32[9,16,128]{2,1,0:T(8,128)S(1)}, u32[]{:S(2)}) copy-start(f32[9,16,128]{2,1,0:T(8,128)S(1)} %dynamic-slice_add_fusion.5) | copy-start | bytes 221188
  68.2 5.3 %collective-permute-start.5 = (f32[9,16,128]{2,1,0:T(8,128)S(1)}, f32[9,16,128]{2,1,0:T(8,128)S(1)}, u32[]{:S(2)}, u32[]{:S(2)}) collective-permute-start(f32[9,16,128]{2,1,0:T(8,128)S(1)} %dynamic-slice_add_fusion.5), channel_id=1, source_target_pairs={{0,8},{1,9},{2,10},{3,11},{4,12},{5,13},{6,14},{7,15},{8,0},{9,1},... | collective-permute-start | bytes 221192 | tf_op jit(solution)/shard_map/ppermute | solution.py:59
  74.4 2.8 %copy-start.8 = (f32[9,16,128]{2,1,0:T(8,128)}, f32[9,16,128]{2,1,0:T(8,128)S(1)}, u32[]{:S(2)}) copy-start(f32[9,16,128]{2,1,0:T(8,128)S(1)} %get-tuple-element.29) | copy-start | bytes 221188
  75.1 5.6 %collective-permute-start.6 = (f32[9,32,128]{2,1,0:T(8,128)}, f32[9,32,128]{2,1,0:T(8,128)}, u32[]{:S(2)}, u32[]{:S(2)}) collective-permute-start(f32[9,32,128]{2,1,0:T(8,128)} %pad_maximum_fusion.5), channel_id=1, source_target_pairs={{0,4},{1,5},{2,6},{3,7},{4,0},{5,1},{6,2},{7,3},{8,12},{9,13},{10,... | collective-permute-start | bytes 442376 | tf_op jit(solution)/shard_map/ppermute | solution.py:59
  83.1 7.0 %collective-permute-start.7 = (f32[9,32,256]{2,1,0:T(8,128)}, f32[9,32,256]{2,1,0:T(8,128)}, u32[]{:S(2)}, u32[]{:S(2)}) collective-permute-start(f32[9,32,256]{2,1,0:T(8,128)} %pad_maximum_fusion.3), channel_id=1, source_target_pairs={{0,2},{1,3},{2,0},{3,1},{4,6},{5,7},{6,4},{7,5},{8,10},{9,11},{10,... | collective-permute-start | bytes 884744 | tf_op jit(solution)/shard_map/ppermute | solution.py:59
  84.7 8.1 %copy-start.13 = (s32[1024]{0:T(1024)S(1)}, s32[1024]{0:T(1024)}, u32[]{:S(2)}) copy-start(s32[1024]{0:T(1024)} %pad_clamp_fusion) | copy-start | bytes 12292
  91.2 1.6 %copy-start.4 = (f32[9,32,256]{2,1,0:T(8,128)}, f32[9,32,256]{2,1,0:T(8,128)S(1)}, u32[]{:S(2)}) copy-start(f32[9,32,256]{2,1,0:T(8,128)S(1)} %get-tuple-element.18) | copy-start | bytes 884740
  92.8 2.9 %collective-permute-start.8 = (f32[9,32,512]{2,1,0:T(8,128)}, f32[9,32,512]{2,1,0:T(8,128)}, u32[]{:S(2)}, u32[]{:S(2)}) collective-permute-start(f32[9,32,512]{2,1,0:T(8,128)} %pad_maximum_fusion.1), channel_id=1, source_target_pairs={{0,1},{1,0},{2,3},{3,2},{4,5},{5,4},{6,7},{7,6},{8,9},{9,8},{10,11... | collective-permute-start | bytes 1769480 | tf_op jit(solution)/shard_map/ppermute | solution.py:59
  97.1 3.8 %copy-start.12 = (pred[4]{0:T(512)(128)(4,1)S(1)}, pred[4]{0:T(512)(128)(4,1)}, u32[]{:S(2)}) copy-start(pred[4]{0:T(512)(128)(4,1)} %copy-done.11) | copy-start | bytes 16
  103.7 1.0 copy-start.16
  106.7 2.2 %collective-permute-start.9 = (f32[9,32,512]{2,1,0:T(8,128)S(1)}, f32[9,32,512]{2,1,0:T(8,128)S(1)}, u32[]{:S(2)}, u32[]{:S(2)}) collective-permute-start(f32[9,32,512]{2,1,0:T(8,128)S(1)} %copy.43), channel_id=1, source_target_pairs={{0,1},{1,0},{2,3},{3,2},{4,5},{5,4},{6,7},{7,6},{8,9},{9,8},{10,11... | collective-permute-start | bytes 1769480 | tf_op jit(solution)/shard_map/ppermute | solution.py:56
  109.3 9.4 %collective-permute-start.10 = (f32[9,32,256]{2,1,0:T(8,128)S(1)}, f32[9,32,256]{2,1,0:T(8,128)S(1)}, u32[]{:S(2)}, u32[]{:S(2)}) collective-permute-start(f32[9,32,256]{2,1,0:T(8,128)S(1)} %constant_dynamic-slice_fusion.2), channel_id=1, source_target_pairs={{0,2},{1,3},{2,0},{3,1},{4,6},{5,7},{6,4},{7,5},{8,10},{9,11},{10,... | collective-permute-start | bytes 884744 | tf_op jit(solution)/shard_map/ppermute | solution.py:56
  118.8 5.6 %collective-permute-start.11 = (f32[9,32,128]{2,1,0:T(8,128)S(1)}, f32[9,32,128]{2,1,0:T(8,128)S(1)}, u32[]{:S(2)}, u32[]{:S(2)}) collective-permute-start(f32[9,32,128]{2,1,0:T(8,128)S(1)} %constant_dynamic-slice_fusion.1), channel_id=1, source_target_pairs={{0,4},{1,5},{2,6},{3,7},{4,0},{5,1},{6,2},{7,3},{8,12},{9,13},{10,... | collective-permute-start | bytes 442376 | tf_op jit(solution)/shard_map/ppermute | solution.py:56
  124.4 5.4 %collective-permute-start.12 = (f32[9,16,128]{2,1,0:T(8,128)S(1)}, f32[9,16,128]{2,1,0:T(8,128)S(1)}, u32[]{:S(2)}, u32[]{:S(2)}) collective-permute-start(f32[9,16,128]{2,1,0:T(8,128)S(1)} %constant_dynamic-slice_fusion), channel_id=1, source_target_pairs={{0,8},{1,9},{2,10},{3,11},{4,12},{5,13},{6,14},{7,15},{8,0},{9,1},... | collective-permute-start | bytes 221192 | tf_op jit(solution)/shard_map/ppermute | solution.py:56
  129.8 5.4 %collective-permute-start.13 = (f32[9,16,128]{2,1,0:T(8,128)S(1)}, f32[9,16,128]{2,1,0:T(8,128)S(1)}, u32[]{:S(2)}, u32[]{:S(2)}) collective-permute-start(f32[9,16,128]{2,1,0:T(8,128)S(1)} %dynamic-slice_add_fusion.4), channel_id=1, source_target_pairs={{0,8},{1,9},{2,10},{3,11},{4,12},{5,13},{6,14},{7,15},{8,0},{9,1},... | collective-permute-start | bytes 221192 | tf_op jit(solution)/shard_map/ppermute | solution.py:59
  135.2 5.4 %collective-permute-start.14 = (f32[9,32,128]{2,1,0:T(8,128)S(1)}, f32[9,32,128]{2,1,0:T(8,128)S(1)}, u32[]{:S(2)}, u32[]{:S(2)}) collective-permute-start(f32[9,32,128]{2,1,0:T(8,128)S(1)} %pad_maximum_fusion.6), channel_id=1, source_target_pairs={{0,4},{1,5},{2,6},{3,7},{4,0},{5,1},{6,2},{7,3},{8,12},{9,13},{10,... | collective-permute-start | bytes 442376 | tf_op jit(solution)/shard_map/ppermute | solution.py:59
  140.7 7.0 %copy-start.17 = (s32[9]{0:T(128)S(1)}, s32[9]{0:T(128)}, u32[]{:S(2)}) copy-start(s32[9]{0:T(128)} %param.18) | copy-start | bytes 112
  140.7 7.0 %copy-start.18 = (f32[4]{0:T(128)S(1)}, f32[4]{0:T(128)}, u32[]{:S(2)}) copy-start(f32[4]{0:T(128)} %param.19) | copy-start | bytes 52
  140.7 7.4 %copy-start.10 = (f32[5,1024]{1,0:T(8,128)S(1)}, f32[5,1024]{1,0:T(8,128)}, u32[]{:S(2)}) copy-start(f32[5,1024]{1,0:T(8,128)} %param.23) | copy-start | bytes 61444
  140.7 6.8 %collective-permute-start.15 = (f32[9,32,256]{2,1,0:T(8,128)S(1)}, f32[9,32,256]{2,1,0:T(8,128)S(1)}, u32[]{:S(2)}, u32[]{:S(2)}) collective-permute-start(f32[9,32,256]{2,1,0:T(8,128)S(1)} %pad_maximum_fusion.4), channel_id=1, source_target_pairs={{0,2},{1,3},{2,0},{3,1},{4,6},{5,7},{6,4},{7,5},{8,10},{9,11},{10,... | collective-permute-start | bytes 884744 | tf_op jit(solution)/shard_map/ppermute | solution.py:59
  147.6 2.1 %collective-permute-start.16 = (f32[9,32,512]{2,1,0:T(8,128)S(1)}, f32[9,32,512]{2,1,0:T(8,128)S(1)}, u32[]{:S(2)}, u32[]{:S(2)}) collective-permute-start(f32[9,32,512]{2,1,0:T(8,128)S(1)} %pad_maximum_fusion.2), channel_id=1, source_target_pairs={{0,1},{1,0},{2,3},{3,2},{4,5},{5,4},{6,7},{7,6},{8,9},{9,8},{10,11... | collective-permute-start | bytes 1769480 | tf_op jit(solution)/shard_map/ppermute | solution.py:59
  (4 other events, 2.9 us)

commit v3 on v1

--- a/solution.py
+++ b/solution.py
@@ -39,24 +39,41 @@
     return plan
 
 
-def table_sum(x, order):
-    steps = []
-    for name in order:
-        n = lax.axis_size(name)
-        for j in range(_bits(n)):
-            steps.append((name, j, n))
-    plan = _split_plan(x.shape, len(steps))
+def table_sum(x, n_rep, n_own):
+    axes = ("rep", "own")
+    count = n_rep * n_own
+    index = lax.axis_index("rep") * n_own + lax.axis_index("own")
+    core = index & 1
+    own_bits = _bits(n_own)
+    rest = list(range(1, own_bits)) + [own_bits + j for j in range(_bits(n_rep))]
+    alt = list(rest)
+    for i in range(0, len(alt) - 1, 2):
+        alt[i], alt[i + 1] = alt[i + 1], alt[i]
+    stages = [(0, 0)] + list(zip(rest, alt))
+    tail = min(2, len(rest))
+    halving = stages[: len(stages) - tail]
+    pairing = stages[len(stages) - tail :]
+
+    def perm_of(p0, p1):
+        return [(i, i ^ (1 << (p0 if i % 2 == 0 else p1))) for i in range(count)]
+
+    def bit_of(p0, p1):
+        return (index >> jnp.where(core == 0, p0, p1)) & 1
+
+    plan = _split_plan(x.shape, len(halving))
     bits = []
     cur = x
-    for (name, j, n), axis in zip(steps, plan):
-        bit = (lax.axis_index(name) >> j) & 1
+    for (p0, p1), axis in zip(halving, plan):
+        bit = bit_of(p0, p1)
         half = cur.shape[axis] // 2
         keep = lax.dynamic_slice_in_dim(cur, bit * half, half, axis)
         send = lax.dynamic_slice_in_dim(cur, (1 - bit) * half, half, axis)
-        cur = keep + lax.ppermute(send, name, _pair_perm(n, j))
+        cur = keep + lax.ppermute(send, axes, perm_of(p0, p1))
         bits.append(bit)
-    for (name, j, n), axis, bit in reversed(list(zip(steps, plan, bits))):
-        other = lax.ppermute(cur, name, _pair_perm(n, j))
+    for p0, p1 in pairing:
+        cur = cur + lax.ppermute(cur, axes, perm_of(p0, p1))
+    for (p0, p1), axis, bit in reversed(list(zip(halving, plan, bits))):
+        other = lax.ppermute(cur, axes, perm_of(p0, p1))
         low = jnp.where(bit == 0, cur, other)
         high = jnp.where(bit == 0, other, cur)
         cur = jnp.concatenate([low, high], axis=axis)
@@ -76,21 +93,24 @@
     vector_momentum,
 ):
     replicas = lax.axis_size("rep")
+    n_own = lax.axis_size("own")
     matrix_count = start_basis.shape[0]
-    order = ("own", "rep")
     selector = (tile_matrix[:, None] == jnp.arange(matrix_count, dtype=jnp.int32)[None, :]).astype(
         jnp.float32
     )
     combined = gradient[0].astype(jnp.float32) + feedback[0]
     q_tiles = jnp.take(start_basis, tile_matrix, axis=0)
     first_local = jnp.einsum("tkd,tds->tks", combined, q_tiles, precision=TOP_PRECISION)
-    vector_summed = swap_sum(vector_grad[0], "rep")
-    first_left = swap_sum(first_local, "rep") / replicas
+    left_size = first_local.size
+    carried = jnp.concatenate([first_local.reshape(-1), vector_grad[0].reshape(-1)])
+    carried = swap_sum(carried, "rep")
+    first_left = carried[:left_size].reshape(first_local.shape) / replicas
+    vector_summed = carried[left_size:].reshape(vector_grad.shape[1:])
     mix_first = jnp.take(inverse_gram_factors[0], tile_matrix, axis=0)
     first_ortho = jnp.einsum("tks,tsa->tka", first_left, mix_first, precision=TOP_PRECISION)
     first_parts = jnp.einsum("tkd,tks->tsd", combined, first_ortho, precision=TOP_PRECISION)
     first_table = jnp.einsum("tm,tsd->msd", selector, first_parts, precision=TOP_PRECISION)
-    first_table = table_sum(first_table, order) / replicas
+    first_table = table_sum(first_table, replicas, n_own) / replicas
     first_rows = jnp.take(first_table, tile_matrix, axis=0)
     mix_right = jnp.take(inverse_gram_factors[1], tile_matrix, axis=0)
     right_rows = jnp.einsum("tjw,tjd->twd", mix_right, first_rows, precision=TOP_PRECISION)
@@ -100,7 +120,7 @@
     second_ortho = jnp.einsum("tks,tsa->tka", second_left, mix_second, precision=TOP_PRECISION)
     second_parts = jnp.einsum("tkd,tks->tsd", combined, second_ortho, precision=TOP_PRECISION)
     second_table = jnp.einsum("tm,tsd->msd", selector, second_parts, precision=TOP_PRECISION)
-    second_table = table_sum(second_table, order) / replicas
+    second_table = table_sum(second_table, replicas, n_own) / replicas
     back_rows = jnp.take(second_table, tile_matrix, axis=0)
     approximation = jnp.einsum("tks,tsd->tkd", second_ortho, back_rows, precision=TOP_PRECISION)
     new_feedback = (combined - approximation)[None]

time: 146 us -> 136 us (0.932)
  waiting for transfers between devices: 69.8 us -> 62.1 us
  starting transfers between devices: 37.4 us -> 31.1 us
  other arithmetic: 12.2 us -> 14.8 us
    ppermute x20 -> x16, starting transfers between devices: 31.6 us -> 26.2 us  [the longest x4 10.1 us: table_sum(): cur = cur + lax.ppermute(cur, axes, perm_of(p0, p1))]
    ppermute x20 -> x16, waiting for transfers between devices: 65.2 us -> 61.1 us  [the longest x6 21 us: table_sum(): other = lax.ppermute(cur, axes, perm_of(p0, p1))]
    ppermute x3 -> x2, waiting for transfers between devices: 4.55 us -> 0.98 us  [swap_sum(): x = x + lax.ppermute(x, axis, _pair_perm(n, j))]
    select_n x10 -> x6, other arithmetic: 2.59 us -> 3.61 us  [table_sum(): low = jnp.where(bit == 0, cur, other)]
    ppermute x3 -> x2, starting transfers between devices: 5.88 us -> 4.92 us  [swap_sum(): x = x + lax.ppermute(x, axis, _pair_perm(n, j))]
    add x10 -> x11, other arithmetic: 4.24 us -> 4.3 us  [the longest x6 4.2 us: table_sum(): cur = keep + lax.ppermute(send, axes, perm_of(p0, p1))]
  transfers between devices with their start and end apart: 23 -> 18, of which waited for: 22 -> 17; matrix products, arithmetic and copies ran while one was open for 4% -> 5% of each run, Pallas kernels for 0% -> 0%
where the time goes in v3:
time: 136 us
  waiting for transfers between devices  62.1 us (46%)
  starting transfers between devices  31.1 us (23%)
  local copies, waits for them, and re-layouts  14.8 us (11%)
  other arithmetic  14.8 us (11%)
  matrix products  11.9 us (9%)
    ppermute x6, waiting for transfers between devices, table_sum(): other = lax.ppermute(cur, axes, perm_of(p0, p1))  21 us
    ppermute x6, waiting for transfers between devices, table_sum(): cur = keep + lax.ppermute(send, axes, perm_of(p0, p1))  20.6 us
    ppermute x4, waiting for transfers between devices, table_sum(): cur = cur + lax.ppermute(cur, axes, perm_of(p0, p1))  19.6 us
    ppermute x4, starting transfers between devices, table_sum(): cur = cur + lax.ppermute(cur, axes, perm_of(p0, p1))  10.1 us
    ppermute x6, starting transfers between devices, table_sum(): other = lax.ppermute(cur, axes, perm_of(p0, p1))  8.21 us
    ppermute x6, starting transfers between devices, table_sum(): cur = keep + lax.ppermute(send, axes, perm_of(p0, p1))  7.9 us
    ppermute x2, starting transfers between devices, swap_sum(): x = x + lax.ppermute(x, axis, _pair_perm(n, j))  4.92 us
    add x6, other arithmetic, table_sum(): cur = keep + lax.ppermute(send, axes, perm_of(p0, p1))  4.2 us
  transfers between devices with their start and end apart: 18, of which 17 were waited for; matrix products, arithmetic and copies ran while one was open for 5% of the time, Pallas kernels for 0%

profile of v3, /device:TPU:0, one launch (start us, length us, event | category | flops | bytes accessed | tf_op | source)
XLA Modules:
  0.0 135.8 jit_solution(16051694536411560621)
XLA Ops:
  4.7 3.0 %collective-permute-start = (f32[13312]{0:T(1024)S(1)}, f32[13312]{0:T(1024)S(1)}, u32[]{:S(2)}, u32[]{:S(2)}) collective-permute-start(f32[13312]{0:T(1024)S(1)} %pad_maximum_fusion.4), channel_id=1, source_target_pairs={{0,16},{16,0},{1,17},{17,1},{2,18},{18,2},{3,19},{19,3},{4,20},{20... | collective-permute-start | bytes 159752 | tf_op jit(solution)/shard_map/ppermute | solution.py:20
  7.7 1.8 %slice_bitcast_fusion.2 = (f32[9,32,32]{2,1,0:T(8,128)}, f32[9,32,32]{2,1,0:T(8,128)}, f32[9,32,32]{2,1,0:T(8,128)S(1)}) fusion(f32[3,9,32,32]{3,2,1,0:T(8,128)} %param.21), kind=kLoop, calls=%fused_computation.53 | loop fusion | bytes 221184 | tf_op jit(solution)/shard_map/squeeze | solution.py:115
  14.4 2.1 %collective-permute-done.1 = f32[9,32,512]{2,1,0:T(8,128)} collective-permute-done((f32[9,32,512]{2,1,0:T(8,128)S(1)}, f32[9,32,512]{2,1,0:T(8,128)}, u32[]{:S(2)}, u32[]{:S(2)}) %collective-permute-start.1) | collective-permute-done | bytes 589856 | tf_op jit(solution)/shard_map/ppermute | solution.py:71
  16.5 1.8 %copy_add_fusion.1 = f32[9,32,512]{2,1,0:T(8,128)S(1)} fusion(f32[9,32,512]{2,1,0:T(8,128)} %collective-permute-done.1, f32[9,32,512]{2,0,1:T(8,128)} %get-tuple-element.7), kind=kLoop, calls=%fused_computation.25 | loop fusion | flops 147456 | bytes 1769472 | tf_op jit(solution)/shard_map/add | solution.py:71
  19.0 1.8 %collective-permute-start.2 = (f32[9,32,256]{2,1,0:T(8,128)}, f32[9,32,256]{2,1,0:T(8,128)}, u32[]{:S(2)}, u32[]{:S(2)}) collective-permute-start(f32[9,32,256]{2,1,0:T(8,128)} %constant_dynamic-slice_fusion.5), channel_id=1, source_target_pairs={{0,2},{1,5},{2,0},{3,7},{4,6},{5,1},{6,4},{7,3},{8,10},{9,13},{10,... | collective-permute-start | bytes 884744 | tf_op jit(solution)/shard_map/ppermute | solution.py:71
  20.8 5.2 %collective-permute-done.2 = f32[9,32,256]{2,1,0:T(8,128)} collective-permute-done((f32[9,32,256]{2,1,0:T(8,128)}, f32[9,32,256]{2,1,0:T(8,128)}, u32[]{:S(2)}, u32[]{:S(2)}) %collective-permute-start.2) | collective-permute-done | bytes 294944 | tf_op jit(solution)/shard_map/ppermute | solution.py:71
  27.8 1.9 %collective-permute-start.3 = (f32[9,32,128]{2,1,0:T(8,128)S(1)}, f32[9,32,128]{2,1,0:T(8,128)S(1)}, u32[]{:S(2)}, u32[]{:S(2)}) collective-permute-start(f32[9,32,128]{2,1,0:T(8,128)S(1)} %constant_dynamic-slice_fusion.4), channel_id=1, source_target_pairs={{0,4},{1,3},{2,6},{3,1},{4,0},{5,7},{6,2},{7,5},{8,12},{9,11},{10,... | collective-permute-start | bytes 442376 | tf_op jit(solution)/shard_map/ppermute | solution.py:71
  29.7 3.3 %collective-permute-done.3 = f32[9,32,128]{2,1,0:T(8,128)S(1)} collective-permute-done((f32[9,32,128]{2,1,0:T(8,128)S(1)}, f32[9,32,128]{2,1,0:T(8,128)S(1)}, u32[]{:S(2)}, u32[]{:S(2)}) %collective-permute-start.3) | collective-permute-done | bytes 147488 | tf_op jit(solution)/shard_map/ppermute | solution.py:71
  33.9 2.9 %collective-permute-start.4 = (f32[9,32,128]{2,1,0:T(8,128)S(1)}, f32[9,32,128]{2,1,0:T(8,128)S(1)}, u32[]{:S(2)}, u32[]{:S(2)}) collective-permute-start(f32[9,32,128]{2,1,0:T(8,128)S(1)} %dynamic-slice_add_fusion.3), channel_id=1, source_target_pairs={{0,8},{1,17},{2,10},{3,19},{4,12},{5,21},{6,14},{7,23},{8,0},{9,25... | collective-permute-start | bytes 442376 | tf_op jit(solution)/shard_map/ppermute | solution.py:74
  36.9 6.5 %collective-permute-done.4 = f32[9,32,128]{2,1,0:T(8,128)S(1)} collective-permute-done((f32[9,32,128]{2,1,0:T(8,128)S(1)}, f32[9,32,128]{2,1,0:T(8,128)S(1)}, u32[]{:S(2)}, u32[]{:S(2)}) %collective-permute-start.4) | collective-permute-done | bytes 147488 | tf_op jit(solution)/shard_map/ppermute | solution.py:74
  43.4 2.1 %collective-permute-start.5 = (f32[9,32,128]{2,1,0:T(8,128)S(1)}, f32[9,32,128]{2,1,0:T(8,128)S(1)}, u32[]{:S(2)}, u32[]{:S(2)}) collective-permute-start(f32[9,32,128]{2,1,0:T(8,128)S(1)} %add.100), channel_id=1, source_target_pairs={{0,16},{1,9},{2,18},{3,11},{4,20},{5,13},{6,22},{7,15},{8,24},{9,1... | collective-permute-start | bytes 442376 | tf_op jit(solution)/shard_map/ppermute | solution.py:74
  45.5 3.1 %collective-permute-done.5 = f32[9,32,128]{2,1,0:T(8,128)S(1)} collective-permute-done((f32[9,32,128]{2,1,0:T(8,128)S(1)}, f32[9,32,128]{2,1,0:T(8,128)S(1)}, u32[]{:S(2)}, u32[]{:S(2)}) %collective-permute-start.5) | collective-permute-done | bytes 147488 | tf_op jit(solution)/shard_map/ppermute | solution.py:74
  48.7 2.3 %collective-permute-start.6 = (f32[9,32,128]{2,1,0:T(8,128)S(1)}, f32[9,32,128]{2,1,0:T(8,128)S(1)}, u32[]{:S(2)}, u32[]{:S(2)}) collective-permute-start(f32[9,32,128]{2,1,0:T(8,128)S(1)} %add.101), channel_id=1, source_target_pairs={{0,4},{1,3},{2,6},{3,1},{4,0},{5,7},{6,2},{7,5},{8,12},{9,11},{10,... | collective-permute-start | bytes 442376 | tf_op jit(solution)/shard_map/ppermute | solution.py:76
  51.0 4.7 %collective-permute-done.6 = f32[9,32,128]{2,1,0:T(8,128)S(1)} collective-permute-done((f32[9,32,128]{2,1,0:T(8,128)S(1)}, f32[9,32,128]{2,1,0:T(8,128)S(1)}, u32[]{:S(2)}, u32[]{:S(2)}) %collective-permute-start.6) | collective-permute-done | bytes 147488 | tf_op jit(solution)/shard_map/ppermute | solution.py:76
  56.4 1.9 %collective-permute-start.7 = (f32[9,32,256]{2,1,0:T(8,128)S(1)}, f32[9,32,256]{2,1,0:T(8,128)}, u32[]{:S(2)}, u32[]{:S(2)}) collective-permute-start(f32[9,32,256]{2,1,0:T(8,128)S(1)} %pad_maximum_fusion.2), channel_id=1, source_target_pairs={{0,2},{1,5},{2,0},{3,7},{4,6},{5,1},{6,4},{7,3},{8,10},{9,13},{10,... | collective-permute-start | bytes 884744 | tf_op jit(solution)/shard_map/ppermute | solution.py:76
  58.3 5.0 %collective-permute-done.7 = f32[9,32,256]{2,1,0:T(8,128)} collective-permute-done((f32[9,32,256]{2,1,0:T(8,128)S(1)}, f32[9,32,256]{2,1,0:T(8,128)}, u32[]{:S(2)}, u32[]{:S(2)}) %collective-permute-start.7) | collective-permute-done | bytes 294944 | tf_op jit(solution)/shard_map/ppermute | solution.py:76
  69.9 1.8 %gather_fusion.3 = f32[4,32,1024]{2,1,0:T(8,128)S(1)} fusion(f32[9,32,1024]{2,1,0:T(8,128)} %maximum_multiply_fusion, s32[1024]{0:T(1024)S(1)} %pad_clamp_fusion), kind=kCustom, calls=%fused_computation.1.clone | custom fusion | bytes 1048592 | tf_op jit(solution)/shard_map/jit(_take)/gather | solution.py:114
  73.6 1.9 %collective-permute-start.9 = (f32[4,64,32]{1,2,0:T(8,128)S(1)}, f32[4,64,32]{1,2,0:T(8,128)S(1)}, u32[]{:S(2)}, u32[]{:S(2)}) collective-permute-start(f32[4,64,32]{1,2,0:T(8,128)S(1)} %fusion.2), channel_id=1, source_target_pairs={{0,16},{16,0},{1,17},{17,1},{2,18},{18,2},{3,19},{19,3},{4,20},{20... | collective-permute-start | bytes 98312 | tf_op jit(solution)/shard_map/ppermute | solution.py:20
  81.0 2.0 %collective-permute-done.10 = f32[9,32,512]{2,1,0:T(8,128)S(1)} collective-permute-done((f32[9,32,512]{2,1,0:T(8,128)S(1)}, f32[9,32,512]{2,1,0:T(8,128)S(1)}, u32[]{:S(2)}, u32[]{:S(2)}) %collective-permute-start.10) | collective-permute-done | bytes 589856 | tf_op jit(solution)/shard_map/ppermute | solution.py:71
  83.5 1.9 %collective-permute-start.11 = (f32[9,32,256]{2,1,0:T(8,128)S(1)}, f32[9,32,256]{2,1,0:T(8,128)S(1)}, u32[]{:S(2)}, u32[]{:S(2)}) collective-permute-start(f32[9,32,256]{2,1,0:T(8,128)S(1)} %constant_dynamic-slice_fusion.1), channel_id=1, source_target_pairs={{0,2},{1,5},{2,0},{3,7},{4,6},{5,1},{6,4},{7,3},{8,10},{9,13},{10,... | collective-permute-start | bytes 884744 | tf_op jit(solution)/shard_map/ppermute | solution.py:71
  85.4 4.9 %collective-permute-done.11 = f32[9,32,256]{2,1,0:T(8,128)S(1)} collective-permute-done((f32[9,32,256]{2,1,0:T(8,128)S(1)}, f32[9,32,256]{2,1,0:T(8,128)S(1)}, u32[]{:S(2)}, u32[]{:S(2)}) %collective-permute-start.11) | collective-permute-done | bytes 294944 | tf_op jit(solution)/shard_map/ppermute | solution.py:71
  90.3 2.1 %collective-permute-start.12 = (f32[9,32,128]{2,1,0:T(8,128)S(1)}, f32[9,32,128]{2,1,0:T(8,128)S(1)}, u32[]{:S(2)}, u32[]{:S(2)}) collective-permute-start(f32[9,32,128]{2,1,0:T(8,128)S(1)} %constant_dynamic-slice_fusion), channel_id=1, source_target_pairs={{0,4},{1,3},{2,6},{3,1},{4,0},{5,7},{6,2},{7,5},{8,12},{9,11},{10,... | collective-permute-start | bytes 442376 | tf_op jit(solution)/shard_map/ppermute | solution.py:71
  92.4 3.1 %collective-permute-done.12 = f32[9,32,128]{2,1,0:T(8,128)S(1)} collective-permute-done((f32[9,32,128]{2,1,0:T(8,128)S(1)}, f32[9,32,128]{2,1,0:T(8,128)S(1)}, u32[]{:S(2)}, u32[]{:S(2)}) %collective-permute-start.12) | collective-permute-done | bytes 147488 | tf_op jit(solution)/shard_map/ppermute | solution.py:71
  95.6 3.4 %collective-permute-start.13 = (f32[9,32,128]{2,1,0:T(8,128)S(1)}, f32[9,32,128]{2,1,0:T(8,128)S(1)}, u32[]{:S(2)}, u32[]{:S(2)}) collective-permute-start(f32[9,32,128]{2,1,0:T(8,128)S(1)} %dynamic-slice_add_fusion.2), channel_id=1, source_target_pairs={{0,8},{1,17},{2,10},{3,19},{4,12},{5,21},{6,14},{7,23},{8,0},{9,25... | collective-permute-start | bytes 442376 | tf_op jit(solution)/shard_map/ppermute | solution.py:74
  99.0 6.3 %collective-permute-done.13 = f32[9,32,128]{2,1,0:T(8,128)S(1)} collective-permute-done((f32[9,32,128]{2,1,0:T(8,128)S(1)}, f32[9,32,128]{2,1,0:T(8,128)S(1)}, u32[]{:S(2)}, u32[]{:S(2)}) %collective-permute-start.13) | collective-permute-done | bytes 147488 | tf_op jit(solution)/shard_map/ppermute | solution.py:74
  106.9 3.6 %collective-permute-done.14 = f32[9,32,128]{2,1,0:T(8,128)S(1)} collective-permute-done((f32[9,32,128]{2,1,0:T(8,128)S(1)}, f32[9,32,128]{2,1,0:T(8,128)S(1)}, u32[]{:S(2)}, u32[]{:S(2)}) %collective-permute-start.14) | collective-permute-done | bytes 147488 | tf_op jit(solution)/shard_map/ppermute | solution.py:74
  110.6 2.4 %collective-permute-start.15 = (f32[9,32,128]{2,1,0:T(8,128)S(1)}, f32[9,32,128]{2,1,0:T(8,128)S(1)}, u32[]{:S(2)}, u32[]{:S(2)}) collective-permute-start(f32[9,32,128]{2,1,0:T(8,128)S(1)} %add.107), channel_id=1, source_target_pairs={{0,4},{1,3},{2,6},{3,1},{4,0},{5,7},{6,2},{7,5},{8,12},{9,11},{10,... | collective-permute-start | bytes 442376 | tf_op jit(solution)/shard_map/ppermute | solution.py:76
  113.0 4.7 %collective-permute-done.15 = f32[9,32,128]{2,1,0:T(8,128)S(1)} collective-permute-done((f32[9,32,128]{2,1,0:T(8,128)S(1)}, f32[9,32,128]{2,1,0:T(8,128)S(1)}, u32[]{:S(2)}, u32[]{:S(2)}) %collective-permute-start.15) | collective-permute-done | bytes 147488 | tf_op jit(solution)/shard_map/ppermute | solution.py:76
  117.8 1.6 %collective-permute-start.16 = (f32[9,32,256]{2,1,0:T(8,128)S(1)}, f32[9,32,256]{2,1,0:T(8,128)S(1)}, u32[]{:S(2)}, u32[]{:S(2)}) collective-permute-start(f32[9,32,256]{2,1,0:T(8,128)S(1)} %pad_maximum_fusion.3), channel_id=1, source_target_pairs={{0,2},{1,5},{2,0},{3,7},{4,6},{5,1},{6,4},{7,3},{8,10},{9,13},{10,... | collective-permute-start | bytes 884744 | tf_op jit(solution)/shard_map/ppermute | solution.py:76
  119.4 5.2 %collective-permute-done.16 = f32[9,32,256]{2,1,0:T(8,128)S(1)} collective-permute-done((f32[9,32,256]{2,1,0:T(8,128)S(1)}, f32[9,32,256]{2,1,0:T(8,128)S(1)}, u32[]{:S(2)}, u32[]{:S(2)}) %collective-permute-start.16) | collective-permute-done | bytes 294944 | tf_op jit(solution)/shard_map/ppermute | solution.py:76
  130.2 1.8 %gather_fusion.5 = f32[4,32,1024]{2,1,0:T(8,128)S(1)} fusion(f32[9,32,1024]{2,1,0:T(8,128)} %maximum_multiply_fusion.1, s32[1024]{0:T(1024)S(1)} %pad_clamp_fusion), kind=kCustom, calls=%fused_computation.4.clone | custom fusion | bytes 1048592 | tf_op jit(solution)/shard_map/jit(_take)/gather | solution.py:124
  132.1 3.8 %multiply_add_fusion = (f32[4,64,1024]{2,1,0:T(8,128)}, f32[1,4,64,1024]{3,2,1,0:T(8,128)}) fusion(f32[4,64,1024]{2,1,0:T(8,128)} %param.16, f32[4]{0:T(128)S(1)} %convolution_bitcast_fusion, f32[1,4,64,1024]{3,2,1,0:T(8,128)S(1)} %copy-done.1, bf16[1,4,64,1024]{3,2,1,0:T(8,128)(2,1)S(1)} %copy-done.2, f32[4,64,32]{1,2,0:T(8,128)S(1)} %fusion.24, ...), kind=kOutput, calls=%fused_computation.20 | convolution fusion | flops 102367232 | bytes 5275668 | tf_op jit(solution)/shard_map/tks,tsd->tkd/dot_general | solution.py:125
  (82 shorter events, 34.6 us)
Async XLA Ops:
  0.6 1.4 %copy-start = (f32[9,1024,32]{1,2,0:T(8,128)S(1)}, f32[9,1024,32]{1,2,0:T(8,128)}, u32[]{:S(2)}) copy-start(f32[9,1024,32]{1,2,0:T(8,128)} %param.20) | copy-start | bytes 3538948
  2.1 1.2 copy-start.1
  2.1 1.3 copy-start.2
  3.4 1.2 copy-start.5
  4.7 5.4 %collective-permute-start = (f32[13312]{0:T(1024)S(1)}, f32[13312]{0:T(1024)S(1)}, u32[]{:S(2)}, u32[]{:S(2)}) collective-permute-start(f32[13312]{0:T(1024)S(1)} %pad_maximum_fusion.4), channel_id=1, source_target_pairs={{0,16},{16,0},{1,17},{17,1},{2,18},{18,2},{3,19},{19,3},{4,20},{20... | collective-permute-start | bytes 159752 | tf_op jit(solution)/shard_map/ppermute | solution.py:20
  10.2 1.2 copy-start.6
  14.3 2.2 %collective-permute-start.1 = (f32[9,32,512]{2,1,0:T(8,128)S(1)}, f32[9,32,512]{2,1,0:T(8,128)}, u32[]{:S(2)}, u32[]{:S(2)}) collective-permute-start(f32[9,32,512]{2,1,0:T(8,128)S(1)} %copy.43), channel_id=1, source_target_pairs={{0,1},{1,0},{2,3},{3,2},{4,5},{5,4},{6,7},{7,6},{8,9},{9,8},{10,11... | collective-permute-start | bytes 1769480 | tf_op jit(solution)/shard_map/ppermute | solution.py:71
  19.0 7.0 %collective-permute-start.2 = (f32[9,32,256]{2,1,0:T(8,128)}, f32[9,32,256]{2,1,0:T(8,128)}, u32[]{:S(2)}, u32[]{:S(2)}) collective-permute-start(f32[9,32,256]{2,1,0:T(8,128)} %constant_dynamic-slice_fusion.5), channel_id=1, source_target_pairs={{0,2},{1,5},{2,0},{3,7},{4,6},{5,1},{6,4},{7,3},{8,10},{9,13},{10,... | collective-permute-start | bytes 884744 | tf_op jit(solution)/shard_map/ppermute | solution.py:71
  27.1 0.7 copy-start.4
  27.8 5.2 %collective-permute-start.3 = (f32[9,32,128]{2,1,0:T(8,128)S(1)}, f32[9,32,128]{2,1,0:T(8,128)S(1)}, u32[]{:S(2)}, u32[]{:S(2)}) collective-permute-start(f32[9,32,128]{2,1,0:T(8,128)S(1)} %constant_dynamic-slice_fusion.4), channel_id=1, source_target_pairs={{0,4},{1,3},{2,6},{3,1},{4,0},{5,7},{6,2},{7,5},{8,12},{9,11},{10,... | collective-permute-start | bytes 442376 | tf_op jit(solution)/shard_map/ppermute | solution.py:71
  33.9 9.4 %collective-permute-start.4 = (f32[9,32,128]{2,1,0:T(8,128)S(1)}, f32[9,32,128]{2,1,0:T(8,128)S(1)}, u32[]{:S(2)}, u32[]{:S(2)}) collective-permute-start(f32[9,32,128]{2,1,0:T(8,128)S(1)} %dynamic-slice_add_fusion.3), channel_id=1, source_target_pairs={{0,8},{1,17},{2,10},{3,19},{4,12},{5,21},{6,14},{7,23},{8,0},{9,25... | collective-permute-start | bytes 442376 | tf_op jit(solution)/shard_map/ppermute | solution.py:74
  43.4 5.3 %collective-permute-start.5 = (f32[9,32,128]{2,1,0:T(8,128)S(1)}, f32[9,32,128]{2,1,0:T(8,128)S(1)}, u32[]{:S(2)}, u32[]{:S(2)}) collective-permute-start(f32[9,32,128]{2,1,0:T(8,128)S(1)} %add.100), channel_id=1, source_target_pairs={{0,16},{1,9},{2,18},{3,11},{4,20},{5,13},{6,22},{7,15},{8,24},{9,1... | collective-permute-start | bytes 442376 | tf_op jit(solution)/shard_map/ppermute | solution.py:74
  48.7 7.0 %collective-permute-start.6 = (f32[9,32,128]{2,1,0:T(8,128)S(1)}, f32[9,32,128]{2,1,0:T(8,128)S(1)}, u32[]{:S(2)}, u32[]{:S(2)}) collective-permute-start(f32[9,32,128]{2,1,0:T(8,128)S(1)} %add.101), channel_id=1, source_target_pairs={{0,4},{1,3},{2,6},{3,1},{4,0},{5,7},{6,2},{7,5},{8,12},{9,11},{10,... | collective-permute-start | bytes 442376 | tf_op jit(solution)/shard_map/ppermute | solution.py:76
  55.7 0.7 copy-start.3
  56.4 6.9 %collective-permute-start.7 = (f32[9,32,256]{2,1,0:T(8,128)S(1)}, f32[9,32,256]{2,1,0:T(8,128)}, u32[]{:S(2)}, u32[]{:S(2)}) collective-permute-start(f32[9,32,256]{2,1,0:T(8,128)S(1)} %pad_maximum_fusion.2), channel_id=1, source_target_pairs={{0,2},{1,5},{2,0},{3,7},{4,6},{5,1},{6,4},{7,3},{8,10},{9,13},{10,... | collective-permute-start | bytes 884744 | tf_op jit(solution)/shard_map/ppermute | solution.py:76
  65.2 2.3 %collective-permute-start.8 = (f32[9,32,512]{2,1,0:T(8,128)}, f32[9,32,512]{2,1,0:T(8,128)}, u32[]{:S(2)}, u32[]{:S(2)}) collective-permute-start(f32[9,32,512]{2,1,0:T(8,128)} %pad_maximum_fusion), channel_id=1, source_target_pairs={{0,1},{1,0},{2,3},{3,2},{4,5},{5,4},{6,7},{7,6},{8,9},{9,8},{10,11... | collective-permute-start | bytes 1769480 | tf_op jit(solution)/shard_map/ppermute | solution.py:76
  73.6 4.3 %collective-permute-start.9 = (f32[4,64,32]{1,2,0:T(8,128)S(1)}, f32[4,64,32]{1,2,0:T(8,128)S(1)}, u32[]{:S(2)}, u32[]{:S(2)}) collective-permute-start(f32[4,64,32]{1,2,0:T(8,128)S(1)} %fusion.2), channel_id=1, source_target_pairs={{0,16},{16,0},{1,17},{17,1},{2,18},{18,2},{3,19},{19,3},{4,20},{20... | collective-permute-start | bytes 98312 | tf_op jit(solution)/shard_map/ppermute | solution.py:20
  81.0 2.1 %collective-permute-start.10 = (f32[9,32,512]{2,1,0:T(8,128)S(1)}, f32[9,32,512]{2,1,0:T(8,128)S(1)}, u32[]{:S(2)}, u32[]{:S(2)}) collective-permute-start(f32[9,32,512]{2,1,0:T(8,128)S(1)} %copy.48), channel_id=1, source_target_pairs={{0,1},{1,0},{2,3},{3,2},{4,5},{5,4},{6,7},{7,6},{8,9},{9,8},{10,11... | collective-permute-start | bytes 1769480 | tf_op jit(solution)/shard_map/ppermute | solution.py:71
  83.5 6.8 %collective-permute-start.11 = (f32[9,32,256]{2,1,0:T(8,128)S(1)}, f32[9,32,256]{2,1,0:T(8,128)S(1)}, u32[]{:S(2)}, u32[]{:S(2)}) collective-permute-start(f32[9,32,256]{2,1,0:T(8,128)S(1)} %constant_dynamic-slice_fusion.1), channel_id=1, source_target_pairs={{0,2},{1,5},{2,0},{3,7},{4,6},{5,1},{6,4},{7,3},{8,10},{9,13},{10,... | collective-permute-start | bytes 884744 | tf_op jit(solution)/shard_map/ppermute | solution.py:71
  90.3 5.2 %collective-permute-start.12 = (f32[9,32,128]{2,1,0:T(8,128)S(1)}, f32[9,32,128]{2,1,0:T(8,128)S(1)}, u32[]{:S(2)}, u32[]{:S(2)}) collective-permute-start(f32[9,32,128]{2,1,0:T(8,128)S(1)} %constant_dynamic-slice_fusion), channel_id=1, source_target_pairs={{0,4},{1,3},{2,6},{3,1},{4,0},{5,7},{6,2},{7,5},{8,12},{9,11},{10,... | collective-permute-start | bytes 442376 | tf_op jit(solution)/shard_map/ppermute | solution.py:71
  95.6 9.7 %collective-permute-start.13 = (f32[9,32,128]{2,1,0:T(8,128)S(1)}, f32[9,32,128]{2,1,0:T(8,128)S(1)}, u32[]{:S(2)}, u32[]{:S(2)}) collective-permute-start(f32[9,32,128]{2,1,0:T(8,128)S(1)} %dynamic-slice_add_fusion.2), channel_id=1, source_target_pairs={{0,8},{1,17},{2,10},{3,19},{4,12},{5,21},{6,14},{7,23},{8,0},{9,25... | collective-permute-start | bytes 442376 | tf_op jit(solution)/shard_map/ppermute | solution.py:74
  105.3 5.2 %collective-permute-start.14 = (f32[9,32,128]{2,1,0:T(8,128)S(1)}, f32[9,32,128]{2,1,0:T(8,128)S(1)}, u32[]{:S(2)}, u32[]{:S(2)}) collective-permute-start(f32[9,32,128]{2,1,0:T(8,128)S(1)} %add.106), channel_id=1, source_target_pairs={{0,16},{1,9},{2,18},{3,11},{4,20},{5,13},{6,22},{7,15},{8,24},{9,1... | collective-permute-start | bytes 442376 | tf_op jit(solution)/shard_map/ppermute | solution.py:74
  110.6 7.1 %collective-permute-start.15 = (f32[9,32,128]{2,1,0:T(8,128)S(1)}, f32[9,32,128]{2,1,0:T(8,128)S(1)}, u32[]{:S(2)}, u32[]{:S(2)}) collective-permute-start(f32[9,32,128]{2,1,0:T(8,128)S(1)} %add.107), channel_id=1, source_target_pairs={{0,4},{1,3},{2,6},{3,1},{4,0},{5,7},{6,2},{7,5},{8,12},{9,11},{10,... | collective-permute-start | bytes 442376 | tf_op jit(solution)/shard_map/ppermute | solution.py:76
  117.7 7.8 %copy-start.7 = (s32[9]{0:T(128)S(1)}, s32[9]{0:T(128)}, u32[]{:S(2)}) copy-start(s32[9]{0:T(128)} %param.18) | copy-start | bytes 112
  117.7 7.8 %copy-start.8 = (f32[4]{0:T(128)S(1)}, f32[4]{0:T(128)}, u32[]{:S(2)}) copy-start(f32[4]{0:T(128)} %param.19) | copy-start | bytes 52
  117.8 6.8 %collective-permute-start.16 = (f32[9,32,256]{2,1,0:T(8,128)S(1)}, f32[9,32,256]{2,1,0:T(8,128)S(1)}, u32[]{:S(2)}, u32[]{:S(2)}) collective-permute-start(f32[9,32,256]{2,1,0:T(8,128)S(1)} %pad_maximum_fusion.3), channel_id=1, source_target_pairs={{0,2},{1,5},{2,0},{3,7},{4,6},{5,1},{6,4},{7,3},{8,10},{9,13},{10,... | collective-permute-start | bytes 884744 | tf_op jit(solution)/shard_map/ppermute | solution.py:76
  125.5 2.3 %collective-permute-start.17 = (f32[9,32,512]{2,1,0:T(8,128)}, f32[9,32,512]{2,1,0:T(8,128)}, u32[]{:S(2)}, u32[]{:S(2)}) collective-permute-start(f32[9,32,512]{2,1,0:T(8,128)} %pad_maximum_fusion.1), channel_id=1, source_target_pairs={{0,1},{1,0},{2,3},{3,2},{4,5},{5,4},{6,7},{7,6},{8,9},{9,8},{10,11... | collective-permute-start | bytes 1769480 | tf_op jit(solution)/shard_map/ppermute | solution.py:76

commit v4 on v3

--- a/solution.py
+++ b/solution.py
@@ -39,7 +39,7 @@
     return plan
 
 
-def table_sum(x, n_rep, n_own):
+def table_rows(x, rows, n_rep, n_own):
     axes = ("rep", "own")
     count = n_rep * n_own
     index = lax.axis_index("rep") * n_own + lax.axis_index("own")
@@ -72,11 +72,17 @@
         bits.append(bit)
     for p0, p1 in pairing:
         cur = cur + lax.ppermute(cur, axes, perm_of(p0, p1))
-    for (p0, p1), axis, bit in reversed(list(zip(halving, plan, bits))):
+    steps_back = list(reversed(list(zip(halving, plan, bits))))
+    for index_step, ((p0, p1), axis, bit) in enumerate(steps_back):
         other = lax.ppermute(cur, axes, perm_of(p0, p1))
+        if index_step == len(steps_back) - 1:
+            cur = jnp.take(cur, rows, axis=0)
+            other = jnp.take(other, rows, axis=0)
         low = jnp.where(bit == 0, cur, other)
         high = jnp.where(bit == 0, other, cur)
         cur = jnp.concatenate([low, high], axis=axis)
+    if not steps_back:
+        cur = jnp.take(cur, rows, axis=0)
     return cur
 
 
@@ -110,8 +116,7 @@
     first_ortho = jnp.einsum("tks,tsa->tka", first_left, mix_first, precision=TOP_PRECISION)
     first_parts = jnp.einsum("tkd,tks->tsd", combined, first_ortho, precision=TOP_PRECISION)
     first_table = jnp.einsum("tm,tsd->msd", selector, first_parts, precision=TOP_PRECISION)
-    first_table = table_sum(first_table, replicas, n_own) / replicas
-    first_rows = jnp.take(first_table, tile_matrix, axis=0)
+    first_rows = table_rows(first_table, tile_matrix, replicas, n_own) / replicas
     mix_right = jnp.take(inverse_gram_factors[1], tile_matrix, axis=0)
     right_rows = jnp.einsum("tjw,tjd->twd", mix_right, first_rows, precision=TOP_PRECISION)
     second_local = jnp.einsum("tkd,tsd->tks", combined, right_rows, precision=TOP_PRECISION)
@@ -120,8 +125,7 @@
     second_ortho = jnp.einsum("tks,tsa->tka", second_left, mix_second, precision=TOP_PRECISION)
     second_parts = jnp.einsum("tkd,tks->tsd", combined, second_ortho, precision=TOP_PRECISION)
     second_table = jnp.einsum("tm,tsd->msd", selector, second_parts, precision=TOP_PRECISION)
-    second_table = table_sum(second_table, replicas, n_own) / replicas
-    back_rows = jnp.take(second_table, tile_matrix, axis=0)
+    back_rows = table_rows(second_table, tile_matrix, replicas, n_own) / replicas
     approximation = jnp.einsum("tks,tsd->tkd", second_ortho, back_rows, precision=TOP_PRECISION)
     new_feedback = (combined - approximation)[None]
     group_select = (

time: 136 us -> 166 us (1.22)
  waiting for transfers between devices: 62.1 us -> 89.9 us
  local copies, waits for them, and re-layouts: 14.8 us -> 17.3 us
    ppermute x16, waiting for transfers between devices: 61.1 us -> 88.7 us  [the longest x4 31.9 us: table_rows(): cur = cur + lax.ppermute(cur, axes, perm_of(p0, p1))]
    div x2 -> x0, other arithmetic: 2.27 us -> none  [the longest x1 1.14 us: local(): first_table = table_sum(first_table, replicas, n_own) / replicas]
    gather x2 -> x4, local copies, waits for them, and re-layouts: 3.7 us -> 5.78 us  [the longest x2 3.25 us: table_rows(): other = jnp.take(other, rows, axis=0)]
    dynamic_slice x8, local copies, waits for them, and re-layouts: 2.93 us -> 1.02 us  [table_rows(): send = lax.dynamic_slice_in_dim(cur, (1 - bit) * half, half, axis)]
    unnamed x18 -> x22, local copies, waits for them, and re-layouts: 2.15 us -> 3.77 us
  transfers between devices with their start and end apart: 18 -> 18, of which waited for: 17 -> 15; matrix products, arithmetic and copies ran while one was open for 5% -> 6% of each run, Pallas kernels for 0% -> 0%
where the time goes in v4:
time: 166 us; the launch traced here: 165 us
  waiting for transfers between devices  89.9 us (54%)
  starting transfers between devices  31.7 us (19%)
  local copies, waits for them, and re-layouts  17.3 us (10%)
  other arithmetic  13.2 us (8%)
  matrix products  11.9 us (7%)
    ppermute x4, waiting for transfers between devices, table_rows(): cur = cur + lax.ppermute(cur, axes, perm_of(p0, p1))  31.9 us
    ppermute x6, waiting for transfers between devices, table_rows(): other = lax.ppermute(cur, axes, perm_of(p0, p1))  28.8 us
    ppermute x6, waiting for transfers between devices, table_rows(): cur = keep + lax.ppermute(send, axes, perm_of(p0, p1))  28 us
    ppermute x4, starting transfers between devices, table_rows(): cur = cur + lax.ppermute(cur, axes, perm_of(p0, p1))  10.2 us
    ppermute x6, starting transfers between devices, table_rows(): cur = keep + lax.ppermute(send, axes, perm_of(p0, p1))  8.4 us
    ppermute x6, starting transfers between devices, table_rows(): other = lax.ppermute(cur, axes, perm_of(p0, p1))  8.16 us
    ppermute x2, starting transfers between devices, swap_sum(): x = x + lax.ppermute(x, axis, _pair_perm(n, j))  4.85 us
    add x6, other arithmetic, table_rows(): cur = keep + lax.ppermute(send, axes, perm_of(p0, p1))  4.65 us
  transfers between devices with their start and end apart: 18, of which 15 were waited for; matrix products, arithmetic and copies ran while one was open for 6% of the time, Pallas kernels for 0%

profile of v4, /device:TPU:0, one launch (start us, length us, event | category | flops | bytes accessed | tf_op | source)
XLA Modules:
  0.0 165.1 jit_solution(3622710604670193519)
XLA Ops:
  4.7 3.0 %collective-permute-start = (f32[13312]{0:T(1024)S(1)}, f32[13312]{0:T(1024)S(1)}, u32[]{:S(2)}, u32[]{:S(2)}) collective-permute-start(f32[13312]{0:T(1024)S(1)} %pad_maximum_fusion.4), channel_id=1, source_target_pairs={{0,16},{16,0},{1,17},{17,1},{2,18},{18,2},{3,19},{19,3},{4,20},{20... | collective-permute-start | bytes 159752 | tf_op jit(solution)/shard_map/ppermute | solution.py:20
  7.7 1.8 %slice_bitcast_fusion.2 = (f32[9,32,32]{2,1,0:T(8,128)}, f32[9,32,32]{2,1,0:T(8,128)}, f32[9,32,32]{2,1,0:T(8,128)S(1)}) fusion(f32[3,9,32,32]{3,2,1,0:T(8,128)} %param.21), kind=kLoop, calls=%fused_computation.59 | loop fusion | bytes 221184 | tf_op jit(solution)/shard_map/squeeze | solution.py:120
  15.2 2.1 %collective-permute-done.1 = f32[9,32,512]{2,1,0:T(8,128)} collective-permute-done((f32[9,32,512]{2,1,0:T(8,128)S(1)}, f32[9,32,512]{2,1,0:T(8,128)}, u32[]{:S(2)}, u32[]{:S(2)}) %collective-permute-start.1) | collective-permute-done | bytes 589856 | tf_op jit(solution)/shard_map/ppermute | solution.py:71
  17.3 1.8 %copy_add_fusion.1 = f32[9,32,512]{2,0,1:T(8,128)S(1)} fusion(f32[9,32,512]{2,1,0:T(8,128)} %collective-permute-done.1, f32[9,32,1024]{2,0,1:T(8,128)} %copy-done.3, s32[]{:T(128)S(6)} %select_n.123), kind=kLoop, calls=%fused_computation.23 | loop fusion | flops 147456 | bytes 1769476 | tf_op jit(solution)/shard_map/add | solution.py:71
  20.2 1.9 %collective-permute-start.2 = (f32[9,32,256]{2,0,1:T(8,128)S(1)}, f32[9,32,256]{2,0,1:T(8,128)}, u32[]{:S(2)}, u32[]{:S(2)}) collective-permute-start(f32[9,32,256]{2,0,1:T(8,128)S(1)} %constant_dynamic-slice_fusion.4), channel_id=1, source_target_pairs={{0,2},{1,5},{2,0},{3,7},{4,6},{5,1},{6,4},{7,3},{8,10},{9,13},{10,... | collective-permute-start | bytes 884744 | tf_op jit(solution)/shard_map/ppermute | solution.py:71
  22.0 7.5 %collective-permute-done.2 = f32[9,32,256]{2,0,1:T(8,128)} collective-permute-done((f32[9,32,256]{2,0,1:T(8,128)S(1)}, f32[9,32,256]{2,0,1:T(8,128)}, u32[]{:S(2)}, u32[]{:S(2)}) %collective-permute-start.2) | collective-permute-done | bytes 294944 | tf_op jit(solution)/shard_map/ppermute | solution.py:71
  30.8 1.9 %collective-permute-start.3 = (f32[9,32,128]{2,0,1:T(8,128)S(1)}, f32[9,32,128]{2,0,1:T(8,128)}, u32[]{:S(2)}, u32[]{:S(2)}) collective-permute-start(f32[9,32,128]{2,0,1:T(8,128)S(1)} %constant_dynamic-slice_fusion.3), channel_id=1, source_target_pairs={{0,4},{1,3},{2,6},{3,1},{4,0},{5,7},{6,2},{7,5},{8,12},{9,11},{10,... | collective-permute-start | bytes 442376 | tf_op jit(solution)/shard_map/ppermute | solution.py:71
  32.8 4.6 %collective-permute-done.3 = f32[9,32,128]{2,0,1:T(8,128)} collective-permute-done((f32[9,32,128]{2,0,1:T(8,128)S(1)}, f32[9,32,128]{2,0,1:T(8,128)}, u32[]{:S(2)}, u32[]{:S(2)}) %collective-permute-start.3) | collective-permute-done | bytes 147488 | tf_op jit(solution)/shard_map/ppermute | solution.py:71
  38.4 2.9 %collective-permute-start.4 = (f32[9,32,128]{2,0,1:T(8,128)S(1)}, f32[9,32,128]{2,0,1:T(8,128)S(1)}, u32[]{:S(2)}, u32[]{:S(2)}) collective-permute-start(f32[9,32,128]{2,0,1:T(8,128)S(1)} %dynamic-slice_add_fusion.3), channel_id=1, source_target_pairs={{0,8},{1,17},{2,10},{3,19},{4,12},{5,21},{6,14},{7,23},{8,0},{9,25... | collective-permute-start | bytes 442376 | tf_op jit(solution)/shard_map/ppermute | solution.py:74
  41.3 11.4 %collective-permute-done.4 = f32[9,32,128]{2,0,1:T(8,128)S(1)} collective-permute-done((f32[9,32,128]{2,0,1:T(8,128)S(1)}, f32[9,32,128]{2,0,1:T(8,128)S(1)}, u32[]{:S(2)}, u32[]{:S(2)}) %collective-permute-start.4) | collective-permute-done | bytes 147488 | tf_op jit(solution)/shard_map/ppermute | solution.py:74
  52.8 2.1 %collective-permute-start.5 = (f32[9,32,128]{2,0,1:T(8,128)S(1)}, f32[9,32,128]{2,0,1:T(8,128)S(1)}, u32[]{:S(2)}, u32[]{:S(2)}) collective-permute-start(f32[9,32,128]{2,0,1:T(8,128)S(1)} %add.100), channel_id=1, source_target_pairs={{0,16},{1,9},{2,18},{3,11},{4,20},{5,13},{6,22},{7,15},{8,24},{9,1... | collective-permute-start | bytes 442376 | tf_op jit(solution)/shard_map/ppermute | solution.py:74
  54.9 4.4 %collective-permute-done.5 = f32[9,32,128]{2,0,1:T(8,128)S(1)} collective-permute-done((f32[9,32,128]{2,0,1:T(8,128)S(1)}, f32[9,32,128]{2,0,1:T(8,128)S(1)}, u32[]{:S(2)}, u32[]{:S(2)}) %collective-permute-start.5) | collective-permute-done | bytes 147488 | tf_op jit(solution)/shard_map/ppermute | solution.py:74
  59.3 2.3 %collective-permute-start.6 = (f32[9,32,128]{2,0,1:T(8,128)S(1)}, f32[9,32,128]{2,0,1:T(8,128)}, u32[]{:S(2)}, u32[]{:S(2)}) collective-permute-start(f32[9,32,128]{2,0,1:T(8,128)S(1)} %add.101), channel_id=1, source_target_pairs={{0,4},{1,3},{2,6},{3,1},{4,0},{5,7},{6,2},{7,5},{8,12},{9,11},{10,... | collective-permute-start | bytes 442376 | tf_op jit(solution)/shard_map/ppermute | solution.py:77
  61.6 6.3 %collective-permute-done.6 = f32[9,32,128]{2,0,1:T(8,128)} collective-permute-done((f32[9,32,128]{2,0,1:T(8,128)S(1)}, f32[9,32,128]{2,0,1:T(8,128)}, u32[]{:S(2)}, u32[]{:S(2)}) %collective-permute-start.6) | collective-permute-done | bytes 147488 | tf_op jit(solution)/shard_map/ppermute | solution.py:77
  69.7 1.8 %collective-permute-start.7 = (f32[9,32,256]{2,0,1:T(8,128)}, f32[9,32,256]{2,0,1:T(8,128)}, u32[]{:S(2)}, u32[]{:S(2)}) collective-permute-start(f32[9,32,256]{2,0,1:T(8,128)} %pad_maximum_fusion.2), channel_id=1, source_target_pairs={{0,2},{1,5},{2,0},{3,7},{4,6},{5,1},{6,4},{7,3},{8,10},{9,13},{10,... | collective-permute-start | bytes 884744 | tf_op jit(solution)/shard_map/ppermute | solution.py:77
  71.5 7.7 %collective-permute-done.7 = f32[9,32,256]{2,0,1:T(8,128)} collective-permute-done((f32[9,32,256]{2,0,1:T(8,128)}, f32[9,32,256]{2,0,1:T(8,128)}, u32[]{:S(2)}, u32[]{:S(2)}) %collective-permute-start.7) | collective-permute-done | bytes 294944 | tf_op jit(solution)/shard_map/ppermute | solution.py:77
  83.7 1.6 gather_fusion.4
  88.2 1.8 %collective-permute-start.9 = (f32[4,64,32]{1,2,0:T(8,128)S(1)}, f32[4,64,32]{1,2,0:T(8,128)S(1)}, u32[]{:S(2)}, u32[]{:S(2)}) collective-permute-start(f32[4,64,32]{1,2,0:T(8,128)S(1)} %fusion.2), channel_id=1, source_target_pairs={{0,16},{16,0},{1,17},{17,1},{2,18},{18,2},{3,19},{19,3},{4,20},{20... | collective-permute-start | bytes 98312 | tf_op jit(solution)/shard_map/ppermute | solution.py:20
  95.7 2.0 %collective-permute-done.10 = f32[9,32,512]{2,1,0:T(8,128)S(1)} collective-permute-done((f32[9,32,512]{2,1,0:T(8,128)S(1)}, f32[9,32,512]{2,1,0:T(8,128)S(1)}, u32[]{:S(2)}, u32[]{:S(2)}) %collective-permute-start.10) | collective-permute-done | bytes 589856 | tf_op jit(solution)/shard_map/ppermute | solution.py:71
  98.2 1.8 %collective-permute-start.11 = (f32[9,32,256]{2,0,1:T(8,128)S(1)}, f32[9,32,256]{2,0,1:T(8,128)S(1)}, u32[]{:S(2)}, u32[]{:S(2)}) collective-permute-start(f32[9,32,256]{2,0,1:T(8,128)S(1)} %constant_dynamic-slice_fusion.1), channel_id=1, source_target_pairs={{0,2},{1,5},{2,0},{3,7},{4,6},{5,1},{6,4},{7,3},{8,10},{9,13},{10,... | collective-permute-start | bytes 884744 | tf_op jit(solution)/shard_map/ppermute | solution.py:71
  100.0 7.4 %collective-permute-done.11 = f32[9,32,256]{2,0,1:T(8,128)S(1)} collective-permute-done((f32[9,32,256]{2,0,1:T(8,128)S(1)}, f32[9,32,256]{2,0,1:T(8,128)S(1)}, u32[]{:S(2)}, u32[]{:S(2)}) %collective-permute-start.11) | collective-permute-done | bytes 294944 | tf_op jit(solution)/shard_map/ppermute | solution.py:71
  107.6 2.6 %collective-permute-start.12 = (f32[9,32,128]{2,0,1:T(8,128)S(1)}, f32[9,32,128]{2,0,1:T(8,128)S(1)}, u32[]{:S(2)}, u32[]{:S(2)}) collective-permute-start(f32[9,32,128]{2,0,1:T(8,128)S(1)} %constant_dynamic-slice_fusion), channel_id=1, source_target_pairs={{0,4},{1,3},{2,6},{3,1},{4,0},{5,7},{6,2},{7,5},{8,12},{9,11},{10,... | collective-permute-start | bytes 442376 | tf_op jit(solution)/shard_map/ppermute | solution.py:71
  110.2 4.4 %collective-permute-done.12 = f32[9,32,128]{2,0,1:T(8,128)S(1)} collective-permute-done((f32[9,32,128]{2,0,1:T(8,128)S(1)}, f32[9,32,128]{2,0,1:T(8,128)S(1)}, u32[]{:S(2)}, u32[]{:S(2)}) %collective-permute-start.12) | collective-permute-done | bytes 147488 | tf_op jit(solution)/shard_map/ppermute | solution.py:71
  114.6 3.6 %collective-permute-start.13 = (f32[9,32,128]{2,0,1:T(8,128)S(1)}, f32[9,32,128]{2,0,1:T(8,128)S(1)}, u32[]{:S(2)}, u32[]{:S(2)}) collective-permute-start(f32[9,32,128]{2,0,1:T(8,128)S(1)} %dynamic-slice_add_fusion.2), channel_id=1, source_target_pairs={{0,8},{1,17},{2,10},{3,19},{4,12},{5,21},{6,14},{7,23},{8,0},{9,25... | collective-permute-start | bytes 442376 | tf_op jit(solution)/shard_map/ppermute | solution.py:74
  118.2 11.2 %collective-permute-done.13 = f32[9,32,128]{2,0,1:T(8,128)S(1)} collective-permute-done((f32[9,32,128]{2,0,1:T(8,128)S(1)}, f32[9,32,128]{2,0,1:T(8,128)S(1)}, u32[]{:S(2)}, u32[]{:S(2)}) %collective-permute-start.13) | collective-permute-done | bytes 147488 | tf_op jit(solution)/shard_map/ppermute | solution.py:74
  131.0 4.9 %collective-permute-done.14 = f32[9,32,128]{2,0,1:T(8,128)S(1)} collective-permute-done((f32[9,32,128]{2,0,1:T(8,128)S(1)}, f32[9,32,128]{2,0,1:T(8,128)S(1)}, u32[]{:S(2)}, u32[]{:S(2)}) %collective-permute-start.14) | collective-permute-done | bytes 147488 | tf_op jit(solution)/shard_map/ppermute | solution.py:74
  135.9 2.4 %collective-permute-start.15 = (f32[9,32,128]{2,0,1:T(8,128)S(1)}, f32[9,32,128]{2,0,1:T(8,128)S(1)}, u32[]{:S(2)}, u32[]{:S(2)}) collective-permute-start(f32[9,32,128]{2,0,1:T(8,128)S(1)} %add.107), channel_id=1, source_target_pairs={{0,4},{1,3},{2,6},{3,1},{4,0},{5,7},{6,2},{7,5},{8,12},{9,11},{10,... | collective-permute-start | bytes 442376 | tf_op jit(solution)/shard_map/ppermute | solution.py:77
  138.3 7.2 %collective-permute-done.15 = f32[9,32,128]{2,0,1:T(8,128)S(1)} collective-permute-done((f32[9,32,128]{2,0,1:T(8,128)S(1)}, f32[9,32,128]{2,0,1:T(8,128)S(1)}, u32[]{:S(2)}, u32[]{:S(2)}) %collective-permute-start.15) | collective-permute-done | bytes 147488 | tf_op jit(solution)/shard_map/ppermute | solution.py:77
  145.5 1.6 collective-permute-start.16
  147.1 7.7 %collective-permute-done.16 = f32[9,32,256]{2,0,1:T(8,128)S(1)} collective-permute-done((f32[9,32,256]{2,0,1:T(8,128)S(1)}, f32[9,32,256]{2,0,1:T(8,128)S(1)}, u32[]{:S(2)}, u32[]{:S(2)}) %collective-permute-start.16) | collective-permute-done | bytes 294944 | tf_op jit(solution)/shard_map/ppermute | solution.py:77
  158.6 1.6 gather_fusion.7
  161.3 3.7 %multiply_add_fusion = (f32[4,64,1024]{2,1,0:T(8,128)}, f32[1,4,64,1024]{3,2,1,0:T(8,128)}) fusion(f32[4,64,1024]{2,1,0:T(8,128)} %param.16, f32[4]{0:T(128)S(1)} %convolution_bitcast_fusion, f32[1,4,64,1024]{3,2,1,0:T(8,128)S(1)} %copy-done.1, bf16[1,4,64,1024]{3,2,1,0:T(8,128)(2,1)S(1)} %copy-done.2, f32[4,64,32]{1,2,0:T(8,128)S(1)} %fusion.24, ...), kind=kOutput, calls=%fused_computation.24 | convolution fusion | flops 102498304 | bytes 5275664 | tf_op jit(solution)/shard_map/tks,tsd->tkd/dot_general | solution.py:129
  (88 shorter events, 34.9 us)
Async XLA Ops:
  0.6 1.4 copy-start
  2.1 1.2 copy-start.1
  2.1 1.3 copy-start.2
  3.4 1.3 copy-start.6
  4.6 7.4 %copy-start.8 = (s32[4]{0:T(128)S(1)}, s32[4]{0:T(128)}, u32[]{:S(2)}) copy-start(s32[4]{0:T(128)} %param.17) | copy-start | bytes 52
  4.7 5.4 %collective-permute-start = (f32[13312]{0:T(1024)S(1)}, f32[13312]{0:T(1024)S(1)}, u32[]{:S(2)}, u32[]{:S(2)}) collective-permute-start(f32[13312]{0:T(1024)S(1)} %pad_maximum_fusion.4), channel_id=1, source_target_pairs={{0,16},{16,0},{1,17},{17,1},{2,18},{18,2},{3,19},{19,3},{4,20},{20... | collective-permute-start | bytes 159752 | tf_op jit(solution)/shard_map/ppermute | solution.py:20
  10.1 0.6 copy-start.5
  13.3 1.3 copy-start.3
  15.1 2.2 %collective-permute-start.1 = (f32[9,32,512]{2,1,0:T(8,128)S(1)}, f32[9,32,512]{2,1,0:T(8,128)}, u32[]{:S(2)}, u32[]{:S(2)}) collective-permute-start(f32[9,32,512]{2,1,0:T(8,128)S(1)} %copy.25), channel_id=1, source_target_pairs={{0,1},{1,0},{2,3},{3,2},{4,5},{5,4},{6,7},{7,6},{8,9},{9,8},{10,11... | collective-permute-start | bytes 1769480 | tf_op jit(solution)/shard_map/ppermute | solution.py:71
  19.2 1.0 copy-start.4
  20.2 9.4 %collective-permute-start.2 = (f32[9,32,256]{2,0,1:T(8,128)S(1)}, f32[9,32,256]{2,0,1:T(8,128)}, u32[]{:S(2)}, u32[]{:S(2)}) collective-permute-start(f32[9,32,256]{2,0,1:T(8,128)S(1)} %constant_dynamic-slice_fusion.4), channel_id=1, source_target_pairs={{0,2},{1,5},{2,0},{3,7},{4,6},{5,1},{6,4},{7,3},{8,10},{9,13},{10,... | collective-permute-start | bytes 884744 | tf_op jit(solution)/shard_map/ppermute | solution.py:71
  30.8 6.5 %collective-permute-start.3 = (f32[9,32,128]{2,0,1:T(8,128)S(1)}, f32[9,32,128]{2,0,1:T(8,128)}, u32[]{:S(2)}, u32[]{:S(2)}) collective-permute-start(f32[9,32,128]{2,0,1:T(8,128)S(1)} %constant_dynamic-slice_fusion.3), channel_id=1, source_target_pairs={{0,4},{1,3},{2,6},{3,1},{4,0},{5,7},{6,2},{7,5},{8,12},{9,11},{10,... | collective-permute-start | bytes 442376 | tf_op jit(solution)/shard_map/ppermute | solution.py:71
  38.4 14.4 %collective-permute-start.4 = (f32[9,32,128]{2,0,1:T(8,128)S(1)}, f32[9,32,128]{2,0,1:T(8,128)S(1)}, u32[]{:S(2)}, u32[]{:S(2)}) collective-permute-start(f32[9,32,128]{2,0,1:T(8,128)S(1)} %dynamic-slice_add_fusion.3), channel_id=1, source_target_pairs={{0,8},{1,17},{2,10},{3,19},{4,12},{5,21},{6,14},{7,23},{8,0},{9,25... | collective-permute-start | bytes 442376 | tf_op jit(solution)/shard_map/ppermute | solution.py:74
  52.8 6.5 %collective-permute-start.5 = (f32[9,32,128]{2,0,1:T(8,128)S(1)}, f32[9,32,128]{2,0,1:T(8,128)S(1)}, u32[]{:S(2)}, u32[]{:S(2)}) collective-permute-start(f32[9,32,128]{2,0,1:T(8,128)S(1)} %add.100), channel_id=1, source_target_pairs={{0,16},{1,9},{2,18},{3,11},{4,20},{5,13},{6,22},{7,15},{8,24},{9,1... | collective-permute-start | bytes 442376 | tf_op jit(solution)/shard_map/ppermute | solution.py:74
  59.3 8.6 %collective-permute-start.6 = (f32[9,32,128]{2,0,1:T(8,128)S(1)}, f32[9,32,128]{2,0,1:T(8,128)}, u32[]{:S(2)}, u32[]{:S(2)}) collective-permute-start(f32[9,32,128]{2,0,1:T(8,128)S(1)} %add.101), channel_id=1, source_target_pairs={{0,4},{1,3},{2,6},{3,1},{4,0},{5,7},{6,2},{7,5},{8,12},{9,11},{10,... | collective-permute-start | bytes 442376 | tf_op jit(solution)/shard_map/ppermute | solution.py:77
  69.7 9.5 %collective-permute-start.7 = (f32[9,32,256]{2,0,1:T(8,128)}, f32[9,32,256]{2,0,1:T(8,128)}, u32[]{:S(2)}, u32[]{:S(2)}) collective-permute-start(f32[9,32,256]{2,0,1:T(8,128)} %pad_maximum_fusion.2), channel_id=1, source_target_pairs={{0,2},{1,5},{2,0},{3,7},{4,6},{5,1},{6,4},{7,3},{8,10},{9,13},{10,... | collective-permute-start | bytes 884744 | tf_op jit(solution)/shard_map/ppermute | solution.py:77
  80.9 2.8 %collective-permute-start.8 = (f32[9,32,512]{2,1,0:T(8,128)S(1)}, f32[9,32,512]{2,1,0:T(8,128)}, u32[]{:S(2)}, u32[]{:S(2)}) collective-permute-start(f32[9,32,512]{2,1,0:T(8,128)S(1)} %copy.27), channel_id=1, source_target_pairs={{0,1},{1,0},{2,3},{3,2},{4,5},{5,4},{6,7},{7,6},{8,9},{9,8},{10,11... | collective-permute-start | bytes 1769480 | tf_op jit(solution)/shard_map/ppermute | solution.py:77
  88.2 4.6 %collective-permute-start.9 = (f32[4,64,32]{1,2,0:T(8,128)S(1)}, f32[4,64,32]{1,2,0:T(8,128)S(1)}, u32[]{:S(2)}, u32[]{:S(2)}) collective-permute-start(f32[4,64,32]{1,2,0:T(8,128)S(1)} %fusion.2), channel_id=1, source_target_pairs={{0,16},{16,0},{1,17},{17,1},{2,18},{18,2},{3,19},{19,3},{4,20},{20... | collective-permute-start | bytes 98312 | tf_op jit(solution)/shard_map/ppermute | solution.py:20
  95.6 2.1 %collective-permute-start.10 = (f32[9,32,512]{2,1,0:T(8,128)S(1)}, f32[9,32,512]{2,1,0:T(8,128)S(1)}, u32[]{:S(2)}, u32[]{:S(2)}) collective-permute-start(f32[9,32,512]{2,1,0:T(8,128)S(1)} %copy.32), channel_id=1, source_target_pairs={{0,1},{1,0},{2,3},{3,2},{4,5},{5,4},{6,7},{7,6},{8,9},{9,8},{10,11... | collective-permute-start | bytes 1769480 | tf_op jit(solution)/shard_map/ppermute | solution.py:71
  98.2 9.2 %collective-permute-start.11 = (f32[9,32,256]{2,0,1:T(8,128)S(1)}, f32[9,32,256]{2,0,1:T(8,128)S(1)}, u32[]{:S(2)}, u32[]{:S(2)}) collective-permute-start(f32[9,32,256]{2,0,1:T(8,128)S(1)} %constant_dynamic-slice_fusion.1), channel_id=1, source_target_pairs={{0,2},{1,5},{2,0},{3,7},{4,6},{5,1},{6,4},{7,3},{8,10},{9,13},{10,... | collective-permute-start | bytes 884744 | tf_op jit(solution)/shard_map/ppermute | solution.py:71
  107.6 7.0 %collective-permute-start.12 = (f32[9,32,128]{2,0,1:T(8,128)S(1)}, f32[9,32,128]{2,0,1:T(8,128)S(1)}, u32[]{:S(2)}, u32[]{:S(2)}) collective-permute-start(f32[9,32,128]{2,0,1:T(8,128)S(1)} %constant_dynamic-slice_fusion), channel_id=1, source_target_pairs={{0,4},{1,3},{2,6},{3,1},{4,0},{5,7},{6,2},{7,5},{8,12},{9,11},{10,... | collective-permute-start | bytes 442376 | tf_op jit(solution)/shard_map/ppermute | solution.py:71
  114.6 14.9 %collective-permute-start.13 = (f32[9,32,128]{2,0,1:T(8,128)S(1)}, f32[9,32,128]{2,0,1:T(8,128)S(1)}, u32[]{:S(2)}, u32[]{:S(2)}) collective-permute-start(f32[9,32,128]{2,0,1:T(8,128)S(1)} %dynamic-slice_add_fusion.2), channel_id=1, source_target_pairs={{0,8},{1,17},{2,10},{3,19},{4,12},{5,21},{6,14},{7,23},{8,0},{9,25... | collective-permute-start | bytes 442376 | tf_op jit(solution)/shard_map/ppermute | solution.py:74
  129.5 6.4 %collective-permute-start.14 = (f32[9,32,128]{2,0,1:T(8,128)S(1)}, f32[9,32,128]{2,0,1:T(8,128)S(1)}, u32[]{:S(2)}, u32[]{:S(2)}) collective-permute-start(f32[9,32,128]{2,0,1:T(8,128)S(1)} %add.106), channel_id=1, source_target_pairs={{0,16},{1,9},{2,18},{3,11},{4,20},{5,13},{6,22},{7,15},{8,24},{9,1... | collective-permute-start | bytes 442376 | tf_op jit(solution)/shard_map/ppermute | solution.py:74
  135.9 9.5 %collective-permute-start.15 = (f32[9,32,128]{2,0,1:T(8,128)S(1)}, f32[9,32,128]{2,0,1:T(8,128)S(1)}, u32[]{:S(2)}, u32[]{:S(2)}) collective-permute-start(f32[9,32,128]{2,0,1:T(8,128)S(1)} %add.107), channel_id=1, source_target_pairs={{0,4},{1,3},{2,6},{3,1},{4,0},{5,7},{6,2},{7,5},{8,12},{9,11},{10,... | collective-permute-start | bytes 442376 | tf_op jit(solution)/shard_map/ppermute | solution.py:77
  145.5 9.2 %collective-permute-start.16 = (f32[9,32,256]{2,0,1:T(8,128)S(1)}, f32[9,32,256]{2,0,1:T(8,128)S(1)}, u32[]{:S(2)}, u32[]{:S(2)}) collective-permute-start(f32[9,32,256]{2,0,1:T(8,128)S(1)} %pad_maximum_fusion.3), channel_id=1, source_target_pairs={{0,2},{1,5},{2,0},{3,7},{4,6},{5,1},{6,4},{7,3},{8,10},{9,13},{10,... | collective-permute-start | bytes 884744 | tf_op jit(solution)/shard_map/ppermute | solution.py:77
  154.9 0.7 copy-start.9
  154.9 0.7 copy-start.10
  154.9 1.8 %copy-start.7 = (f32[5,1024]{1,0:T(8,128)S(1)}, f32[5,1024]{1,0:T(8,128)}, u32[]{:S(2)}) copy-start(f32[5,1024]{1,0:T(8,128)} %param.23) | copy-start | bytes 61444
  155.5 3.2 %collective-permute-start.17 = (f32[9,32,512]{2,1,0:T(8,128)S(1)}, f32[9,32,512]{2,1,0:T(8,128)}, u32[]{:S(2)}, u32[]{:S(2)}) collective-permute-start(f32[9,32,512]{2,1,0:T(8,128)S(1)} %copy.34), channel_id=1, source_target_pairs={{0,1},{1,0},{2,3},{3,2},{4,5},{5,4},{6,7},{7,6},{8,9},{9,8},{10,11... | collective-permute-start | bytes 1769480 | tf_op jit(solution)/shard_map/ppermute | solution.py:77

commit v5 on v4

--- a/solution.py
+++ b/solution.py
@@ -39,6 +39,10 @@
     return plan
 
 
+def _pick_rows(table, rows):
+    return jnp.stack([lax.dynamic_index_in_dim(table, rows[i], 0, keepdims=False) for i in range(rows.shape[0])])
+
+
 def table_rows(x, rows, n_rep, n_own):
     axes = ("rep", "own")
     count = n_rep * n_own
@@ -76,13 +80,13 @@
     for index_step, ((p0, p1), axis, bit) in enumerate(steps_back):
         other = lax.ppermute(cur, axes, perm_of(p0, p1))
         if index_step == len(steps_back) - 1:
-            cur = jnp.take(cur, rows, axis=0)
-            other = jnp.take(other, rows, axis=0)
+            cur = _pick_rows(cur, rows)
+            other = _pick_rows(other, rows)
         low = jnp.where(bit == 0, cur, other)
         high = jnp.where(bit == 0, other, cur)
         cur = jnp.concatenate([low, high], axis=axis)
     if not steps_back:
-        cur = jnp.take(cur, rows, axis=0)
+        cur = _pick_rows(cur, rows)
     return cur
 
 

time: 166 us -> 137 us (0.83)
  waiting for transfers between devices: 89.9 us -> 61.6 us
  between operations: 1.12 us -> 8.69 us
  local copies, waits for them, and re-layouts: 17.3 us -> 13.7 us
  other arithmetic: 13.2 us -> 10.3 us
    ppermute x4, waiting for transfers between devices: 31.9 us -> 19.6 us  [table_rows(): cur = cur + lax.ppermute(cur, axes, perm_of(p0, p1))]
    ppermute x6, waiting for transfers between devices: 28.8 us -> 20 us  [table_rows(): other = lax.ppermute(cur, axes, perm_of(p0, p1))]
    ppermute x6, waiting for transfers between devices: 28 us -> 20.7 us  [table_rows(): cur = keep + lax.ppermute(send, axes, perm_of(p0, p1))]
    gather x4 -> x0, local copies, waits for them, and re-layouts: 5.78 us -> none  [the longest x2 3.25 us: table_rows(): other = jnp.take(other, rows, axis=0)]
    dynamic_slice x0 -> x4, local copies, waits for them, and re-layouts: none -> 3.35 us  [the longest x2 1.92 us: _pick_rows(): lax.dynamic_index_in_dim(table, rows[i], 0, keepdims=False)]
    select_n x6, other arithmetic: 4.46 us -> 1.25 us  [table_rows(): low = jnp.where(bit == 0, cur, other)]
    unnamed x22 -> x20, local copies, waits for them, and re-layouts: 3.77 us -> 2.16 us
  transfers between devices with their start and end apart: 18 -> 18, of which waited for: 15 -> 16; matrix products, arithmetic and copies ran while one was open for 6% -> 6% of each run, Pallas kernels for 0% -> 0%
where the time goes in v5:
time: 137 us; the launch traced here: 136 us
  waiting for transfers between devices  61.6 us (45%)
  starting transfers between devices  31 us (23%)
  local copies, waits for them, and re-layouts  13.7 us (10%)
  matrix products  10.7 us (8%)
  other arithmetic  10.3 us (8%)
  between operations  8.69 us (6%)
    ppermute x6, waiting for transfers between devices, table_rows(): cur = keep + lax.ppermute(send, axes, perm_of(p0, p1))  20.7 us
    ppermute x6, waiting for transfers between devices, table_rows(): other = lax.ppermute(cur, axes, perm_of(p0, p1))  20 us
    ppermute x4, waiting for transfers between devices, table_rows(): cur = cur + lax.ppermute(cur, axes, perm_of(p0, p1))  19.6 us
    ppermute x4, starting transfers between devices, table_rows(): cur = cur + lax.ppermute(cur, axes, perm_of(p0, p1))  10 us
    ppermute x6, starting transfers between devices, table_rows(): other = lax.ppermute(cur, axes, perm_of(p0, p1))  8.21 us
    ppermute x6, starting transfers between devices, table_rows(): cur = keep + lax.ppermute(send, axes, perm_of(p0, p1))  7.78 us
    ppermute x2, starting transfers between devices, swap_sum(): x = x + lax.ppermute(x, axis, _pair_perm(n, j))  4.92 us
    add x6, other arithmetic, table_rows(): cur = keep + lax.ppermute(send, axes, perm_of(p0, p1))  4.2 us
  transfers between devices with their start and end apart: 18, of which 16 were waited for; matrix products, arithmetic and copies ran while one was open for 6% of the time, Pallas kernels for 0%

profile of v5, /device:TPU:0, one launch (start us, length us, event | category | flops | bytes accessed | tf_op | source)
XLA Modules:
  0.0 135.9 jit_solution(12731355271626729492)
XLA Ops:
  4.7 3.0 %collective-permute-start = (f32[13312]{0:T(1024)S(1)}, f32[13312]{0:T(1024)S(1)}, u32[]{:S(2)}, u32[]{:S(2)}) collective-permute-start(f32[13312]{0:T(1024)S(1)} %pad_maximum_fusion.8), channel_id=1, source_target_pairs={{0,16},{16,0},{1,17},{17,1},{2,18},{18,2},{3,19},{19,3},{4,20},{20... | collective-permute-start | bytes 159752 | tf_op jit(solution)/shard_map/ppermute | solution.py:20
  7.7 1.8 %slice_bitcast_fusion.2 = (f32[9,32,32]{2,1,0:T(8,128)}, f32[9,32,32]{2,1,0:T(8,128)}, f32[9,32,32]{2,1,0:T(8,128)S(1)}) fusion(f32[3,9,32,32]{3,2,1,0:T(8,128)} %param.19), kind=kLoop, calls=%fused_computation.71 | loop fusion | bytes 221184 | tf_op jit(solution)/shard_map/squeeze | solution.py:124
  14.4 2.1 %collective-permute-done.1 = f32[9,32,512]{2,1,0:T(8,128)} collective-permute-done((f32[9,32,512]{2,1,0:T(8,128)S(1)}, f32[9,32,512]{2,1,0:T(8,128)}, u32[]{:S(2)}, u32[]{:S(2)}) %collective-permute-start.1) | collective-permute-done | bytes 589856 | tf_op jit(solution)/shard_map/ppermute | solution.py:75
  16.5 1.8 %copy_add_fusion.1 = f32[9,32,512]{2,1,0:T(8,128)S(1)} fusion(f32[9,32,512]{2,1,0:T(8,128)} %collective-permute-done.1, f32[9,32,512]{2,0,1:T(8,128)} %get-tuple-element.6), kind=kLoop, calls=%fused_computation.37 | loop fusion | flops 147456 | bytes 1769472 | tf_op jit(solution)/shard_map/add | solution.py:75
  19.0 1.8 %collective-permute-start.2 = (f32[9,32,256]{2,1,0:T(8,128)}, f32[9,32,256]{2,1,0:T(8,128)}, u32[]{:S(2)}, u32[]{:S(2)}) collective-permute-start(f32[9,32,256]{2,1,0:T(8,128)} %constant_dynamic-slice_fusion.13), channel_id=1, source_target_pairs={{0,2},{1,5},{2,0},{3,7},{4,6},{5,1},{6,4},{7,3},{8,10},{9,13},{10,... | collective-permute-start | bytes 884744 | tf_op jit(solution)/shard_map/ppermute | solution.py:75
  20.8 5.2 %collective-permute-done.2 = f32[9,32,256]{2,1,0:T(8,128)} collective-permute-done((f32[9,32,256]{2,1,0:T(8,128)}, f32[9,32,256]{2,1,0:T(8,128)}, u32[]{:S(2)}, u32[]{:S(2)}) %collective-permute-start.2) | collective-permute-done | bytes 294944 | tf_op jit(solution)/shard_map/ppermute | solution.py:75
  27.8 1.9 %collective-permute-start.3 = (f32[9,32,128]{2,1,0:T(8,128)S(1)}, f32[9,32,128]{2,1,0:T(8,128)S(1)}, u32[]{:S(2)}, u32[]{:S(2)}) collective-permute-start(f32[9,32,128]{2,1,0:T(8,128)S(1)} %constant_dynamic-slice_fusion.12), channel_id=1, source_target_pairs={{0,4},{1,3},{2,6},{3,1},{4,0},{5,7},{6,2},{7,5},{8,12},{9,11},{10,... | collective-permute-start | bytes 442376 | tf_op jit(solution)/shard_map/ppermute | solution.py:75
  29.7 3.3 %collective-permute-done.3 = f32[9,32,128]{2,1,0:T(8,128)S(1)} collective-permute-done((f32[9,32,128]{2,1,0:T(8,128)S(1)}, f32[9,32,128]{2,1,0:T(8,128)S(1)}, u32[]{:S(2)}, u32[]{:S(2)}) %collective-permute-start.3) | collective-permute-done | bytes 147488 | tf_op jit(solution)/shard_map/ppermute | solution.py:75
  33.9 2.9 %collective-permute-start.4 = (f32[9,32,128]{2,1,0:T(8,128)S(1)}, f32[9,32,128]{2,1,0:T(8,128)S(1)}, u32[]{:S(2)}, u32[]{:S(2)}) collective-permute-start(f32[9,32,128]{2,1,0:T(8,128)S(1)} %dynamic-slice_add_fusion.3), channel_id=1, source_target_pairs={{0,8},{1,17},{2,10},{3,19},{4,12},{5,21},{6,14},{7,23},{8,0},{9,25... | collective-permute-start | bytes 442376 | tf_op jit(solution)/shard_map/ppermute | solution.py:78
  36.9 6.5 %collective-permute-done.4 = f32[9,32,128]{2,1,0:T(8,128)S(1)} collective-permute-done((f32[9,32,128]{2,1,0:T(8,128)S(1)}, f32[9,32,128]{2,1,0:T(8,128)S(1)}, u32[]{:S(2)}, u32[]{:S(2)}) %collective-permute-start.4) | collective-permute-done | bytes 147488 | tf_op jit(solution)/shard_map/ppermute | solution.py:78
  43.4 2.1 %collective-permute-start.5 = (f32[9,32,128]{2,1,0:T(8,128)S(1)}, f32[9,32,128]{2,1,0:T(8,128)S(1)}, u32[]{:S(2)}, u32[]{:S(2)}) collective-permute-start(f32[9,32,128]{2,1,0:T(8,128)S(1)} %add.122), channel_id=1, source_target_pairs={{0,16},{1,9},{2,18},{3,11},{4,20},{5,13},{6,22},{7,15},{8,24},{9,1... | collective-permute-start | bytes 442376 | tf_op jit(solution)/shard_map/ppermute | solution.py:78
  45.5 3.1 %collective-permute-done.5 = f32[9,32,128]{2,1,0:T(8,128)S(1)} collective-permute-done((f32[9,32,128]{2,1,0:T(8,128)S(1)}, f32[9,32,128]{2,1,0:T(8,128)S(1)}, u32[]{:S(2)}, u32[]{:S(2)}) %collective-permute-start.5) | collective-permute-done | bytes 147488 | tf_op jit(solution)/shard_map/ppermute | solution.py:78
  48.7 2.3 %collective-permute-start.6 = (f32[9,32,128]{2,1,0:T(8,128)S(1)}, f32[9,32,128]{2,1,0:T(8,128)S(1)}, u32[]{:S(2)}, u32[]{:S(2)}) collective-permute-start(f32[9,32,128]{2,1,0:T(8,128)S(1)} %add.123), channel_id=1, source_target_pairs={{0,4},{1,3},{2,6},{3,1},{4,0},{5,7},{6,2},{7,5},{8,12},{9,11},{10,... | collective-permute-start | bytes 442376 | tf_op jit(solution)/shard_map/ppermute | solution.py:81
  51.0 4.7 %collective-permute-done.6 = f32[9,32,128]{2,1,0:T(8,128)S(1)} collective-permute-done((f32[9,32,128]{2,1,0:T(8,128)S(1)}, f32[9,32,128]{2,1,0:T(8,128)S(1)}, u32[]{:S(2)}, u32[]{:S(2)}) %collective-permute-start.6) | collective-permute-done | bytes 147488 | tf_op jit(solution)/shard_map/ppermute | solution.py:81
  56.4 1.9 %collective-permute-start.7 = (f32[9,32,256]{2,1,0:T(8,128)S(1)}, f32[9,32,256]{2,1,0:T(8,128)}, u32[]{:S(2)}, u32[]{:S(2)}) collective-permute-start(f32[9,32,256]{2,1,0:T(8,128)S(1)} %pad_maximum_fusion.2), channel_id=1, source_target_pairs={{0,2},{1,5},{2,0},{3,7},{4,6},{5,1},{6,4},{7,3},{8,10},{9,13},{10,... | collective-permute-start | bytes 884744 | tf_op jit(solution)/shard_map/ppermute | solution.py:81
  58.3 5.0 %collective-permute-done.7 = f32[9,32,256]{2,1,0:T(8,128)} collective-permute-done((f32[9,32,256]{2,1,0:T(8,128)S(1)}, f32[9,32,256]{2,1,0:T(8,128)}, u32[]{:S(2)}, u32[]{:S(2)}) %collective-permute-start.7) | collective-permute-done | bytes 294944 | tf_op jit(solution)/shard_map/ppermute | solution.py:81
  77.8 1.9 %collective-permute-start.9 = (f32[4,64,32]{1,2,0:T(8,128)S(1)}, f32[4,64,32]{1,2,0:T(8,128)S(1)}, u32[]{:S(2)}, u32[]{:S(2)}) collective-permute-start(f32[4,64,32]{1,2,0:T(8,128)S(1)} %fusion.2), channel_id=1, source_target_pairs={{0,16},{16,0},{1,17},{17,1},{2,18},{18,2},{3,19},{19,3},{4,20},{20... | collective-permute-start | bytes 98312 | tf_op jit(solution)/shard_map/ppermute | solution.py:20
  85.6 2.0 %collective-permute-done.10 = f32[9,32,512]{2,1,0:T(8,128)S(1)} collective-permute-done((f32[9,32,512]{2,1,0:T(8,128)S(1)}, f32[9,32,512]{2,1,0:T(8,128)S(1)}, u32[]{:S(2)}, u32[]{:S(2)}) %collective-permute-start.10) | collective-permute-done | bytes 589856 | tf_op jit(solution)/shard_map/ppermute | solution.py:75
  88.1 1.8 %collective-permute-start.11 = (f32[9,32,256]{2,1,0:T(8,128)S(1)}, f32[9,32,256]{2,1,0:T(8,128)S(1)}, u32[]{:S(2)}, u32[]{:S(2)}) collective-permute-start(f32[9,32,256]{2,1,0:T(8,128)S(1)} %constant_dynamic-slice_fusion.5), channel_id=1, source_target_pairs={{0,2},{1,5},{2,0},{3,7},{4,6},{5,1},{6,4},{7,3},{8,10},{9,13},{10,... | collective-permute-start | bytes 884744 | tf_op jit(solution)/shard_map/ppermute | solution.py:75
  89.9 4.9 %collective-permute-done.11 = f32[9,32,256]{2,1,0:T(8,128)S(1)} collective-permute-done((f32[9,32,256]{2,1,0:T(8,128)S(1)}, f32[9,32,256]{2,1,0:T(8,128)S(1)}, u32[]{:S(2)}, u32[]{:S(2)}) %collective-permute-start.11) | collective-permute-done | bytes 294944 | tf_op jit(solution)/shard_map/ppermute | solution.py:75
  94.9 2.1 %collective-permute-start.12 = (f32[9,32,128]{2,1,0:T(8,128)S(1)}, f32[9,32,128]{2,1,0:T(8,128)S(1)}, u32[]{:S(2)}, u32[]{:S(2)}) collective-permute-start(f32[9,32,128]{2,1,0:T(8,128)S(1)} %constant_dynamic-slice_fusion.4), channel_id=1, source_target_pairs={{0,4},{1,3},{2,6},{3,1},{4,0},{5,7},{6,2},{7,5},{8,12},{9,11},{10,... | collective-permute-start | bytes 442376 | tf_op jit(solution)/shard_map/ppermute | solution.py:75
  97.0 3.2 %collective-permute-done.12 = f32[9,32,128]{2,1,0:T(8,128)S(1)} collective-permute-done((f32[9,32,128]{2,1,0:T(8,128)S(1)}, f32[9,32,128]{2,1,0:T(8,128)S(1)}, u32[]{:S(2)}, u32[]{:S(2)}) %collective-permute-start.12) | collective-permute-done | bytes 147488 | tf_op jit(solution)/shard_map/ppermute | solution.py:75
  100.2 3.4 %collective-permute-start.13 = (f32[9,32,128]{2,1,0:T(8,128)S(1)}, f32[9,32,128]{2,1,0:T(8,128)S(1)}, u32[]{:S(2)}, u32[]{:S(2)}) collective-permute-start(f32[9,32,128]{2,1,0:T(8,128)S(1)} %dynamic-slice_add_fusion.2), channel_id=1, source_target_pairs={{0,8},{1,17},{2,10},{3,19},{4,12},{5,21},{6,14},{7,23},{8,0},{9,25... | collective-permute-start | bytes 442376 | tf_op jit(solution)/shard_map/ppermute | solution.py:78
  103.6 6.3 %collective-permute-done.13 = f32[9,32,128]{2,1,0:T(8,128)S(1)} collective-permute-done((f32[9,32,128]{2,1,0:T(8,128)S(1)}, f32[9,32,128]{2,1,0:T(8,128)S(1)}, u32[]{:S(2)}, u32[]{:S(2)}) %collective-permute-start.13) | collective-permute-done | bytes 147488 | tf_op jit(solution)/shard_map/ppermute | solution.py:78
  109.9 1.6 %collective-permute-start.14 = (f32[9,32,128]{2,1,0:T(8,128)S(1)}, f32[9,32,128]{2,1,0:T(8,128)S(1)}, u32[]{:S(2)}, u32[]{:S(2)}) collective-permute-start(f32[9,32,128]{2,1,0:T(8,128)S(1)} %add.132), channel_id=1, source_target_pairs={{0,16},{1,9},{2,18},{3,11},{4,20},{5,13},{6,22},{7,15},{8,24},{9,1... | collective-permute-start | bytes 442376 | tf_op jit(solution)/shard_map/ppermute | solution.py:78
  111.5 3.7 %collective-permute-done.14 = f32[9,32,128]{2,1,0:T(8,128)S(1)} collective-permute-done((f32[9,32,128]{2,1,0:T(8,128)S(1)}, f32[9,32,128]{2,1,0:T(8,128)S(1)}, u32[]{:S(2)}, u32[]{:S(2)}) %collective-permute-start.14) | collective-permute-done | bytes 147488 | tf_op jit(solution)/shard_map/ppermute | solution.py:78
  115.1 2.4 %collective-permute-start.15 = (f32[9,32,128]{2,1,0:T(8,128)S(1)}, f32[9,32,128]{2,1,0:T(8,128)S(1)}, u32[]{:S(2)}, u32[]{:S(2)}) collective-permute-start(f32[9,32,128]{2,1,0:T(8,128)S(1)} %add.133), channel_id=1, source_target_pairs={{0,4},{1,3},{2,6},{3,1},{4,0},{5,7},{6,2},{7,5},{8,12},{9,11},{10,... | collective-permute-start | bytes 442376 | tf_op jit(solution)/shard_map/ppermute | solution.py:81
  117.5 4.7 %collective-permute-done.15 = f32[9,32,128]{2,1,0:T(8,128)S(1)} collective-permute-done((f32[9,32,128]{2,1,0:T(8,128)S(1)}, f32[9,32,128]{2,1,0:T(8,128)S(1)}, u32[]{:S(2)}, u32[]{:S(2)}) %collective-permute-start.15) | collective-permute-done | bytes 147488 | tf_op jit(solution)/shard_map/ppermute | solution.py:81
  122.3 1.6 %collective-permute-start.16 = (f32[9,32,256]{2,1,0:T(8,128)S(1)}, f32[9,32,256]{2,1,0:T(8,128)S(1)}, u32[]{:S(2)}, u32[]{:S(2)}) collective-permute-start(f32[9,32,256]{2,1,0:T(8,128)S(1)} %pad_maximum_fusion.3), channel_id=1, source_target_pairs={{0,2},{1,5},{2,0},{3,7},{4,6},{5,1},{6,4},{7,3},{8,10},{9,13},{10,... | collective-permute-start | bytes 884744 | tf_op jit(solution)/shard_map/ppermute | solution.py:81
  124.1 5.0 %collective-permute-done.16 = f32[9,32,256]{2,1,0:T(8,128)S(1)} collective-permute-done((f32[9,32,256]{2,1,0:T(8,128)S(1)}, f32[9,32,256]{2,1,0:T(8,128)S(1)}, u32[]{:S(2)}, u32[]{:S(2)}) %collective-permute-start.16) | collective-permute-done | bytes 294944 | tf_op jit(solution)/shard_map/ppermute | solution.py:81
  130.3 1.5 %multiply_add_fusion.1 = f32[5,1024]{1,0:T(8,128)} fusion(f32[5,1024]{1,0:T(8,128)S(1)} %div.29, f32[5,1024]{1,0:T(8,128)} %param.21), kind=kLoop, calls=%fused_computation.100 | loop fusion | flops 10240 | bytes 61440 | tf_op jit(solution)/shard_map/add | solution.py:141
  133.4 2.5 %multiply_add_fusion = (f32[4,64,1024]{2,1,0:T(8,128)}, f32[1,4,64,1024]{3,2,1,0:T(8,128)}) fusion(f32[4,64,1024]{2,1,0:T(8,128)S(1)} %copy-done.5, f32[4]{0:T(128)S(1)} %convolution_bitcast_fusion, f32[1,4,64,1024]{3,2,1,0:T(8,128)S(1)} %copy-done.1, bf16[1,4,64,1024]{3,2,1,0:T(8,128)(2,1)S(1)} %copy-done.2, f32[4,64,32]{1,2,0:T(8,128)S(1)} %fusion.36, ...), kind=kOutput, calls=%fused_computation.16 | convolution fusion | flops 102498304 | bytes 5275664 | tf_op jit(solution)/shard_map/tks,tsd->tkd/dot_general | solution.py:133
  (85 shorter events, 29.2 us)
Async XLA Ops:
  0.6 1.4 %copy-start = (f32[9,1024,32]{1,2,0:T(8,128)S(1)}, f32[9,1024,32]{1,2,0:T(8,128)}, u32[]{:S(2)}) copy-start(f32[9,1024,32]{1,2,0:T(8,128)} %param.18) | copy-start | bytes 3538948
  2.1 1.2 copy-start.1
  2.1 1.3 copy-start.2
  3.4 1.3 copy-start.6
  4.6 6.8 %copy-start.7 = (s32[4]{0:T(128)S(1)}, s32[4]{0:T(128)}, u32[]{:S(2)}) copy-start(s32[4]{0:T(128)} %param.15) | copy-start | bytes 52
  4.7 5.4 %collective-permute-start = (f32[13312]{0:T(1024)S(1)}, f32[13312]{0:T(1024)S(1)}, u32[]{:S(2)}, u32[]{:S(2)}) collective-permute-start(f32[13312]{0:T(1024)S(1)} %pad_maximum_fusion.8), channel_id=1, source_target_pairs={{0,16},{16,0},{1,17},{17,1},{2,18},{18,2},{3,19},{19,3},{4,20},{20... | collective-permute-start | bytes 159752 | tf_op jit(solution)/shard_map/ppermute | solution.py:20
  14.3 2.2 %collective-permute-start.1 = (f32[9,32,512]{2,1,0:T(8,128)S(1)}, f32[9,32,512]{2,1,0:T(8,128)}, u32[]{:S(2)}, u32[]{:S(2)}) collective-permute-start(f32[9,32,512]{2,1,0:T(8,128)S(1)} %copy.46), channel_id=1, source_target_pairs={{0,1},{1,0},{2,3},{3,2},{4,5},{5,4},{6,7},{7,6},{8,9},{9,8},{10,11... | collective-permute-start | bytes 1769480 | tf_op jit(solution)/shard_map/ppermute | solution.py:75
  19.0 7.0 %collective-permute-start.2 = (f32[9,32,256]{2,1,0:T(8,128)}, f32[9,32,256]{2,1,0:T(8,128)}, u32[]{:S(2)}, u32[]{:S(2)}) collective-permute-start(f32[9,32,256]{2,1,0:T(8,128)} %constant_dynamic-slice_fusion.13), channel_id=1, source_target_pairs={{0,2},{1,5},{2,0},{3,7},{4,6},{5,1},{6,4},{7,3},{8,10},{9,13},{10,... | collective-permute-start | bytes 884744 | tf_op jit(solution)/shard_map/ppermute | solution.py:75
  27.1 0.7 copy-start.4
  27.8 5.2 %collective-permute-start.3 = (f32[9,32,128]{2,1,0:T(8,128)S(1)}, f32[9,32,128]{2,1,0:T(8,128)S(1)}, u32[]{:S(2)}, u32[]{:S(2)}) collective-permute-start(f32[9,32,128]{2,1,0:T(8,128)S(1)} %constant_dynamic-slice_fusion.12), channel_id=1, source_target_pairs={{0,4},{1,3},{2,6},{3,1},{4,0},{5,7},{6,2},{7,5},{8,12},{9,11},{10,... | collective-permute-start | bytes 442376 | tf_op jit(solution)/shard_map/ppermute | solution.py:75
  33.9 9.4 %collective-permute-start.4 = (f32[9,32,128]{2,1,0:T(8,128)S(1)}, f32[9,32,128]{2,1,0:T(8,128)S(1)}, u32[]{:S(2)}, u32[]{:S(2)}) collective-permute-start(f32[9,32,128]{2,1,0:T(8,128)S(1)} %dynamic-slice_add_fusion.3), channel_id=1, source_target_pairs={{0,8},{1,17},{2,10},{3,19},{4,12},{5,21},{6,14},{7,23},{8,0},{9,25... | collective-permute-start | bytes 442376 | tf_op jit(solution)/shard_map/ppermute | solution.py:78
  43.4 5.3 %collective-permute-start.5 = (f32[9,32,128]{2,1,0:T(8,128)S(1)}, f32[9,32,128]{2,1,0:T(8,128)S(1)}, u32[]{:S(2)}, u32[]{:S(2)}) collective-permute-start(f32[9,32,128]{2,1,0:T(8,128)S(1)} %add.122), channel_id=1, source_target_pairs={{0,16},{1,9},{2,18},{3,11},{4,20},{5,13},{6,22},{7,15},{8,24},{9,1... | collective-permute-start | bytes 442376 | tf_op jit(solution)/shard_map/ppermute | solution.py:78
  48.7 7.0 %collective-permute-start.6 = (f32[9,32,128]{2,1,0:T(8,128)S(1)}, f32[9,32,128]{2,1,0:T(8,128)S(1)}, u32[]{:S(2)}, u32[]{:S(2)}) collective-permute-start(f32[9,32,128]{2,1,0:T(8,128)S(1)} %add.123), channel_id=1, source_target_pairs={{0,4},{1,3},{2,6},{3,1},{4,0},{5,7},{6,2},{7,5},{8,12},{9,11},{10,... | collective-permute-start | bytes 442376 | tf_op jit(solution)/shard_map/ppermute | solution.py:81
  55.7 0.7 copy-start.3
  56.4 6.9 %collective-permute-start.7 = (f32[9,32,256]{2,1,0:T(8,128)S(1)}, f32[9,32,256]{2,1,0:T(8,128)}, u32[]{:S(2)}, u32[]{:S(2)}) collective-permute-start(f32[9,32,256]{2,1,0:T(8,128)S(1)} %pad_maximum_fusion.2), channel_id=1, source_target_pairs={{0,2},{1,5},{2,0},{3,7},{4,6},{5,1},{6,4},{7,3},{8,10},{9,13},{10,... | collective-permute-start | bytes 884744 | tf_op jit(solution)/shard_map/ppermute | solution.py:81
  65.2 9.8 %collective-permute-start.8 = (f32[9,32,512]{2,1,0:T(8,128)}, f32[9,32,512]{2,1,0:T(8,128)}, u32[]{:S(2)}, u32[]{:S(2)}) collective-permute-start(f32[9,32,512]{2,1,0:T(8,128)} %pad_maximum_fusion), channel_id=1, source_target_pairs={{0,1},{1,0},{2,3},{3,2},{4,5},{5,4},{6,7},{7,6},{8,9},{9,8},{10,11... | collective-permute-start | bytes 1769480 | tf_op jit(solution)/shard_map/ppermute | solution.py:81
  77.8 4.7 %collective-permute-start.9 = (f32[4,64,32]{1,2,0:T(8,128)S(1)}, f32[4,64,32]{1,2,0:T(8,128)S(1)}, u32[]{:S(2)}, u32[]{:S(2)}) collective-permute-start(f32[4,64,32]{1,2,0:T(8,128)S(1)} %fusion.2), channel_id=1, source_target_pairs={{0,16},{16,0},{1,17},{17,1},{2,18},{18,2},{3,19},{19,3},{4,20},{20... | collective-permute-start | bytes 98312 | tf_op jit(solution)/shard_map/ppermute | solution.py:20
  85.5 2.1 %collective-permute-start.10 = (f32[9,32,512]{2,1,0:T(8,128)S(1)}, f32[9,32,512]{2,1,0:T(8,128)S(1)}, u32[]{:S(2)}, u32[]{:S(2)}) collective-permute-start(f32[9,32,512]{2,1,0:T(8,128)S(1)} %copy.51), channel_id=1, source_target_pairs={{0,1},{1,0},{2,3},{3,2},{4,5},{5,4},{6,7},{7,6},{8,9},{9,8},{10,11... | collective-permute-start | bytes 1769480 | tf_op jit(solution)/shard_map/ppermute | solution.py:75
  88.0 35.9 %copy-start.8 = (s32[9]{0:T(128)S(1)}, s32[9]{0:T(128)}, u32[]{:S(2)}) copy-start(s32[9]{0:T(128)} %param.16) | copy-start | bytes 112
  88.0 35.9 %copy-start.9 = (f32[4]{0:T(128)S(1)}, f32[4]{0:T(128)}, u32[]{:S(2)}) copy-start(f32[4]{0:T(128)} %param.17) | copy-start | bytes 52
  88.1 6.8 %collective-permute-start.11 = (f32[9,32,256]{2,1,0:T(8,128)S(1)}, f32[9,32,256]{2,1,0:T(8,128)S(1)}, u32[]{:S(2)}, u32[]{:S(2)}) collective-permute-start(f32[9,32,256]{2,1,0:T(8,128)S(1)} %constant_dynamic-slice_fusion.5), channel_id=1, source_target_pairs={{0,2},{1,5},{2,0},{3,7},{4,6},{5,1},{6,4},{7,3},{8,10},{9,13},{10,... | collective-permute-start | bytes 884744 | tf_op jit(solution)/shard_map/ppermute | solution.py:75
  94.9 5.2 %collective-permute-start.12 = (f32[9,32,128]{2,1,0:T(8,128)S(1)}, f32[9,32,128]{2,1,0:T(8,128)S(1)}, u32[]{:S(2)}, u32[]{:S(2)}) collective-permute-start(f32[9,32,128]{2,1,0:T(8,128)S(1)} %constant_dynamic-slice_fusion.4), channel_id=1, source_target_pairs={{0,4},{1,3},{2,6},{3,1},{4,0},{5,7},{6,2},{7,5},{8,12},{9,11},{10,... | collective-permute-start | bytes 442376 | tf_op jit(solution)/shard_map/ppermute | solution.py:75
  100.2 9.7 %collective-permute-start.13 = (f32[9,32,128]{2,1,0:T(8,128)S(1)}, f32[9,32,128]{2,1,0:T(8,128)S(1)}, u32[]{:S(2)}, u32[]{:S(2)}) collective-permute-start(f32[9,32,128]{2,1,0:T(8,128)S(1)} %dynamic-slice_add_fusion.2), channel_id=1, source_target_pairs={{0,8},{1,17},{2,10},{3,19},{4,12},{5,21},{6,14},{7,23},{8,0},{9,25... | collective-permute-start | bytes 442376 | tf_op jit(solution)/shard_map/ppermute | solution.py:78
  109.9 5.2 %collective-permute-start.14 = (f32[9,32,128]{2,1,0:T(8,128)S(1)}, f32[9,32,128]{2,1,0:T(8,128)S(1)}, u32[]{:S(2)}, u32[]{:S(2)}) collective-permute-start(f32[9,32,128]{2,1,0:T(8,128)S(1)} %add.132), channel_id=1, source_target_pairs={{0,16},{1,9},{2,18},{3,11},{4,20},{5,13},{6,22},{7,15},{8,24},{9,1... | collective-permute-start | bytes 442376 | tf_op jit(solution)/shard_map/ppermute | solution.py:78
  115.1 7.1 %collective-permute-start.15 = (f32[9,32,128]{2,1,0:T(8,128)S(1)}, f32[9,32,128]{2,1,0:T(8,128)S(1)}, u32[]{:S(2)}, u32[]{:S(2)}) collective-permute-start(f32[9,32,128]{2,1,0:T(8,128)S(1)} %add.133), channel_id=1, source_target_pairs={{0,4},{1,3},{2,6},{3,1},{4,0},{5,7},{6,2},{7,5},{8,12},{9,11},{10,... | collective-permute-start | bytes 442376 | tf_op jit(solution)/shard_map/ppermute | solution.py:81
  122.3 6.8 %collective-permute-start.16 = (f32[9,32,256]{2,1,0:T(8,128)S(1)}, f32[9,32,256]{2,1,0:T(8,128)S(1)}, u32[]{:S(2)}, u32[]{:S(2)}) collective-permute-start(f32[9,32,256]{2,1,0:T(8,128)S(1)} %pad_maximum_fusion.3), channel_id=1, source_target_pairs={{0,2},{1,5},{2,0},{3,7},{4,6},{5,1},{6,4},{7,3},{8,10},{9,13},{10,... | collective-permute-start | bytes 884744 | tf_op jit(solution)/shard_map/ppermute | solution.py:81
  130.0 2.3 %collective-permute-start.17 = (f32[9,32,512]{2,1,0:T(8,128)}, f32[9,32,512]{2,1,0:T(8,128)}, u32[]{:S(2)}, u32[]{:S(2)}) collective-permute-start(f32[9,32,512]{2,1,0:T(8,128)} %pad_maximum_fusion.1), channel_id=1, source_target_pairs={{0,1},{1,0},{2,3},{3,2},{4,5},{5,4},{6,7},{7,6},{8,9},{9,8},{10,11... | collective-permute-start | bytes 1769480 | tf_op jit(solution)/shard_map/ppermute | solution.py:81
  130.2 3.2 %copy-start.5 = (f32[4,64,1024]{2,1,0:T(8,128)S(1)}, f32[4,64,1024]{2,1,0:T(8,128)}, u32[]{:S(2)}) copy-start(f32[4,64,1024]{2,1,0:T(8,128)} %param.14) | copy-start | bytes 3145732

commit v6 on v5

--- a/solution.py
+++ b/solution.py
@@ -41,6 +41,14 @@
 
 def _pick_rows(table, rows):
     return jnp.stack([lax.dynamic_index_in_dim(table, rows[i], 0, keepdims=False) for i in range(rows.shape[0])])
+
+
+def _scatter_rows(parts, rows, count):
+    table = jnp.zeros((count,) + parts.shape[1:], parts.dtype)
+    for i in range(parts.shape[0]):
+        slab = lax.dynamic_index_in_dim(table, rows[i], 0, keepdims=True)
+        table = lax.dynamic_update_index_in_dim(table, slab + parts[i : i + 1], rows[i], 0)
+    return table
 
 
 def table_rows(x, rows, n_rep, n_own):
@@ -109,26 +117,26 @@
         jnp.float32
     )
     combined = gradient[0].astype(jnp.float32) + feedback[0]
-    q_tiles = jnp.take(start_basis, tile_matrix, axis=0)
+    q_tiles = _pick_rows(start_basis, tile_matrix)
     first_local = jnp.einsum("tkd,tds->tks", combined, q_tiles, precision=TOP_PRECISION)
     left_size = first_local.size
     carried = jnp.concatenate([first_local.reshape(-1), vector_grad[0].reshape(-1)])
     carried = swap_sum(carried, "rep")
     first_left = carried[:left_size].reshape(first_local.shape) / replicas
     vector_summed = carried[left_size:].reshape(vector_grad.shape[1:])
-    mix_first = jnp.take(inverse_gram_factors[0], tile_matrix, axis=0)
+    mix_first = _pick_rows(inverse_gram_factors[0], tile_matrix)
     first_ortho = jnp.einsum("tks,tsa->tka", first_left, mix_first, precision=TOP_PRECISION)
     first_parts = jnp.einsum("tkd,tks->tsd", combined, first_ortho, precision=TOP_PRECISION)
-    first_table = jnp.einsum("tm,tsd->msd", selector, first_parts, precision=TOP_PRECISION)
+    first_table = _scatter_rows(first_parts, tile_matrix, matrix_count)
     first_rows = table_rows(first_table, tile_matrix, replicas, n_own) / replicas
-    mix_right = jnp.take(inverse_gram_factors[1], tile_matrix, axis=0)
+    mix_right = _pick_rows(inverse_gram_factors[1], tile_matrix)
     right_rows = jnp.einsum("tjw,tjd->twd", mix_right, first_rows, precision=TOP_PRECISION)
     second_local = jnp.einsum("tkd,tsd->tks", combined, right_rows, precision=TOP_PRECISION)
     second_left = swap_sum(second_local, "rep") / replicas
-    mix_second = jnp.take(inverse_gram_factors[2], tile_matrix, axis=0)
+    mix_second = _pick_rows(inverse_gram_factors[2], tile_matrix)
     second_ortho = jnp.einsum("tks,tsa->tka", second_left, mix_second, precision=TOP_PRECISION)
     second_parts = jnp.einsum("tkd,tks->tsd", combined, second_ortho, precision=TOP_PRECISION)
-    second_table = jnp.einsum("tm,tsd->msd", selector, second_parts, precision=TOP_PRECISION)
+    second_table = _scatter_rows(second_parts, tile_matrix, matrix_count)
     back_rows = table_rows(second_table, tile_matrix, replicas, n_own) / replicas
     approximation = jnp.einsum("tks,tsd->tkd", second_ortho, back_rows, precision=TOP_PRECISION)
     new_feedback = (combined - approximation)[None]

time: 137 us -> 124 us (0.905)
  local copies, waits for them, and re-layouts: 13.7 us -> 6.04 us
  other arithmetic: 10.3 us -> 2.77 us
  waiting for transfers between devices: 61.6 us -> 64.8 us
  matrix products: 10.7 us -> 8.8 us
    gather x4 -> x0, local copies, waits for them, and re-layouts: 4.05 us -> none  [the longest x1 1.46 us: local(): mix_right = jnp.take(inverse_gram_factors[1], tile_matrix, axis=0)]
    add x6, other arithmetic: 4.2 us -> 1.42 us  [table_rows(): cur = keep + lax.ppermute(send, axes, perm_of(p0, p1))]
    dot_general x2 -> x0, matrix products: 2.72 us -> none  [the longest x1 1.36 us: local(): jnp.einsum('tm,tsd->msd', selector, second_parts, precision=TOP_PRECISION)]
    ppermute x2, waiting for transfers between devices: 1.3 us -> 3.56 us  [swap_sum(): x = x + lax.ppermute(x, axis, _pair_perm(n, j))]
    unnamed x20 -> x18, local copies, waits for them, and re-layouts: 2.16 us -> 0.05 us
    squeeze x1 -> x0, local copies, waits for them, and re-layouts: 1.78 us -> none  [local(): mix_right = jnp.take(inverse_gram_factors[1], tile_matrix, axis=0)]
    ppermute x6, waiting for transfers between devices: 20 us -> 21.7 us  [table_rows(): other = lax.ppermute(cur, axes, perm_of(p0, p1))]
    concatenate x6, other arithmetic: 1.88 us -> 0.21 us  [table_rows(): cur = jnp.concatenate([low, high], axis=axis)]
  transfers between devices with their start and end apart: 18 -> 18, of which waited for: 16 -> 18; matrix products, arithmetic and copies ran while one was open for 6% -> 2% of each run, Pallas kernels for 0% -> 0%
where the time goes in v6:
time: 124 us; the launch traced here: 123 us
  waiting for transfers between devices  64.8 us (52%)
  starting transfers between devices  31.9 us (26%)
  between operations  8.87 us (7%)
  matrix products  8.8 us (7%)
  local copies, waits for them, and re-layouts  6.04 us (5%)
  other arithmetic  2.77 us (2%)
    ppermute x6, waiting for transfers between devices, table_rows(): other = lax.ppermute(cur, axes, perm_of(p0, p1))  21.7 us
    ppermute x6, waiting for transfers between devices, table_rows(): cur = keep + lax.ppermute(send, axes, perm_of(p0, p1))  19.9 us
    ppermute x4, waiting for transfers between devices, table_rows(): cur = cur + lax.ppermute(cur, axes, perm_of(p0, p1))  19.6 us
    ppermute x4, starting transfers between devices, table_rows(): cur = cur + lax.ppermute(cur, axes, perm_of(p0, p1))  10.3 us
    ppermute x6, starting transfers between devices, table_rows(): cur = keep + lax.ppermute(send, axes, perm_of(p0, p1))  8.41 us
    ppermute x6, starting transfers between devices, table_rows(): other = lax.ppermute(cur, axes, perm_of(p0, p1))  8.28 us
    ppermute x2, starting transfers between devices, swap_sum(): x = x + lax.ppermute(x, axis, _pair_perm(n, j))  4.92 us
    ppermute x2, waiting for transfers between devices, swap_sum(): x = x + lax.ppermute(x, axis, _pair_perm(n, j))  3.56 us
  transfers between devices with their start and end apart: 18, of which 18 were waited for; matrix products, arithmetic and copies ran while one was open for 2% of the time, Pallas kernels for 0%

profile of v6, /device:TPU:0, one launch (start us, length us, event | category | flops | bytes accessed | tf_op | source)
XLA Modules:
  0.0 123.2 jit_solution(1760911508745645723)
XLA Ops:
  0.7 1.4 %fusion.89 = (s32[1]{0:T(128)}, s32[1]{0:T(128)}, s32[1]{0:T(128)}, s32[1]{0:T(128)}) fusion(s32[4]{0:T(128)} %param.13), kind=kLoop, calls=%fused_computation.178 | loop fusion | bytes 32 | tf_op jit(solution)/shard_map/slice | solution.py:43
  11.0 2.2 %fusion.6 = f32[4,64,32]{2,1,0:T(8,128)S(1)} fusion(f32[1,1024,32]{1,2,0:T(8,128)S(1)} %get-tuple-element.5, f32[1,1024,32]{1,2,0:T(8,128)S(1)} %get-tuple-element.6, f32[1,1024,32]{1,2,0:T(8,128)S(1)} %get-tuple-element.4, f32[1,1024,32]{1,2,0:T(8,128)S(1)} %get-tuple-element.3, f32[1,4,64,1024]{3,2,1,0:T(8,128)S(1)} %copy-done.1, ...), kind=kOutput, calls=%fused_computation.9 | convolution fusion | flops 101580800 | bytes 2129920 | tf_op jit(solution)/shard_map/tkd,tds->tks/dot_general | solution.py:121
  13.3 3.0 %collective-permute-start = (f32[13312]{0:T(1024)S(1)}, f32[13312]{0:T(1024)S(1)}, u32[]{:S(2)}, u32[]{:S(2)}) collective-permute-start(f32[13312]{0:T(1024)S(1)} %pad_maximum_fusion.8), channel_id=1, source_target_pairs={{0,16},{16,0},{1,17},{17,1},{2,18},{18,2},{3,19},{19,3},{4,20},{20... | collective-permute-start | bytes 159752 | tf_op jit(solution)/shard_map/ppermute | solution.py:20
  20.1 2.1 %collective-permute-done.1 = f32[9,32,512]{2,1,0:T(8,128)} collective-permute-done((f32[9,32,512]{2,1,0:T(8,128)S(1)}, f32[9,32,512]{2,1,0:T(8,128)}, u32[]{:S(2)}, u32[]{:S(2)}) %collective-permute-start.1) | collective-permute-done | bytes 589856 | tf_op jit(solution)/shard_map/ppermute | solution.py:83
  23.4 2.1 %collective-permute-start.2 = (f32[9,32,256]{2,1,0:T(8,128)S(1)}, f32[9,32,256]{2,1,0:T(8,128)S(1)}, u32[]{:S(2)}, u32[]{:S(2)}) collective-permute-start(f32[9,32,256]{2,1,0:T(8,128)S(1)} %constant_dynamic-slice_fusion.16), channel_id=1, source_target_pairs={{0,2},{1,5},{2,0},{3,7},{4,6},{5,1},{6,4},{7,3},{8,10},{9,13},{10,... | collective-permute-start | bytes 884744 | tf_op jit(solution)/shard_map/ppermute | solution.py:83
  25.5 4.7 %collective-permute-done.2 = f32[9,32,256]{2,1,0:T(8,128)S(1)} collective-permute-done((f32[9,32,256]{2,1,0:T(8,128)S(1)}, f32[9,32,256]{2,1,0:T(8,128)S(1)}, u32[]{:S(2)}, u32[]{:S(2)}) %collective-permute-start.2) | collective-permute-done | bytes 294944 | tf_op jit(solution)/shard_map/ppermute | solution.py:83
  30.3 2.1 %collective-permute-start.3 = (f32[9,32,128]{2,1,0:T(8,128)S(1)}, f32[9,32,128]{2,1,0:T(8,128)S(1)}, u32[]{:S(2)}, u32[]{:S(2)}) collective-permute-start(f32[9,32,128]{2,1,0:T(8,128)S(1)} %constant_dynamic-slice_fusion.15), channel_id=1, source_target_pairs={{0,4},{1,3},{2,6},{3,1},{4,0},{5,7},{6,2},{7,5},{8,12},{9,11},{10,... | collective-permute-start | bytes 442376 | tf_op jit(solution)/shard_map/ppermute | solution.py:83
  32.4 3.1 %collective-permute-done.3 = f32[9,32,128]{2,1,0:T(8,128)S(1)} collective-permute-done((f32[9,32,128]{2,1,0:T(8,128)S(1)}, f32[9,32,128]{2,1,0:T(8,128)S(1)}, u32[]{:S(2)}, u32[]{:S(2)}) %collective-permute-start.3) | collective-permute-done | bytes 147488 | tf_op jit(solution)/shard_map/ppermute | solution.py:83
  35.6 3.1 %collective-permute-start.4 = (f32[9,32,128]{2,1,0:T(8,128)S(1)}, f32[9,32,128]{2,1,0:T(8,128)S(1)}, u32[]{:S(2)}, u32[]{:S(2)}) collective-permute-start(f32[9,32,128]{2,1,0:T(8,128)S(1)} %dynamic-slice_add_fusion.5), channel_id=1, source_target_pairs={{0,8},{1,17},{2,10},{3,19},{4,12},{5,21},{6,14},{7,23},{8,0},{9,25... | collective-permute-start | bytes 442376 | tf_op jit(solution)/shard_map/ppermute | solution.py:86
  38.7 6.4 %collective-permute-done.4 = f32[9,32,128]{2,1,0:T(8,128)S(1)} collective-permute-done((f32[9,32,128]{2,1,0:T(8,128)S(1)}, f32[9,32,128]{2,1,0:T(8,128)S(1)}, u32[]{:S(2)}, u32[]{:S(2)}) %collective-permute-start.4) | collective-permute-done | bytes 147488 | tf_op jit(solution)/shard_map/ppermute | solution.py:86
  45.1 2.2 %collective-permute-start.5 = (f32[9,32,128]{2,1,0:T(8,128)S(1)}, f32[9,32,128]{2,1,0:T(8,128)S(1)}, u32[]{:S(2)}, u32[]{:S(2)}) collective-permute-start(f32[9,32,128]{2,1,0:T(8,128)S(1)} %add.177), channel_id=1, source_target_pairs={{0,16},{1,9},{2,18},{3,11},{4,20},{5,13},{6,22},{7,15},{8,24},{9,1... | collective-permute-start | bytes 442376 | tf_op jit(solution)/shard_map/ppermute | solution.py:86
  47.3 3.1 %collective-permute-done.5 = f32[9,32,128]{2,1,0:T(8,128)S(1)} collective-permute-done((f32[9,32,128]{2,1,0:T(8,128)S(1)}, f32[9,32,128]{2,1,0:T(8,128)S(1)}, u32[]{:S(2)}, u32[]{:S(2)}) %collective-permute-start.5) | collective-permute-done | bytes 147488 | tf_op jit(solution)/shard_map/ppermute | solution.py:86
  50.5 2.3 %collective-permute-start.6 = (f32[9,32,128]{2,1,0:T(8,128)S(1)}, f32[9,32,128]{2,1,0:T(8,128)S(1)}, u32[]{:S(2)}, u32[]{:S(2)}) collective-permute-start(f32[9,32,128]{2,1,0:T(8,128)S(1)} %add.178), channel_id=1, source_target_pairs={{0,4},{1,3},{2,6},{3,1},{4,0},{5,7},{6,2},{7,5},{8,12},{9,11},{10,... | collective-permute-start | bytes 442376 | tf_op jit(solution)/shard_map/ppermute | solution.py:89
  52.8 4.7 %collective-permute-done.6 = f32[9,32,128]{2,1,0:T(8,128)S(1)} collective-permute-done((f32[9,32,128]{2,1,0:T(8,128)S(1)}, f32[9,32,128]{2,1,0:T(8,128)S(1)}, u32[]{:S(2)}, u32[]{:S(2)}) %collective-permute-start.6) | collective-permute-done | bytes 147488 | tf_op jit(solution)/shard_map/ppermute | solution.py:89
  57.5 1.9 %collective-permute-start.7 = (f32[9,32,256]{2,1,0:T(8,128)S(1)}, f32[9,32,256]{2,1,0:T(8,128)S(1)}, u32[]{:S(2)}, u32[]{:S(2)}) collective-permute-start(f32[9,32,256]{2,1,0:T(8,128)S(1)} %pad_maximum_fusion.2), channel_id=1, source_target_pairs={{0,2},{1,5},{2,0},{3,7},{4,6},{5,1},{6,4},{7,3},{8,10},{9,13},{10,... | collective-permute-start | bytes 884744 | tf_op jit(solution)/shard_map/ppermute | solution.py:89
  59.4 4.9 %collective-permute-done.7 = f32[9,32,256]{2,1,0:T(8,128)S(1)} collective-permute-done((f32[9,32,256]{2,1,0:T(8,128)S(1)}, f32[9,32,256]{2,1,0:T(8,128)S(1)}, u32[]{:S(2)}, u32[]{:S(2)}) %collective-permute-start.7) | collective-permute-done | bytes 294944 | tf_op jit(solution)/shard_map/ppermute | solution.py:89
  69.4 1.9 %collective-permute-start.9 = (f32[4,64,32]{1,2,0:T(8,128)S(1)}, f32[4,64,32]{1,2,0:T(8,128)S(1)}, u32[]{:S(2)}, u32[]{:S(2)}) collective-permute-start(f32[4,64,32]{1,2,0:T(8,128)S(1)} %fusion.2), channel_id=1, source_target_pairs={{0,16},{16,0},{1,17},{17,1},{2,18},{18,2},{3,19},{19,3},{4,20},{20... | collective-permute-start | bytes 98312 | tf_op jit(solution)/shard_map/ppermute | solution.py:20
  71.6 2.2 %collective-permute-done.9 = f32[4,64,32]{1,2,0:T(8,128)S(1)} collective-permute-done((f32[4,64,32]{1,2,0:T(8,128)S(1)}, f32[4,64,32]{1,2,0:T(8,128)S(1)}, u32[]{:S(2)}, u32[]{:S(2)}) %collective-permute-start.9) | collective-permute-done | bytes 32800 | tf_op jit(solution)/shard_map/ppermute | solution.py:20
  75.0 2.0 %collective-permute-done.10 = f32[9,32,512]{2,1,0:T(8,128)S(1)} collective-permute-done((f32[9,32,512]{2,1,0:T(8,128)S(1)}, f32[9,32,512]{2,1,0:T(8,128)S(1)}, u32[]{:S(2)}, u32[]{:S(2)}) %collective-permute-start.10) | collective-permute-done | bytes 589856 | tf_op jit(solution)/shard_map/ppermute | solution.py:83
  77.2 1.9 %collective-permute-start.11 = (f32[9,32,256]{2,1,0:T(8,128)S(1)}, f32[9,32,256]{2,1,0:T(8,128)S(1)}, u32[]{:S(2)}, u32[]{:S(2)}) collective-permute-start(f32[9,32,256]{2,1,0:T(8,128)S(1)} %constant_dynamic-slice_fusion.1), channel_id=1, source_target_pairs={{0,2},{1,5},{2,0},{3,7},{4,6},{5,1},{6,4},{7,3},{8,10},{9,13},{10,... | collective-permute-start | bytes 884744 | tf_op jit(solution)/shard_map/ppermute | solution.py:83
  79.1 4.9 %collective-permute-done.11 = f32[9,32,256]{2,1,0:T(8,128)S(1)} collective-permute-done((f32[9,32,256]{2,1,0:T(8,128)S(1)}, f32[9,32,256]{2,1,0:T(8,128)S(1)}, u32[]{:S(2)}, u32[]{:S(2)}) %collective-permute-start.11) | collective-permute-done | bytes 294944 | tf_op jit(solution)/shard_map/ppermute | solution.py:83
  84.0 2.1 %collective-permute-start.12 = (f32[9,32,128]{2,1,0:T(8,128)S(1)}, f32[9,32,128]{2,1,0:T(8,128)S(1)}, u32[]{:S(2)}, u32[]{:S(2)}) collective-permute-start(f32[9,32,128]{2,1,0:T(8,128)S(1)} %constant_dynamic-slice_fusion), channel_id=1, source_target_pairs={{0,4},{1,3},{2,6},{3,1},{4,0},{5,7},{6,2},{7,5},{8,12},{9,11},{10,... | collective-permute-start | bytes 442376 | tf_op jit(solution)/shard_map/ppermute | solution.py:83
  86.1 3.1 %collective-permute-done.12 = f32[9,32,128]{2,1,0:T(8,128)S(1)} collective-permute-done((f32[9,32,128]{2,1,0:T(8,128)S(1)}, f32[9,32,128]{2,1,0:T(8,128)S(1)}, u32[]{:S(2)}, u32[]{:S(2)}) %collective-permute-start.12) | collective-permute-done | bytes 147488 | tf_op jit(solution)/shard_map/ppermute | solution.py:83
  89.3 3.5 %collective-permute-start.13 = (f32[9,32,128]{2,1,0:T(8,128)S(1)}, f32[9,32,128]{2,1,0:T(8,128)S(1)}, u32[]{:S(2)}, u32[]{:S(2)}) collective-permute-start(f32[9,32,128]{2,1,0:T(8,128)S(1)} %dynamic-slice_add_fusion.4), channel_id=1, source_target_pairs={{0,8},{1,17},{2,10},{3,19},{4,12},{5,21},{6,14},{7,23},{8,0},{9,25... | collective-permute-start | bytes 442376 | tf_op jit(solution)/shard_map/ppermute | solution.py:86
  92.7 6.4 %collective-permute-done.13 = f32[9,32,128]{2,1,0:T(8,128)S(1)} collective-permute-done((f32[9,32,128]{2,1,0:T(8,128)S(1)}, f32[9,32,128]{2,1,0:T(8,128)S(1)}, u32[]{:S(2)}, u32[]{:S(2)}) %collective-permute-start.13) | collective-permute-done | bytes 147488 | tf_op jit(solution)/shard_map/ppermute | solution.py:86
  99.2 1.6 %collective-permute-start.14 = (f32[9,32,128]{2,1,0:T(8,128)S(1)}, f32[9,32,128]{2,1,0:T(8,128)S(1)}, u32[]{:S(2)}, u32[]{:S(2)}) collective-permute-start(f32[9,32,128]{2,1,0:T(8,128)S(1)} %add.186), channel_id=1, source_target_pairs={{0,16},{1,9},{2,18},{3,11},{4,20},{5,13},{6,22},{7,15},{8,24},{9,1... | collective-permute-start | bytes 442376 | tf_op jit(solution)/shard_map/ppermute | solution.py:86
  100.7 3.7 %collective-permute-done.14 = f32[9,32,128]{2,1,0:T(8,128)S(1)} collective-permute-done((f32[9,32,128]{2,1,0:T(8,128)S(1)}, f32[9,32,128]{2,1,0:T(8,128)S(1)}, u32[]{:S(2)}, u32[]{:S(2)}) %collective-permute-start.14) | collective-permute-done | bytes 147488 | tf_op jit(solution)/shard_map/ppermute | solution.py:86
  104.4 2.4 %collective-permute-start.15 = (f32[9,32,128]{2,1,0:T(8,128)S(1)}, f32[9,32,128]{2,1,0:T(8,128)S(1)}, u32[]{:S(2)}, u32[]{:S(2)}) collective-permute-start(f32[9,32,128]{2,1,0:T(8,128)S(1)} %add.187), channel_id=1, source_target_pairs={{0,4},{1,3},{2,6},{3,1},{4,0},{5,7},{6,2},{7,5},{8,12},{9,11},{10,... | collective-permute-start | bytes 442376 | tf_op jit(solution)/shard_map/ppermute | solution.py:89
  106.8 4.7 %collective-permute-done.15 = f32[9,32,128]{2,1,0:T(8,128)S(1)} collective-permute-done((f32[9,32,128]{2,1,0:T(8,128)S(1)}, f32[9,32,128]{2,1,0:T(8,128)S(1)}, u32[]{:S(2)}, u32[]{:S(2)}) %collective-permute-start.15) | collective-permute-done | bytes 147488 | tf_op jit(solution)/shard_map/ppermute | solution.py:89
  111.6 1.5 %collective-permute-start.16 = (f32[9,32,256]{2,1,0:T(8,128)S(1)}, f32[9,32,256]{2,1,0:T(8,128)S(1)}, u32[]{:S(2)}, u32[]{:S(2)}) collective-permute-start(f32[9,32,256]{2,1,0:T(8,128)S(1)} %pad_maximum_fusion.3), channel_id=1, source_target_pairs={{0,2},{1,5},{2,0},{3,7},{4,6},{5,1},{6,4},{7,3},{8,10},{9,13},{10,... | collective-permute-start | bytes 884744 | tf_op jit(solution)/shard_map/ppermute | solution.py:89
  113.3 5.1 %collective-permute-done.16 = f32[9,32,256]{2,1,0:T(8,128)S(1)} collective-permute-done((f32[9,32,256]{2,1,0:T(8,128)S(1)}, f32[9,32,256]{2,1,0:T(8,128)S(1)}, u32[]{:S(2)}, u32[]{:S(2)}) %collective-permute-start.16) | collective-permute-done | bytes 294944 | tf_op jit(solution)/shard_map/ppermute | solution.py:89
  120.7 2.6 %multiply_add_fusion = (f32[4,64,1024]{2,1,0:T(8,128)}, f32[1,4,64,1024]{3,2,1,0:T(8,128)}) fusion(f32[4,64,1024]{2,1,0:T(8,128)S(1)} %copy-done.3, f32[4]{0:T(128)S(1)} %convolution_bitcast_fusion, f32[1,4,64,1024]{3,2,1,0:T(8,128)S(1)} %copy-done.1, bf16[1,4,64,1024]{3,2,1,0:T(8,128)(2,1)S(1)} %copy-done.2, f32[4,64,32]{1,2,0:T(8,128)S(1)} %fusion.57, ...), kind=kOutput, calls=%fused_computation.12 | convolution fusion | flops 102498304 | bytes 5275664 | tf_op jit(solution)/shard_map/tks,tsd->tkd/dot_general | solution.py:141
  (90 shorter events, 15.5 us)
Async XLA Ops:
  0.6 112.5 %copy-start = (f32[4]{0:T(128)S(1)}, f32[4]{0:T(128)}, u32[]{:S(2)}) copy-start(f32[4]{0:T(128)} %param.15) | copy-start | bytes 52
  0.6 10.3 %copy-start.1 = (f32[1,4,64,1024]{3,2,1,0:T(8,128)S(1)}, f32[1,4,64,1024]{3,2,1,0:T(8,128)}, u32[]{:S(2)}) copy-start(f32[1,4,64,1024]{3,2,1,0:T(8,128)} %param.11) | copy-start | bytes 3145732
  11.0 2.3 %copy-start.5 = (f32[1,5,1024]{2,0,1:T(1,128)S(1)}, f32[1,5,1024]{2,0,1:T(1,128)}, u32[]{:S(2)}) copy-start(f32[1,5,1024]{2,0,1:T(1,128)} %param.18) | copy-start | bytes 61444
  11.0 5.4 %copy-start.4 = (f32[3,9,32,32]{3,2,1,0:T(8,128)S(1)}, f32[3,9,32,32]{3,2,1,0:T(8,128)}, u32[]{:S(2)}) copy-start(f32[3,9,32,32]{3,2,1,0:T(8,128)} %param.17) | copy-start | bytes 331780
  13.2 5.8 %copy-start.2 = (bf16[1,4,64,1024]{3,2,1,0:T(8,128)(2,1)S(1)}, bf16[1,4,64,1024]{3,2,1,0:T(8,128)(2,1)}, u32[]{:S(2)}) copy-start(bf16[1,4,64,1024]{3,2,1,0:T(8,128)(2,1)} %param.10) | copy-start | bytes 1572868
  13.3 5.1 %collective-permute-start = (f32[13312]{0:T(1024)S(1)}, f32[13312]{0:T(1024)S(1)}, u32[]{:S(2)}, u32[]{:S(2)}) collective-permute-start(f32[13312]{0:T(1024)S(1)} %pad_maximum_fusion.8), channel_id=1, source_target_pairs={{0,16},{16,0},{1,17},{17,1},{2,18},{18,2},{3,19},{19,3},{4,20},{20... | collective-permute-start | bytes 159752 | tf_op jit(solution)/shard_map/ppermute | solution.py:20
  20.0 2.2 %collective-permute-start.1 = (f32[9,32,512]{2,1,0:T(8,128)S(1)}, f32[9,32,512]{2,1,0:T(8,128)}, u32[]{:S(2)}, u32[]{:S(2)}) collective-permute-start(f32[9,32,512]{2,1,0:T(8,128)S(1)} %constant_dynamic-slice_fusion.17), channel_id=1, source_target_pairs={{0,1},{1,0},{2,3},{3,2},{4,5},{5,4},{6,7},{7,6},{8,9},{9,8},{10,11... | collective-permute-start | bytes 1769480 | tf_op jit(solution)/shard_map/ppermute | solution.py:83
  23.4 6.8 %collective-permute-start.2 = (f32[9,32,256]{2,1,0:T(8,128)S(1)}, f32[9,32,256]{2,1,0:T(8,128)S(1)}, u32[]{:S(2)}, u32[]{:S(2)}) collective-permute-start(f32[9,32,256]{2,1,0:T(8,128)S(1)} %constant_dynamic-slice_fusion.16), channel_id=1, source_target_pairs={{0,2},{1,5},{2,0},{3,7},{4,6},{5,1},{6,4},{7,3},{8,10},{9,13},{10,... | collective-permute-start | bytes 884744 | tf_op jit(solution)/shard_map/ppermute | solution.py:83
  30.3 5.3 %collective-permute-start.3 = (f32[9,32,128]{2,1,0:T(8,128)S(1)}, f32[9,32,128]{2,1,0:T(8,128)S(1)}, u32[]{:S(2)}, u32[]{:S(2)}) collective-permute-start(f32[9,32,128]{2,1,0:T(8,128)S(1)} %constant_dynamic-slice_fusion.15), channel_id=1, source_target_pairs={{0,4},{1,3},{2,6},{3,1},{4,0},{5,7},{6,2},{7,5},{8,12},{9,11},{10,... | collective-permute-start | bytes 442376 | tf_op jit(solution)/shard_map/ppermute | solution.py:83
  35.6 9.5 %collective-permute-start.4 = (f32[9,32,128]{2,1,0:T(8,128)S(1)}, f32[9,32,128]{2,1,0:T(8,128)S(1)}, u32[]{:S(2)}, u32[]{:S(2)}) collective-permute-start(f32[9,32,128]{2,1,0:T(8,128)S(1)} %dynamic-slice_add_fusion.5), channel_id=1, source_target_pairs={{0,8},{1,17},{2,10},{3,19},{4,12},{5,21},{6,14},{7,23},{8,0},{9,25... | collective-permute-start | bytes 442376 | tf_op jit(solution)/shard_map/ppermute | solution.py:86
  45.1 5.3 %collective-permute-start.5 = (f32[9,32,128]{2,1,0:T(8,128)S(1)}, f32[9,32,128]{2,1,0:T(8,128)S(1)}, u32[]{:S(2)}, u32[]{:S(2)}) collective-permute-start(f32[9,32,128]{2,1,0:T(8,128)S(1)} %add.177), channel_id=1, source_target_pairs={{0,16},{1,9},{2,18},{3,11},{4,20},{5,13},{6,22},{7,15},{8,24},{9,1... | collective-permute-start | bytes 442376 | tf_op jit(solution)/shard_map/ppermute | solution.py:86
  50.5 7.0 %collective-permute-start.6 = (f32[9,32,128]{2,1,0:T(8,128)S(1)}, f32[9,32,128]{2,1,0:T(8,128)S(1)}, u32[]{:S(2)}, u32[]{:S(2)}) collective-permute-start(f32[9,32,128]{2,1,0:T(8,128)S(1)} %add.178), channel_id=1, source_target_pairs={{0,4},{1,3},{2,6},{3,1},{4,0},{5,7},{6,2},{7,5},{8,12},{9,11},{10,... | collective-permute-start | bytes 442376 | tf_op jit(solution)/shard_map/ppermute | solution.py:89
  57.5 6.8 %collective-permute-start.7 = (f32[9,32,256]{2,1,0:T(8,128)S(1)}, f32[9,32,256]{2,1,0:T(8,128)S(1)}, u32[]{:S(2)}, u32[]{:S(2)}) collective-permute-start(f32[9,32,256]{2,1,0:T(8,128)S(1)} %pad_maximum_fusion.2), channel_id=1, source_target_pairs={{0,2},{1,5},{2,0},{3,7},{4,6},{5,1},{6,4},{7,3},{8,10},{9,13},{10,... | collective-permute-start | bytes 884744 | tf_op jit(solution)/shard_map/ppermute | solution.py:89
  64.4 2.2 %collective-permute-start.8 = (f32[9,32,512]{2,1,0:T(8,128)S(1)}, f32[9,32,512]{2,1,0:T(8,128)}, u32[]{:S(2)}, u32[]{:S(2)}) collective-permute-start(f32[9,32,512]{2,1,0:T(8,128)S(1)} %pad_maximum_fusion), channel_id=1, source_target_pairs={{0,1},{1,0},{2,3},{3,2},{4,5},{5,4},{6,7},{7,6},{8,9},{9,8},{10,11... | collective-permute-start | bytes 1769480 | tf_op jit(solution)/shard_map/ppermute | solution.py:89
  69.4 4.3 %collective-permute-start.9 = (f32[4,64,32]{1,2,0:T(8,128)S(1)}, f32[4,64,32]{1,2,0:T(8,128)S(1)}, u32[]{:S(2)}, u32[]{:S(2)}) collective-permute-start(f32[4,64,32]{1,2,0:T(8,128)S(1)} %fusion.2), channel_id=1, source_target_pairs={{0,16},{16,0},{1,17},{17,1},{2,18},{18,2},{3,19},{19,3},{4,20},{20... | collective-permute-start | bytes 98312 | tf_op jit(solution)/shard_map/ppermute | solution.py:20
  75.0 2.1 %collective-permute-start.10 = (f32[9,32,512]{2,1,0:T(8,128)S(1)}, f32[9,32,512]{2,1,0:T(8,128)S(1)}, u32[]{:S(2)}, u32[]{:S(2)}) collective-permute-start(f32[9,32,512]{2,1,0:T(8,128)S(1)} %constant_dynamic-slice_fusion.2), channel_id=1, source_target_pairs={{0,1},{1,0},{2,3},{3,2},{4,5},{5,4},{6,7},{7,6},{8,9},{9,8},{10,11... | collective-permute-start | bytes 1769480 | tf_op jit(solution)/shard_map/ppermute | solution.py:83
  77.2 6.8 %collective-permute-start.11 = (f32[9,32,256]{2,1,0:T(8,128)S(1)}, f32[9,32,256]{2,1,0:T(8,128)S(1)}, u32[]{:S(2)}, u32[]{:S(2)}) collective-permute-start(f32[9,32,256]{2,1,0:T(8,128)S(1)} %constant_dynamic-slice_fusion.1), channel_id=1, source_target_pairs={{0,2},{1,5},{2,0},{3,7},{4,6},{5,1},{6,4},{7,3},{8,10},{9,13},{10,... | collective-permute-start | bytes 884744 | tf_op jit(solution)/shard_map/ppermute | solution.py:83
  84.0 29.1 %copy-start.8 = (s32[9]{0:T(128)S(1)}, s32[9]{0:T(128)}, u32[]{:S(2)}) copy-start(s32[9]{0:T(128)} %param.14) | copy-start | bytes 112
  84.0 5.2 %collective-permute-start.12 = (f32[9,32,128]{2,1,0:T(8,128)S(1)}, f32[9,32,128]{2,1,0:T(8,128)S(1)}, u32[]{:S(2)}, u32[]{:S(2)}) collective-permute-start(f32[9,32,128]{2,1,0:T(8,128)S(1)} %constant_dynamic-slice_fusion), channel_id=1, source_target_pairs={{0,4},{1,3},{2,6},{3,1},{4,0},{5,7},{6,2},{7,5},{8,12},{9,11},{10,... | collective-permute-start | bytes 442376 | tf_op jit(solution)/shard_map/ppermute | solution.py:83
  89.3 9.9 %collective-permute-start.13 = (f32[9,32,128]{2,1,0:T(8,128)S(1)}, f32[9,32,128]{2,1,0:T(8,128)S(1)}, u32[]{:S(2)}, u32[]{:S(2)}) collective-permute-start(f32[9,32,128]{2,1,0:T(8,128)S(1)} %dynamic-slice_add_fusion.4), channel_id=1, source_target_pairs={{0,8},{1,17},{2,10},{3,19},{4,12},{5,21},{6,14},{7,23},{8,0},{9,25... | collective-permute-start | bytes 442376 | tf_op jit(solution)/shard_map/ppermute | solution.py:86
  99.2 5.2 %collective-permute-start.14 = (f32[9,32,128]{2,1,0:T(8,128)S(1)}, f32[9,32,128]{2,1,0:T(8,128)S(1)}, u32[]{:S(2)}, u32[]{:S(2)}) collective-permute-start(f32[9,32,128]{2,1,0:T(8,128)S(1)} %add.186), channel_id=1, source_target_pairs={{0,16},{1,9},{2,18},{3,11},{4,20},{5,13},{6,22},{7,15},{8,24},{9,1... | collective-permute-start | bytes 442376 | tf_op jit(solution)/shard_map/ppermute | solution.py:86
  104.4 7.1 %collective-permute-start.15 = (f32[9,32,128]{2,1,0:T(8,128)S(1)}, f32[9,32,128]{2,1,0:T(8,128)S(1)}, u32[]{:S(2)}, u32[]{:S(2)}) collective-permute-start(f32[9,32,128]{2,1,0:T(8,128)S(1)} %add.187), channel_id=1, source_target_pairs={{0,4},{1,3},{2,6},{3,1},{4,0},{5,7},{6,2},{7,5},{8,12},{9,11},{10,... | collective-permute-start | bytes 442376 | tf_op jit(solution)/shard_map/ppermute | solution.py:89
  111.6 6.8 %collective-permute-start.16 = (f32[9,32,256]{2,1,0:T(8,128)S(1)}, f32[9,32,256]{2,1,0:T(8,128)S(1)}, u32[]{:S(2)}, u32[]{:S(2)}) collective-permute-start(f32[9,32,256]{2,1,0:T(8,128)S(1)} %pad_maximum_fusion.3), channel_id=1, source_target_pairs={{0,2},{1,5},{2,0},{3,7},{4,6},{5,1},{6,4},{7,3},{8,10},{9,13},{10,... | collective-permute-start | bytes 884744 | tf_op jit(solution)/shard_map/ppermute | solution.py:89
  113.3 5.3 %copy-start.7 = (s32[4]{0:T(128)S(1)}, s32[4]{0:T(128)}, u32[]{:S(2)}) copy-start(s32[4]{0:T(128)} %param.13) | copy-start | bytes 52
  113.3 5.5 %copy-start.6 = (f32[5,1024]{1,0:T(8,128)S(1)}, f32[5,1024]{1,0:T(8,128)}, u32[]{:S(2)}) copy-start(f32[5,1024]{1,0:T(8,128)} %param.19) | copy-start | bytes 61444
  118.5 2.1 %collective-permute-start.17 = (f32[9,32,512]{2,1,0:T(8,128)S(1)}, f32[9,32,512]{2,1,0:T(8,128)S(1)}, u32[]{:S(2)}, u32[]{:S(2)}) collective-permute-start(f32[9,32,512]{2,1,0:T(8,128)S(1)} %pad_maximum_fusion.1), channel_id=1, source_target_pairs={{0,1},{1,0},{2,3},{3,2},{4,5},{5,4},{6,7},{7,6},{8,9},{9,8},{10,11... | collective-permute-start | bytes 1769480 | tf_op jit(solution)/shard_map/ppermute | solution.py:89
  119.4 1.2 copy-start.3

commit v7 on v6

--- a/solution.py
+++ b/solution.py
@@ -117,23 +117,23 @@
         jnp.float32
     )
     combined = gradient[0].astype(jnp.float32) + feedback[0]
-    q_tiles = _pick_rows(start_basis, tile_matrix)
+    q_tiles = start_basis.at[tile_matrix].get(mode="promise_in_bounds")
     first_local = jnp.einsum("tkd,tds->tks", combined, q_tiles, precision=TOP_PRECISION)
     left_size = first_local.size
     carried = jnp.concatenate([first_local.reshape(-1), vector_grad[0].reshape(-1)])
     carried = swap_sum(carried, "rep")
     first_left = carried[:left_size].reshape(first_local.shape) / replicas
     vector_summed = carried[left_size:].reshape(vector_grad.shape[1:])
-    mix_first = _pick_rows(inverse_gram_factors[0], tile_matrix)
+    mix_first = inverse_gram_factors[0].at[tile_matrix].get(mode="promise_in_bounds")
     first_ortho = jnp.einsum("tks,tsa->tka", first_left, mix_first, precision=TOP_PRECISION)
     first_parts = jnp.einsum("tkd,tks->tsd", combined, first_ortho, precision=TOP_PRECISION)
     first_table = _scatter_rows(first_parts, tile_matrix, matrix_count)
     first_rows = table_rows(first_table, tile_matrix, replicas, n_own) / replicas
-    mix_right = _pick_rows(inverse_gram_factors[1], tile_matrix)
+    mix_right = inverse_gram_factors[1].at[tile_matrix].get(mode="promise_in_bounds")
     right_rows = jnp.einsum("tjw,tjd->twd", mix_right, first_rows, precision=TOP_PRECISION)
     second_local = jnp.einsum("tkd,tsd->tks", combined, right_rows, precision=TOP_PRECISION)
     second_left = swap_sum(second_local, "rep") / replicas
-    mix_second = _pick_rows(inverse_gram_factors[2], tile_matrix)
+    mix_second = inverse_gram_factors[2].at[tile_matrix].get(mode="promise_in_bounds")
     second_ortho = jnp.einsum("tks,tsa->tka", second_left, mix_second, precision=TOP_PRECISION)
     second_parts = jnp.einsum("tkd,tks->tsd", combined, second_ortho, precision=TOP_PRECISION)
     second_table = _scatter_rows(second_parts, tile_matrix, matrix_count)

time: 124 us -> 132 us (1.065)
  starting transfers between devices: 31.9 us -> 23.9 us
  local copies, waits for them, and re-layouts: 6.04 us -> 13.4 us
  other arithmetic: 2.77 us -> 8.99 us
  waiting for transfers between devices: 64.8 us -> 69 us
    gather x0 -> x4, local copies, waits for them, and re-layouts: none -> 4.05 us  [the longest x1 1.46 us: local(): inverse_gram_factors[1].at[tile_matrix].get(mode='promise_in_bounds')]
    ppermute x4, starting transfers between devices: 10.3 us -> 6.44 us  [table_rows(): cur = cur + lax.ppermute(cur, axes, perm_of(p0, p1))]
    unnamed x18 -> x22, local copies, waits for them, and re-layouts: 0.05 us -> 3.71 us
    ppermute x4, waiting for transfers between devices: 19.6 us -> 23.1 us  [table_rows(): cur = cur + lax.ppermute(cur, axes, perm_of(p0, p1))]
    add x6, other arithmetic: 1.42 us -> 3.45 us  [table_rows(): cur = keep + lax.ppermute(send, axes, perm_of(p0, p1))]
    ppermute x6, waiting for transfers between devices: 19.9 us -> 21.8 us  [table_rows(): cur = keep + lax.ppermute(send, axes, perm_of(p0, p1))]
    squeeze x0 -> x1, local copies, waits for them, and re-layouts: none -> 1.79 us  [local(): inverse_gram_factors[0].at[tile_matrix].get(mode='promise_in_bounds')]
    ppermute x6, starting transfers between devices: 8.41 us -> 6.71 us  [table_rows(): cur = keep + lax.ppermute(send, axes, perm_of(p0, p1))]
  transfers between devices with their start and end apart: 18 -> 18, of which waited for: 18 -> 17; matrix products, arithmetic and copies ran while one was open for 2% -> 6% of each run, Pallas kernels for 0% -> 0%
where the time goes in v7:
time: 132 us
  waiting for transfers between devices  69 us (52%)
  starting transfers between devices  23.9 us (18%)
  local copies, waits for them, and re-layouts  13.4 us (10%)
  other arithmetic  8.99 us (7%)
  between operations  8.65 us (7%)
  matrix products  7.72 us (6%)
    ppermute x4, waiting for transfers between devices, table_rows(): cur = cur + lax.ppermute(cur, axes, perm_of(p0, p1))  23.1 us
    ppermute x6, waiting for transfers between devices, table_rows(): cur = keep + lax.ppermute(send, axes, perm_of(p0, p1))  21.8 us
    ppermute x6, waiting for transfers between devices, table_rows(): other = lax.ppermute(cur, axes, perm_of(p0, p1))  21.5 us
    ppermute x6, starting transfers between devices, table_rows(): other = lax.ppermute(cur, axes, perm_of(p0, p1))  7.4 us
    ppermute x6, starting transfers between devices, table_rows(): cur = keep + lax.ppermute(send, axes, perm_of(p0, p1))  6.71 us
    ppermute x4, starting transfers between devices, table_rows(): cur = cur + lax.ppermute(cur, axes, perm_of(p0, p1))  6.44 us
    unnamed x22, local copies, waits for them, and re-layouts  3.71 us
    add x6, other arithmetic, table_rows(): cur = keep + lax.ppermute(send, axes, perm_of(p0, p1))  3.45 us
  transfers between devices with their start and end apart: 18, of which 17 were waited for; matrix products, arithmetic and copies ran while one was open for 6% of the time, Pallas kernels for 0%

profile of v7, /device:TPU:0, one launch (start us, length us, event | category | flops | bytes accessed | tf_op | source)
XLA Modules:
  0.0 131.7 jit_solution(14480287313229539200)
XLA Ops:
  4.5 3.0 %collective-permute-start = (f32[13312]{0:T(1024)S(1)}, f32[13312]{0:T(1024)S(1)}, u32[]{:S(2)}, u32[]{:S(2)}) collective-permute-start(f32[13312]{0:T(1024)S(1)} %pad_maximum_fusion.8), channel_id=1, source_target_pairs={{0,16},{16,0},{1,17},{17,1},{2,18},{18,2},{3,19},{19,3},{4,20},{20... | collective-permute-start | bytes 159752 | tf_op jit(solution)/shard_map/ppermute | solution.py:20
  7.5 1.8 %slice_bitcast_fusion.1 = (f32[9,32,32]{2,1,0:T(8,128)S(1)}, f32[9,32,32]{2,1,0:T(8,128)}, f32[9,32,32]{2,1,0:T(8,128)}) fusion(f32[3,9,32,32]{3,2,1,0:T(8,128)} %param.17), kind=kLoop, calls=%fused_computation.63 | loop fusion | bytes 221184 | tf_op jit(solution)/shard_map/squeeze | solution.py:127
  20.7 2.1 %collective-permute-done.1 = f32[9,32,512]{2,1,0:T(8,128)} collective-permute-done((f32[9,32,512]{2,1,0:T(8,128)S(1)}, f32[9,32,512]{2,1,0:T(8,128)}, u32[]{:S(2)}, u32[]{:S(2)}) %collective-permute-start.1) | collective-permute-done | bytes 589856 | tf_op jit(solution)/shard_map/ppermute | solution.py:83
  22.8 1.3 %dynamic-slice_add_fusion.1 = f32[9,32,512]{2,1,0:T(8,128)S(1)} fusion(f32[9,32,512]{2,1,0:T(8,128)} %collective-permute-done.1, f32[9,32,1024]{2,1,0:T(8,128)} %copy-done.3, s32[]{:T(128)S(6)} %select_n.154), kind=kLoop, calls=%fused_computation.37 | loop fusion | flops 147456 | bytes 1769476 | tf_op jit(solution)/shard_map/add | solution.py:83
  24.9 1.5 %collective-permute-start.2 = (f32[9,32,256]{2,1,0:T(8,128)}, f32[9,32,256]{2,1,0:T(8,128)}, u32[]{:S(2)}, u32[]{:S(2)}) collective-permute-start(f32[9,32,256]{2,1,0:T(8,128)} %constant_dynamic-slice_fusion.12), channel_id=1, source_target_pairs={{0,2},{1,5},{2,0},{3,7},{4,6},{5,1},{6,4},{7,3},{8,10},{9,13},{10,... | collective-permute-start | bytes 884744 | tf_op jit(solution)/shard_map/ppermute | solution.py:83
  26.4 5.5 %collective-permute-done.2 = f32[9,32,256]{2,1,0:T(8,128)} collective-permute-done((f32[9,32,256]{2,1,0:T(8,128)}, f32[9,32,256]{2,1,0:T(8,128)}, u32[]{:S(2)}, u32[]{:S(2)}) %collective-permute-start.2) | collective-permute-done | bytes 294944 | tf_op jit(solution)/shard_map/ppermute | solution.py:83
  33.7 1.6 %collective-permute-start.3 = (f32[9,32,128]{2,1,0:T(8,128)S(1)}, f32[9,32,128]{2,1,0:T(8,128)S(1)}, u32[]{:S(2)}, u32[]{:S(2)}) collective-permute-start(f32[9,32,128]{2,1,0:T(8,128)S(1)} %constant_dynamic-slice_fusion.11), channel_id=1, source_target_pairs={{0,4},{1,3},{2,6},{3,1},{4,0},{5,7},{6,2},{7,5},{8,12},{9,11},{10,... | collective-permute-start | bytes 442376 | tf_op jit(solution)/shard_map/ppermute | solution.py:83
  35.3 3.6 %collective-permute-done.3 = f32[9,32,128]{2,1,0:T(8,128)S(1)} collective-permute-done((f32[9,32,128]{2,1,0:T(8,128)S(1)}, f32[9,32,128]{2,1,0:T(8,128)S(1)}, u32[]{:S(2)}, u32[]{:S(2)}) %collective-permute-start.3) | collective-permute-done | bytes 147488 | tf_op jit(solution)/shard_map/ppermute | solution.py:83
  39.8 2.7 %collective-permute-start.4 = (f32[9,32,128]{2,1,0:T(8,128)S(1)}, f32[9,32,128]{2,1,0:T(8,128)S(1)}, u32[]{:S(2)}, u32[]{:S(2)}) collective-permute-start(f32[9,32,128]{2,1,0:T(8,128)S(1)} %dynamic-slice_add_fusion.5), channel_id=1, source_target_pairs={{0,8},{1,17},{2,10},{3,19},{4,12},{5,21},{6,14},{7,23},{8,0},{9,25... | collective-permute-start | bytes 442376 | tf_op jit(solution)/shard_map/ppermute | solution.py:86
  42.5 7.1 %collective-permute-done.4 = f32[9,32,128]{2,1,0:T(8,128)S(1)} collective-permute-done((f32[9,32,128]{2,1,0:T(8,128)S(1)}, f32[9,32,128]{2,1,0:T(8,128)S(1)}, u32[]{:S(2)}, u32[]{:S(2)}) %collective-permute-start.4) | collective-permute-done | bytes 147488 | tf_op jit(solution)/shard_map/ppermute | solution.py:86
  49.6 5.1 %collective-permute-done.5 = f32[9,32,128]{2,1,0:T(8,128)S(1)} collective-permute-done((f32[9,32,128]{2,1,0:T(8,128)S(1)}, f32[9,32,128]{2,1,0:T(8,128)S(1)}, u32[]{:S(2)}, u32[]{:S(2)}) %collective-permute-start.5) | collective-permute-done | bytes 147488 | tf_op jit(solution)/shard_map/ppermute | solution.py:86
  54.8 1.8 %collective-permute-start.6 = (f32[9,32,128]{2,1,0:T(8,128)S(1)}, f32[9,32,128]{2,1,0:T(8,128)S(1)}, u32[]{:S(2)}, u32[]{:S(2)}) collective-permute-start(f32[9,32,128]{2,1,0:T(8,128)S(1)} %add.167), channel_id=1, source_target_pairs={{0,4},{1,3},{2,6},{3,1},{4,0},{5,7},{6,2},{7,5},{8,12},{9,11},{10,... | collective-permute-start | bytes 442376 | tf_op jit(solution)/shard_map/ppermute | solution.py:89
  56.5 5.0 %collective-permute-done.6 = f32[9,32,128]{2,1,0:T(8,128)S(1)} collective-permute-done((f32[9,32,128]{2,1,0:T(8,128)S(1)}, f32[9,32,128]{2,1,0:T(8,128)S(1)}, u32[]{:S(2)}, u32[]{:S(2)}) %collective-permute-start.6) | collective-permute-done | bytes 147488 | tf_op jit(solution)/shard_map/ppermute | solution.py:89
  62.3 1.6 %collective-permute-start.7 = (f32[9,32,256]{2,1,0:T(8,128)S(1)}, f32[9,32,256]{2,1,0:T(8,128)}, u32[]{:S(2)}, u32[]{:S(2)}) collective-permute-start(f32[9,32,256]{2,1,0:T(8,128)S(1)} %pad_maximum_fusion.2), channel_id=1, source_target_pairs={{0,2},{1,5},{2,0},{3,7},{4,6},{5,1},{6,4},{7,3},{8,10},{9,13},{10,... | collective-permute-start | bytes 884744 | tf_op jit(solution)/shard_map/ppermute | solution.py:89
  63.9 5.3 %collective-permute-done.7 = f32[9,32,256]{2,1,0:T(8,128)} collective-permute-done((f32[9,32,256]{2,1,0:T(8,128)S(1)}, f32[9,32,256]{2,1,0:T(8,128)}, u32[]{:S(2)}, u32[]{:S(2)}) %collective-permute-start.7) | collective-permute-done | bytes 294944 | tf_op jit(solution)/shard_map/ppermute | solution.py:89
  71.1 1.5 %gather_fusion = f32[4,32,32]{2,1,0:T(8,128)S(1)} fusion(f32[9,32,32]{2,1,0:T(8,128)} %get-tuple-element.30, s32[1024]{0:T(1024)S(1)} %pad_clamp_fusion), kind=kCustom, calls=%fused_computation | custom fusion | bytes 32784 | tf_op jit(solution)/shard_map/gather | solution.py:132
  76.5 1.5 %gather_fusion.3 = f32[4,32,32]{2,1,0:T(8,128)S(1)} fusion(f32[9,32,32]{2,1,0:T(8,128)} %get-tuple-element.31, s32[1024]{0:T(1024)S(1)} %pad_clamp_fusion), kind=kCustom, calls=%fused_computation.3 | custom fusion | bytes 32784 | tf_op jit(solution)/shard_map/gather | solution.py:136
  78.0 2.6 %collective-permute-done.9 = f32[4,64,32]{1,2,0:T(8,128)S(1)} collective-permute-done((f32[4,64,32]{1,2,0:T(8,128)S(1)}, f32[4,64,32]{1,2,0:T(8,128)S(1)}, u32[]{:S(2)}, u32[]{:S(2)}) %collective-permute-start.9) | collective-permute-done | bytes 32800 | tf_op jit(solution)/shard_map/ppermute | solution.py:20
  81.9 2.0 %collective-permute-done.10 = f32[9,32,512]{2,1,0:T(8,128)S(1)} collective-permute-done((f32[9,32,512]{2,1,0:T(8,128)S(1)}, f32[9,32,512]{2,1,0:T(8,128)S(1)}, u32[]{:S(2)}, u32[]{:S(2)}) %collective-permute-start.10) | collective-permute-done | bytes 589856 | tf_op jit(solution)/shard_map/ppermute | solution.py:83
  84.1 1.7 %collective-permute-start.11 = (f32[9,32,256]{2,1,0:T(8,128)S(1)}, f32[9,32,256]{2,1,0:T(8,128)S(1)}, u32[]{:S(2)}, u32[]{:S(2)}) collective-permute-start(f32[9,32,256]{2,1,0:T(8,128)S(1)} %constant_dynamic-slice_fusion.1), channel_id=1, source_target_pairs={{0,2},{1,5},{2,0},{3,7},{4,6},{5,1},{6,4},{7,3},{8,10},{9,13},{10,... | collective-permute-start | bytes 884744 | tf_op jit(solution)/shard_map/ppermute | solution.py:83
  85.7 5.1 %collective-permute-done.11 = f32[9,32,256]{2,1,0:T(8,128)S(1)} collective-permute-done((f32[9,32,256]{2,1,0:T(8,128)S(1)}, f32[9,32,256]{2,1,0:T(8,128)S(1)}, u32[]{:S(2)}, u32[]{:S(2)}) %collective-permute-start.11) | collective-permute-done | bytes 294944 | tf_op jit(solution)/shard_map/ppermute | solution.py:83
  91.0 1.8 %collective-permute-start.12 = (f32[9,32,128]{2,1,0:T(8,128)S(1)}, f32[9,32,128]{2,1,0:T(8,128)S(1)}, u32[]{:S(2)}, u32[]{:S(2)}) collective-permute-start(f32[9,32,128]{2,1,0:T(8,128)S(1)} %constant_dynamic-slice_fusion), channel_id=1, source_target_pairs={{0,4},{1,3},{2,6},{3,1},{4,0},{5,7},{6,2},{7,5},{8,12},{9,11},{10,... | collective-permute-start | bytes 442376 | tf_op jit(solution)/shard_map/ppermute | solution.py:83
  92.7 3.5 %collective-permute-done.12 = f32[9,32,128]{2,1,0:T(8,128)S(1)} collective-permute-done((f32[9,32,128]{2,1,0:T(8,128)S(1)}, f32[9,32,128]{2,1,0:T(8,128)S(1)}, u32[]{:S(2)}, u32[]{:S(2)}) %collective-permute-start.12) | collective-permute-done | bytes 147488 | tf_op jit(solution)/shard_map/ppermute | solution.py:83
  96.2 3.1 %collective-permute-start.13 = (f32[9,32,128]{2,1,0:T(8,128)S(1)}, f32[9,32,128]{2,1,0:T(8,128)S(1)}, u32[]{:S(2)}, u32[]{:S(2)}) collective-permute-start(f32[9,32,128]{2,1,0:T(8,128)S(1)} %dynamic-slice_add_fusion.4), channel_id=1, source_target_pairs={{0,8},{1,17},{2,10},{3,19},{4,12},{5,21},{6,14},{7,23},{8,0},{9,25... | collective-permute-start | bytes 442376 | tf_op jit(solution)/shard_map/ppermute | solution.py:86
  99.3 6.3 %collective-permute-done.13 = f32[9,32,128]{2,1,0:T(8,128)S(1)} collective-permute-done((f32[9,32,128]{2,1,0:T(8,128)S(1)}, f32[9,32,128]{2,1,0:T(8,128)S(1)}, u32[]{:S(2)}, u32[]{:S(2)}) %collective-permute-start.13) | collective-permute-done | bytes 147488 | tf_op jit(solution)/shard_map/ppermute | solution.py:86
  106.2 4.6 %collective-permute-done.14 = f32[9,32,128]{2,1,0:T(8,128)S(1)} collective-permute-done((f32[9,32,128]{2,1,0:T(8,128)S(1)}, f32[9,32,128]{2,1,0:T(8,128)S(1)}, u32[]{:S(2)}, u32[]{:S(2)}) %collective-permute-start.14) | collective-permute-done | bytes 147488 | tf_op jit(solution)/shard_map/ppermute | solution.py:86
  110.9 2.4 %collective-permute-start.15 = (f32[9,32,128]{2,1,0:T(8,128)S(1)}, f32[9,32,128]{2,1,0:T(8,128)S(1)}, u32[]{:S(2)}, u32[]{:S(2)}) collective-permute-start(f32[9,32,128]{2,1,0:T(8,128)S(1)} %add.176), channel_id=1, source_target_pairs={{0,4},{1,3},{2,6},{3,1},{4,0},{5,7},{6,2},{7,5},{8,12},{9,11},{10,... | collective-permute-start | bytes 442376 | tf_op jit(solution)/shard_map/ppermute | solution.py:89
  113.3 4.7 %collective-permute-done.15 = f32[9,32,128]{2,1,0:T(8,128)S(1)} collective-permute-done((f32[9,32,128]{2,1,0:T(8,128)S(1)}, f32[9,32,128]{2,1,0:T(8,128)S(1)}, u32[]{:S(2)}, u32[]{:S(2)}) %collective-permute-start.15) | collective-permute-done | bytes 147488 | tf_op jit(solution)/shard_map/ppermute | solution.py:89
  118.0 1.6 %collective-permute-start.16 = (f32[9,32,256]{2,1,0:T(8,128)S(1)}, f32[9,32,256]{2,1,0:T(8,128)S(1)}, u32[]{:S(2)}, u32[]{:S(2)}) collective-permute-start(f32[9,32,256]{2,1,0:T(8,128)S(1)} %pad_maximum_fusion.3), channel_id=1, source_target_pairs={{0,2},{1,5},{2,0},{3,7},{4,6},{5,1},{6,4},{7,3},{8,10},{9,13},{10,... | collective-permute-start | bytes 884744 | tf_op jit(solution)/shard_map/ppermute | solution.py:89
  119.9 4.9 %collective-permute-done.16 = f32[9,32,256]{2,1,0:T(8,128)S(1)} collective-permute-done((f32[9,32,256]{2,1,0:T(8,128)S(1)}, f32[9,32,256]{2,1,0:T(8,128)S(1)}, u32[]{:S(2)}, u32[]{:S(2)}) %collective-permute-start.16) | collective-permute-done | bytes 294944 | tf_op jit(solution)/shard_map/ppermute | solution.py:89
  126.0 1.4 %multiply_add_fusion.1 = f32[5,1024]{1,0:T(8,128)} fusion(f32[5,1024]{1,0:T(8,128)S(1)} %div.29, f32[5,1024]{1,0:T(8,128)} %param.19), kind=kLoop, calls=%fused_computation.100 | loop fusion | flops 10240 | bytes 61440 | tf_op jit(solution)/shard_map/add | solution.py:149
  129.1 2.5 %multiply_add_fusion = (f32[4,64,1024]{2,1,0:T(8,128)}, f32[1,4,64,1024]{3,2,1,0:T(8,128)}) fusion(f32[4,64,1024]{2,1,0:T(8,128)S(1)} %copy-done.6, f32[4]{0:T(128)S(1)} %convolution_bitcast_fusion, f32[1,4,64,1024]{3,2,1,0:T(8,128)S(1)} %copy-done.1, bf16[1,4,64,1024]{3,2,1,0:T(8,128)(2,1)S(1)} %copy-done.2, f32[4,64,32]{1,2,0:T(8,128)S(1)} %fusion.35, ...), kind=kOutput, calls=%fused_computation.16 | convolution fusion | flops 102498304 | bytes 5275664 | tf_op jit(solution)/shard_map/tks,tsd->tkd/dot_general | solution.py:141
  (92 shorter events, 22.8 us)
Async XLA Ops:
  0.6 1.3 copy-start
  1.9 1.2 copy-start.1
  1.9 1.4 %copy-start.2 = (bf16[1,4,64,1024]{3,2,1,0:T(8,128)(2,1)S(1)}, bf16[1,4,64,1024]{3,2,1,0:T(8,128)(2,1)}, u32[]{:S(2)}) copy-start(bf16[1,4,64,1024]{3,2,1,0:T(8,128)(2,1)} %param.10) | copy-start | bytes 1572868
  3.3 1.2 copy-start.7
  3.3 6.0 %copy-start.8 = (s32[4]{0:T(128)S(1)}, s32[4]{0:T(128)}, u32[]{:S(2)}) copy-start(s32[4]{0:T(128)} %param.13) | copy-start | bytes 52
  4.5 13.5 %collective-permute-start = (f32[13312]{0:T(1024)S(1)}, f32[13312]{0:T(1024)S(1)}, u32[]{:S(2)}, u32[]{:S(2)}) collective-permute-start(f32[13312]{0:T(1024)S(1)} %pad_maximum_fusion.8), channel_id=1, source_target_pairs={{0,16},{16,0},{1,17},{17,1},{2,18},{18,2},{3,19},{19,3},{4,20},{20... | collective-permute-start | bytes 159752 | tf_op jit(solution)/shard_map/ppermute | solution.py:20
  19.5 1.0 copy-start.3
  20.6 2.2 %collective-permute-start.1 = (f32[9,32,512]{2,1,0:T(8,128)S(1)}, f32[9,32,512]{2,1,0:T(8,128)}, u32[]{:S(2)}, u32[]{:S(2)}) collective-permute-start(f32[9,32,512]{2,1,0:T(8,128)S(1)} %constant_dynamic-slice_fusion.13), channel_id=1, source_target_pairs={{0,1},{1,0},{2,3},{3,2},{4,5},{5,4},{6,7},{7,6},{8,9},{9,8},{10,11... | collective-permute-start | bytes 1769480 | tf_op jit(solution)/shard_map/ppermute | solution.py:83
  24.9 7.0 %collective-permute-start.2 = (f32[9,32,256]{2,1,0:T(8,128)}, f32[9,32,256]{2,1,0:T(8,128)}, u32[]{:S(2)}, u32[]{:S(2)}) collective-permute-start(f32[9,32,256]{2,1,0:T(8,128)} %constant_dynamic-slice_fusion.12), channel_id=1, source_target_pairs={{0,2},{1,5},{2,0},{3,7},{4,6},{5,1},{6,4},{7,3},{8,10},{9,13},{10,... | collective-permute-start | bytes 884744 | tf_op jit(solution)/shard_map/ppermute | solution.py:83
  32.9 0.7 copy-start.5
  33.7 5.2 %collective-permute-start.3 = (f32[9,32,128]{2,1,0:T(8,128)S(1)}, f32[9,32,128]{2,1,0:T(8,128)S(1)}, u32[]{:S(2)}, u32[]{:S(2)}) collective-permute-start(f32[9,32,128]{2,1,0:T(8,128)S(1)} %constant_dynamic-slice_fusion.11), channel_id=1, source_target_pairs={{0,4},{1,3},{2,6},{3,1},{4,0},{5,7},{6,2},{7,5},{8,12},{9,11},{10,... | collective-permute-start | bytes 442376 | tf_op jit(solution)/shard_map/ppermute | solution.py:83
  39.8 9.7 %collective-permute-start.4 = (f32[9,32,128]{2,1,0:T(8,128)S(1)}, f32[9,32,128]{2,1,0:T(8,128)S(1)}, u32[]{:S(2)}, u32[]{:S(2)}) collective-permute-start(f32[9,32,128]{2,1,0:T(8,128)S(1)} %dynamic-slice_add_fusion.5), channel_id=1, source_target_pairs={{0,8},{1,17},{2,10},{3,19},{4,12},{5,21},{6,14},{7,23},{8,0},{9,25... | collective-permute-start | bytes 442376 | tf_op jit(solution)/shard_map/ppermute | solution.py:86
  49.6 5.2 %collective-permute-start.5 = (f32[9,32,128]{2,1,0:T(8,128)S(1)}, f32[9,32,128]{2,1,0:T(8,128)S(1)}, u32[]{:S(2)}, u32[]{:S(2)}) collective-permute-start(f32[9,32,128]{2,1,0:T(8,128)S(1)} %add.166), channel_id=1, source_target_pairs={{0,16},{1,9},{2,18},{3,11},{4,20},{5,13},{6,22},{7,15},{8,24},{9,1... | collective-permute-start | bytes 442376 | tf_op jit(solution)/shard_map/ppermute | solution.py:86
  54.8 6.8 %collective-permute-start.6 = (f32[9,32,128]{2,1,0:T(8,128)S(1)}, f32[9,32,128]{2,1,0:T(8,128)S(1)}, u32[]{:S(2)}, u32[]{:S(2)}) collective-permute-start(f32[9,32,128]{2,1,0:T(8,128)S(1)} %add.167), channel_id=1, source_target_pairs={{0,4},{1,3},{2,6},{3,1},{4,0},{5,7},{6,2},{7,5},{8,12},{9,11},{10,... | collective-permute-start | bytes 442376 | tf_op jit(solution)/shard_map/ppermute | solution.py:89
  61.6 0.7 copy-start.4
  62.3 6.9 %collective-permute-start.7 = (f32[9,32,256]{2,1,0:T(8,128)S(1)}, f32[9,32,256]{2,1,0:T(8,128)}, u32[]{:S(2)}, u32[]{:S(2)}) collective-permute-start(f32[9,32,256]{2,1,0:T(8,128)S(1)} %pad_maximum_fusion.2), channel_id=1, source_target_pairs={{0,2},{1,5},{2,0},{3,7},{4,6},{5,1},{6,4},{7,3},{8,10},{9,13},{10,... | collective-permute-start | bytes 884744 | tf_op jit(solution)/shard_map/ppermute | solution.py:89
  71.1 2.3 %collective-permute-start.8 = (f32[9,32,512]{2,1,0:T(8,128)}, f32[9,32,512]{2,1,0:T(8,128)}, u32[]{:S(2)}, u32[]{:S(2)}) collective-permute-start(f32[9,32,512]{2,1,0:T(8,128)} %pad_maximum_fusion), channel_id=1, source_target_pairs={{0,1},{1,0},{2,3},{3,2},{4,5},{5,4},{6,7},{7,6},{8,9},{9,8},{10,11... | collective-permute-start | bytes 1769480 | tf_op jit(solution)/shard_map/ppermute | solution.py:89
  76.2 4.3 %collective-permute-start.9 = (f32[4,64,32]{1,2,0:T(8,128)S(1)}, f32[4,64,32]{1,2,0:T(8,128)S(1)}, u32[]{:S(2)}, u32[]{:S(2)}) collective-permute-start(f32[4,64,32]{1,2,0:T(8,128)S(1)} %fusion.2), channel_id=1, source_target_pairs={{0,16},{16,0},{1,17},{17,1},{2,18},{18,2},{3,19},{19,3},{4,20},{20... | collective-permute-start | bytes 98312 | tf_op jit(solution)/shard_map/ppermute | solution.py:20
  81.9 2.1 %collective-permute-start.10 = (f32[9,32,512]{2,1,0:T(8,128)S(1)}, f32[9,32,512]{2,1,0:T(8,128)S(1)}, u32[]{:S(2)}, u32[]{:S(2)}) collective-permute-start(f32[9,32,512]{2,1,0:T(8,128)S(1)} %constant_dynamic-slice_fusion.2), channel_id=1, source_target_pairs={{0,1},{1,0},{2,3},{3,2},{4,5},{5,4},{6,7},{7,6},{8,9},{9,8},{10,11... | collective-permute-start | bytes 1769480 | tf_op jit(solution)/shard_map/ppermute | solution.py:83
  84.1 6.8 %collective-permute-start.11 = (f32[9,32,256]{2,1,0:T(8,128)S(1)}, f32[9,32,256]{2,1,0:T(8,128)S(1)}, u32[]{:S(2)}, u32[]{:S(2)}) collective-permute-start(f32[9,32,256]{2,1,0:T(8,128)S(1)} %constant_dynamic-slice_fusion.1), channel_id=1, source_target_pairs={{0,2},{1,5},{2,0},{3,7},{4,6},{5,1},{6,4},{7,3},{8,10},{9,13},{10,... | collective-permute-start | bytes 884744 | tf_op jit(solution)/shard_map/ppermute | solution.py:83
  90.9 28.7 %copy-start.9 = (s32[9]{0:T(128)S(1)}, s32[9]{0:T(128)}, u32[]{:S(2)}) copy-start(s32[9]{0:T(128)} %param.14) | copy-start | bytes 112
  91.0 28.7 %copy-start.10 = (f32[4]{0:T(128)S(1)}, f32[4]{0:T(128)}, u32[]{:S(2)}) copy-start(f32[4]{0:T(128)} %param.15) | copy-start | bytes 52
  91.0 5.2 %collective-permute-start.12 = (f32[9,32,128]{2,1,0:T(8,128)S(1)}, f32[9,32,128]{2,1,0:T(8,128)S(1)}, u32[]{:S(2)}, u32[]{:S(2)}) collective-permute-start(f32[9,32,128]{2,1,0:T(8,128)S(1)} %constant_dynamic-slice_fusion), channel_id=1, source_target_pairs={{0,4},{1,3},{2,6},{3,1},{4,0},{5,7},{6,2},{7,5},{8,12},{9,11},{10,... | collective-permute-start | bytes 442376 | tf_op jit(solution)/shard_map/ppermute | solution.py:83
  96.2 9.4 %collective-permute-start.13 = (f32[9,32,128]{2,1,0:T(8,128)S(1)}, f32[9,32,128]{2,1,0:T(8,128)S(1)}, u32[]{:S(2)}, u32[]{:S(2)}) collective-permute-start(f32[9,32,128]{2,1,0:T(8,128)S(1)} %dynamic-slice_add_fusion.4), channel_id=1, source_target_pairs={{0,8},{1,17},{2,10},{3,19},{4,12},{5,21},{6,14},{7,23},{8,0},{9,25... | collective-permute-start | bytes 442376 | tf_op jit(solution)/shard_map/ppermute | solution.py:86
  105.6 5.2 %collective-permute-start.14 = (f32[9,32,128]{2,1,0:T(8,128)S(1)}, f32[9,32,128]{2,1,0:T(8,128)S(1)}, u32[]{:S(2)}, u32[]{:S(2)}) collective-permute-start(f32[9,32,128]{2,1,0:T(8,128)S(1)} %add.175), channel_id=1, source_target_pairs={{0,16},{1,9},{2,18},{3,11},{4,20},{5,13},{6,22},{7,15},{8,24},{9,1... | collective-permute-start | bytes 442376 | tf_op jit(solution)/shard_map/ppermute | solution.py:86
  110.9 7.1 %collective-permute-start.15 = (f32[9,32,128]{2,1,0:T(8,128)S(1)}, f32[9,32,128]{2,1,0:T(8,128)S(1)}, u32[]{:S(2)}, u32[]{:S(2)}) collective-permute-start(f32[9,32,128]{2,1,0:T(8,128)S(1)} %add.176), channel_id=1, source_target_pairs={{0,4},{1,3},{2,6},{3,1},{4,0},{5,7},{6,2},{7,5},{8,12},{9,11},{10,... | collective-permute-start | bytes 442376 | tf_op jit(solution)/shard_map/ppermute | solution.py:89
  118.0 6.8 %collective-permute-start.16 = (f32[9,32,256]{2,1,0:T(8,128)S(1)}, f32[9,32,256]{2,1,0:T(8,128)S(1)}, u32[]{:S(2)}, u32[]{:S(2)}) collective-permute-start(f32[9,32,256]{2,1,0:T(8,128)S(1)} %pad_maximum_fusion.3), channel_id=1, source_target_pairs={{0,2},{1,5},{2,0},{3,7},{4,6},{5,1},{6,4},{7,3},{8,10},{9,13},{10,... | collective-permute-start | bytes 884744 | tf_op jit(solution)/shard_map/ppermute | solution.py:89
  125.8 2.3 %collective-permute-start.17 = (f32[9,32,512]{2,1,0:T(8,128)}, f32[9,32,512]{2,1,0:T(8,128)}, u32[]{:S(2)}, u32[]{:S(2)}) collective-permute-start(f32[9,32,512]{2,1,0:T(8,128)} %pad_maximum_fusion.1), channel_id=1, source_target_pairs={{0,1},{1,0},{2,3},{3,2},{4,5},{5,4},{6,7},{7,6},{8,9},{9,8},{10,11... | collective-permute-start | bytes 1769480 | tf_op jit(solution)/shard_map/ppermute | solution.py:89
  127.4 1.8 %copy-start.6 = (f32[4,64,1024]{2,1,0:T(8,128)S(1)}, f32[4,64,1024]{2,1,0:T(8,128)}, u32[]{:S(2)}) copy-start(f32[4,64,1024]{2,1,0:T(8,128)} %param.12) | copy-start | bytes 3145732

commit v8 on v7

--- a/solution.py
+++ b/solution.py
@@ -44,10 +44,11 @@
 
 
 def _scatter_rows(parts, rows, count):
-    table = jnp.zeros((count,) + parts.shape[1:], parts.dtype)
+    slots = jnp.arange(count, dtype=rows.dtype)[:, None, None]
+    table = None
     for i in range(parts.shape[0]):
-        slab = lax.dynamic_index_in_dim(table, rows[i], 0, keepdims=True)
-        table = lax.dynamic_update_index_in_dim(table, slab + parts[i : i + 1], rows[i], 0)
+        term = jnp.where(slots == rows[i], parts[i][None], 0.0)
+        table = term if table is None else table + term
     return table
 
 

time: 132 us -> 134 us (1.015)
  other arithmetic: 8.99 us -> 12.1 us
    eq x0 -> x2, other arithmetic: none -> 2.39 us  [_scatter_rows(): term = jnp.where(slots == rows[i], parts[i][None], 0.0)]
    unnamed x22 -> x34, local copies, waits for them, and re-layouts: 3.71 us -> 3.75 us
  transfers between devices with their start and end apart: 18 -> 18, of which waited for: 17 -> 16; matrix products, arithmetic and copies ran while one was open for 6% -> 8% of each run, Pallas kernels for 0% -> 0%
where the time goes in v8:
time: 134 us
  waiting for transfers between devices  68.5 us (51%)
  starting transfers between devices  23.8 us (18%)
  local copies, waits for them, and re-layouts  13.3 us (10%)
  other arithmetic  12.1 us (9%)
  between operations  8.36 us (6%)
  matrix products  7.72 us (6%)
    ppermute x4, waiting for transfers between devices, table_rows(): cur = cur + lax.ppermute(cur, axes, perm_of(p0, p1))  23.1 us
    ppermute x6, waiting for transfers between devices, table_rows(): cur = keep + lax.ppermute(send, axes, perm_of(p0, p1))  21.8 us
    ppermute x6, waiting for transfers between devices, table_rows(): other = lax.ppermute(cur, axes, perm_of(p0, p1))  20.7 us
    ppermute x6, starting transfers between devices, table_rows(): other = lax.ppermute(cur, axes, perm_of(p0, p1))  7.37 us
    ppermute x6, starting transfers between devices, table_rows(): cur = keep + lax.ppermute(send, axes, perm_of(p0, p1))  6.65 us
    ppermute x4, starting transfers between devices, table_rows(): cur = cur + lax.ppermute(cur, axes, perm_of(p0, p1))  6.44 us
    unnamed x34, local copies, waits for them, and re-layouts  3.75 us
    add x6, other arithmetic, table_rows(): cur = keep + lax.ppermute(send, axes, perm_of(p0, p1))  3.45 us
  transfers between devices with their start and end apart: 18, of which 16 were waited for; matrix products, arithmetic and copies ran while one was open for 8% of the time, Pallas kernels for 0%

profile of v8, /device:TPU:0, one launch (start us, length us, event | category | flops | bytes accessed | tf_op | source)
XLA Modules:
  0.0 133.8 jit_solution(7372599511462912830)
XLA Ops:
  4.5 3.0 %collective-permute-start = (f32[13312]{0:T(1024)S(1)}, f32[13312]{0:T(1024)S(1)}, u32[]{:S(2)}, u32[]{:S(2)}) collective-permute-start(f32[13312]{0:T(1024)S(1)} %pad_maximum_fusion.8), channel_id=1, source_target_pairs={{0,16},{16,0},{1,17},{17,1},{2,18},{18,2},{3,19},{19,3},{4,20},{20... | collective-permute-start | bytes 159752 | tf_op jit(solution)/shard_map/ppermute | solution.py:20
  8.2 1.8 %slice_bitcast_fusion.1 = (f32[9,32,32]{2,1,0:T(8,128)S(1)}, f32[9,32,32]{2,1,0:T(8,128)}, f32[9,32,32]{2,1,0:T(8,128)}) fusion(f32[3,9,32,32]{3,2,1,0:T(8,128)} %param.17), kind=kLoop, calls=%fused_computation.65 | loop fusion | bytes 221184 | tf_op jit(solution)/shard_map/squeeze | solution.py:128
  15.9 2.1 %collective-permute-done.1 = f32[9,32,512]{2,1,0:T(8,128)} collective-permute-done((f32[9,32,512]{2,1,0:T(8,128)S(1)}, f32[9,32,512]{2,1,0:T(8,128)}, u32[]{:S(2)}, u32[]{:S(2)}) %collective-permute-start.1) | collective-permute-done | bytes 589856 | tf_op jit(solution)/shard_map/ppermute | solution.py:84
  18.0 1.3 %dynamic-slice_add_fusion.1 = f32[9,32,512]{2,1,0:T(8,128)S(1)} fusion(f32[9,32,512]{2,1,0:T(8,128)} %collective-permute-done.1, f32[9,32,1024]{2,1,0:T(8,128)} %copy-done.3, s32[]{:T(128)S(6)} %select_n.161), kind=kLoop, calls=%fused_computation.39 | loop fusion | flops 147456 | bytes 1769476 | tf_op jit(solution)/shard_map/add | solution.py:84
  20.1 1.5 %collective-permute-start.2 = (f32[9,32,256]{2,1,0:T(8,128)}, f32[9,32,256]{2,1,0:T(8,128)}, u32[]{:S(2)}, u32[]{:S(2)}) collective-permute-start(f32[9,32,256]{2,1,0:T(8,128)} %constant_dynamic-slice_fusion.12), channel_id=1, source_target_pairs={{0,2},{1,5},{2,0},{3,7},{4,6},{5,1},{6,4},{7,3},{8,10},{9,13},{10,... | collective-permute-start | bytes 884744 | tf_op jit(solution)/shard_map/ppermute | solution.py:84
  21.6 5.5 %collective-permute-done.2 = f32[9,32,256]{2,1,0:T(8,128)} collective-permute-done((f32[9,32,256]{2,1,0:T(8,128)}, f32[9,32,256]{2,1,0:T(8,128)}, u32[]{:S(2)}, u32[]{:S(2)}) %collective-permute-start.2) | collective-permute-done | bytes 294944 | tf_op jit(solution)/shard_map/ppermute | solution.py:84
  28.9 1.6 %collective-permute-start.3 = (f32[9,32,128]{2,1,0:T(8,128)S(1)}, f32[9,32,128]{2,1,0:T(8,128)S(1)}, u32[]{:S(2)}, u32[]{:S(2)}) collective-permute-start(f32[9,32,128]{2,1,0:T(8,128)S(1)} %constant_dynamic-slice_fusion.11), channel_id=1, source_target_pairs={{0,4},{1,3},{2,6},{3,1},{4,0},{5,7},{6,2},{7,5},{8,12},{9,11},{10,... | collective-permute-start | bytes 442376 | tf_op jit(solution)/shard_map/ppermute | solution.py:84
  30.5 3.6 %collective-permute-done.3 = f32[9,32,128]{2,1,0:T(8,128)S(1)} collective-permute-done((f32[9,32,128]{2,1,0:T(8,128)S(1)}, f32[9,32,128]{2,1,0:T(8,128)S(1)}, u32[]{:S(2)}, u32[]{:S(2)}) %collective-permute-start.3) | collective-permute-done | bytes 147488 | tf_op jit(solution)/shard_map/ppermute | solution.py:84
  35.0 2.7 %collective-permute-start.4 = (f32[9,32,128]{2,1,0:T(8,128)S(1)}, f32[9,32,128]{2,1,0:T(8,128)S(1)}, u32[]{:S(2)}, u32[]{:S(2)}) collective-permute-start(f32[9,32,128]{2,1,0:T(8,128)S(1)} %dynamic-slice_add_fusion.5), channel_id=1, source_target_pairs={{0,8},{1,17},{2,10},{3,19},{4,12},{5,21},{6,14},{7,23},{8,0},{9,25... | collective-permute-start | bytes 442376 | tf_op jit(solution)/shard_map/ppermute | solution.py:87
  37.7 7.1 %collective-permute-done.4 = f32[9,32,128]{2,1,0:T(8,128)S(1)} collective-permute-done((f32[9,32,128]{2,1,0:T(8,128)S(1)}, f32[9,32,128]{2,1,0:T(8,128)S(1)}, u32[]{:S(2)}, u32[]{:S(2)}) %collective-permute-start.4) | collective-permute-done | bytes 147488 | tf_op jit(solution)/shard_map/ppermute | solution.py:87
  44.9 5.1 %collective-permute-done.5 = f32[9,32,128]{2,1,0:T(8,128)S(1)} collective-permute-done((f32[9,32,128]{2,1,0:T(8,128)S(1)}, f32[9,32,128]{2,1,0:T(8,128)S(1)}, u32[]{:S(2)}, u32[]{:S(2)}) %collective-permute-start.5) | collective-permute-done | bytes 147488 | tf_op jit(solution)/shard_map/ppermute | solution.py:87
  50.0 1.8 %collective-permute-start.6 = (f32[9,32,128]{2,1,0:T(8,128)S(1)}, f32[9,32,128]{2,1,0:T(8,128)S(1)}, u32[]{:S(2)}, u32[]{:S(2)}) collective-permute-start(f32[9,32,128]{2,1,0:T(8,128)S(1)} %add.143), channel_id=1, source_target_pairs={{0,4},{1,3},{2,6},{3,1},{4,0},{5,7},{6,2},{7,5},{8,12},{9,11},{10,... | collective-permute-start | bytes 442376 | tf_op jit(solution)/shard_map/ppermute | solution.py:90
  51.8 5.0 %collective-permute-done.6 = f32[9,32,128]{2,1,0:T(8,128)S(1)} collective-permute-done((f32[9,32,128]{2,1,0:T(8,128)S(1)}, f32[9,32,128]{2,1,0:T(8,128)S(1)}, u32[]{:S(2)}, u32[]{:S(2)}) %collective-permute-start.6) | collective-permute-done | bytes 147488 | tf_op jit(solution)/shard_map/ppermute | solution.py:90
  57.5 1.6 %collective-permute-start.7 = (f32[9,32,256]{2,1,0:T(8,128)S(1)}, f32[9,32,256]{2,1,0:T(8,128)}, u32[]{:S(2)}, u32[]{:S(2)}) collective-permute-start(f32[9,32,256]{2,1,0:T(8,128)S(1)} %pad_maximum_fusion.2), channel_id=1, source_target_pairs={{0,2},{1,5},{2,0},{3,7},{4,6},{5,1},{6,4},{7,3},{8,10},{9,13},{10,... | collective-permute-start | bytes 884744 | tf_op jit(solution)/shard_map/ppermute | solution.py:90
  59.1 5.3 %collective-permute-done.7 = f32[9,32,256]{2,1,0:T(8,128)} collective-permute-done((f32[9,32,256]{2,1,0:T(8,128)S(1)}, f32[9,32,256]{2,1,0:T(8,128)}, u32[]{:S(2)}, u32[]{:S(2)}) %collective-permute-start.7) | collective-permute-done | bytes 294944 | tf_op jit(solution)/shard_map/ppermute | solution.py:90
  71.1 1.5 %gather_fusion = f32[4,32,32]{2,1,0:T(8,128)S(1)} fusion(f32[9,32,32]{2,1,0:T(8,128)} %get-tuple-element.38, s32[1024]{0:T(1024)S(1)} %pad_clamp_fusion), kind=kCustom, calls=%fused_computation | custom fusion | bytes 32784 | tf_op jit(solution)/shard_map/gather | solution.py:133
  78.1 1.5 %gather_fusion.3 = f32[4,32,32]{2,1,0:T(8,128)S(1)} fusion(f32[9,32,32]{2,1,0:T(8,128)} %get-tuple-element.39, s32[1024]{0:T(1024)S(1)} %pad_clamp_fusion), kind=kCustom, calls=%fused_computation.3 | custom fusion | bytes 32784 | tf_op jit(solution)/shard_map/gather | solution.py:137
  79.5 2.8 %collective-permute-done.9 = f32[4,64,32]{1,2,0:T(8,128)S(1)} collective-permute-done((f32[4,64,32]{1,2,0:T(8,128)S(1)}, f32[4,64,32]{1,2,0:T(8,128)S(1)}, u32[]{:S(2)}, u32[]{:S(2)}) %collective-permute-start.9) | collective-permute-done | bytes 32800 | tf_op jit(solution)/shard_map/ppermute | solution.py:20
  84.1 2.0 %collective-permute-done.10 = f32[9,32,512]{2,1,0:T(8,128)S(1)} collective-permute-done((f32[9,32,512]{2,1,0:T(8,128)S(1)}, f32[9,32,512]{2,1,0:T(8,128)S(1)}, u32[]{:S(2)}, u32[]{:S(2)}) %collective-permute-start.10) | collective-permute-done | bytes 589856 | tf_op jit(solution)/shard_map/ppermute | solution.py:84
  86.2 1.6 %collective-permute-start.11 = (f32[9,32,256]{2,1,0:T(8,128)S(1)}, f32[9,32,256]{2,1,0:T(8,128)S(1)}, u32[]{:S(2)}, u32[]{:S(2)}) collective-permute-start(f32[9,32,256]{2,1,0:T(8,128)S(1)} %constant_dynamic-slice_fusion.5), channel_id=1, source_target_pairs={{0,2},{1,5},{2,0},{3,7},{4,6},{5,1},{6,4},{7,3},{8,10},{9,13},{10,... | collective-permute-start | bytes 884744 | tf_op jit(solution)/shard_map/ppermute | solution.py:84
  87.8 5.2 %collective-permute-done.11 = f32[9,32,256]{2,1,0:T(8,128)S(1)} collective-permute-done((f32[9,32,256]{2,1,0:T(8,128)S(1)}, f32[9,32,256]{2,1,0:T(8,128)S(1)}, u32[]{:S(2)}, u32[]{:S(2)}) %collective-permute-start.11) | collective-permute-done | bytes 294944 | tf_op jit(solution)/shard_map/ppermute | solution.py:84
  93.1 1.8 %collective-permute-start.12 = (f32[9,32,128]{2,1,0:T(8,128)S(1)}, f32[9,32,128]{2,1,0:T(8,128)S(1)}, u32[]{:S(2)}, u32[]{:S(2)}) collective-permute-start(f32[9,32,128]{2,1,0:T(8,128)S(1)} %constant_dynamic-slice_fusion.4), channel_id=1, source_target_pairs={{0,4},{1,3},{2,6},{3,1},{4,0},{5,7},{6,2},{7,5},{8,12},{9,11},{10,... | collective-permute-start | bytes 442376 | tf_op jit(solution)/shard_map/ppermute | solution.py:84
  94.8 3.5 %collective-permute-done.12 = f32[9,32,128]{2,1,0:T(8,128)S(1)} collective-permute-done((f32[9,32,128]{2,1,0:T(8,128)S(1)}, f32[9,32,128]{2,1,0:T(8,128)S(1)}, u32[]{:S(2)}, u32[]{:S(2)}) %collective-permute-start.12) | collective-permute-done | bytes 147488 | tf_op jit(solution)/shard_map/ppermute | solution.py:84
  98.3 3.1 %collective-permute-start.13 = (f32[9,32,128]{2,1,0:T(8,128)S(1)}, f32[9,32,128]{2,1,0:T(8,128)S(1)}, u32[]{:S(2)}, u32[]{:S(2)}) collective-permute-start(f32[9,32,128]{2,1,0:T(8,128)S(1)} %dynamic-slice_add_fusion.4), channel_id=1, source_target_pairs={{0,8},{1,17},{2,10},{3,19},{4,12},{5,21},{6,14},{7,23},{8,0},{9,25... | collective-permute-start | bytes 442376 | tf_op jit(solution)/shard_map/ppermute | solution.py:87
  101.4 6.3 %collective-permute-done.13 = f32[9,32,128]{2,1,0:T(8,128)S(1)} collective-permute-done((f32[9,32,128]{2,1,0:T(8,128)S(1)}, f32[9,32,128]{2,1,0:T(8,128)S(1)}, u32[]{:S(2)}, u32[]{:S(2)}) %collective-permute-start.13) | collective-permute-done | bytes 147488 | tf_op jit(solution)/shard_map/ppermute | solution.py:87
  108.4 4.6 %collective-permute-done.14 = f32[9,32,128]{2,1,0:T(8,128)S(1)} collective-permute-done((f32[9,32,128]{2,1,0:T(8,128)S(1)}, f32[9,32,128]{2,1,0:T(8,128)S(1)}, u32[]{:S(2)}, u32[]{:S(2)}) %collective-permute-start.14) | collective-permute-done | bytes 147488 | tf_op jit(solution)/shard_map/ppermute | solution.py:87
  113.0 2.4 %collective-permute-start.15 = (f32[9,32,128]{2,1,0:T(8,128)S(1)}, f32[9,32,128]{2,1,0:T(8,128)S(1)}, u32[]{:S(2)}, u32[]{:S(2)}) collective-permute-start(f32[9,32,128]{2,1,0:T(8,128)S(1)} %add.156), channel_id=1, source_target_pairs={{0,4},{1,3},{2,6},{3,1},{4,0},{5,7},{6,2},{7,5},{8,12},{9,11},{10,... | collective-permute-start | bytes 442376 | tf_op jit(solution)/shard_map/ppermute | solution.py:90
  115.4 4.7 %collective-permute-done.15 = f32[9,32,128]{2,1,0:T(8,128)S(1)} collective-permute-done((f32[9,32,128]{2,1,0:T(8,128)S(1)}, f32[9,32,128]{2,1,0:T(8,128)S(1)}, u32[]{:S(2)}, u32[]{:S(2)}) %collective-permute-start.15) | collective-permute-done | bytes 147488 | tf_op jit(solution)/shard_map/ppermute | solution.py:90
  120.2 1.6 %collective-permute-start.16 = (f32[9,32,256]{2,1,0:T(8,128)S(1)}, f32[9,32,256]{2,1,0:T(8,128)S(1)}, u32[]{:S(2)}, u32[]{:S(2)}) collective-permute-start(f32[9,32,256]{2,1,0:T(8,128)S(1)} %pad_maximum_fusion.3), channel_id=1, source_target_pairs={{0,2},{1,5},{2,0},{3,7},{4,6},{5,1},{6,4},{7,3},{8,10},{9,13},{10,... | collective-permute-start | bytes 884744 | tf_op jit(solution)/shard_map/ppermute | solution.py:90
  122.0 5.0 %collective-permute-done.16 = f32[9,32,256]{2,1,0:T(8,128)S(1)} collective-permute-done((f32[9,32,256]{2,1,0:T(8,128)S(1)}, f32[9,32,256]{2,1,0:T(8,128)S(1)}, u32[]{:S(2)}, u32[]{:S(2)}) %collective-permute-start.16) | collective-permute-done | bytes 294944 | tf_op jit(solution)/shard_map/ppermute | solution.py:90
  128.1 1.4 %multiply_add_fusion.1 = f32[5,1024]{1,0:T(8,128)} fusion(f32[5,1024]{1,0:T(8,128)S(1)} %div.29, f32[5,1024]{1,0:T(8,128)} %param.19), kind=kLoop, calls=%fused_computation.96 | loop fusion | flops 10240 | bytes 61440 | tf_op jit(solution)/shard_map/add | solution.py:150
  131.3 2.5 %multiply_add_fusion = (f32[4,64,1024]{2,1,0:T(8,128)}, f32[1,4,64,1024]{3,2,1,0:T(8,128)}) fusion(f32[4,64,1024]{2,1,0:T(8,128)S(1)} %copy-done.6, f32[4]{0:T(128)S(1)} %convolution_bitcast_fusion, f32[1,4,64,1024]{3,2,1,0:T(8,128)S(1)} %copy-done.1, bf16[1,4,64,1024]{3,2,1,0:T(8,128)(2,1)S(1)} %copy-done.2, f32[4,64,32]{1,2,0:T(8,128)S(1)} %fusion.29, ...), kind=kOutput, calls=%fused_computation.18 | convolution fusion | flops 102498304 | bytes 5275664 | tf_op jit(solution)/shard_map/tks,tsd->tkd/dot_general | solution.py:142
  (100 shorter events, 25.0 us)
Async XLA Ops:
  0.6 1.3 copy-start
  1.9 1.2 copy-start.1
  1.9 1.4 %copy-start.2 = (bf16[1,4,64,1024]{3,2,1,0:T(8,128)(2,1)S(1)}, bf16[1,4,64,1024]{3,2,1,0:T(8,128)(2,1)}, u32[]{:S(2)}) copy-start(bf16[1,4,64,1024]{3,2,1,0:T(8,128)(2,1)} %param.10) | copy-start | bytes 1572868
  3.3 1.2 copy-start.7
  3.3 4.2 %copy-start.8 = (s32[4]{0:T(128)S(1)}, s32[4]{0:T(128)}, u32[]{:S(2)}) copy-start(s32[4]{0:T(128)} %param.13) | copy-start | bytes 52
  4.5 8.4 %collective-permute-start = (f32[13312]{0:T(1024)S(1)}, f32[13312]{0:T(1024)S(1)}, u32[]{:S(2)}, u32[]{:S(2)}) collective-permute-start(f32[13312]{0:T(1024)S(1)} %pad_maximum_fusion.8), channel_id=1, source_target_pairs={{0,16},{16,0},{1,17},{17,1},{2,18},{18,2},{3,19},{19,3},{4,20},{20... | collective-permute-start | bytes 159752 | tf_op jit(solution)/shard_map/ppermute | solution.py:20
  11.2 3.0 %copy-start.9 = (pred[9]{0:T(512)(128)(4,1)}, pred[9]{0:T(512)(128)(4,1)S(1)}, u32[]{:S(2)}) copy-start(pred[9]{0:T(512)(128)(4,1)S(1)} %get-tuple-element.51) | copy-start | bytes 31
  12.4 1.9 %copy-start.11 = (pred[9]{0:T(512)(128)(4,1)}, pred[9]{0:T(512)(128)(4,1)S(1)}, u32[]{:S(2)}) copy-start(pred[9]{0:T(512)(128)(4,1)S(1)} %get-tuple-element.48) | copy-start | bytes 31
  12.4 1.9 %copy-start.13 = (pred[9]{0:T(512)(128)(4,1)}, pred[9]{0:T(512)(128)(4,1)S(1)}, u32[]{:S(2)}) copy-start(pred[9]{0:T(512)(128)(4,1)S(1)} %get-tuple-element.49) | copy-start | bytes 31
  14.7 1.1 copy-start.3
  15.8 2.2 %collective-permute-start.1 = (f32[9,32,512]{2,1,0:T(8,128)S(1)}, f32[9,32,512]{2,1,0:T(8,128)}, u32[]{:S(2)}, u32[]{:S(2)}) collective-permute-start(f32[9,32,512]{2,1,0:T(8,128)S(1)} %constant_dynamic-slice_fusion.13), channel_id=1, source_target_pairs={{0,1},{1,0},{2,3},{3,2},{4,5},{5,4},{6,7},{7,6},{8,9},{9,8},{10,11... | collective-permute-start | bytes 1769480 | tf_op jit(solution)/shard_map/ppermute | solution.py:84
  20.1 7.0 %collective-permute-start.2 = (f32[9,32,256]{2,1,0:T(8,128)}, f32[9,32,256]{2,1,0:T(8,128)}, u32[]{:S(2)}, u32[]{:S(2)}) collective-permute-start(f32[9,32,256]{2,1,0:T(8,128)} %constant_dynamic-slice_fusion.12), channel_id=1, source_target_pairs={{0,2},{1,5},{2,0},{3,7},{4,6},{5,1},{6,4},{7,3},{8,10},{9,13},{10,... | collective-permute-start | bytes 884744 | tf_op jit(solution)/shard_map/ppermute | solution.py:84
  28.9 5.2 %collective-permute-start.3 = (f32[9,32,128]{2,1,0:T(8,128)S(1)}, f32[9,32,128]{2,1,0:T(8,128)S(1)}, u32[]{:S(2)}, u32[]{:S(2)}) collective-permute-start(f32[9,32,128]{2,1,0:T(8,128)S(1)} %constant_dynamic-slice_fusion.11), channel_id=1, source_target_pairs={{0,4},{1,3},{2,6},{3,1},{4,0},{5,7},{6,2},{7,5},{8,12},{9,11},{10,... | collective-permute-start | bytes 442376 | tf_op jit(solution)/shard_map/ppermute | solution.py:84
  35.0 9.7 %collective-permute-start.4 = (f32[9,32,128]{2,1,0:T(8,128)S(1)}, f32[9,32,128]{2,1,0:T(8,128)S(1)}, u32[]{:S(2)}, u32[]{:S(2)}) collective-permute-start(f32[9,32,128]{2,1,0:T(8,128)S(1)} %dynamic-slice_add_fusion.5), channel_id=1, source_target_pairs={{0,8},{1,17},{2,10},{3,19},{4,12},{5,21},{6,14},{7,23},{8,0},{9,25... | collective-permute-start | bytes 442376 | tf_op jit(solution)/shard_map/ppermute | solution.py:87
  44.8 5.2 %collective-permute-start.5 = (f32[9,32,128]{2,1,0:T(8,128)S(1)}, f32[9,32,128]{2,1,0:T(8,128)S(1)}, u32[]{:S(2)}, u32[]{:S(2)}) collective-permute-start(f32[9,32,128]{2,1,0:T(8,128)S(1)} %add.142), channel_id=1, source_target_pairs={{0,16},{1,9},{2,18},{3,11},{4,20},{5,13},{6,22},{7,15},{8,24},{9,1... | collective-permute-start | bytes 442376 | tf_op jit(solution)/shard_map/ppermute | solution.py:87
  50.0 6.8 %collective-permute-start.6 = (f32[9,32,128]{2,1,0:T(8,128)S(1)}, f32[9,32,128]{2,1,0:T(8,128)S(1)}, u32[]{:S(2)}, u32[]{:S(2)}) collective-permute-start(f32[9,32,128]{2,1,0:T(8,128)S(1)} %add.143), channel_id=1, source_target_pairs={{0,4},{1,3},{2,6},{3,1},{4,0},{5,7},{6,2},{7,5},{8,12},{9,11},{10,... | collective-permute-start | bytes 442376 | tf_op jit(solution)/shard_map/ppermute | solution.py:90
  57.5 6.9 %collective-permute-start.7 = (f32[9,32,256]{2,1,0:T(8,128)S(1)}, f32[9,32,256]{2,1,0:T(8,128)}, u32[]{:S(2)}, u32[]{:S(2)}) collective-permute-start(f32[9,32,256]{2,1,0:T(8,128)S(1)} %pad_maximum_fusion.2), channel_id=1, source_target_pairs={{0,2},{1,5},{2,0},{3,7},{4,6},{5,1},{6,4},{7,3},{8,10},{9,13},{10,... | collective-permute-start | bytes 884744 | tf_op jit(solution)/shard_map/ppermute | solution.py:90
  66.4 8.7 %collective-permute-start.8 = (f32[9,32,512]{2,1,0:T(8,128)}, f32[9,32,512]{2,1,0:T(8,128)}, u32[]{:S(2)}, u32[]{:S(2)}) collective-permute-start(f32[9,32,512]{2,1,0:T(8,128)} %pad_maximum_fusion), channel_id=1, source_target_pairs={{0,1},{1,0},{2,3},{3,2},{4,5},{5,4},{6,7},{7,6},{8,9},{9,8},{10,11... | collective-permute-start | bytes 1769480 | tf_op jit(solution)/shard_map/ppermute | solution.py:90
  77.8 4.6 %collective-permute-start.9 = (f32[4,64,32]{1,2,0:T(8,128)S(1)}, f32[4,64,32]{1,2,0:T(8,128)S(1)}, u32[]{:S(2)}, u32[]{:S(2)}) collective-permute-start(f32[4,64,32]{1,2,0:T(8,128)S(1)} %fusion.2), channel_id=1, source_target_pairs={{0,16},{16,0},{1,17},{17,1},{2,18},{18,2},{3,19},{19,3},{4,20},{20... | collective-permute-start | bytes 98312 | tf_op jit(solution)/shard_map/ppermute | solution.py:20
  82.7 0.8 copy-start.10
  82.7 0.8 copy-start.12
  84.0 2.1 %collective-permute-start.10 = (f32[9,32,512]{2,1,0:T(8,128)S(1)}, f32[9,32,512]{2,1,0:T(8,128)S(1)}, u32[]{:S(2)}, u32[]{:S(2)}) collective-permute-start(f32[9,32,512]{2,1,0:T(8,128)S(1)} %constant_dynamic-slice_fusion.6), channel_id=1, source_target_pairs={{0,1},{1,0},{2,3},{3,2},{4,5},{5,4},{6,7},{7,6},{8,9},{9,8},{10,11... | collective-permute-start | bytes 1769480 | tf_op jit(solution)/shard_map/ppermute | solution.py:84
  86.2 6.8 %collective-permute-start.11 = (f32[9,32,256]{2,1,0:T(8,128)S(1)}, f32[9,32,256]{2,1,0:T(8,128)S(1)}, u32[]{:S(2)}, u32[]{:S(2)}) collective-permute-start(f32[9,32,256]{2,1,0:T(8,128)S(1)} %constant_dynamic-slice_fusion.5), channel_id=1, source_target_pairs={{0,2},{1,5},{2,0},{3,7},{4,6},{5,1},{6,4},{7,3},{8,10},{9,13},{10,... | collective-permute-start | bytes 884744 | tf_op jit(solution)/shard_map/ppermute | solution.py:84
  93.1 28.7 %copy-start.15 = (s32[9]{0:T(128)S(1)}, s32[9]{0:T(128)}, u32[]{:S(2)}) copy-start(s32[9]{0:T(128)} %param.14) | copy-start | bytes 112
  93.1 28.7 %copy-start.16 = (f32[4]{0:T(128)S(1)}, f32[4]{0:T(128)}, u32[]{:S(2)}) copy-start(f32[4]{0:T(128)} %param.15) | copy-start | bytes 52
  93.1 5.2 %collective-permute-start.12 = (f32[9,32,128]{2,1,0:T(8,128)S(1)}, f32[9,32,128]{2,1,0:T(8,128)S(1)}, u32[]{:S(2)}, u32[]{:S(2)}) collective-permute-start(f32[9,32,128]{2,1,0:T(8,128)S(1)} %constant_dynamic-slice_fusion.4), channel_id=1, source_target_pairs={{0,4},{1,3},{2,6},{3,1},{4,0},{5,7},{6,2},{7,5},{8,12},{9,11},{10,... | collective-permute-start | bytes 442376 | tf_op jit(solution)/shard_map/ppermute | solution.py:84
  98.3 9.4 %collective-permute-start.13 = (f32[9,32,128]{2,1,0:T(8,128)S(1)}, f32[9,32,128]{2,1,0:T(8,128)S(1)}, u32[]{:S(2)}, u32[]{:S(2)}) collective-permute-start(f32[9,32,128]{2,1,0:T(8,128)S(1)} %dynamic-slice_add_fusion.4), channel_id=1, source_target_pairs={{0,8},{1,17},{2,10},{3,19},{4,12},{5,21},{6,14},{7,23},{8,0},{9,25... | collective-permute-start | bytes 442376 | tf_op jit(solution)/shard_map/ppermute | solution.py:87
  107.8 5.2 %collective-permute-start.14 = (f32[9,32,128]{2,1,0:T(8,128)S(1)}, f32[9,32,128]{2,1,0:T(8,128)S(1)}, u32[]{:S(2)}, u32[]{:S(2)}) collective-permute-start(f32[9,32,128]{2,1,0:T(8,128)S(1)} %add.155), channel_id=1, source_target_pairs={{0,16},{1,9},{2,18},{3,11},{4,20},{5,13},{6,22},{7,15},{8,24},{9,1... | collective-permute-start | bytes 442376 | tf_op jit(solution)/shard_map/ppermute | solution.py:87
  113.0 7.1 %collective-permute-start.15 = (f32[9,32,128]{2,1,0:T(8,128)S(1)}, f32[9,32,128]{2,1,0:T(8,128)S(1)}, u32[]{:S(2)}, u32[]{:S(2)}) collective-permute-start(f32[9,32,128]{2,1,0:T(8,128)S(1)} %add.156), channel_id=1, source_target_pairs={{0,4},{1,3},{2,6},{3,1},{4,0},{5,7},{6,2},{7,5},{8,12},{9,11},{10,... | collective-permute-start | bytes 442376 | tf_op jit(solution)/shard_map/ppermute | solution.py:90
  120.2 6.8 %collective-permute-start.16 = (f32[9,32,256]{2,1,0:T(8,128)S(1)}, f32[9,32,256]{2,1,0:T(8,128)S(1)}, u32[]{:S(2)}, u32[]{:S(2)}) collective-permute-start(f32[9,32,256]{2,1,0:T(8,128)S(1)} %pad_maximum_fusion.3), channel_id=1, source_target_pairs={{0,2},{1,5},{2,0},{3,7},{4,6},{5,1},{6,4},{7,3},{8,10},{9,13},{10,... | collective-permute-start | bytes 884744 | tf_op jit(solution)/shard_map/ppermute | solution.py:90
  127.9 2.3 %collective-permute-start.17 = (f32[9,32,512]{2,1,0:T(8,128)}, f32[9,32,512]{2,1,0:T(8,128)}, u32[]{:S(2)}, u32[]{:S(2)}) collective-permute-start(f32[9,32,512]{2,1,0:T(8,128)} %pad_maximum_fusion.1), channel_id=1, source_target_pairs={{0,1},{1,0},{2,3},{3,2},{4,5},{5,4},{6,7},{7,6},{8,9},{9,8},{10,11... | collective-permute-start | bytes 1769480 | tf_op jit(solution)/shard_map/ppermute | solution.py:90
  129.5 1.8 %copy-start.6 = (f32[4,64,1024]{2,1,0:T(8,128)S(1)}, f32[4,64,1024]{2,1,0:T(8,128)}, u32[]{:S(2)}) copy-start(f32[4,64,1024]{2,1,0:T(8,128)} %param.12) | copy-start | bytes 3145732
  (3 other events, 2.2 us)

commit v9 on v8

--- a/solution.py
+++ b/solution.py
@@ -37,10 +37,6 @@
         dims[axis] //= 2
         plan.append(axis)
     return plan
-
-
-def _pick_rows(table, rows):
-    return jnp.stack([lax.dynamic_index_in_dim(table, rows[i], 0, keepdims=False) for i in range(rows.shape[0])])
 
 
 def _scatter_rows(parts, rows, count):
@@ -85,18 +81,12 @@
         bits.append(bit)
     for p0, p1 in pairing:
         cur = cur + lax.ppermute(cur, axes, perm_of(p0, p1))
-    steps_back = list(reversed(list(zip(halving, plan, bits))))
-    for index_step, ((p0, p1), axis, bit) in enumerate(steps_back):
+    for (p0, p1), axis, bit in reversed(list(zip(halving, plan, bits))):
         other = lax.ppermute(cur, axes, perm_of(p0, p1))
-        if index_step == len(steps_back) - 1:
-            cur = _pick_rows(cur, rows)
-            other = _pick_rows(other, rows)
         low = jnp.where(bit == 0, cur, other)
         high = jnp.where(bit == 0, other, cur)
         cur = jnp.concatenate([low, high], axis=axis)
-    if not steps_back:
-        cur = _pick_rows(cur, rows)
-    return cur
+    return cur.at[rows].get(mode="promise_in_bounds")
 
 
 def local(

time: 134 us -> 136 us (1.015)
  between operations: 8.36 us -> 1.18 us
  other arithmetic: 12.1 us -> 16.8 us
  local copies, waits for them, and re-layouts: 13.3 us -> 15.1 us
    gather x0 -> x2, local copies, waits for them, and re-layouts: none -> 3.7 us  [table_rows(): return cur.at[rows].get(mode='promise_in_bounds')]
    select_n x6, other arithmetic: 1.25 us -> 3.61 us  [table_rows(): low = jnp.where(bit == 0, cur, other)]
    concatenate x6, other arithmetic: 1.88 us -> 4.09 us  [table_rows(): cur = jnp.concatenate([low, high], axis=axis)]
    dynamic_slice x2 -> x0, local copies, waits for them, and re-layouts: 1.92 us -> none  [_pick_rows(): lax.dynamic_index_in_dim(table, rows[i], 0, keepdims=False)]
    unnamed x34 -> x32, local copies, waits for them, and re-layouts: 3.75 us -> 3.73 us
  transfers between devices with their start and end apart: 18 -> 18, of which waited for: 16 -> 17; matrix products, arithmetic and copies ran while one was open for 8% -> 8% of each run, Pallas kernels for 0% -> 0%
where the time goes in v9:
time: 136 us; the launch traced here: 135 us
  waiting for transfers between devices  69.2 us (51%)
  starting transfers between devices  23.7 us (17%)
  other arithmetic  16.8 us (12%)
  local copies, waits for them, and re-layouts  15.1 us (11%)
  matrix products  8.94 us (7%)
    ppermute x4, waiting for transfers between devices, table_rows(): cur = cur + lax.ppermute(cur, axes, perm_of(p0, p1))  23.1 us
    ppermute x6, waiting for transfers between devices, table_rows(): cur = keep + lax.ppermute(send, axes, perm_of(p0, p1))  21.8 us
    ppermute x6, waiting for transfers between devices, table_rows(): other = lax.ppermute(cur, axes, perm_of(p0, p1))  21.6 us
    ppermute x6, starting transfers between devices, table_rows(): other = lax.ppermute(cur, axes, perm_of(p0, p1))  7.35 us
    ppermute x6, starting transfers between devices, table_rows(): cur = keep + lax.ppermute(send, axes, perm_of(p0, p1))  6.66 us
    ppermute x4, starting transfers between devices, table_rows(): cur = cur + lax.ppermute(cur, axes, perm_of(p0, p1))  6.44 us
    concatenate x6, other arithmetic, table_rows(): cur = jnp.concatenate([low, high], axis=axis)  4.09 us
    dot_general x1, matrix products, local(): jnp.einsum('tks,tsd->tkd', second_ortho, back_rows, precision=TOP_PRECISION)  3.75 us
  transfers between devices with their start and end apart: 18, of which 17 were waited for; matrix products, arithmetic and copies ran while one was open for 8% of the time, Pallas kernels for 0%

profile of v9, /device:TPU:0, one launch (start us, length us, event | category | flops | bytes accessed | tf_op | source)
XLA Modules:
  0.0 134.9 jit_solution(6806459660306968341)
XLA Ops:
  4.5 3.0 %collective-permute-start = (f32[13312]{0:T(1024)S(1)}, f32[13312]{0:T(1024)S(1)}, u32[]{:S(2)}, u32[]{:S(2)}) collective-permute-start(f32[13312]{0:T(1024)S(1)} %pad_maximum_fusion.6), channel_id=1, source_target_pairs={{0,16},{16,0},{1,17},{17,1},{2,18},{18,2},{3,19},{19,3},{4,20},{20... | collective-permute-start | bytes 159752 | tf_op jit(solution)/shard_map/ppermute | solution.py:20
  8.2 1.8 %slice_bitcast_fusion.1 = (f32[9,32,32]{2,1,0:T(8,128)S(1)}, f32[9,32,32]{2,1,0:T(8,128)}, f32[9,32,32]{2,1,0:T(8,128)}) fusion(f32[3,9,32,32]{3,2,1,0:T(8,128)} %param.17), kind=kLoop, calls=%fused_computation.45 | loop fusion | bytes 221184 | tf_op jit(solution)/shard_map/squeeze | solution.py:118
  16.0 2.1 %collective-permute-done.1 = f32[9,32,512]{2,1,0:T(8,128)} collective-permute-done((f32[9,32,512]{2,1,0:T(8,128)S(1)}, f32[9,32,512]{2,1,0:T(8,128)}, u32[]{:S(2)}, u32[]{:S(2)}) %collective-permute-start.1) | collective-permute-done | bytes 589856 | tf_op jit(solution)/shard_map/ppermute | solution.py:80
  20.2 1.5 %collective-permute-start.2 = (f32[9,32,256]{2,1,0:T(8,128)}, f32[9,32,256]{2,1,0:T(8,128)}, u32[]{:S(2)}, u32[]{:S(2)}) collective-permute-start(f32[9,32,256]{2,1,0:T(8,128)} %constant_dynamic-slice_fusion.4), channel_id=1, source_target_pairs={{0,2},{1,5},{2,0},{3,7},{4,6},{5,1},{6,4},{7,3},{8,10},{9,13},{10,... | collective-permute-start | bytes 884744 | tf_op jit(solution)/shard_map/ppermute | solution.py:80
  21.7 5.5 %collective-permute-done.2 = f32[9,32,256]{2,1,0:T(8,128)} collective-permute-done((f32[9,32,256]{2,1,0:T(8,128)}, f32[9,32,256]{2,1,0:T(8,128)}, u32[]{:S(2)}, u32[]{:S(2)}) %collective-permute-start.2) | collective-permute-done | bytes 294944 | tf_op jit(solution)/shard_map/ppermute | solution.py:80
  29.0 1.6 %collective-permute-start.3 = (f32[9,32,128]{2,1,0:T(8,128)S(1)}, f32[9,32,128]{2,1,0:T(8,128)S(1)}, u32[]{:S(2)}, u32[]{:S(2)}) collective-permute-start(f32[9,32,128]{2,1,0:T(8,128)S(1)} %constant_dynamic-slice_fusion.3), channel_id=1, source_target_pairs={{0,4},{1,3},{2,6},{3,1},{4,0},{5,7},{6,2},{7,5},{8,12},{9,11},{10,... | collective-permute-start | bytes 442376 | tf_op jit(solution)/shard_map/ppermute | solution.py:80
  30.6 3.6 %collective-permute-done.3 = f32[9,32,128]{2,1,0:T(8,128)S(1)} collective-permute-done((f32[9,32,128]{2,1,0:T(8,128)S(1)}, f32[9,32,128]{2,1,0:T(8,128)S(1)}, u32[]{:S(2)}, u32[]{:S(2)}) %collective-permute-start.3) | collective-permute-done | bytes 147488 | tf_op jit(solution)/shard_map/ppermute | solution.py:80
  35.1 2.7 %collective-permute-start.4 = (f32[9,32,128]{2,1,0:T(8,128)S(1)}, f32[9,32,128]{2,1,0:T(8,128)S(1)}, u32[]{:S(2)}, u32[]{:S(2)}) collective-permute-start(f32[9,32,128]{2,1,0:T(8,128)S(1)} %dynamic-slice_add_fusion.5), channel_id=1, source_target_pairs={{0,8},{1,17},{2,10},{3,19},{4,12},{5,21},{6,14},{7,23},{8,0},{9,25... | collective-permute-start | bytes 442376 | tf_op jit(solution)/shard_map/ppermute | solution.py:83
  37.8 7.1 %collective-permute-done.4 = f32[9,32,128]{2,1,0:T(8,128)S(1)} collective-permute-done((f32[9,32,128]{2,1,0:T(8,128)S(1)}, f32[9,32,128]{2,1,0:T(8,128)S(1)}, u32[]{:S(2)}, u32[]{:S(2)}) %collective-permute-start.4) | collective-permute-done | bytes 147488 | tf_op jit(solution)/shard_map/ppermute | solution.py:83
  44.9 5.1 %collective-permute-done.5 = f32[9,32,128]{2,1,0:T(8,128)S(1)} collective-permute-done((f32[9,32,128]{2,1,0:T(8,128)S(1)}, f32[9,32,128]{2,1,0:T(8,128)S(1)}, u32[]{:S(2)}, u32[]{:S(2)}) %collective-permute-start.5) | collective-permute-done | bytes 147488 | tf_op jit(solution)/shard_map/ppermute | solution.py:83
  50.1 1.8 %collective-permute-start.6 = (f32[9,32,128]{2,1,0:T(8,128)S(1)}, f32[9,32,128]{2,1,0:T(8,128)S(1)}, u32[]{:S(2)}, u32[]{:S(2)}) collective-permute-start(f32[9,32,128]{2,1,0:T(8,128)S(1)} %add.120), channel_id=1, source_target_pairs={{0,4},{1,3},{2,6},{3,1},{4,0},{5,7},{6,2},{7,5},{8,12},{9,11},{10,... | collective-permute-start | bytes 442376 | tf_op jit(solution)/shard_map/ppermute | solution.py:85
  51.8 5.0 %collective-permute-done.6 = f32[9,32,128]{2,1,0:T(8,128)S(1)} collective-permute-done((f32[9,32,128]{2,1,0:T(8,128)S(1)}, f32[9,32,128]{2,1,0:T(8,128)S(1)}, u32[]{:S(2)}, u32[]{:S(2)}) %collective-permute-start.6) | collective-permute-done | bytes 147488 | tf_op jit(solution)/shard_map/ppermute | solution.py:85
  57.6 1.6 %collective-permute-start.7 = (f32[9,32,256]{2,1,0:T(8,128)S(1)}, f32[9,32,256]{2,1,0:T(8,128)}, u32[]{:S(2)}, u32[]{:S(2)}) collective-permute-start(f32[9,32,256]{2,1,0:T(8,128)S(1)} %pad_maximum_fusion.4), channel_id=1, source_target_pairs={{0,2},{1,5},{2,0},{3,7},{4,6},{5,1},{6,4},{7,3},{8,10},{9,13},{10,... | collective-permute-start | bytes 884744 | tf_op jit(solution)/shard_map/ppermute | solution.py:85
  59.2 5.3 %collective-permute-done.7 = f32[9,32,256]{2,1,0:T(8,128)} collective-permute-done((f32[9,32,256]{2,1,0:T(8,128)S(1)}, f32[9,32,256]{2,1,0:T(8,128)}, u32[]{:S(2)}, u32[]{:S(2)}) %collective-permute-start.7) | collective-permute-done | bytes 294944 | tf_op jit(solution)/shard_map/ppermute | solution.py:85
  66.4 1.5 %gather_fusion = f32[4,32,32]{2,1,0:T(8,128)S(1)} fusion(f32[9,32,32]{2,1,0:T(8,128)} %get-tuple-element.22, s32[1024]{0:T(1024)S(1)} %pad_clamp_fusion), kind=kCustom, calls=%fused_computation | custom fusion | bytes 32784 | tf_op jit(solution)/shard_map/gather | solution.py:123
  71.2 1.8 %gather_fusion.3 = f32[4,32,1024]{2,1,0:T(8,128)S(1)} fusion(f32[9,32,1024]{2,1,0:T(8,128)} %pad_maximum_fusion, s32[1024]{0:T(1024)S(1)} %pad_clamp_fusion), kind=kCustom, calls=%fused_computation.3 | custom fusion | bytes 1048592 | tf_op jit(solution)/shard_map/gather | solution.py:89
  75.0 1.5 %gather_fusion.4 = f32[4,32,32]{2,1,0:T(8,128)S(1)} fusion(f32[9,32,32]{2,1,0:T(8,128)} %get-tuple-element.23, s32[1024]{0:T(1024)S(1)} %pad_clamp_fusion), kind=kCustom, calls=%fused_computation.4 | custom fusion | bytes 32784 | tf_op jit(solution)/shard_map/gather | solution.py:127
  76.5 2.6 %collective-permute-done.9 = f32[4,64,32]{1,2,0:T(8,128)S(1)} collective-permute-done((f32[4,64,32]{1,2,0:T(8,128)S(1)}, f32[4,64,32]{1,2,0:T(8,128)S(1)}, u32[]{:S(2)}, u32[]{:S(2)}) %collective-permute-start.9) | collective-permute-done | bytes 32800 | tf_op jit(solution)/shard_map/ppermute | solution.py:20
  80.8 2.0 %collective-permute-done.10 = f32[9,32,512]{2,1,0:T(8,128)S(1)} collective-permute-done((f32[9,32,512]{2,1,0:T(8,128)S(1)}, f32[9,32,512]{2,1,0:T(8,128)S(1)}, u32[]{:S(2)}, u32[]{:S(2)}) %collective-permute-start.10) | collective-permute-done | bytes 589856 | tf_op jit(solution)/shard_map/ppermute | solution.py:80
  82.9 1.6 %collective-permute-start.11 = (f32[9,32,256]{2,1,0:T(8,128)S(1)}, f32[9,32,256]{2,1,0:T(8,128)S(1)}, u32[]{:S(2)}, u32[]{:S(2)}) collective-permute-start(f32[9,32,256]{2,1,0:T(8,128)S(1)} %constant_dynamic-slice_fusion.1), channel_id=1, source_target_pairs={{0,2},{1,5},{2,0},{3,7},{4,6},{5,1},{6,4},{7,3},{8,10},{9,13},{10,... | collective-permute-start | bytes 884744 | tf_op jit(solution)/shard_map/ppermute | solution.py:80
  84.5 5.2 %collective-permute-done.11 = f32[9,32,256]{2,1,0:T(8,128)S(1)} collective-permute-done((f32[9,32,256]{2,1,0:T(8,128)S(1)}, f32[9,32,256]{2,1,0:T(8,128)S(1)}, u32[]{:S(2)}, u32[]{:S(2)}) %collective-permute-start.11) | collective-permute-done | bytes 294944 | tf_op jit(solution)/shard_map/ppermute | solution.py:80
  89.8 1.8 %collective-permute-start.12 = (f32[9,32,128]{2,1,0:T(8,128)S(1)}, f32[9,32,128]{2,1,0:T(8,128)S(1)}, u32[]{:S(2)}, u32[]{:S(2)}) collective-permute-start(f32[9,32,128]{2,1,0:T(8,128)S(1)} %constant_dynamic-slice_fusion), channel_id=1, source_target_pairs={{0,4},{1,3},{2,6},{3,1},{4,0},{5,7},{6,2},{7,5},{8,12},{9,11},{10,... | collective-permute-start | bytes 442376 | tf_op jit(solution)/shard_map/ppermute | solution.py:80
  91.5 3.5 %collective-permute-done.12 = f32[9,32,128]{2,1,0:T(8,128)S(1)} collective-permute-done((f32[9,32,128]{2,1,0:T(8,128)S(1)}, f32[9,32,128]{2,1,0:T(8,128)S(1)}, u32[]{:S(2)}, u32[]{:S(2)}) %collective-permute-start.12) | collective-permute-done | bytes 147488 | tf_op jit(solution)/shard_map/ppermute | solution.py:80
  95.0 3.1 %collective-permute-start.13 = (f32[9,32,128]{2,1,0:T(8,128)S(1)}, f32[9,32,128]{2,1,0:T(8,128)S(1)}, u32[]{:S(2)}, u32[]{:S(2)}) collective-permute-start(f32[9,32,128]{2,1,0:T(8,128)S(1)} %dynamic-slice_add_fusion.4), channel_id=1, source_target_pairs={{0,8},{1,17},{2,10},{3,19},{4,12},{5,21},{6,14},{7,23},{8,0},{9,25... | collective-permute-start | bytes 442376 | tf_op jit(solution)/shard_map/ppermute | solution.py:83
  98.1 6.3 %collective-permute-done.13 = f32[9,32,128]{2,1,0:T(8,128)S(1)} collective-permute-done((f32[9,32,128]{2,1,0:T(8,128)S(1)}, f32[9,32,128]{2,1,0:T(8,128)S(1)}, u32[]{:S(2)}, u32[]{:S(2)}) %collective-permute-start.13) | collective-permute-done | bytes 147488 | tf_op jit(solution)/shard_map/ppermute | solution.py:83
  105.0 4.6 %collective-permute-done.14 = f32[9,32,128]{2,1,0:T(8,128)S(1)} collective-permute-done((f32[9,32,128]{2,1,0:T(8,128)S(1)}, f32[9,32,128]{2,1,0:T(8,128)S(1)}, u32[]{:S(2)}, u32[]{:S(2)}) %collective-permute-start.14) | collective-permute-done | bytes 147488 | tf_op jit(solution)/shard_map/ppermute | solution.py:83
  109.7 2.4 %collective-permute-start.15 = (f32[9,32,128]{2,1,0:T(8,128)S(1)}, f32[9,32,128]{2,1,0:T(8,128)S(1)}, u32[]{:S(2)}, u32[]{:S(2)}) collective-permute-start(f32[9,32,128]{2,1,0:T(8,128)S(1)} %add.129), channel_id=1, source_target_pairs={{0,4},{1,3},{2,6},{3,1},{4,0},{5,7},{6,2},{7,5},{8,12},{9,11},{10,... | collective-permute-start | bytes 442376 | tf_op jit(solution)/shard_map/ppermute | solution.py:85
  112.1 4.7 %collective-permute-done.15 = f32[9,32,128]{2,1,0:T(8,128)S(1)} collective-permute-done((f32[9,32,128]{2,1,0:T(8,128)S(1)}, f32[9,32,128]{2,1,0:T(8,128)S(1)}, u32[]{:S(2)}, u32[]{:S(2)}) %collective-permute-start.15) | collective-permute-done | bytes 147488 | tf_op jit(solution)/shard_map/ppermute | solution.py:85
  116.8 1.6 %collective-permute-start.16 = (f32[9,32,256]{2,1,0:T(8,128)S(1)}, f32[9,32,256]{2,1,0:T(8,128)S(1)}, u32[]{:S(2)}, u32[]{:S(2)}) collective-permute-start(f32[9,32,256]{2,1,0:T(8,128)S(1)} %pad_maximum_fusion.5), channel_id=1, source_target_pairs={{0,2},{1,5},{2,0},{3,7},{4,6},{5,1},{6,4},{7,3},{8,10},{9,13},{10,... | collective-permute-start | bytes 884744 | tf_op jit(solution)/shard_map/ppermute | solution.py:85
  118.5 5.2 %collective-permute-done.16 = f32[9,32,256]{2,1,0:T(8,128)S(1)} collective-permute-done((f32[9,32,256]{2,1,0:T(8,128)S(1)}, f32[9,32,256]{2,1,0:T(8,128)S(1)}, u32[]{:S(2)}, u32[]{:S(2)}) %collective-permute-start.16) | collective-permute-done | bytes 294944 | tf_op jit(solution)/shard_map/ppermute | solution.py:85
  129.3 1.8 %gather_fusion.5 = f32[4,32,1024]{2,1,0:T(8,128)S(1)} fusion(f32[9,32,1024]{2,1,0:T(8,128)} %pad_maximum_fusion.1, s32[1024]{0:T(1024)S(1)} %pad_clamp_fusion), kind=kCustom, calls=%fused_computation.5 | custom fusion | bytes 1048592 | tf_op jit(solution)/shard_map/gather | solution.py:89
  131.2 3.7 %multiply_add_fusion = (f32[4,64,1024]{2,1,0:T(8,128)}, f32[1,4,64,1024]{3,2,1,0:T(8,128)}) fusion(f32[4,64,1024]{2,1,0:T(8,128)} %param.12, f32[4]{0:T(128)S(1)} %convolution_bitcast_fusion, f32[1,4,64,1024]{3,2,1,0:T(8,128)S(1)} %copy-done.1, bf16[1,4,64,1024]{3,2,1,0:T(8,128)(2,1)S(1)} %copy-done.2, f32[4,64,32]{1,2,0:T(8,128)S(1)} %fusion.15, ...), kind=kOutput, calls=%fused_computation.22 | convolution fusion | flops 102367232 | bytes 5275664 | tf_op jit(solution)/shard_map/tks,tsd->tkd/dot_general | solution.py:132
  (98 shorter events, 31.2 us)
Async XLA Ops:
  0.6 1.3 copy-start
  1.9 1.2 copy-start.1
  1.9 1.4 %copy-start.2 = (bf16[1,4,64,1024]{3,2,1,0:T(8,128)(2,1)S(1)}, bf16[1,4,64,1024]{3,2,1,0:T(8,128)(2,1)}, u32[]{:S(2)}) copy-start(bf16[1,4,64,1024]{3,2,1,0:T(8,128)(2,1)} %param.10) | copy-start | bytes 1572868
  3.3 1.2 copy-start.6
  3.3 4.2 %copy-start.7 = (s32[4]{0:T(128)S(1)}, s32[4]{0:T(128)}, u32[]{:S(2)}) copy-start(s32[4]{0:T(128)} %param.13) | copy-start | bytes 52
  4.5 8.6 %collective-permute-start = (f32[13312]{0:T(1024)S(1)}, f32[13312]{0:T(1024)S(1)}, u32[]{:S(2)}, u32[]{:S(2)}) collective-permute-start(f32[13312]{0:T(1024)S(1)} %pad_maximum_fusion.6), channel_id=1, source_target_pairs={{0,16},{16,0},{1,17},{17,1},{2,18},{18,2},{3,19},{19,3},{4,20},{20... | collective-permute-start | bytes 159752 | tf_op jit(solution)/shard_map/ppermute | solution.py:20
  11.3 3.0 %copy-start.8 = (pred[9]{0:T(512)(128)(4,1)}, pred[9]{0:T(512)(128)(4,1)S(1)}, u32[]{:S(2)}) copy-start(pred[9]{0:T(512)(128)(4,1)S(1)} %get-tuple-element.35) | copy-start | bytes 31
  12.5 1.9 %copy-start.10 = (pred[9]{0:T(512)(128)(4,1)}, pred[9]{0:T(512)(128)(4,1)S(1)}, u32[]{:S(2)}) copy-start(pred[9]{0:T(512)(128)(4,1)S(1)} %get-tuple-element.32) | copy-start | bytes 31
  12.5 1.9 %copy-start.12 = (pred[9]{0:T(512)(128)(4,1)}, pred[9]{0:T(512)(128)(4,1)S(1)}, u32[]{:S(2)}) copy-start(pred[9]{0:T(512)(128)(4,1)S(1)} %get-tuple-element.33) | copy-start | bytes 31
  14.8 1.0 copy-start.3
  15.9 2.2 %collective-permute-start.1 = (f32[9,32,512]{2,1,0:T(8,128)S(1)}, f32[9,32,512]{2,1,0:T(8,128)}, u32[]{:S(2)}, u32[]{:S(2)}) collective-permute-start(f32[9,32,512]{2,1,0:T(8,128)S(1)} %constant_dynamic-slice_fusion.5), channel_id=1, source_target_pairs={{0,1},{1,0},{2,3},{3,2},{4,5},{5,4},{6,7},{7,6},{8,9},{9,8},{10,11... | collective-permute-start | bytes 1769480 | tf_op jit(solution)/shard_map/ppermute | solution.py:80
  20.2 7.0 %collective-permute-start.2 = (f32[9,32,256]{2,1,0:T(8,128)}, f32[9,32,256]{2,1,0:T(8,128)}, u32[]{:S(2)}, u32[]{:S(2)}) collective-permute-start(f32[9,32,256]{2,1,0:T(8,128)} %constant_dynamic-slice_fusion.4), channel_id=1, source_target_pairs={{0,2},{1,5},{2,0},{3,7},{4,6},{5,1},{6,4},{7,3},{8,10},{9,13},{10,... | collective-permute-start | bytes 884744 | tf_op jit(solution)/shard_map/ppermute | solution.py:80
  29.0 5.2 %collective-permute-start.3 = (f32[9,32,128]{2,1,0:T(8,128)S(1)}, f32[9,32,128]{2,1,0:T(8,128)S(1)}, u32[]{:S(2)}, u32[]{:S(2)}) collective-permute-start(f32[9,32,128]{2,1,0:T(8,128)S(1)} %constant_dynamic-slice_fusion.3), channel_id=1, source_target_pairs={{0,4},{1,3},{2,6},{3,1},{4,0},{5,7},{6,2},{7,5},{8,12},{9,11},{10,... | collective-permute-start | bytes 442376 | tf_op jit(solution)/shard_map/ppermute | solution.py:80
  35.1 9.7 %collective-permute-start.4 = (f32[9,32,128]{2,1,0:T(8,128)S(1)}, f32[9,32,128]{2,1,0:T(8,128)S(1)}, u32[]{:S(2)}, u32[]{:S(2)}) collective-permute-start(f32[9,32,128]{2,1,0:T(8,128)S(1)} %dynamic-slice_add_fusion.5), channel_id=1, source_target_pairs={{0,8},{1,17},{2,10},{3,19},{4,12},{5,21},{6,14},{7,23},{8,0},{9,25... | collective-permute-start | bytes 442376 | tf_op jit(solution)/shard_map/ppermute | solution.py:83
  44.9 5.2 %collective-permute-start.5 = (f32[9,32,128]{2,1,0:T(8,128)S(1)}, f32[9,32,128]{2,1,0:T(8,128)S(1)}, u32[]{:S(2)}, u32[]{:S(2)}) collective-permute-start(f32[9,32,128]{2,1,0:T(8,128)S(1)} %add.119), channel_id=1, source_target_pairs={{0,16},{1,9},{2,18},{3,11},{4,20},{5,13},{6,22},{7,15},{8,24},{9,1... | collective-permute-start | bytes 442376 | tf_op jit(solution)/shard_map/ppermute | solution.py:83
  50.1 6.8 %collective-permute-start.6 = (f32[9,32,128]{2,1,0:T(8,128)S(1)}, f32[9,32,128]{2,1,0:T(8,128)S(1)}, u32[]{:S(2)}, u32[]{:S(2)}) collective-permute-start(f32[9,32,128]{2,1,0:T(8,128)S(1)} %add.120), channel_id=1, source_target_pairs={{0,4},{1,3},{2,6},{3,1},{4,0},{5,7},{6,2},{7,5},{8,12},{9,11},{10,... | collective-permute-start | bytes 442376 | tf_op jit(solution)/shard_map/ppermute | solution.py:85
  57.6 6.9 %collective-permute-start.7 = (f32[9,32,256]{2,1,0:T(8,128)S(1)}, f32[9,32,256]{2,1,0:T(8,128)}, u32[]{:S(2)}, u32[]{:S(2)}) collective-permute-start(f32[9,32,256]{2,1,0:T(8,128)S(1)} %pad_maximum_fusion.4), channel_id=1, source_target_pairs={{0,2},{1,5},{2,0},{3,7},{4,6},{5,1},{6,4},{7,3},{8,10},{9,13},{10,... | collective-permute-start | bytes 884744 | tf_op jit(solution)/shard_map/ppermute | solution.py:85
  66.4 2.3 %collective-permute-start.8 = (f32[9,32,512]{2,1,0:T(8,128)}, f32[9,32,512]{2,1,0:T(8,128)}, u32[]{:S(2)}, u32[]{:S(2)}) collective-permute-start(f32[9,32,512]{2,1,0:T(8,128)} %pad_maximum_fusion.2), channel_id=1, source_target_pairs={{0,1},{1,0},{2,3},{3,2},{4,5},{5,4},{6,7},{7,6},{8,9},{9,8},{10,11... | collective-permute-start | bytes 1769480 | tf_op jit(solution)/shard_map/ppermute | solution.py:85
  74.7 4.3 %collective-permute-start.9 = (f32[4,64,32]{1,2,0:T(8,128)S(1)}, f32[4,64,32]{1,2,0:T(8,128)S(1)}, u32[]{:S(2)}, u32[]{:S(2)}) collective-permute-start(f32[4,64,32]{1,2,0:T(8,128)S(1)} %fusion.2), channel_id=1, source_target_pairs={{0,16},{16,0},{1,17},{17,1},{2,18},{18,2},{3,19},{19,3},{4,20},{20... | collective-permute-start | bytes 98312 | tf_op jit(solution)/shard_map/ppermute | solution.py:20
  79.4 0.8 copy-start.9
  79.4 0.8 copy-start.11
  79.4 0.8 copy-start.13
  80.7 2.1 %collective-permute-start.10 = (f32[9,32,512]{2,1,0:T(8,128)S(1)}, f32[9,32,512]{2,1,0:T(8,128)S(1)}, u32[]{:S(2)}, u32[]{:S(2)}) collective-permute-start(f32[9,32,512]{2,1,0:T(8,128)S(1)} %constant_dynamic-slice_fusion.2), channel_id=1, source_target_pairs={{0,1},{1,0},{2,3},{3,2},{4,5},{5,4},{6,7},{7,6},{8,9},{9,8},{10,11... | collective-permute-start | bytes 1769480 | tf_op jit(solution)/shard_map/ppermute | solution.py:80
  82.9 6.8 %collective-permute-start.11 = (f32[9,32,256]{2,1,0:T(8,128)S(1)}, f32[9,32,256]{2,1,0:T(8,128)S(1)}, u32[]{:S(2)}, u32[]{:S(2)}) collective-permute-start(f32[9,32,256]{2,1,0:T(8,128)S(1)} %constant_dynamic-slice_fusion.1), channel_id=1, source_target_pairs={{0,2},{1,5},{2,0},{3,7},{4,6},{5,1},{6,4},{7,3},{8,10},{9,13},{10,... | collective-permute-start | bytes 884744 | tf_op jit(solution)/shard_map/ppermute | solution.py:80
  89.8 5.2 %collective-permute-start.12 = (f32[9,32,128]{2,1,0:T(8,128)S(1)}, f32[9,32,128]{2,1,0:T(8,128)S(1)}, u32[]{:S(2)}, u32[]{:S(2)}) collective-permute-start(f32[9,32,128]{2,1,0:T(8,128)S(1)} %constant_dynamic-slice_fusion), channel_id=1, source_target_pairs={{0,4},{1,3},{2,6},{3,1},{4,0},{5,7},{6,2},{7,5},{8,12},{9,11},{10,... | collective-permute-start | bytes 442376 | tf_op jit(solution)/shard_map/ppermute | solution.py:80
  95.0 9.4 %collective-permute-start.13 = (f32[9,32,128]{2,1,0:T(8,128)S(1)}, f32[9,32,128]{2,1,0:T(8,128)S(1)}, u32[]{:S(2)}, u32[]{:S(2)}) collective-permute-start(f32[9,32,128]{2,1,0:T(8,128)S(1)} %dynamic-slice_add_fusion.4), channel_id=1, source_target_pairs={{0,8},{1,17},{2,10},{3,19},{4,12},{5,21},{6,14},{7,23},{8,0},{9,25... | collective-permute-start | bytes 442376 | tf_op jit(solution)/shard_map/ppermute | solution.py:83
  104.4 5.2 %collective-permute-start.14 = (f32[9,32,128]{2,1,0:T(8,128)S(1)}, f32[9,32,128]{2,1,0:T(8,128)S(1)}, u32[]{:S(2)}, u32[]{:S(2)}) collective-permute-start(f32[9,32,128]{2,1,0:T(8,128)S(1)} %add.128), channel_id=1, source_target_pairs={{0,16},{1,9},{2,18},{3,11},{4,20},{5,13},{6,22},{7,15},{8,24},{9,1... | collective-permute-start | bytes 442376 | tf_op jit(solution)/shard_map/ppermute | solution.py:83
  109.7 7.1 %collective-permute-start.15 = (f32[9,32,128]{2,1,0:T(8,128)S(1)}, f32[9,32,128]{2,1,0:T(8,128)S(1)}, u32[]{:S(2)}, u32[]{:S(2)}) collective-permute-start(f32[9,32,128]{2,1,0:T(8,128)S(1)} %add.129), channel_id=1, source_target_pairs={{0,4},{1,3},{2,6},{3,1},{4,0},{5,7},{6,2},{7,5},{8,12},{9,11},{10,... | collective-permute-start | bytes 442376 | tf_op jit(solution)/shard_map/ppermute | solution.py:85
  116.8 7.8 %copy-start.14 = (s32[9]{0:T(128)S(1)}, s32[9]{0:T(128)}, u32[]{:S(2)}) copy-start(s32[9]{0:T(128)} %param.14) | copy-start | bytes 112
  116.8 7.8 %copy-start.15 = (f32[4]{0:T(128)S(1)}, f32[4]{0:T(128)}, u32[]{:S(2)}) copy-start(f32[4]{0:T(128)} %param.15) | copy-start | bytes 52
  116.8 6.8 %collective-permute-start.16 = (f32[9,32,256]{2,1,0:T(8,128)S(1)}, f32[9,32,256]{2,1,0:T(8,128)S(1)}, u32[]{:S(2)}, u32[]{:S(2)}) collective-permute-start(f32[9,32,256]{2,1,0:T(8,128)S(1)} %pad_maximum_fusion.5), channel_id=1, source_target_pairs={{0,2},{1,5},{2,0},{3,7},{4,6},{5,1},{6,4},{7,3},{8,10},{9,13},{10,... | collective-permute-start | bytes 884744 | tf_op jit(solution)/shard_map/ppermute | solution.py:85
  124.6 2.3 %collective-permute-start.17 = (f32[9,32,512]{2,1,0:T(8,128)}, f32[9,32,512]{2,1,0:T(8,128)}, u32[]{:S(2)}, u32[]{:S(2)}) collective-permute-start(f32[9,32,512]{2,1,0:T(8,128)} %pad_maximum_fusion.3), channel_id=1, source_target_pairs={{0,1},{1,0},{2,3},{3,2},{4,5},{5,4},{6,7},{7,6},{8,9},{9,8},{10,11... | collective-permute-start | bytes 1769480 | tf_op jit(solution)/shard_map/ppermute | solution.py:85
  (2 other events, 1.4 us)

commit v10 on v7

--- a/solution.py
+++ b/solution.py
@@ -39,15 +39,25 @@
     return plan
 
 
+def _scalar_rows(rows, count):
+    width = max(1, (count - 1).bit_length())
+    n = rows.shape[0]
+    if n * width > 31:
+        return [rows[i] for i in range(n)]
+    fields = jnp.left_shift(rows, jnp.arange(n, dtype=rows.dtype) * width)
+    packed = jnp.sum(fields)
+    return [(packed >> (i * width)) & ((1 << width) - 1) for i in range(n)]
+
+
 def _pick_rows(table, rows):
-    return jnp.stack([lax.dynamic_index_in_dim(table, rows[i], 0, keepdims=False) for i in range(rows.shape[0])])
+    return jnp.stack([lax.dynamic_index_in_dim(table, r, 0, keepdims=False) for r in rows])
 
 
 def _scatter_rows(parts, rows, count):
     table = jnp.zeros((count,) + parts.shape[1:], parts.dtype)
-    for i in range(parts.shape[0]):
-        slab = lax.dynamic_index_in_dim(table, rows[i], 0, keepdims=True)
-        table = lax.dynamic_update_index_in_dim(table, slab + parts[i : i + 1], rows[i], 0)
+    for i, r in enumerate(rows):
+        slab = lax.dynamic_index_in_dim(table, r, 0, keepdims=True)
+        table = lax.dynamic_update_index_in_dim(table, slab + parts[i : i + 1], r, 0)
     return table
 
 
@@ -117,27 +127,28 @@
         jnp.float32
     )
     combined = gradient[0].astype(jnp.float32) + feedback[0]
-    q_tiles = start_basis.at[tile_matrix].get(mode="promise_in_bounds")
+    tile_rows = _scalar_rows(tile_matrix, matrix_count)
+    q_tiles = _pick_rows(start_basis, tile_rows)
     first_local = jnp.einsum("tkd,tds->tks", combined, q_tiles, precision=TOP_PRECISION)
     left_size = first_local.size
     carried = jnp.concatenate([first_local.reshape(-1), vector_grad[0].reshape(-1)])
     carried = swap_sum(carried, "rep")
     first_left = carried[:left_size].reshape(first_local.shape) / replicas
     vector_summed = carried[left_size:].reshape(vector_grad.shape[1:])
-    mix_first = inverse_gram_factors[0].at[tile_matrix].get(mode="promise_in_bounds")
+    mix_first = _pick_rows(inverse_gram_factors[0], tile_rows)
     first_ortho = jnp.einsum("tks,tsa->tka", first_left, mix_first, precision=TOP_PRECISION)
     first_parts = jnp.einsum("tkd,tks->tsd", combined, first_ortho, precision=TOP_PRECISION)
-    first_table = _scatter_rows(first_parts, tile_matrix, matrix_count)
-    first_rows = table_rows(first_table, tile_matrix, replicas, n_own) / replicas
-    mix_right = inverse_gram_factors[1].at[tile_matrix].get(mode="promise_in_bounds")
+    first_table = _scatter_rows(first_parts, tile_rows, matrix_count)
+    first_rows = table_rows(first_table, tile_rows, replicas, n_own) / replicas
+    mix_right = _pick_rows(inverse_gram_factors[1], tile_rows)
     right_rows = jnp.einsum("tjw,tjd->twd", mix_right, first_rows, precision=TOP_PRECISION)
     second_local = jnp.einsum("tkd,tsd->tks", combined, right_rows, precision=TOP_PRECISION)
     second_left = swap_sum(second_local, "rep") / replicas
-    mix_second = inverse_gram_factors[2].at[tile_matrix].get(mode="promise_in_bounds")
+    mix_second = _pick_rows(inverse_gram_factors[2], tile_rows)
     second_ortho = jnp.einsum("tks,tsa->tka", second_left, mix_second, precision=TOP_PRECISION)
     second_parts = jnp.einsum("tkd,tks->tsd", combined, second_ortho, precision=TOP_PRECISION)
-    second_table = _scatter_rows(second_parts, tile_matrix, matrix_count)
-    back_rows = table_rows(second_table, tile_matrix, replicas, n_own) / replicas
+    second_table = _scatter_rows(second_parts, tile_rows, matrix_count)
+    back_rows = table_rows(second_table, tile_rows, replicas, n_own) / replicas
     approximation = jnp.einsum("tks,tsd->tkd", second_ortho, back_rows, precision=TOP_PRECISION)
     new_feedback = (combined - approximation)[None]
     group_select = (

time: 132 us -> 119 us (0.902)
  local copies, waits for them, and re-layouts: 13.4 us -> 4.62 us
  starting transfers between devices: 23.9 us -> 32 us
  between operations: 8.65 us -> 3.74 us
  other arithmetic: 8.99 us -> 4.15 us
  waiting for transfers between devices: 69 us -> 64.8 us
    gather x4 -> x0, local copies, waits for them, and re-layouts: 4.05 us -> none  [the longest x1 1.46 us: local(): inverse_gram_factors[1].at[tile_matrix].get(mode='promise_in_bounds')]
    ppermute x4, starting transfers between devices: 6.44 us -> 10.2 us  [table_rows(): cur = cur + lax.ppermute(cur, axes, perm_of(p0, p1))]
    unnamed x22 -> x18, local copies, waits for them, and re-layouts: 3.71 us -> 0.05 us
    ppermute x4, waiting for transfers between devices: 23.1 us -> 19.6 us  [table_rows(): cur = cur + lax.ppermute(cur, axes, perm_of(p0, p1))]
    add x6, other arithmetic: 3.45 us -> 1.42 us  [table_rows(): cur = keep + lax.ppermute(send, axes, perm_of(p0, p1))]
    ppermute x6, waiting for transfers between devices: 21.8 us -> 19.9 us  [table_rows(): cur = keep + lax.ppermute(send, axes, perm_of(p0, p1))]
    squeeze x1 -> x0, local copies, waits for them, and re-layouts: 1.79 us -> none  [local(): inverse_gram_factors[0].at[tile_matrix].get(mode='promise_in_bounds')]
    ppermute x6, starting transfers between devices: 6.71 us -> 8.49 us  [table_rows(): cur = keep + lax.ppermute(send, axes, perm_of(p0, p1))]
  transfers between devices with their start and end apart: 18 -> 18, of which waited for: 17 -> 18; matrix products, arithmetic and copies ran while one was open for 6% -> 2% of each run, Pallas kernels for 0% -> 0%
where the time goes in v10:
time: 119 us; the launch traced here: 118 us
  waiting for transfers between devices  64.8 us (54%)
  starting transfers between devices  32 us (27%)
  matrix products  8.8 us (7%)
  local copies, waits for them, and re-layouts  4.62 us (4%)
  other arithmetic  4.15 us (3%)
  between operations  3.74 us (3%)
    ppermute x6, waiting for transfers between devices, table_rows(): other = lax.ppermute(cur, axes, perm_of(p0, p1))  21.7 us
    ppermute x6, waiting for transfers between devices, table_rows(): cur = keep + lax.ppermute(send, axes, perm_of(p0, p1))  19.9 us
    ppermute x4, waiting for transfers between devices, table_rows(): cur = cur + lax.ppermute(cur, axes, perm_of(p0, p1))  19.6 us
    ppermute x4, starting transfers between devices, table_rows(): cur = cur + lax.ppermute(cur, axes, perm_of(p0, p1))  10.2 us
    ppermute x6, starting transfers between devices, table_rows(): cur = keep + lax.ppermute(send, axes, perm_of(p0, p1))  8.49 us
    ppermute x6, starting transfers between devices, table_rows(): other = lax.ppermute(cur, axes, perm_of(p0, p1))  8.36 us
    ppermute x2, starting transfers between devices, swap_sum(): x = x + lax.ppermute(x, axis, _pair_perm(n, j))  4.88 us
    ppermute x2, waiting for transfers between devices, swap_sum(): x = x + lax.ppermute(x, axis, _pair_perm(n, j))  3.6 us
  transfers between devices with their start and end apart: 18, of which 18 were waited for; matrix products, arithmetic and copies ran while one was open for 2% of the time, Pallas kernels for 0%

profile of v10, /device:TPU:0, one launch (start us, length us, event | category | flops | bytes accessed | tf_op | source)
XLA Modules:
  0.0 118.0 jit_solution(7767248055521372524)
XLA Ops:
  5.8 2.2 %fusion.6 = f32[4,64,32]{2,1,0:T(8,128)S(1)} fusion(f32[1,1024,32]{1,2,0:T(8,128)S(1)} %get-tuple-element.5, f32[1,1024,32]{1,2,0:T(8,128)S(1)} %get-tuple-element.6, f32[1,1024,32]{1,2,0:T(8,128)S(1)} %get-tuple-element.4, f32[1,1024,32]{1,2,0:T(8,128)S(1)} %get-tuple-element.3, f32[1,4,64,1024]{3,2,1,0:T(8,128)S(1)} %copy-done.1, ...), kind=kOutput, calls=%fused_computation.9 | convolution fusion | flops 101580800 | bytes 2129920 | tf_op jit(solution)/shard_map/tkd,tds->tks/dot_general | solution.py:132
  8.1 3.0 %collective-permute-start = (f32[13312]{0:T(1024)S(1)}, f32[13312]{0:T(1024)S(1)}, u32[]{:S(2)}, u32[]{:S(2)}) collective-permute-start(f32[13312]{0:T(1024)S(1)} %pad_maximum_fusion.8), channel_id=1, source_target_pairs={{0,16},{16,0},{1,17},{17,1},{2,18},{18,2},{3,19},{19,3},{4,20},{20... | collective-permute-start | bytes 159752 | tf_op jit(solution)/shard_map/ppermute | solution.py:20
  11.9 1.4 %collective-permute-done = f32[13312]{0:T(1024)S(1)} collective-permute-done((f32[13312]{0:T(1024)S(1)}, f32[13312]{0:T(1024)S(1)}, u32[]{:S(2)}, u32[]{:S(2)}) %collective-permute-start) | collective-permute-done | bytes 53280 | tf_op jit(solution)/shard_map/ppermute | solution.py:20
  14.9 2.1 %collective-permute-done.1 = f32[9,32,512]{2,1,0:T(8,128)} collective-permute-done((f32[9,32,512]{2,1,0:T(8,128)S(1)}, f32[9,32,512]{2,1,0:T(8,128)}, u32[]{:S(2)}, u32[]{:S(2)}) %collective-permute-start.1) | collective-permute-done | bytes 589856 | tf_op jit(solution)/shard_map/ppermute | solution.py:93
  18.2 2.1 %collective-permute-start.2 = (f32[9,32,256]{2,1,0:T(8,128)S(1)}, f32[9,32,256]{2,1,0:T(8,128)S(1)}, u32[]{:S(2)}, u32[]{:S(2)}) collective-permute-start(f32[9,32,256]{2,1,0:T(8,128)S(1)} %constant_dynamic-slice_fusion.16), channel_id=1, source_target_pairs={{0,2},{1,5},{2,0},{3,7},{4,6},{5,1},{6,4},{7,3},{8,10},{9,13},{10,... | collective-permute-start | bytes 884744 | tf_op jit(solution)/shard_map/ppermute | solution.py:93
  20.3 4.7 %collective-permute-done.2 = f32[9,32,256]{2,1,0:T(8,128)S(1)} collective-permute-done((f32[9,32,256]{2,1,0:T(8,128)S(1)}, f32[9,32,256]{2,1,0:T(8,128)S(1)}, u32[]{:S(2)}, u32[]{:S(2)}) %collective-permute-start.2) | collective-permute-done | bytes 294944 | tf_op jit(solution)/shard_map/ppermute | solution.py:93
  25.1 2.2 %collective-permute-start.3 = (f32[9,32,128]{2,1,0:T(8,128)S(1)}, f32[9,32,128]{2,1,0:T(8,128)S(1)}, u32[]{:S(2)}, u32[]{:S(2)}) collective-permute-start(f32[9,32,128]{2,1,0:T(8,128)S(1)} %constant_dynamic-slice_fusion.15), channel_id=1, source_target_pairs={{0,4},{1,3},{2,6},{3,1},{4,0},{5,7},{6,2},{7,5},{8,12},{9,11},{10,... | collective-permute-start | bytes 442376 | tf_op jit(solution)/shard_map/ppermute | solution.py:93
  27.3 3.1 %collective-permute-done.3 = f32[9,32,128]{2,1,0:T(8,128)S(1)} collective-permute-done((f32[9,32,128]{2,1,0:T(8,128)S(1)}, f32[9,32,128]{2,1,0:T(8,128)S(1)}, u32[]{:S(2)}, u32[]{:S(2)}) %collective-permute-start.3) | collective-permute-done | bytes 147488 | tf_op jit(solution)/shard_map/ppermute | solution.py:93
  30.4 3.1 %collective-permute-start.4 = (f32[9,32,128]{2,1,0:T(8,128)S(1)}, f32[9,32,128]{2,1,0:T(8,128)S(1)}, u32[]{:S(2)}, u32[]{:S(2)}) collective-permute-start(f32[9,32,128]{2,1,0:T(8,128)S(1)} %dynamic-slice_add_fusion.5), channel_id=1, source_target_pairs={{0,8},{1,17},{2,10},{3,19},{4,12},{5,21},{6,14},{7,23},{8,0},{9,25... | collective-permute-start | bytes 442376 | tf_op jit(solution)/shard_map/ppermute | solution.py:96
  33.5 6.4 %collective-permute-done.4 = f32[9,32,128]{2,1,0:T(8,128)S(1)} collective-permute-done((f32[9,32,128]{2,1,0:T(8,128)S(1)}, f32[9,32,128]{2,1,0:T(8,128)S(1)}, u32[]{:S(2)}, u32[]{:S(2)}) %collective-permute-start.4) | collective-permute-done | bytes 147488 | tf_op jit(solution)/shard_map/ppermute | solution.py:96
  39.9 2.2 %collective-permute-start.5 = (f32[9,32,128]{2,1,0:T(8,128)S(1)}, f32[9,32,128]{2,1,0:T(8,128)S(1)}, u32[]{:S(2)}, u32[]{:S(2)}) collective-permute-start(f32[9,32,128]{2,1,0:T(8,128)S(1)} %add.177), channel_id=1, source_target_pairs={{0,16},{1,9},{2,18},{3,11},{4,20},{5,13},{6,22},{7,15},{8,24},{9,1... | collective-permute-start | bytes 442376 | tf_op jit(solution)/shard_map/ppermute | solution.py:96
  42.1 3.1 %collective-permute-done.5 = f32[9,32,128]{2,1,0:T(8,128)S(1)} collective-permute-done((f32[9,32,128]{2,1,0:T(8,128)S(1)}, f32[9,32,128]{2,1,0:T(8,128)S(1)}, u32[]{:S(2)}, u32[]{:S(2)}) %collective-permute-start.5) | collective-permute-done | bytes 147488 | tf_op jit(solution)/shard_map/ppermute | solution.py:96
  45.3 2.3 %collective-permute-start.6 = (f32[9,32,128]{2,1,0:T(8,128)S(1)}, f32[9,32,128]{2,1,0:T(8,128)S(1)}, u32[]{:S(2)}, u32[]{:S(2)}) collective-permute-start(f32[9,32,128]{2,1,0:T(8,128)S(1)} %add.178), channel_id=1, source_target_pairs={{0,4},{1,3},{2,6},{3,1},{4,0},{5,7},{6,2},{7,5},{8,12},{9,11},{10,... | collective-permute-start | bytes 442376 | tf_op jit(solution)/shard_map/ppermute | solution.py:99
  47.6 4.7 %collective-permute-done.6 = f32[9,32,128]{2,1,0:T(8,128)S(1)} collective-permute-done((f32[9,32,128]{2,1,0:T(8,128)S(1)}, f32[9,32,128]{2,1,0:T(8,128)S(1)}, u32[]{:S(2)}, u32[]{:S(2)}) %collective-permute-start.6) | collective-permute-done | bytes 147488 | tf_op jit(solution)/shard_map/ppermute | solution.py:99
  52.4 1.9 %collective-permute-start.7 = (f32[9,32,256]{2,1,0:T(8,128)S(1)}, f32[9,32,256]{2,1,0:T(8,128)S(1)}, u32[]{:S(2)}, u32[]{:S(2)}) collective-permute-start(f32[9,32,256]{2,1,0:T(8,128)S(1)} %pad_maximum_fusion.2), channel_id=1, source_target_pairs={{0,2},{1,5},{2,0},{3,7},{4,6},{5,1},{6,4},{7,3},{8,10},{9,13},{10,... | collective-permute-start | bytes 884744 | tf_op jit(solution)/shard_map/ppermute | solution.py:99
  54.3 4.9 %collective-permute-done.7 = f32[9,32,256]{2,1,0:T(8,128)S(1)} collective-permute-done((f32[9,32,256]{2,1,0:T(8,128)S(1)}, f32[9,32,256]{2,1,0:T(8,128)S(1)}, u32[]{:S(2)}, u32[]{:S(2)}) %collective-permute-start.7) | collective-permute-done | bytes 294944 | tf_op jit(solution)/shard_map/ppermute | solution.py:99
  64.2 1.9 %collective-permute-start.9 = (f32[4,64,32]{1,2,0:T(8,128)S(1)}, f32[4,64,32]{1,2,0:T(8,128)S(1)}, u32[]{:S(2)}, u32[]{:S(2)}) collective-permute-start(f32[4,64,32]{1,2,0:T(8,128)S(1)} %fusion.2), channel_id=1, source_target_pairs={{0,16},{16,0},{1,17},{17,1},{2,18},{18,2},{3,19},{19,3},{4,20},{20... | collective-permute-start | bytes 98312 | tf_op jit(solution)/shard_map/ppermute | solution.py:20
  66.4 2.2 %collective-permute-done.9 = f32[4,64,32]{1,2,0:T(8,128)S(1)} collective-permute-done((f32[4,64,32]{1,2,0:T(8,128)S(1)}, f32[4,64,32]{1,2,0:T(8,128)S(1)}, u32[]{:S(2)}, u32[]{:S(2)}) %collective-permute-start.9) | collective-permute-done | bytes 32800 | tf_op jit(solution)/shard_map/ppermute | solution.py:20
  69.9 2.0 %collective-permute-done.10 = f32[9,32,512]{2,1,0:T(8,128)S(1)} collective-permute-done((f32[9,32,512]{2,1,0:T(8,128)S(1)}, f32[9,32,512]{2,1,0:T(8,128)S(1)}, u32[]{:S(2)}, u32[]{:S(2)}) %collective-permute-start.10) | collective-permute-done | bytes 589856 | tf_op jit(solution)/shard_map/ppermute | solution.py:93
  72.0 1.9 %collective-permute-start.11 = (f32[9,32,256]{2,1,0:T(8,128)S(1)}, f32[9,32,256]{2,1,0:T(8,128)S(1)}, u32[]{:S(2)}, u32[]{:S(2)}) collective-permute-start(f32[9,32,256]{2,1,0:T(8,128)S(1)} %constant_dynamic-slice_fusion.1), channel_id=1, source_target_pairs={{0,2},{1,5},{2,0},{3,7},{4,6},{5,1},{6,4},{7,3},{8,10},{9,13},{10,... | collective-permute-start | bytes 884744 | tf_op jit(solution)/shard_map/ppermute | solution.py:93
  73.9 4.9 %collective-permute-done.11 = f32[9,32,256]{2,1,0:T(8,128)S(1)} collective-permute-done((f32[9,32,256]{2,1,0:T(8,128)S(1)}, f32[9,32,256]{2,1,0:T(8,128)S(1)}, u32[]{:S(2)}, u32[]{:S(2)}) %collective-permute-start.11) | collective-permute-done | bytes 294944 | tf_op jit(solution)/shard_map/ppermute | solution.py:93
  78.9 2.1 %collective-permute-start.12 = (f32[9,32,128]{2,1,0:T(8,128)S(1)}, f32[9,32,128]{2,1,0:T(8,128)S(1)}, u32[]{:S(2)}, u32[]{:S(2)}) collective-permute-start(f32[9,32,128]{2,1,0:T(8,128)S(1)} %constant_dynamic-slice_fusion), channel_id=1, source_target_pairs={{0,4},{1,3},{2,6},{3,1},{4,0},{5,7},{6,2},{7,5},{8,12},{9,11},{10,... | collective-permute-start | bytes 442376 | tf_op jit(solution)/shard_map/ppermute | solution.py:93
  81.0 3.1 %collective-permute-done.12 = f32[9,32,128]{2,1,0:T(8,128)S(1)} collective-permute-done((f32[9,32,128]{2,1,0:T(8,128)S(1)}, f32[9,32,128]{2,1,0:T(8,128)S(1)}, u32[]{:S(2)}, u32[]{:S(2)}) %collective-permute-start.12) | collective-permute-done | bytes 147488 | tf_op jit(solution)/shard_map/ppermute | solution.py:93
  84.2 3.4 %collective-permute-start.13 = (f32[9,32,128]{2,1,0:T(8,128)S(1)}, f32[9,32,128]{2,1,0:T(8,128)S(1)}, u32[]{:S(2)}, u32[]{:S(2)}) collective-permute-start(f32[9,32,128]{2,1,0:T(8,128)S(1)} %dynamic-slice_add_fusion.4), channel_id=1, source_target_pairs={{0,8},{1,17},{2,10},{3,19},{4,12},{5,21},{6,14},{7,23},{8,0},{9,25... | collective-permute-start | bytes 442376 | tf_op jit(solution)/shard_map/ppermute | solution.py:96
  87.6 6.4 %collective-permute-done.13 = f32[9,32,128]{2,1,0:T(8,128)S(1)} collective-permute-done((f32[9,32,128]{2,1,0:T(8,128)S(1)}, f32[9,32,128]{2,1,0:T(8,128)S(1)}, u32[]{:S(2)}, u32[]{:S(2)}) %collective-permute-start.13) | collective-permute-done | bytes 147488 | tf_op jit(solution)/shard_map/ppermute | solution.py:96
  94.0 1.6 %collective-permute-start.14 = (f32[9,32,128]{2,1,0:T(8,128)S(1)}, f32[9,32,128]{2,1,0:T(8,128)S(1)}, u32[]{:S(2)}, u32[]{:S(2)}) collective-permute-start(f32[9,32,128]{2,1,0:T(8,128)S(1)} %add.186), channel_id=1, source_target_pairs={{0,16},{1,9},{2,18},{3,11},{4,20},{5,13},{6,22},{7,15},{8,24},{9,1... | collective-permute-start | bytes 442376 | tf_op jit(solution)/shard_map/ppermute | solution.py:96
  95.5 3.7 %collective-permute-done.14 = f32[9,32,128]{2,1,0:T(8,128)S(1)} collective-permute-done((f32[9,32,128]{2,1,0:T(8,128)S(1)}, f32[9,32,128]{2,1,0:T(8,128)S(1)}, u32[]{:S(2)}, u32[]{:S(2)}) %collective-permute-start.14) | collective-permute-done | bytes 147488 | tf_op jit(solution)/shard_map/ppermute | solution.py:96
  99.2 2.4 %collective-permute-start.15 = (f32[9,32,128]{2,1,0:T(8,128)S(1)}, f32[9,32,128]{2,1,0:T(8,128)S(1)}, u32[]{:S(2)}, u32[]{:S(2)}) collective-permute-start(f32[9,32,128]{2,1,0:T(8,128)S(1)} %add.187), channel_id=1, source_target_pairs={{0,4},{1,3},{2,6},{3,1},{4,0},{5,7},{6,2},{7,5},{8,12},{9,11},{10,... | collective-permute-start | bytes 442376 | tf_op jit(solution)/shard_map/ppermute | solution.py:99
  101.6 4.7 %collective-permute-done.15 = f32[9,32,128]{2,1,0:T(8,128)S(1)} collective-permute-done((f32[9,32,128]{2,1,0:T(8,128)S(1)}, f32[9,32,128]{2,1,0:T(8,128)S(1)}, u32[]{:S(2)}, u32[]{:S(2)}) %collective-permute-start.15) | collective-permute-done | bytes 147488 | tf_op jit(solution)/shard_map/ppermute | solution.py:99
  106.4 1.6 %collective-permute-start.16 = (f32[9,32,256]{2,1,0:T(8,128)S(1)}, f32[9,32,256]{2,1,0:T(8,128)S(1)}, u32[]{:S(2)}, u32[]{:S(2)}) collective-permute-start(f32[9,32,256]{2,1,0:T(8,128)S(1)} %pad_maximum_fusion.3), channel_id=1, source_target_pairs={{0,2},{1,5},{2,0},{3,7},{4,6},{5,1},{6,4},{7,3},{8,10},{9,13},{10,... | collective-permute-start | bytes 884744 | tf_op jit(solution)/shard_map/ppermute | solution.py:99
  108.2 5.0 %collective-permute-done.16 = f32[9,32,256]{2,1,0:T(8,128)S(1)} collective-permute-done((f32[9,32,256]{2,1,0:T(8,128)S(1)}, f32[9,32,256]{2,1,0:T(8,128)S(1)}, u32[]{:S(2)}, u32[]{:S(2)}) %collective-permute-start.16) | collective-permute-done | bytes 294944 | tf_op jit(solution)/shard_map/ppermute | solution.py:99
  115.5 2.6 %multiply_add_fusion = (f32[4,64,1024]{2,1,0:T(8,128)}, f32[1,4,64,1024]{3,2,1,0:T(8,128)}) fusion(f32[4,64,1024]{2,1,0:T(8,128)S(1)} %copy-done.3, f32[4]{0:T(128)S(1)} %convolution_bitcast_fusion, f32[1,4,64,1024]{3,2,1,0:T(8,128)S(1)} %copy-done.1, bf16[1,4,64,1024]{3,2,1,0:T(8,128)(2,1)S(1)} %copy-done.2, f32[4,64,32]{1,2,0:T(8,128)S(1)} %fusion.57, ...), kind=kOutput, calls=%fused_computation.12 | convolution fusion | flops 102498304 | bytes 5275664 | tf_op jit(solution)/shard_map/tks,tsd->tkd/dot_general | solution.py:152
  (90 shorter events, 15.5 us)
Async XLA Ops:
  0.6 107.3 %copy-start = (f32[4]{0:T(128)S(1)}, f32[4]{0:T(128)}, u32[]{:S(2)}) copy-start(f32[4]{0:T(128)} %param.15) | copy-start | bytes 52
  0.6 5.1 %copy-start.1 = (f32[1,4,64,1024]{3,2,1,0:T(8,128)S(1)}, f32[1,4,64,1024]{3,2,1,0:T(8,128)}, u32[]{:S(2)}) copy-start(f32[1,4,64,1024]{3,2,1,0:T(8,128)} %param.11) | copy-start | bytes 3145732
  5.8 2.3 %copy-start.5 = (f32[1,5,1024]{2,0,1:T(1,128)S(1)}, f32[1,5,1024]{2,0,1:T(1,128)}, u32[]{:S(2)}) copy-start(f32[1,5,1024]{2,0,1:T(1,128)} %param.18) | copy-start | bytes 61444
  5.8 5.4 %copy-start.4 = (f32[3,9,32,32]{3,2,1,0:T(8,128)S(1)}, f32[3,9,32,32]{3,2,1,0:T(8,128)}, u32[]{:S(2)}) copy-start(f32[3,9,32,32]{3,2,1,0:T(8,128)} %param.17) | copy-start | bytes 331780
  8.0 5.8 %copy-start.2 = (bf16[1,4,64,1024]{3,2,1,0:T(8,128)(2,1)S(1)}, bf16[1,4,64,1024]{3,2,1,0:T(8,128)(2,1)}, u32[]{:S(2)}) copy-start(bf16[1,4,64,1024]{3,2,1,0:T(8,128)(2,1)} %param.10) | copy-start | bytes 1572868
  8.1 5.1 %collective-permute-start = (f32[13312]{0:T(1024)S(1)}, f32[13312]{0:T(1024)S(1)}, u32[]{:S(2)}, u32[]{:S(2)}) collective-permute-start(f32[13312]{0:T(1024)S(1)} %pad_maximum_fusion.8), channel_id=1, source_target_pairs={{0,16},{16,0},{1,17},{17,1},{2,18},{18,2},{3,19},{19,3},{4,20},{20... | collective-permute-start | bytes 159752 | tf_op jit(solution)/shard_map/ppermute | solution.py:20
  14.8 2.2 %collective-permute-start.1 = (f32[9,32,512]{2,1,0:T(8,128)S(1)}, f32[9,32,512]{2,1,0:T(8,128)}, u32[]{:S(2)}, u32[]{:S(2)}) collective-permute-start(f32[9,32,512]{2,1,0:T(8,128)S(1)} %constant_dynamic-slice_fusion.17), channel_id=1, source_target_pairs={{0,1},{1,0},{2,3},{3,2},{4,5},{5,4},{6,7},{7,6},{8,9},{9,8},{10,11... | collective-permute-start | bytes 1769480 | tf_op jit(solution)/shard_map/ppermute | solution.py:93
  18.2 6.8 %collective-permute-start.2 = (f32[9,32,256]{2,1,0:T(8,128)S(1)}, f32[9,32,256]{2,1,0:T(8,128)S(1)}, u32[]{:S(2)}, u32[]{:S(2)}) collective-permute-start(f32[9,32,256]{2,1,0:T(8,128)S(1)} %constant_dynamic-slice_fusion.16), channel_id=1, source_target_pairs={{0,2},{1,5},{2,0},{3,7},{4,6},{5,1},{6,4},{7,3},{8,10},{9,13},{10,... | collective-permute-start | bytes 884744 | tf_op jit(solution)/shard_map/ppermute | solution.py:93
  25.1 5.3 %collective-permute-start.3 = (f32[9,32,128]{2,1,0:T(8,128)S(1)}, f32[9,32,128]{2,1,0:T(8,128)S(1)}, u32[]{:S(2)}, u32[]{:S(2)}) collective-permute-start(f32[9,32,128]{2,1,0:T(8,128)S(1)} %constant_dynamic-slice_fusion.15), channel_id=1, source_target_pairs={{0,4},{1,3},{2,6},{3,1},{4,0},{5,7},{6,2},{7,5},{8,12},{9,11},{10,... | collective-permute-start | bytes 442376 | tf_op jit(solution)/shard_map/ppermute | solution.py:93
  30.4 9.4 %collective-permute-start.4 = (f32[9,32,128]{2,1,0:T(8,128)S(1)}, f32[9,32,128]{2,1,0:T(8,128)S(1)}, u32[]{:S(2)}, u32[]{:S(2)}) collective-permute-start(f32[9,32,128]{2,1,0:T(8,128)S(1)} %dynamic-slice_add_fusion.5), channel_id=1, source_target_pairs={{0,8},{1,17},{2,10},{3,19},{4,12},{5,21},{6,14},{7,23},{8,0},{9,25... | collective-permute-start | bytes 442376 | tf_op jit(solution)/shard_map/ppermute | solution.py:96
  39.9 5.3 %collective-permute-start.5 = (f32[9,32,128]{2,1,0:T(8,128)S(1)}, f32[9,32,128]{2,1,0:T(8,128)S(1)}, u32[]{:S(2)}, u32[]{:S(2)}) collective-permute-start(f32[9,32,128]{2,1,0:T(8,128)S(1)} %add.177), channel_id=1, source_target_pairs={{0,16},{1,9},{2,18},{3,11},{4,20},{5,13},{6,22},{7,15},{8,24},{9,1... | collective-permute-start | bytes 442376 | tf_op jit(solution)/shard_map/ppermute | solution.py:96
  45.3 7.0 %collective-permute-start.6 = (f32[9,32,128]{2,1,0:T(8,128)S(1)}, f32[9,32,128]{2,1,0:T(8,128)S(1)}, u32[]{:S(2)}, u32[]{:S(2)}) collective-permute-start(f32[9,32,128]{2,1,0:T(8,128)S(1)} %add.178), channel_id=1, source_target_pairs={{0,4},{1,3},{2,6},{3,1},{4,0},{5,7},{6,2},{7,5},{8,12},{9,11},{10,... | collective-permute-start | bytes 442376 | tf_op jit(solution)/shard_map/ppermute | solution.py:99
  52.4 6.8 %collective-permute-start.7 = (f32[9,32,256]{2,1,0:T(8,128)S(1)}, f32[9,32,256]{2,1,0:T(8,128)S(1)}, u32[]{:S(2)}, u32[]{:S(2)}) collective-permute-start(f32[9,32,256]{2,1,0:T(8,128)S(1)} %pad_maximum_fusion.2), channel_id=1, source_target_pairs={{0,2},{1,5},{2,0},{3,7},{4,6},{5,1},{6,4},{7,3},{8,10},{9,13},{10,... | collective-permute-start | bytes 884744 | tf_op jit(solution)/shard_map/ppermute | solution.py:99
  59.3 2.2 %collective-permute-start.8 = (f32[9,32,512]{2,1,0:T(8,128)S(1)}, f32[9,32,512]{2,1,0:T(8,128)}, u32[]{:S(2)}, u32[]{:S(2)}) collective-permute-start(f32[9,32,512]{2,1,0:T(8,128)S(1)} %pad_maximum_fusion), channel_id=1, source_target_pairs={{0,1},{1,0},{2,3},{3,2},{4,5},{5,4},{6,7},{7,6},{8,9},{9,8},{10,11... | collective-permute-start | bytes 1769480 | tf_op jit(solution)/shard_map/ppermute | solution.py:99
  64.2 4.3 %collective-permute-start.9 = (f32[4,64,32]{1,2,0:T(8,128)S(1)}, f32[4,64,32]{1,2,0:T(8,128)S(1)}, u32[]{:S(2)}, u32[]{:S(2)}) collective-permute-start(f32[4,64,32]{1,2,0:T(8,128)S(1)} %fusion.2), channel_id=1, source_target_pairs={{0,16},{16,0},{1,17},{17,1},{2,18},{18,2},{3,19},{19,3},{4,20},{20... | collective-permute-start | bytes 98312 | tf_op jit(solution)/shard_map/ppermute | solution.py:20
  69.8 2.1 %collective-permute-start.10 = (f32[9,32,512]{2,1,0:T(8,128)S(1)}, f32[9,32,512]{2,1,0:T(8,128)S(1)}, u32[]{:S(2)}, u32[]{:S(2)}) collective-permute-start(f32[9,32,512]{2,1,0:T(8,128)S(1)} %constant_dynamic-slice_fusion.2), channel_id=1, source_target_pairs={{0,1},{1,0},{2,3},{3,2},{4,5},{5,4},{6,7},{7,6},{8,9},{9,8},{10,11... | collective-permute-start | bytes 1769480 | tf_op jit(solution)/shard_map/ppermute | solution.py:93
  72.0 6.8 %collective-permute-start.11 = (f32[9,32,256]{2,1,0:T(8,128)S(1)}, f32[9,32,256]{2,1,0:T(8,128)S(1)}, u32[]{:S(2)}, u32[]{:S(2)}) collective-permute-start(f32[9,32,256]{2,1,0:T(8,128)S(1)} %constant_dynamic-slice_fusion.1), channel_id=1, source_target_pairs={{0,2},{1,5},{2,0},{3,7},{4,6},{5,1},{6,4},{7,3},{8,10},{9,13},{10,... | collective-permute-start | bytes 884744 | tf_op jit(solution)/shard_map/ppermute | solution.py:93
  78.9 29.1 %copy-start.7 = (s32[9]{0:T(128)S(1)}, s32[9]{0:T(128)}, u32[]{:S(2)}) copy-start(s32[9]{0:T(128)} %param.14) | copy-start | bytes 112
  78.9 5.3 %collective-permute-start.12 = (f32[9,32,128]{2,1,0:T(8,128)S(1)}, f32[9,32,128]{2,1,0:T(8,128)S(1)}, u32[]{:S(2)}, u32[]{:S(2)}) collective-permute-start(f32[9,32,128]{2,1,0:T(8,128)S(1)} %constant_dynamic-slice_fusion), channel_id=1, source_target_pairs={{0,4},{1,3},{2,6},{3,1},{4,0},{5,7},{6,2},{7,5},{8,12},{9,11},{10,... | collective-permute-start | bytes 442376 | tf_op jit(solution)/shard_map/ppermute | solution.py:93
  84.2 9.8 %collective-permute-start.13 = (f32[9,32,128]{2,1,0:T(8,128)S(1)}, f32[9,32,128]{2,1,0:T(8,128)S(1)}, u32[]{:S(2)}, u32[]{:S(2)}) collective-permute-start(f32[9,32,128]{2,1,0:T(8,128)S(1)} %dynamic-slice_add_fusion.4), channel_id=1, source_target_pairs={{0,8},{1,17},{2,10},{3,19},{4,12},{5,21},{6,14},{7,23},{8,0},{9,25... | collective-permute-start | bytes 442376 | tf_op jit(solution)/shard_map/ppermute | solution.py:96
  94.0 5.2 %collective-permute-start.14 = (f32[9,32,128]{2,1,0:T(8,128)S(1)}, f32[9,32,128]{2,1,0:T(8,128)S(1)}, u32[]{:S(2)}, u32[]{:S(2)}) collective-permute-start(f32[9,32,128]{2,1,0:T(8,128)S(1)} %add.186), channel_id=1, source_target_pairs={{0,16},{1,9},{2,18},{3,11},{4,20},{5,13},{6,22},{7,15},{8,24},{9,1... | collective-permute-start | bytes 442376 | tf_op jit(solution)/shard_map/ppermute | solution.py:96
  99.2 7.1 %collective-permute-start.15 = (f32[9,32,128]{2,1,0:T(8,128)S(1)}, f32[9,32,128]{2,1,0:T(8,128)S(1)}, u32[]{:S(2)}, u32[]{:S(2)}) collective-permute-start(f32[9,32,128]{2,1,0:T(8,128)S(1)} %add.187), channel_id=1, source_target_pairs={{0,4},{1,3},{2,6},{3,1},{4,0},{5,7},{6,2},{7,5},{8,12},{9,11},{10,... | collective-permute-start | bytes 442376 | tf_op jit(solution)/shard_map/ppermute | solution.py:99
  106.4 6.8 %collective-permute-start.16 = (f32[9,32,256]{2,1,0:T(8,128)S(1)}, f32[9,32,256]{2,1,0:T(8,128)S(1)}, u32[]{:S(2)}, u32[]{:S(2)}) collective-permute-start(f32[9,32,256]{2,1,0:T(8,128)S(1)} %pad_maximum_fusion.3), channel_id=1, source_target_pairs={{0,2},{1,5},{2,0},{3,7},{4,6},{5,1},{6,4},{7,3},{8,10},{9,13},{10,... | collective-permute-start | bytes 884744 | tf_op jit(solution)/shard_map/ppermute | solution.py:99
  108.1 5.2 %copy-start.8 = (s32[4]{0:T(128)S(1)}, s32[4]{0:T(128)}, u32[]{:S(2)}) copy-start(s32[4]{0:T(128)} %param.13) | copy-start | bytes 52
  108.2 5.4 %copy-start.6 = (f32[5,1024]{1,0:T(8,128)S(1)}, f32[5,1024]{1,0:T(8,128)}, u32[]{:S(2)}) copy-start(f32[5,1024]{1,0:T(8,128)} %param.19) | copy-start | bytes 61444
  113.3 2.1 %collective-permute-start.17 = (f32[9,32,512]{2,1,0:T(8,128)S(1)}, f32[9,32,512]{2,1,0:T(8,128)S(1)}, u32[]{:S(2)}, u32[]{:S(2)}) collective-permute-start(f32[9,32,512]{2,1,0:T(8,128)S(1)} %pad_maximum_fusion.1), channel_id=1, source_target_pairs={{0,1},{1,0},{2,3},{3,2},{4,5},{5,4},{6,7},{7,6},{8,9},{9,8},{10,11... | collective-permute-start | bytes 1769480 | tf_op jit(solution)/shard_map/ppermute | solution.py:99
  114.2 1.2 %copy-start.3 = (f32[4,64,1024]{2,1,0:T(8,128)S(1)}, f32[4,64,1024]{2,1,0:T(8,128)}, u32[]{:S(2)}) copy-start(f32[4,64,1024]{2,1,0:T(8,128)} %param.12) | copy-start | bytes 3145732

commit v11 on v10

--- a/solution.py
+++ b/solution.py
@@ -72,7 +72,7 @@
     for i in range(0, len(alt) - 1, 2):
         alt[i], alt[i + 1] = alt[i + 1], alt[i]
     stages = [(0, 0)] + list(zip(rest, alt))
-    tail = min(2, len(rest))
+    tail = min(3, len(rest))
     halving = stages[: len(stages) - tail]
     pairing = stages[len(stages) - tail :]
 

time: 119 us -> 124 us (1.042)
  waiting for transfers between devices: 64.8 us -> 73.9 us
  starting transfers between devices: 32 us -> 27.8 us
    ppermute x4 -> x6, waiting for transfers between devices: 19.6 us -> 44.7 us  [table_rows(): cur = cur + lax.ppermute(cur, axes, perm_of(p0, p1))]
    ppermute x6 -> x4, waiting for transfers between devices: 21.7 us -> 12.1 us  [table_rows(): other = lax.ppermute(cur, axes, perm_of(p0, p1))]
    ppermute x6 -> x4, waiting for transfers between devices: 19.9 us -> 13.6 us  [table_rows(): cur = keep + lax.ppermute(send, axes, perm_of(p0, p1))]
    ppermute x6 -> x4, starting transfers between devices: 8.36 us -> 3.86 us  [table_rows(): other = lax.ppermute(cur, axes, perm_of(p0, p1))]
    ppermute x4 -> x6, starting transfers between devices: 10.2 us -> 14.6 us  [table_rows(): cur = cur + lax.ppermute(cur, axes, perm_of(p0, p1))]
    ppermute x6 -> x4, starting transfers between devices: 8.49 us -> 4.23 us  [table_rows(): cur = keep + lax.ppermute(send, axes, perm_of(p0, p1))]
  transfers between devices with their start and end apart: 18 -> 16, of which waited for: 18 -> 16; matrix products, arithmetic and copies ran while one was open for 2% -> 2% of each run, Pallas kernels for 0% -> 0%
where the time goes in v11:
time: 124 us; the launch traced here: 123 us
  waiting for transfers between devices  73.9 us (60%)
  starting transfers between devices  27.8 us (22%)
  matrix products  8.8 us (7%)
  local copies, waits for them, and re-layouts  4.58 us (4%)
  other arithmetic  4.17 us (3%)
  between operations  3.7 us (3%)
    ppermute x6, waiting for transfers between devices, table_rows(): cur = cur + lax.ppermute(cur, axes, perm_of(p0, p1))  44.7 us
    ppermute x6, starting transfers between devices, table_rows(): cur = cur + lax.ppermute(cur, axes, perm_of(p0, p1))  14.6 us
    ppermute x4, waiting for transfers between devices, table_rows(): cur = keep + lax.ppermute(send, axes, perm_of(p0, p1))  13.6 us
    ppermute x4, waiting for transfers between devices, table_rows(): other = lax.ppermute(cur, axes, perm_of(p0, p1))  12.1 us
    ppermute x2, starting transfers between devices, swap_sum(): x = x + lax.ppermute(x, axis, _pair_perm(n, j))  5.08 us
    ppermute x4, starting transfers between devices, table_rows(): cur = keep + lax.ppermute(send, axes, perm_of(p0, p1))  4.23 us
    ppermute x4, starting transfers between devices, table_rows(): other = lax.ppermute(cur, axes, perm_of(p0, p1))  3.86 us
    ppermute x2, waiting for transfers between devices, swap_sum(): x = x + lax.ppermute(x, axis, _pair_perm(n, j))  3.51 us
  transfers between devices with their start and end apart: 16, of which 16 were waited for; matrix products, arithmetic and copies ran while one was open for 2% of the time, Pallas kernels for 0%

profile of v11, /device:TPU:0, one launch (start us, length us, event | category | flops | bytes accessed | tf_op | source)
XLA Modules:
  0.0 122.9 jit_solution(11806693522895017967)
XLA Ops:
  0.7 1.4 %shift-left_reduce_fusion = s32[]{:T(128)} fusion(s32[4]{0:T(128)} %param.13), kind=kLoop, calls=%fused_computation.149 | loop fusion | flops 11 | bytes 20 | tf_op jit(solution)/shard_map/reduce_sum | solution.py:48
  4.6 1.1 constant_dynamic-slice_fusion.19
  5.8 2.2 %fusion.6 = f32[4,64,32]{2,1,0:T(8,128)S(1)} fusion(f32[1,1024,32]{1,2,0:T(8,128)S(1)} %get-tuple-element.5, f32[1,1024,32]{1,2,0:T(8,128)S(1)} %get-tuple-element.6, f32[1,1024,32]{1,2,0:T(8,128)S(1)} %get-tuple-element.4, f32[1,1024,32]{1,2,0:T(8,128)S(1)} %get-tuple-element.3, f32[1,4,64,1024]{3,2,1,0:T(8,128)S(1)} %copy-done.1, ...), kind=kOutput, calls=%fused_computation.9 | convolution fusion | flops 101580800 | bytes 2129920 | tf_op jit(solution)/shard_map/tkd,tds->tks/dot_general | solution.py:132
  8.1 3.0 %collective-permute-start = (f32[13312]{0:T(1024)S(1)}, f32[13312]{0:T(1024)S(1)}, u32[]{:S(2)}, u32[]{:S(2)}) collective-permute-start(f32[13312]{0:T(1024)S(1)} %pad_maximum_fusion.6), channel_id=1, source_target_pairs={{0,16},{16,0},{1,17},{17,1},{2,18},{18,2},{3,19},{19,3},{4,20},{20... | collective-permute-start | bytes 159752 | tf_op jit(solution)/shard_map/ppermute | solution.py:20
  11.9 1.4 %collective-permute-done = f32[13312]{0:T(1024)S(1)} collective-permute-done((f32[13312]{0:T(1024)S(1)}, f32[13312]{0:T(1024)S(1)}, u32[]{:S(2)}, u32[]{:S(2)}) %collective-permute-start) | collective-permute-done | bytes 53280 | tf_op jit(solution)/shard_map/ppermute | solution.py:20
  14.9 2.1 %collective-permute-done.1 = f32[9,32,512]{2,1,0:T(8,128)} collective-permute-done((f32[9,32,512]{2,1,0:T(8,128)S(1)}, f32[9,32,512]{2,1,0:T(8,128)}, u32[]{:S(2)}, u32[]{:S(2)}) %collective-permute-start.1) | collective-permute-done | bytes 589856 | tf_op jit(solution)/shard_map/ppermute | solution.py:93
  17.0 1.2 dynamic-slice_add_fusion.1
  18.2 2.1 %collective-permute-start.2 = (f32[9,32,256]{2,1,0:T(8,128)S(1)}, f32[9,32,256]{2,1,0:T(8,128)S(1)}, u32[]{:S(2)}, u32[]{:S(2)}) collective-permute-start(f32[9,32,256]{2,1,0:T(8,128)S(1)} %constant_dynamic-slice_fusion.14), channel_id=1, source_target_pairs={{0,2},{1,5},{2,0},{3,7},{4,6},{5,1},{6,4},{7,3},{8,10},{9,13},{10,... | collective-permute-start | bytes 884744 | tf_op jit(solution)/shard_map/ppermute | solution.py:93
  20.3 4.7 %collective-permute-done.2 = f32[9,32,256]{2,1,0:T(8,128)S(1)} collective-permute-done((f32[9,32,256]{2,1,0:T(8,128)S(1)}, f32[9,32,256]{2,1,0:T(8,128)S(1)}, u32[]{:S(2)}, u32[]{:S(2)}) %collective-permute-start.2) | collective-permute-done | bytes 294944 | tf_op jit(solution)/shard_map/ppermute | solution.py:93
  25.1 2.1 %collective-permute-start.3 = (f32[9,32,256]{2,1,0:T(8,128)S(1)}, f32[9,32,256]{2,1,0:T(8,128)S(1)}, u32[]{:S(2)}, u32[]{:S(2)}) collective-permute-start(f32[9,32,256]{2,1,0:T(8,128)S(1)} %dynamic-slice_add_fusion.3), channel_id=1, source_target_pairs={{0,4},{1,3},{2,6},{3,1},{4,0},{5,7},{6,2},{7,5},{8,12},{9,11},{10,... | collective-permute-start | bytes 884744 | tf_op jit(solution)/shard_map/ppermute | solution.py:96
  27.2 4.7 %collective-permute-done.3 = f32[9,32,256]{2,1,0:T(8,128)S(1)} collective-permute-done((f32[9,32,256]{2,1,0:T(8,128)S(1)}, f32[9,32,256]{2,1,0:T(8,128)S(1)}, u32[]{:S(2)}, u32[]{:S(2)}) %collective-permute-start.3) | collective-permute-done | bytes 294944 | tf_op jit(solution)/shard_map/ppermute | solution.py:96
  32.0 3.1 %collective-permute-start.4 = (f32[9,32,256]{2,1,0:T(8,128)S(1)}, f32[9,32,256]{2,1,0:T(8,128)S(1)}, u32[]{:S(2)}, u32[]{:S(2)}) collective-permute-start(f32[9,32,256]{2,1,0:T(8,128)S(1)} %add.166), channel_id=1, source_target_pairs={{0,8},{1,17},{2,10},{3,19},{4,12},{5,21},{6,14},{7,23},{8,0},{9,25... | collective-permute-start | bytes 884744 | tf_op jit(solution)/shard_map/ppermute | solution.py:96
  35.1 12.7 %collective-permute-done.4 = f32[9,32,256]{2,1,0:T(8,128)S(1)} collective-permute-done((f32[9,32,256]{2,1,0:T(8,128)S(1)}, f32[9,32,256]{2,1,0:T(8,128)S(1)}, u32[]{:S(2)}, u32[]{:S(2)}) %collective-permute-start.4) | collective-permute-done | bytes 294944 | tf_op jit(solution)/shard_map/ppermute | solution.py:96
  47.9 2.2 %collective-permute-start.5 = (f32[9,32,256]{2,1,0:T(8,128)S(1)}, f32[9,32,256]{2,1,0:T(8,128)S(1)}, u32[]{:S(2)}, u32[]{:S(2)}) collective-permute-start(f32[9,32,256]{2,1,0:T(8,128)S(1)} %add.167), channel_id=1, source_target_pairs={{0,16},{1,9},{2,18},{3,11},{4,20},{5,13},{6,22},{7,15},{8,24},{9,1... | collective-permute-start | bytes 884744 | tf_op jit(solution)/shard_map/ppermute | solution.py:96
  50.1 4.7 %collective-permute-done.5 = f32[9,32,256]{2,1,0:T(8,128)S(1)} collective-permute-done((f32[9,32,256]{2,1,0:T(8,128)S(1)}, f32[9,32,256]{2,1,0:T(8,128)S(1)}, u32[]{:S(2)}, u32[]{:S(2)}) %collective-permute-start.5) | collective-permute-done | bytes 294944 | tf_op jit(solution)/shard_map/ppermute | solution.py:96
  54.8 2.1 %collective-permute-start.6 = (f32[9,32,256]{2,1,0:T(8,128)S(1)}, f32[9,32,256]{2,1,0:T(8,128)S(1)}, u32[]{:S(2)}, u32[]{:S(2)}) collective-permute-start(f32[9,32,256]{2,1,0:T(8,128)S(1)} %add.168), channel_id=1, source_target_pairs={{0,2},{1,5},{2,0},{3,7},{4,6},{5,1},{6,4},{7,3},{8,10},{9,13},{10,... | collective-permute-start | bytes 884744 | tf_op jit(solution)/shard_map/ppermute | solution.py:99
  57.0 4.7 %collective-permute-done.6 = f32[9,32,256]{2,1,0:T(8,128)S(1)} collective-permute-done((f32[9,32,256]{2,1,0:T(8,128)S(1)}, f32[9,32,256]{2,1,0:T(8,128)S(1)}, u32[]{:S(2)}, u32[]{:S(2)}) %collective-permute-start.6) | collective-permute-done | bytes 294944 | tf_op jit(solution)/shard_map/ppermute | solution.py:99
  62.7 1.3 %collective-permute-done.7 = f32[9,32,512]{2,1,0:T(8,128)} collective-permute-done((f32[9,32,512]{2,1,0:T(8,128)S(1)}, f32[9,32,512]{2,1,0:T(8,128)}, u32[]{:S(2)}, u32[]{:S(2)}) %collective-permute-start.7) | collective-permute-done | bytes 589856 | tf_op jit(solution)/shard_map/ppermute | solution.py:99
  66.8 2.0 %collective-permute-start.8 = (f32[4,64,32]{1,2,0:T(8,128)S(1)}, f32[4,64,32]{1,2,0:T(8,128)S(1)}, u32[]{:S(2)}, u32[]{:S(2)}) collective-permute-start(f32[4,64,32]{1,2,0:T(8,128)S(1)} %fusion.2), channel_id=1, source_target_pairs={{0,16},{16,0},{1,17},{17,1},{2,18},{18,2},{3,19},{19,3},{4,20},{20... | collective-permute-start | bytes 98312 | tf_op jit(solution)/shard_map/ppermute | solution.py:20
  69.1 2.1 %collective-permute-done.8 = f32[4,64,32]{1,2,0:T(8,128)S(1)} collective-permute-done((f32[4,64,32]{1,2,0:T(8,128)S(1)}, f32[4,64,32]{1,2,0:T(8,128)S(1)}, u32[]{:S(2)}, u32[]{:S(2)}) %collective-permute-start.8) | collective-permute-done | bytes 32800 | tf_op jit(solution)/shard_map/ppermute | solution.py:20
  72.5 2.0 %collective-permute-done.9 = f32[9,32,512]{2,1,0:T(8,128)S(1)} collective-permute-done((f32[9,32,512]{2,1,0:T(8,128)S(1)}, f32[9,32,512]{2,1,0:T(8,128)S(1)}, u32[]{:S(2)}, u32[]{:S(2)}) %collective-permute-start.9) | collective-permute-done | bytes 589856 | tf_op jit(solution)/shard_map/ppermute | solution.py:93
  74.6 2.0 %collective-permute-start.10 = (f32[9,32,256]{2,1,0:T(8,128)S(1)}, f32[9,32,256]{2,1,0:T(8,128)S(1)}, u32[]{:S(2)}, u32[]{:S(2)}) collective-permute-start(f32[9,32,256]{2,1,0:T(8,128)S(1)} %constant_dynamic-slice_fusion), channel_id=1, source_target_pairs={{0,2},{1,5},{2,0},{3,7},{4,6},{5,1},{6,4},{7,3},{8,10},{9,13},{10,... | collective-permute-start | bytes 884744 | tf_op jit(solution)/shard_map/ppermute | solution.py:93
  76.6 4.8 %collective-permute-done.10 = f32[9,32,256]{2,1,0:T(8,128)S(1)} collective-permute-done((f32[9,32,256]{2,1,0:T(8,128)S(1)}, f32[9,32,256]{2,1,0:T(8,128)S(1)}, u32[]{:S(2)}, u32[]{:S(2)}) %collective-permute-start.10) | collective-permute-done | bytes 294944 | tf_op jit(solution)/shard_map/ppermute | solution.py:93
  81.5 2.1 %collective-permute-start.11 = (f32[9,32,256]{2,1,0:T(8,128)S(1)}, f32[9,32,256]{2,1,0:T(8,128)S(1)}, u32[]{:S(2)}, u32[]{:S(2)}) collective-permute-start(f32[9,32,256]{2,1,0:T(8,128)S(1)} %dynamic-slice_add_fusion.2), channel_id=1, source_target_pairs={{0,4},{1,3},{2,6},{3,1},{4,0},{5,7},{6,2},{7,5},{8,12},{9,11},{10,... | collective-permute-start | bytes 884744 | tf_op jit(solution)/shard_map/ppermute | solution.py:96
  83.6 4.7 %collective-permute-done.11 = f32[9,32,256]{2,1,0:T(8,128)S(1)} collective-permute-done((f32[9,32,256]{2,1,0:T(8,128)S(1)}, f32[9,32,256]{2,1,0:T(8,128)S(1)}, u32[]{:S(2)}, u32[]{:S(2)}) %collective-permute-start.11) | collective-permute-done | bytes 294944 | tf_op jit(solution)/shard_map/ppermute | solution.py:96
  88.4 3.4 %collective-permute-start.12 = (f32[9,32,256]{2,1,0:T(8,128)S(1)}, f32[9,32,256]{2,1,0:T(8,128)S(1)}, u32[]{:S(2)}, u32[]{:S(2)}) collective-permute-start(f32[9,32,256]{2,1,0:T(8,128)S(1)} %add.175), channel_id=1, source_target_pairs={{0,8},{1,17},{2,10},{3,19},{4,12},{5,21},{6,14},{7,23},{8,0},{9,25... | collective-permute-start | bytes 884744 | tf_op jit(solution)/shard_map/ppermute | solution.py:96
  91.8 12.6 %collective-permute-done.12 = f32[9,32,256]{2,1,0:T(8,128)S(1)} collective-permute-done((f32[9,32,256]{2,1,0:T(8,128)S(1)}, f32[9,32,256]{2,1,0:T(8,128)S(1)}, u32[]{:S(2)}, u32[]{:S(2)}) %collective-permute-start.12) | collective-permute-done | bytes 294944 | tf_op jit(solution)/shard_map/ppermute | solution.py:96
  104.5 1.6 %collective-permute-start.13 = (f32[9,32,256]{2,1,0:T(8,128)S(1)}, f32[9,32,256]{2,1,0:T(8,128)S(1)}, u32[]{:S(2)}, u32[]{:S(2)}) collective-permute-start(f32[9,32,256]{2,1,0:T(8,128)S(1)} %add.176), channel_id=1, source_target_pairs={{0,16},{1,9},{2,18},{3,11},{4,20},{5,13},{6,22},{7,15},{8,24},{9,1... | collective-permute-start | bytes 884744 | tf_op jit(solution)/shard_map/ppermute | solution.py:96
  106.0 5.2 %collective-permute-done.13 = f32[9,32,256]{2,1,0:T(8,128)S(1)} collective-permute-done((f32[9,32,256]{2,1,0:T(8,128)S(1)}, f32[9,32,256]{2,1,0:T(8,128)S(1)}, u32[]{:S(2)}, u32[]{:S(2)}) %collective-permute-start.13) | collective-permute-done | bytes 294944 | tf_op jit(solution)/shard_map/ppermute | solution.py:96
  111.3 1.6 %collective-permute-start.14 = (f32[9,32,256]{2,1,0:T(8,128)S(1)}, f32[9,32,256]{2,1,0:T(8,128)S(1)}, u32[]{:S(2)}, u32[]{:S(2)}) collective-permute-start(f32[9,32,256]{2,1,0:T(8,128)S(1)} %add.177), channel_id=1, source_target_pairs={{0,2},{1,5},{2,0},{3,7},{4,6},{5,1},{6,4},{7,3},{8,10},{9,13},{10,... | collective-permute-start | bytes 884744 | tf_op jit(solution)/shard_map/ppermute | solution.py:99
  113.1 5.0 %collective-permute-done.14 = f32[9,32,256]{2,1,0:T(8,128)S(1)} collective-permute-done((f32[9,32,256]{2,1,0:T(8,128)S(1)}, f32[9,32,256]{2,1,0:T(8,128)S(1)}, u32[]{:S(2)}, u32[]{:S(2)}) %collective-permute-start.14) | collective-permute-done | bytes 294944 | tf_op jit(solution)/shard_map/ppermute | solution.py:99
  120.4 2.6 %multiply_add_fusion = (f32[4,64,1024]{2,1,0:T(8,128)}, f32[1,4,64,1024]{3,2,1,0:T(8,128)}) fusion(f32[4,64,1024]{2,1,0:T(8,128)S(1)} %copy-done.3, f32[4]{0:T(128)S(1)} %convolution_bitcast_fusion, f32[1,4,64,1024]{3,2,1,0:T(8,128)S(1)} %copy-done.1, bf16[1,4,64,1024]{3,2,1,0:T(8,128)(2,1)S(1)} %copy-done.2, f32[4,64,32]{1,2,0:T(8,128)S(1)} %fusion.57, ...), kind=kOutput, calls=%fused_computation.12 | convolution fusion | flops 102498304 | bytes 5275664 | tf_op jit(solution)/shard_map/tks,tsd->tkd/dot_general | solution.py:152
  (80 shorter events, 10.5 us)
Async XLA Ops:
  0.6 112.3 %copy-start = (f32[4]{0:T(128)S(1)}, f32[4]{0:T(128)}, u32[]{:S(2)}) copy-start(f32[4]{0:T(128)} %param.15) | copy-start | bytes 52
  0.6 5.1 %copy-start.1 = (f32[1,4,64,1024]{3,2,1,0:T(8,128)S(1)}, f32[1,4,64,1024]{3,2,1,0:T(8,128)}, u32[]{:S(2)}) copy-start(f32[1,4,64,1024]{3,2,1,0:T(8,128)} %param.11) | copy-start | bytes 3145732
  5.8 2.3 %copy-start.5 = (f32[1,5,1024]{2,0,1:T(1,128)S(1)}, f32[1,5,1024]{2,0,1:T(1,128)}, u32[]{:S(2)}) copy-start(f32[1,5,1024]{2,0,1:T(1,128)} %param.18) | copy-start | bytes 61444
  5.8 5.4 %copy-start.4 = (f32[3,9,32,32]{3,2,1,0:T(8,128)S(1)}, f32[3,9,32,32]{3,2,1,0:T(8,128)}, u32[]{:S(2)}) copy-start(f32[3,9,32,32]{3,2,1,0:T(8,128)} %param.17) | copy-start | bytes 331780
  8.0 5.8 %copy-start.2 = (bf16[1,4,64,1024]{3,2,1,0:T(8,128)(2,1)S(1)}, bf16[1,4,64,1024]{3,2,1,0:T(8,128)(2,1)}, u32[]{:S(2)}) copy-start(bf16[1,4,64,1024]{3,2,1,0:T(8,128)(2,1)} %param.10) | copy-start | bytes 1572868
  8.1 5.1 %collective-permute-start = (f32[13312]{0:T(1024)S(1)}, f32[13312]{0:T(1024)S(1)}, u32[]{:S(2)}, u32[]{:S(2)}) collective-permute-start(f32[13312]{0:T(1024)S(1)} %pad_maximum_fusion.6), channel_id=1, source_target_pairs={{0,16},{16,0},{1,17},{17,1},{2,18},{18,2},{3,19},{19,3},{4,20},{20... | collective-permute-start | bytes 159752 | tf_op jit(solution)/shard_map/ppermute | solution.py:20
  14.8 2.2 %collective-permute-start.1 = (f32[9,32,512]{2,1,0:T(8,128)S(1)}, f32[9,32,512]{2,1,0:T(8,128)}, u32[]{:S(2)}, u32[]{:S(2)}) collective-permute-start(f32[9,32,512]{2,1,0:T(8,128)S(1)} %constant_dynamic-slice_fusion.15), channel_id=1, source_target_pairs={{0,1},{1,0},{2,3},{3,2},{4,5},{5,4},{6,7},{7,6},{8,9},{9,8},{10,11... | collective-permute-start | bytes 1769480 | tf_op jit(solution)/shard_map/ppermute | solution.py:93
  18.2 6.8 %collective-permute-start.2 = (f32[9,32,256]{2,1,0:T(8,128)S(1)}, f32[9,32,256]{2,1,0:T(8,128)S(1)}, u32[]{:S(2)}, u32[]{:S(2)}) collective-permute-start(f32[9,32,256]{2,1,0:T(8,128)S(1)} %constant_dynamic-slice_fusion.14), channel_id=1, source_target_pairs={{0,2},{1,5},{2,0},{3,7},{4,6},{5,1},{6,4},{7,3},{8,10},{9,13},{10,... | collective-permute-start | bytes 884744 | tf_op jit(solution)/shard_map/ppermute | solution.py:93
  25.1 6.8 %collective-permute-start.3 = (f32[9,32,256]{2,1,0:T(8,128)S(1)}, f32[9,32,256]{2,1,0:T(8,128)S(1)}, u32[]{:S(2)}, u32[]{:S(2)}) collective-permute-start(f32[9,32,256]{2,1,0:T(8,128)S(1)} %dynamic-slice_add_fusion.3), channel_id=1, source_target_pairs={{0,4},{1,3},{2,6},{3,1},{4,0},{5,7},{6,2},{7,5},{8,12},{9,11},{10,... | collective-permute-start | bytes 884744 | tf_op jit(solution)/shard_map/ppermute | solution.py:96
  32.0 15.8 %collective-permute-start.4 = (f32[9,32,256]{2,1,0:T(8,128)S(1)}, f32[9,32,256]{2,1,0:T(8,128)S(1)}, u32[]{:S(2)}, u32[]{:S(2)}) collective-permute-start(f32[9,32,256]{2,1,0:T(8,128)S(1)} %add.166), channel_id=1, source_target_pairs={{0,8},{1,17},{2,10},{3,19},{4,12},{5,21},{6,14},{7,23},{8,0},{9,25... | collective-permute-start | bytes 884744 | tf_op jit(solution)/shard_map/ppermute | solution.py:96
  47.9 6.9 %collective-permute-start.5 = (f32[9,32,256]{2,1,0:T(8,128)S(1)}, f32[9,32,256]{2,1,0:T(8,128)S(1)}, u32[]{:S(2)}, u32[]{:S(2)}) collective-permute-start(f32[9,32,256]{2,1,0:T(8,128)S(1)} %add.167), channel_id=1, source_target_pairs={{0,16},{1,9},{2,18},{3,11},{4,20},{5,13},{6,22},{7,15},{8,24},{9,1... | collective-permute-start | bytes 884744 | tf_op jit(solution)/shard_map/ppermute | solution.py:96
  54.8 6.8 %collective-permute-start.6 = (f32[9,32,256]{2,1,0:T(8,128)S(1)}, f32[9,32,256]{2,1,0:T(8,128)S(1)}, u32[]{:S(2)}, u32[]{:S(2)}) collective-permute-start(f32[9,32,256]{2,1,0:T(8,128)S(1)} %add.168), channel_id=1, source_target_pairs={{0,2},{1,5},{2,0},{3,7},{4,6},{5,1},{6,4},{7,3},{8,10},{9,13},{10,... | collective-permute-start | bytes 884744 | tf_op jit(solution)/shard_map/ppermute | solution.py:99
  61.8 2.2 %collective-permute-start.7 = (f32[9,32,512]{2,1,0:T(8,128)S(1)}, f32[9,32,512]{2,1,0:T(8,128)}, u32[]{:S(2)}, u32[]{:S(2)}) collective-permute-start(f32[9,32,512]{2,1,0:T(8,128)S(1)} %pad_maximum_fusion), channel_id=1, source_target_pairs={{0,1},{1,0},{2,3},{3,2},{4,5},{5,4},{6,7},{7,6},{8,9},{9,8},{10,11... | collective-permute-start | bytes 1769480 | tf_op jit(solution)/shard_map/ppermute | solution.py:99
  66.8 4.4 %collective-permute-start.8 = (f32[4,64,32]{1,2,0:T(8,128)S(1)}, f32[4,64,32]{1,2,0:T(8,128)S(1)}, u32[]{:S(2)}, u32[]{:S(2)}) collective-permute-start(f32[4,64,32]{1,2,0:T(8,128)S(1)} %fusion.2), channel_id=1, source_target_pairs={{0,16},{16,0},{1,17},{17,1},{2,18},{18,2},{3,19},{19,3},{4,20},{20... | collective-permute-start | bytes 98312 | tf_op jit(solution)/shard_map/ppermute | solution.py:20
  72.4 2.1 %collective-permute-start.9 = (f32[9,32,512]{2,1,0:T(8,128)S(1)}, f32[9,32,512]{2,1,0:T(8,128)S(1)}, u32[]{:S(2)}, u32[]{:S(2)}) collective-permute-start(f32[9,32,512]{2,1,0:T(8,128)S(1)} %constant_dynamic-slice_fusion.1), channel_id=1, source_target_pairs={{0,1},{1,0},{2,3},{3,2},{4,5},{5,4},{6,7},{7,6},{8,9},{9,8},{10,11... | collective-permute-start | bytes 1769480 | tf_op jit(solution)/shard_map/ppermute | solution.py:93
  74.6 6.8 %collective-permute-start.10 = (f32[9,32,256]{2,1,0:T(8,128)S(1)}, f32[9,32,256]{2,1,0:T(8,128)S(1)}, u32[]{:S(2)}, u32[]{:S(2)}) collective-permute-start(f32[9,32,256]{2,1,0:T(8,128)S(1)} %constant_dynamic-slice_fusion), channel_id=1, source_target_pairs={{0,2},{1,5},{2,0},{3,7},{4,6},{5,1},{6,4},{7,3},{8,10},{9,13},{10,... | collective-permute-start | bytes 884744 | tf_op jit(solution)/shard_map/ppermute | solution.py:93
  81.5 31.4 %copy-start.7 = (s32[9]{0:T(128)S(1)}, s32[9]{0:T(128)}, u32[]{:S(2)}) copy-start(s32[9]{0:T(128)} %param.14) | copy-start | bytes 112
  81.5 6.8 %collective-permute-start.11 = (f32[9,32,256]{2,1,0:T(8,128)S(1)}, f32[9,32,256]{2,1,0:T(8,128)S(1)}, u32[]{:S(2)}, u32[]{:S(2)}) collective-permute-start(f32[9,32,256]{2,1,0:T(8,128)S(1)} %dynamic-slice_add_fusion.2), channel_id=1, source_target_pairs={{0,4},{1,3},{2,6},{3,1},{4,0},{5,7},{6,2},{7,5},{8,12},{9,11},{10,... | collective-permute-start | bytes 884744 | tf_op jit(solution)/shard_map/ppermute | solution.py:96
  88.4 16.1 %collective-permute-start.12 = (f32[9,32,256]{2,1,0:T(8,128)S(1)}, f32[9,32,256]{2,1,0:T(8,128)S(1)}, u32[]{:S(2)}, u32[]{:S(2)}) collective-permute-start(f32[9,32,256]{2,1,0:T(8,128)S(1)} %add.175), channel_id=1, source_target_pairs={{0,8},{1,17},{2,10},{3,19},{4,12},{5,21},{6,14},{7,23},{8,0},{9,25... | collective-permute-start | bytes 884744 | tf_op jit(solution)/shard_map/ppermute | solution.py:96
  104.5 6.8 %collective-permute-start.13 = (f32[9,32,256]{2,1,0:T(8,128)S(1)}, f32[9,32,256]{2,1,0:T(8,128)S(1)}, u32[]{:S(2)}, u32[]{:S(2)}) collective-permute-start(f32[9,32,256]{2,1,0:T(8,128)S(1)} %add.176), channel_id=1, source_target_pairs={{0,16},{1,9},{2,18},{3,11},{4,20},{5,13},{6,22},{7,15},{8,24},{9,1... | collective-permute-start | bytes 884744 | tf_op jit(solution)/shard_map/ppermute | solution.py:96
  111.3 6.8 %collective-permute-start.14 = (f32[9,32,256]{2,1,0:T(8,128)S(1)}, f32[9,32,256]{2,1,0:T(8,128)S(1)}, u32[]{:S(2)}, u32[]{:S(2)}) collective-permute-start(f32[9,32,256]{2,1,0:T(8,128)S(1)} %add.177), channel_id=1, source_target_pairs={{0,2},{1,5},{2,0},{3,7},{4,6},{5,1},{6,4},{7,3},{8,10},{9,13},{10,... | collective-permute-start | bytes 884744 | tf_op jit(solution)/shard_map/ppermute | solution.py:99
  113.1 5.2 %copy-start.8 = (s32[4]{0:T(128)S(1)}, s32[4]{0:T(128)}, u32[]{:S(2)}) copy-start(s32[4]{0:T(128)} %param.13) | copy-start | bytes 52
  113.1 5.4 %copy-start.6 = (f32[5,1024]{1,0:T(8,128)S(1)}, f32[5,1024]{1,0:T(8,128)}, u32[]{:S(2)}) copy-start(f32[5,1024]{1,0:T(8,128)} %param.19) | copy-start | bytes 61444
  118.2 2.1 %collective-permute-start.15 = (f32[9,32,512]{2,1,0:T(8,128)S(1)}, f32[9,32,512]{2,1,0:T(8,128)S(1)}, u32[]{:S(2)}, u32[]{:S(2)}) collective-permute-start(f32[9,32,512]{2,1,0:T(8,128)S(1)} %pad_maximum_fusion.1), channel_id=1, source_target_pairs={{0,1},{1,0},{2,3},{3,2},{4,5},{5,4},{6,7},{7,6},{8,9},{9,8},{10,11... | collective-permute-start | bytes 1769480 | tf_op jit(solution)/shard_map/ppermute | solution.py:99
  119.1 1.2 copy-start.3

commit v12 on v10

--- a/solution.py
+++ b/solution.py
@@ -4,6 +4,7 @@
 from jax.sharding import PartitionSpec as P
 
 TOP_PRECISION = lax.Precision.HIGHEST
+WIDE_PRECISION = lax.Precision.HIGH
 
 
 def _bits(n):
@@ -129,7 +130,7 @@
     combined = gradient[0].astype(jnp.float32) + feedback[0]
     tile_rows = _scalar_rows(tile_matrix, matrix_count)
     q_tiles = _pick_rows(start_basis, tile_rows)
-    first_local = jnp.einsum("tkd,tds->tks", combined, q_tiles, precision=TOP_PRECISION)
+    first_local = jnp.einsum("tkd,tds->tks", combined, q_tiles, precision=WIDE_PRECISION)
     left_size = first_local.size
     carried = jnp.concatenate([first_local.reshape(-1), vector_grad[0].reshape(-1)])
     carried = swap_sum(carried, "rep")
@@ -137,19 +138,19 @@
     vector_summed = carried[left_size:].reshape(vector_grad.shape[1:])
     mix_first = _pick_rows(inverse_gram_factors[0], tile_rows)
     first_ortho = jnp.einsum("tks,tsa->tka", first_left, mix_first, precision=TOP_PRECISION)
-    first_parts = jnp.einsum("tkd,tks->tsd", combined, first_ortho, precision=TOP_PRECISION)
+    first_parts = jnp.einsum("tkd,tks->tsd", combined, first_ortho, precision=WIDE_PRECISION)
     first_table = _scatter_rows(first_parts, tile_rows, matrix_count)
     first_rows = table_rows(first_table, tile_rows, replicas, n_own) / replicas
     mix_right = _pick_rows(inverse_gram_factors[1], tile_rows)
     right_rows = jnp.einsum("tjw,tjd->twd", mix_right, first_rows, precision=TOP_PRECISION)
-    second_local = jnp.einsum("tkd,tsd->tks", combined, right_rows, precision=TOP_PRECISION)
+    second_local = jnp.einsum("tkd,tsd->tks", combined, right_rows, precision=WIDE_PRECISION)
     second_left = swap_sum(second_local, "rep") / replicas
     mix_second = _pick_rows(inverse_gram_factors[2], tile_rows)
     second_ortho = jnp.einsum("tks,tsa->tka", second_left, mix_second, precision=TOP_PRECISION)
-    second_parts = jnp.einsum("tkd,tks->tsd", combined, second_ortho, precision=TOP_PRECISION)
+    second_parts = jnp.einsum("tkd,tks->tsd", combined, second_ortho, precision=WIDE_PRECISION)
     second_table = _scatter_rows(second_parts, tile_rows, matrix_count)
     back_rows = table_rows(second_table, tile_rows, replicas, n_own) / replicas
-    approximation = jnp.einsum("tks,tsd->tkd", second_ortho, back_rows, precision=TOP_PRECISION)
+    approximation = jnp.einsum("tks,tsd->tkd", second_ortho, back_rows, precision=WIDE_PRECISION)
     new_feedback = (combined - approximation)[None]
     group_select = (
         matrix_group[:, None] == jnp.arange(group_scale.shape[0], dtype=jnp.int32)[None, :]

time: 119 us -> 117 us (0.983)
  matrix products: 8.8 us -> 6.87 us
    dot_general x5, matrix products: 7.25 us -> 5.32 us  [the longest x1 2.17 us: local(): jnp.einsum('tks,tsd->tkd', second_ortho, back_rows, precision=WIDE_PRECIS...]
where the time goes in v12:
time: 117 us; the launch traced here: 116 us
  waiting for transfers between devices  64.8 us (55%)
  starting transfers between devices  31.9 us (27%)
  matrix products  6.87 us (6%)
  local copies, waits for them, and re-layouts  4.61 us (4%)
  other arithmetic  4.15 us (4%)
  between operations  3.73 us (3%)
    ppermute x6, waiting for transfers between devices, table_rows(): other = lax.ppermute(cur, axes, perm_of(p0, p1))  21.8 us
    ppermute x6, waiting for transfers between devices, table_rows(): cur = keep + lax.ppermute(send, axes, perm_of(p0, p1))  19.9 us
    ppermute x4, waiting for transfers between devices, table_rows(): cur = cur + lax.ppermute(cur, axes, perm_of(p0, p1))  19.6 us
    ppermute x4, starting transfers between devices, table_rows(): cur = cur + lax.ppermute(cur, axes, perm_of(p0, p1))  10.3 us
    ppermute x6, starting transfers between devices, table_rows(): cur = keep + lax.ppermute(send, axes, perm_of(p0, p1))  8.42 us
    ppermute x6, starting transfers between devices, table_rows(): other = lax.ppermute(cur, axes, perm_of(p0, p1))  8.25 us
    ppermute x2, starting transfers between devices, swap_sum(): x = x + lax.ppermute(x, axis, _pair_perm(n, j))  4.91 us
    ppermute x2, waiting for transfers between devices, swap_sum(): x = x + lax.ppermute(x, axis, _pair_perm(n, j))  3.56 us
  transfers between devices with their start and end apart: 18, of which 18 were waited for; matrix products, arithmetic and copies ran while one was open for 2% of the time, Pallas kernels for 0%

profile of v12, /device:TPU:0, one launch (start us, length us, event | category | flops | bytes accessed | tf_op | source)
XLA Modules:
  0.0 116.1 jit_solution(9576724895891589507)
XLA Ops:
  5.8 1.7 %fusion.6 = f32[4,64,32]{2,1,0:T(8,128)S(1)} fusion(f32[1,1024,32]{1,2,0:T(8,128)S(1)} %get-tuple-element.5, f32[1,1024,32]{1,2,0:T(8,128)S(1)} %get-tuple-element.6, f32[1,1024,32]{1,2,0:T(8,128)S(1)} %get-tuple-element.4, f32[1,1024,32]{1,2,0:T(8,128)S(1)} %get-tuple-element.3, f32[1,4,64,1024]{3,2,1,0:T(8,128)S(1)} %copy-done.1, ...), kind=kOutput, calls=%fused_computation.9 | convolution fusion | flops 51249152 | bytes 2129920 | tf_op jit(solution)/shard_map/tkd,tds->tks/dot_general | solution.py:133
  7.7 3.0 %collective-permute-start = (f32[13312]{0:T(1024)S(1)}, f32[13312]{0:T(1024)S(1)}, u32[]{:S(2)}, u32[]{:S(2)}) collective-permute-start(f32[13312]{0:T(1024)S(1)} %pad_maximum_fusion.8), channel_id=1, source_target_pairs={{0,16},{16,0},{1,17},{17,1},{2,18},{18,2},{3,19},{19,3},{4,20},{20... | collective-permute-start | bytes 159752 | tf_op jit(solution)/shard_map/ppermute | solution.py:21
  11.4 1.4 %collective-permute-done = f32[13312]{0:T(1024)S(1)} collective-permute-done((f32[13312]{0:T(1024)S(1)}, f32[13312]{0:T(1024)S(1)}, u32[]{:S(2)}, u32[]{:S(2)}) %collective-permute-start) | collective-permute-done | bytes 53280 | tf_op jit(solution)/shard_map/ppermute | solution.py:21
  14.1 2.1 %collective-permute-done.1 = f32[9,32,512]{2,1,0:T(8,128)} collective-permute-done((f32[9,32,512]{2,1,0:T(8,128)S(1)}, f32[9,32,512]{2,1,0:T(8,128)}, u32[]{:S(2)}, u32[]{:S(2)}) %collective-permute-start.1) | collective-permute-done | bytes 589856 | tf_op jit(solution)/shard_map/ppermute | solution.py:94
  17.5 2.1 %collective-permute-start.2 = (f32[9,32,256]{2,1,0:T(8,128)S(1)}, f32[9,32,256]{2,1,0:T(8,128)S(1)}, u32[]{:S(2)}, u32[]{:S(2)}) collective-permute-start(f32[9,32,256]{2,1,0:T(8,128)S(1)} %constant_dynamic-slice_fusion.16), channel_id=1, source_target_pairs={{0,2},{1,5},{2,0},{3,7},{4,6},{5,1},{6,4},{7,3},{8,10},{9,13},{10,... | collective-permute-start | bytes 884744 | tf_op jit(solution)/shard_map/ppermute | solution.py:94
  19.6 4.7 %collective-permute-done.2 = f32[9,32,256]{2,1,0:T(8,128)S(1)} collective-permute-done((f32[9,32,256]{2,1,0:T(8,128)S(1)}, f32[9,32,256]{2,1,0:T(8,128)S(1)}, u32[]{:S(2)}, u32[]{:S(2)}) %collective-permute-start.2) | collective-permute-done | bytes 294944 | tf_op jit(solution)/shard_map/ppermute | solution.py:94
  24.4 2.1 %collective-permute-start.3 = (f32[9,32,128]{2,1,0:T(8,128)S(1)}, f32[9,32,128]{2,1,0:T(8,128)S(1)}, u32[]{:S(2)}, u32[]{:S(2)}) collective-permute-start(f32[9,32,128]{2,1,0:T(8,128)S(1)} %constant_dynamic-slice_fusion.15), channel_id=1, source_target_pairs={{0,4},{1,3},{2,6},{3,1},{4,0},{5,7},{6,2},{7,5},{8,12},{9,11},{10,... | collective-permute-start | bytes 442376 | tf_op jit(solution)/shard_map/ppermute | solution.py:94
  26.5 3.1 %collective-permute-done.3 = f32[9,32,128]{2,1,0:T(8,128)S(1)} collective-permute-done((f32[9,32,128]{2,1,0:T(8,128)S(1)}, f32[9,32,128]{2,1,0:T(8,128)S(1)}, u32[]{:S(2)}, u32[]{:S(2)}) %collective-permute-start.3) | collective-permute-done | bytes 147488 | tf_op jit(solution)/shard_map/ppermute | solution.py:94
  29.6 3.1 %collective-permute-start.4 = (f32[9,32,128]{2,1,0:T(8,128)S(1)}, f32[9,32,128]{2,1,0:T(8,128)S(1)}, u32[]{:S(2)}, u32[]{:S(2)}) collective-permute-start(f32[9,32,128]{2,1,0:T(8,128)S(1)} %dynamic-slice_add_fusion.5), channel_id=1, source_target_pairs={{0,8},{1,17},{2,10},{3,19},{4,12},{5,21},{6,14},{7,23},{8,0},{9,25... | collective-permute-start | bytes 442376 | tf_op jit(solution)/shard_map/ppermute | solution.py:97
  32.7 6.4 %collective-permute-done.4 = f32[9,32,128]{2,1,0:T(8,128)S(1)} collective-permute-done((f32[9,32,128]{2,1,0:T(8,128)S(1)}, f32[9,32,128]{2,1,0:T(8,128)S(1)}, u32[]{:S(2)}, u32[]{:S(2)}) %collective-permute-start.4) | collective-permute-done | bytes 147488 | tf_op jit(solution)/shard_map/ppermute | solution.py:97
  39.2 2.2 %collective-permute-start.5 = (f32[9,32,128]{2,1,0:T(8,128)S(1)}, f32[9,32,128]{2,1,0:T(8,128)S(1)}, u32[]{:S(2)}, u32[]{:S(2)}) collective-permute-start(f32[9,32,128]{2,1,0:T(8,128)S(1)} %add.177), channel_id=1, source_target_pairs={{0,16},{1,9},{2,18},{3,11},{4,20},{5,13},{6,22},{7,15},{8,24},{9,1... | collective-permute-start | bytes 442376 | tf_op jit(solution)/shard_map/ppermute | solution.py:97
  41.4 3.1 %collective-permute-done.5 = f32[9,32,128]{2,1,0:T(8,128)S(1)} collective-permute-done((f32[9,32,128]{2,1,0:T(8,128)S(1)}, f32[9,32,128]{2,1,0:T(8,128)S(1)}, u32[]{:S(2)}, u32[]{:S(2)}) %collective-permute-start.5) | collective-permute-done | bytes 147488 | tf_op jit(solution)/shard_map/ppermute | solution.py:97
  44.6 2.3 %collective-permute-start.6 = (f32[9,32,128]{2,1,0:T(8,128)S(1)}, f32[9,32,128]{2,1,0:T(8,128)S(1)}, u32[]{:S(2)}, u32[]{:S(2)}) collective-permute-start(f32[9,32,128]{2,1,0:T(8,128)S(1)} %add.178), channel_id=1, source_target_pairs={{0,4},{1,3},{2,6},{3,1},{4,0},{5,7},{6,2},{7,5},{8,12},{9,11},{10,... | collective-permute-start | bytes 442376 | tf_op jit(solution)/shard_map/ppermute | solution.py:100
  46.8 4.7 %collective-permute-done.6 = f32[9,32,128]{2,1,0:T(8,128)S(1)} collective-permute-done((f32[9,32,128]{2,1,0:T(8,128)S(1)}, f32[9,32,128]{2,1,0:T(8,128)S(1)}, u32[]{:S(2)}, u32[]{:S(2)}) %collective-permute-start.6) | collective-permute-done | bytes 147488 | tf_op jit(solution)/shard_map/ppermute | solution.py:100
  51.6 1.9 %collective-permute-start.7 = (f32[9,32,256]{2,1,0:T(8,128)S(1)}, f32[9,32,256]{2,1,0:T(8,128)S(1)}, u32[]{:S(2)}, u32[]{:S(2)}) collective-permute-start(f32[9,32,256]{2,1,0:T(8,128)S(1)} %pad_maximum_fusion.2), channel_id=1, source_target_pairs={{0,2},{1,5},{2,0},{3,7},{4,6},{5,1},{6,4},{7,3},{8,10},{9,13},{10,... | collective-permute-start | bytes 884744 | tf_op jit(solution)/shard_map/ppermute | solution.py:100
  53.5 4.9 %collective-permute-done.7 = f32[9,32,256]{2,1,0:T(8,128)S(1)} collective-permute-done((f32[9,32,256]{2,1,0:T(8,128)S(1)}, f32[9,32,256]{2,1,0:T(8,128)S(1)}, u32[]{:S(2)}, u32[]{:S(2)}) %collective-permute-start.7) | collective-permute-done | bytes 294944 | tf_op jit(solution)/shard_map/ppermute | solution.py:100
  63.0 1.9 %collective-permute-start.9 = (f32[4,64,32]{1,2,0:T(8,128)S(1)}, f32[4,64,32]{1,2,0:T(8,128)S(1)}, u32[]{:S(2)}, u32[]{:S(2)}) collective-permute-start(f32[4,64,32]{1,2,0:T(8,128)S(1)} %fusion.2), channel_id=1, source_target_pairs={{0,16},{16,0},{1,17},{17,1},{2,18},{18,2},{3,19},{19,3},{4,20},{20... | collective-permute-start | bytes 98312 | tf_op jit(solution)/shard_map/ppermute | solution.py:21
  65.1 2.2 %collective-permute-done.9 = f32[4,64,32]{1,2,0:T(8,128)S(1)} collective-permute-done((f32[4,64,32]{1,2,0:T(8,128)S(1)}, f32[4,64,32]{1,2,0:T(8,128)S(1)}, u32[]{:S(2)}, u32[]{:S(2)}) %collective-permute-start.9) | collective-permute-done | bytes 32800 | tf_op jit(solution)/shard_map/ppermute | solution.py:21
  68.3 2.0 %collective-permute-done.10 = f32[9,32,512]{2,1,0:T(8,128)S(1)} collective-permute-done((f32[9,32,512]{2,1,0:T(8,128)S(1)}, f32[9,32,512]{2,1,0:T(8,128)S(1)}, u32[]{:S(2)}, u32[]{:S(2)}) %collective-permute-start.10) | collective-permute-done | bytes 589856 | tf_op jit(solution)/shard_map/ppermute | solution.py:94
  70.4 1.9 %collective-permute-start.11 = (f32[9,32,256]{2,1,0:T(8,128)S(1)}, f32[9,32,256]{2,1,0:T(8,128)S(1)}, u32[]{:S(2)}, u32[]{:S(2)}) collective-permute-start(f32[9,32,256]{2,1,0:T(8,128)S(1)} %constant_dynamic-slice_fusion.1), channel_id=1, source_target_pairs={{0,2},{1,5},{2,0},{3,7},{4,6},{5,1},{6,4},{7,3},{8,10},{9,13},{10,... | collective-permute-start | bytes 884744 | tf_op jit(solution)/shard_map/ppermute | solution.py:94
  72.4 4.9 %collective-permute-done.11 = f32[9,32,256]{2,1,0:T(8,128)S(1)} collective-permute-done((f32[9,32,256]{2,1,0:T(8,128)S(1)}, f32[9,32,256]{2,1,0:T(8,128)S(1)}, u32[]{:S(2)}, u32[]{:S(2)}) %collective-permute-start.11) | collective-permute-done | bytes 294944 | tf_op jit(solution)/shard_map/ppermute | solution.py:94
  77.3 2.1 %collective-permute-start.12 = (f32[9,32,128]{2,1,0:T(8,128)S(1)}, f32[9,32,128]{2,1,0:T(8,128)S(1)}, u32[]{:S(2)}, u32[]{:S(2)}) collective-permute-start(f32[9,32,128]{2,1,0:T(8,128)S(1)} %constant_dynamic-slice_fusion), channel_id=1, source_target_pairs={{0,4},{1,3},{2,6},{3,1},{4,0},{5,7},{6,2},{7,5},{8,12},{9,11},{10,... | collective-permute-start | bytes 442376 | tf_op jit(solution)/shard_map/ppermute | solution.py:94
  79.4 3.1 %collective-permute-done.12 = f32[9,32,128]{2,1,0:T(8,128)S(1)} collective-permute-done((f32[9,32,128]{2,1,0:T(8,128)S(1)}, f32[9,32,128]{2,1,0:T(8,128)S(1)}, u32[]{:S(2)}, u32[]{:S(2)}) %collective-permute-start.12) | collective-permute-done | bytes 147488 | tf_op jit(solution)/shard_map/ppermute | solution.py:94
  82.6 3.5 %collective-permute-start.13 = (f32[9,32,128]{2,1,0:T(8,128)S(1)}, f32[9,32,128]{2,1,0:T(8,128)S(1)}, u32[]{:S(2)}, u32[]{:S(2)}) collective-permute-start(f32[9,32,128]{2,1,0:T(8,128)S(1)} %dynamic-slice_add_fusion.4), channel_id=1, source_target_pairs={{0,8},{1,17},{2,10},{3,19},{4,12},{5,21},{6,14},{7,23},{8,0},{9,25... | collective-permute-start | bytes 442376 | tf_op jit(solution)/shard_map/ppermute | solution.py:97
  86.0 6.4 %collective-permute-done.13 = f32[9,32,128]{2,1,0:T(8,128)S(1)} collective-permute-done((f32[9,32,128]{2,1,0:T(8,128)S(1)}, f32[9,32,128]{2,1,0:T(8,128)S(1)}, u32[]{:S(2)}, u32[]{:S(2)}) %collective-permute-start.13) | collective-permute-done | bytes 147488 | tf_op jit(solution)/shard_map/ppermute | solution.py:97
  92.5 1.6 %collective-permute-start.14 = (f32[9,32,128]{2,1,0:T(8,128)S(1)}, f32[9,32,128]{2,1,0:T(8,128)S(1)}, u32[]{:S(2)}, u32[]{:S(2)}) collective-permute-start(f32[9,32,128]{2,1,0:T(8,128)S(1)} %add.186), channel_id=1, source_target_pairs={{0,16},{1,9},{2,18},{3,11},{4,20},{5,13},{6,22},{7,15},{8,24},{9,1... | collective-permute-start | bytes 442376 | tf_op jit(solution)/shard_map/ppermute | solution.py:97
  94.0 3.7 %collective-permute-done.14 = f32[9,32,128]{2,1,0:T(8,128)S(1)} collective-permute-done((f32[9,32,128]{2,1,0:T(8,128)S(1)}, f32[9,32,128]{2,1,0:T(8,128)S(1)}, u32[]{:S(2)}, u32[]{:S(2)}) %collective-permute-start.14) | collective-permute-done | bytes 147488 | tf_op jit(solution)/shard_map/ppermute | solution.py:97
  97.7 2.4 %collective-permute-start.15 = (f32[9,32,128]{2,1,0:T(8,128)S(1)}, f32[9,32,128]{2,1,0:T(8,128)S(1)}, u32[]{:S(2)}, u32[]{:S(2)}) collective-permute-start(f32[9,32,128]{2,1,0:T(8,128)S(1)} %add.187), channel_id=1, source_target_pairs={{0,4},{1,3},{2,6},{3,1},{4,0},{5,7},{6,2},{7,5},{8,12},{9,11},{10,... | collective-permute-start | bytes 442376 | tf_op jit(solution)/shard_map/ppermute | solution.py:100
  100.1 4.7 %collective-permute-done.15 = f32[9,32,128]{2,1,0:T(8,128)S(1)} collective-permute-done((f32[9,32,128]{2,1,0:T(8,128)S(1)}, f32[9,32,128]{2,1,0:T(8,128)S(1)}, u32[]{:S(2)}, u32[]{:S(2)}) %collective-permute-start.15) | collective-permute-done | bytes 147488 | tf_op jit(solution)/shard_map/ppermute | solution.py:100
  104.9 1.5 %collective-permute-start.16 = (f32[9,32,256]{2,1,0:T(8,128)S(1)}, f32[9,32,256]{2,1,0:T(8,128)S(1)}, u32[]{:S(2)}, u32[]{:S(2)}) collective-permute-start(f32[9,32,256]{2,1,0:T(8,128)S(1)} %pad_maximum_fusion.3), channel_id=1, source_target_pairs={{0,2},{1,5},{2,0},{3,7},{4,6},{5,1},{6,4},{7,3},{8,10},{9,13},{10,... | collective-permute-start | bytes 884744 | tf_op jit(solution)/shard_map/ppermute | solution.py:100
  106.6 5.1 %collective-permute-done.16 = f32[9,32,256]{2,1,0:T(8,128)S(1)} collective-permute-done((f32[9,32,256]{2,1,0:T(8,128)S(1)}, f32[9,32,256]{2,1,0:T(8,128)S(1)}, u32[]{:S(2)}, u32[]{:S(2)}) %collective-permute-start.16) | collective-permute-done | bytes 294944 | tf_op jit(solution)/shard_map/ppermute | solution.py:100
  113.9 2.2 %multiply_add_fusion = (f32[4,64,1024]{2,1,0:T(8,128)}, f32[1,4,64,1024]{3,2,1,0:T(8,128)}) fusion(f32[4,64,1024]{2,1,0:T(8,128)S(1)} %copy-done.3, f32[4]{0:T(128)S(1)} %convolution_bitcast_fusion, f32[1,4,64,1024]{3,2,1,0:T(8,128)S(1)} %copy-done.1, bf16[1,4,64,1024]{3,2,1,0:T(8,128)(2,1)S(1)} %copy-done.2, f32[4,64,32]{1,2,0:T(8,128)S(1)} %fusion.57, ...), kind=kOutput, calls=%fused_computation.12 | convolution fusion | flops 52166656 | bytes 5275664 | tf_op jit(solution)/shard_map/tks,tsd->tkd/dot_general | solution.py:153
  (90 shorter events, 14.4 us)
Async XLA Ops:
  0.6 105.7 %copy-start = (f32[4]{0:T(128)S(1)}, f32[4]{0:T(128)}, u32[]{:S(2)}) copy-start(f32[4]{0:T(128)} %param.15) | copy-start | bytes 52
  0.6 5.1 %copy-start.1 = (f32[1,4,64,1024]{3,2,1,0:T(8,128)S(1)}, f32[1,4,64,1024]{3,2,1,0:T(8,128)}, u32[]{:S(2)}) copy-start(f32[1,4,64,1024]{3,2,1,0:T(8,128)} %param.11) | copy-start | bytes 3145732
  5.8 1.8 %copy-start.5 = (f32[1,5,1024]{2,0,1:T(1,128)S(1)}, f32[1,5,1024]{2,0,1:T(1,128)}, u32[]{:S(2)}) copy-start(f32[1,5,1024]{2,0,1:T(1,128)} %param.18) | copy-start | bytes 61444
  5.8 4.9 %copy-start.4 = (f32[3,9,32,32]{3,2,1,0:T(8,128)S(1)}, f32[3,9,32,32]{3,2,1,0:T(8,128)}, u32[]{:S(2)}) copy-start(f32[3,9,32,32]{3,2,1,0:T(8,128)} %param.17) | copy-start | bytes 331780
  7.5 5.8 %copy-start.2 = (bf16[1,4,64,1024]{3,2,1,0:T(8,128)(2,1)S(1)}, bf16[1,4,64,1024]{3,2,1,0:T(8,128)(2,1)}, u32[]{:S(2)}) copy-start(bf16[1,4,64,1024]{3,2,1,0:T(8,128)(2,1)} %param.10) | copy-start | bytes 1572868
  7.7 5.1 %collective-permute-start = (f32[13312]{0:T(1024)S(1)}, f32[13312]{0:T(1024)S(1)}, u32[]{:S(2)}, u32[]{:S(2)}) collective-permute-start(f32[13312]{0:T(1024)S(1)} %pad_maximum_fusion.8), channel_id=1, source_target_pairs={{0,16},{16,0},{1,17},{17,1},{2,18},{18,2},{3,19},{19,3},{4,20},{20... | collective-permute-start | bytes 159752 | tf_op jit(solution)/shard_map/ppermute | solution.py:21
  14.0 2.2 %collective-permute-start.1 = (f32[9,32,512]{2,1,0:T(8,128)S(1)}, f32[9,32,512]{2,1,0:T(8,128)}, u32[]{:S(2)}, u32[]{:S(2)}) collective-permute-start(f32[9,32,512]{2,1,0:T(8,128)S(1)} %constant_dynamic-slice_fusion.17), channel_id=1, source_target_pairs={{0,1},{1,0},{2,3},{3,2},{4,5},{5,4},{6,7},{7,6},{8,9},{9,8},{10,11... | collective-permute-start | bytes 1769480 | tf_op jit(solution)/shard_map/ppermute | solution.py:94
  17.5 6.8 %collective-permute-start.2 = (f32[9,32,256]{2,1,0:T(8,128)S(1)}, f32[9,32,256]{2,1,0:T(8,128)S(1)}, u32[]{:S(2)}, u32[]{:S(2)}) collective-permute-start(f32[9,32,256]{2,1,0:T(8,128)S(1)} %constant_dynamic-slice_fusion.16), channel_id=1, source_target_pairs={{0,2},{1,5},{2,0},{3,7},{4,6},{5,1},{6,4},{7,3},{8,10},{9,13},{10,... | collective-permute-start | bytes 884744 | tf_op jit(solution)/shard_map/ppermute | solution.py:94
  24.4 5.3 %collective-permute-start.3 = (f32[9,32,128]{2,1,0:T(8,128)S(1)}, f32[9,32,128]{2,1,0:T(8,128)S(1)}, u32[]{:S(2)}, u32[]{:S(2)}) collective-permute-start(f32[9,32,128]{2,1,0:T(8,128)S(1)} %constant_dynamic-slice_fusion.15), channel_id=1, source_target_pairs={{0,4},{1,3},{2,6},{3,1},{4,0},{5,7},{6,2},{7,5},{8,12},{9,11},{10,... | collective-permute-start | bytes 442376 | tf_op jit(solution)/shard_map/ppermute | solution.py:94
  29.6 9.5 %collective-permute-start.4 = (f32[9,32,128]{2,1,0:T(8,128)S(1)}, f32[9,32,128]{2,1,0:T(8,128)S(1)}, u32[]{:S(2)}, u32[]{:S(2)}) collective-permute-start(f32[9,32,128]{2,1,0:T(8,128)S(1)} %dynamic-slice_add_fusion.5), channel_id=1, source_target_pairs={{0,8},{1,17},{2,10},{3,19},{4,12},{5,21},{6,14},{7,23},{8,0},{9,25... | collective-permute-start | bytes 442376 | tf_op jit(solution)/shard_map/ppermute | solution.py:97
  39.2 5.3 %collective-permute-start.5 = (f32[9,32,128]{2,1,0:T(8,128)S(1)}, f32[9,32,128]{2,1,0:T(8,128)S(1)}, u32[]{:S(2)}, u32[]{:S(2)}) collective-permute-start(f32[9,32,128]{2,1,0:T(8,128)S(1)} %add.177), channel_id=1, source_target_pairs={{0,16},{1,9},{2,18},{3,11},{4,20},{5,13},{6,22},{7,15},{8,24},{9,1... | collective-permute-start | bytes 442376 | tf_op jit(solution)/shard_map/ppermute | solution.py:97
  44.6 7.0 %collective-permute-start.6 = (f32[9,32,128]{2,1,0:T(8,128)S(1)}, f32[9,32,128]{2,1,0:T(8,128)S(1)}, u32[]{:S(2)}, u32[]{:S(2)}) collective-permute-start(f32[9,32,128]{2,1,0:T(8,128)S(1)} %add.178), channel_id=1, source_target_pairs={{0,4},{1,3},{2,6},{3,1},{4,0},{5,7},{6,2},{7,5},{8,12},{9,11},{10,... | collective-permute-start | bytes 442376 | tf_op jit(solution)/shard_map/ppermute | solution.py:100
  51.6 6.8 %collective-permute-start.7 = (f32[9,32,256]{2,1,0:T(8,128)S(1)}, f32[9,32,256]{2,1,0:T(8,128)S(1)}, u32[]{:S(2)}, u32[]{:S(2)}) collective-permute-start(f32[9,32,256]{2,1,0:T(8,128)S(1)} %pad_maximum_fusion.2), channel_id=1, source_target_pairs={{0,2},{1,5},{2,0},{3,7},{4,6},{5,1},{6,4},{7,3},{8,10},{9,13},{10,... | collective-permute-start | bytes 884744 | tf_op jit(solution)/shard_map/ppermute | solution.py:100
  58.5 2.2 %collective-permute-start.8 = (f32[9,32,512]{2,1,0:T(8,128)S(1)}, f32[9,32,512]{2,1,0:T(8,128)}, u32[]{:S(2)}, u32[]{:S(2)}) collective-permute-start(f32[9,32,512]{2,1,0:T(8,128)S(1)} %pad_maximum_fusion), channel_id=1, source_target_pairs={{0,1},{1,0},{2,3},{3,2},{4,5},{5,4},{6,7},{7,6},{8,9},{9,8},{10,11... | collective-permute-start | bytes 1769480 | tf_op jit(solution)/shard_map/ppermute | solution.py:100
  63.0 4.3 %collective-permute-start.9 = (f32[4,64,32]{1,2,0:T(8,128)S(1)}, f32[4,64,32]{1,2,0:T(8,128)S(1)}, u32[]{:S(2)}, u32[]{:S(2)}) collective-permute-start(f32[4,64,32]{1,2,0:T(8,128)S(1)} %fusion.2), channel_id=1, source_target_pairs={{0,16},{16,0},{1,17},{17,1},{2,18},{18,2},{3,19},{19,3},{4,20},{20... | collective-permute-start | bytes 98312 | tf_op jit(solution)/shard_map/ppermute | solution.py:21
  68.2 2.1 %collective-permute-start.10 = (f32[9,32,512]{2,1,0:T(8,128)S(1)}, f32[9,32,512]{2,1,0:T(8,128)S(1)}, u32[]{:S(2)}, u32[]{:S(2)}) collective-permute-start(f32[9,32,512]{2,1,0:T(8,128)S(1)} %constant_dynamic-slice_fusion.2), channel_id=1, source_target_pairs={{0,1},{1,0},{2,3},{3,2},{4,5},{5,4},{6,7},{7,6},{8,9},{9,8},{10,11... | collective-permute-start | bytes 1769480 | tf_op jit(solution)/shard_map/ppermute | solution.py:94
  70.4 6.8 %collective-permute-start.11 = (f32[9,32,256]{2,1,0:T(8,128)S(1)}, f32[9,32,256]{2,1,0:T(8,128)S(1)}, u32[]{:S(2)}, u32[]{:S(2)}) collective-permute-start(f32[9,32,256]{2,1,0:T(8,128)S(1)} %constant_dynamic-slice_fusion.1), channel_id=1, source_target_pairs={{0,2},{1,5},{2,0},{3,7},{4,6},{5,1},{6,4},{7,3},{8,10},{9,13},{10,... | collective-permute-start | bytes 884744 | tf_op jit(solution)/shard_map/ppermute | solution.py:94
  77.3 29.1 %copy-start.7 = (s32[9]{0:T(128)S(1)}, s32[9]{0:T(128)}, u32[]{:S(2)}) copy-start(s32[9]{0:T(128)} %param.14) | copy-start | bytes 112
  77.3 5.2 %collective-permute-start.12 = (f32[9,32,128]{2,1,0:T(8,128)S(1)}, f32[9,32,128]{2,1,0:T(8,128)S(1)}, u32[]{:S(2)}, u32[]{:S(2)}) collective-permute-start(f32[9,32,128]{2,1,0:T(8,128)S(1)} %constant_dynamic-slice_fusion), channel_id=1, source_target_pairs={{0,4},{1,3},{2,6},{3,1},{4,0},{5,7},{6,2},{7,5},{8,12},{9,11},{10,... | collective-permute-start | bytes 442376 | tf_op jit(solution)/shard_map/ppermute | solution.py:94
  82.6 9.9 %collective-permute-start.13 = (f32[9,32,128]{2,1,0:T(8,128)S(1)}, f32[9,32,128]{2,1,0:T(8,128)S(1)}, u32[]{:S(2)}, u32[]{:S(2)}) collective-permute-start(f32[9,32,128]{2,1,0:T(8,128)S(1)} %dynamic-slice_add_fusion.4), channel_id=1, source_target_pairs={{0,8},{1,17},{2,10},{3,19},{4,12},{5,21},{6,14},{7,23},{8,0},{9,25... | collective-permute-start | bytes 442376 | tf_op jit(solution)/shard_map/ppermute | solution.py:97
  92.5 5.2 %collective-permute-start.14 = (f32[9,32,128]{2,1,0:T(8,128)S(1)}, f32[9,32,128]{2,1,0:T(8,128)S(1)}, u32[]{:S(2)}, u32[]{:S(2)}) collective-permute-start(f32[9,32,128]{2,1,0:T(8,128)S(1)} %add.186), channel_id=1, source_target_pairs={{0,16},{1,9},{2,18},{3,11},{4,20},{5,13},{6,22},{7,15},{8,24},{9,1... | collective-permute-start | bytes 442376 | tf_op jit(solution)/shard_map/ppermute | solution.py:97
  97.7 7.1 %collective-permute-start.15 = (f32[9,32,128]{2,1,0:T(8,128)S(1)}, f32[9,32,128]{2,1,0:T(8,128)S(1)}, u32[]{:S(2)}, u32[]{:S(2)}) collective-permute-start(f32[9,32,128]{2,1,0:T(8,128)S(1)} %add.187), channel_id=1, source_target_pairs={{0,4},{1,3},{2,6},{3,1},{4,0},{5,7},{6,2},{7,5},{8,12},{9,11},{10,... | collective-permute-start | bytes 442376 | tf_op jit(solution)/shard_map/ppermute | solution.py:100
  104.9 6.8 %collective-permute-start.16 = (f32[9,32,256]{2,1,0:T(8,128)S(1)}, f32[9,32,256]{2,1,0:T(8,128)S(1)}, u32[]{:S(2)}, u32[]{:S(2)}) collective-permute-start(f32[9,32,256]{2,1,0:T(8,128)S(1)} %pad_maximum_fusion.3), channel_id=1, source_target_pairs={{0,2},{1,5},{2,0},{3,7},{4,6},{5,1},{6,4},{7,3},{8,10},{9,13},{10,... | collective-permute-start | bytes 884744 | tf_op jit(solution)/shard_map/ppermute | solution.py:100
  106.6 5.3 %copy-start.8 = (s32[4]{0:T(128)S(1)}, s32[4]{0:T(128)}, u32[]{:S(2)}) copy-start(s32[4]{0:T(128)} %param.13) | copy-start | bytes 52
  106.6 5.5 %copy-start.6 = (f32[5,1024]{1,0:T(8,128)S(1)}, f32[5,1024]{1,0:T(8,128)}, u32[]{:S(2)}) copy-start(f32[5,1024]{1,0:T(8,128)} %param.19) | copy-start | bytes 61444
  111.8 2.1 %collective-permute-start.17 = (f32[9,32,512]{2,1,0:T(8,128)S(1)}, f32[9,32,512]{2,1,0:T(8,128)S(1)}, u32[]{:S(2)}, u32[]{:S(2)}) collective-permute-start(f32[9,32,512]{2,1,0:T(8,128)S(1)} %pad_maximum_fusion.1), channel_id=1, source_target_pairs={{0,1},{1,0},{2,3},{3,2},{4,5},{5,4},{6,7},{7,6},{8,9},{9,8},{10,11... | collective-permute-start | bytes 1769480 | tf_op jit(solution)/shard_map/ppermute | solution.py:100
  112.7 1.2 %copy-start.3 = (f32[4,64,1024]{2,1,0:T(8,128)S(1)}, f32[4,64,1024]{2,1,0:T(8,128)}, u32[]{:S(2)}) copy-start(f32[4,64,1024]{2,1,0:T(8,128)} %param.12) | copy-start | bytes 3145732

commit v13 on v12

--- a/solution.py
+++ b/solution.py
@@ -137,28 +137,31 @@
     first_left = carried[:left_size].reshape(first_local.shape) / replicas
     vector_summed = carried[left_size:].reshape(vector_grad.shape[1:])
     mix_first = _pick_rows(inverse_gram_factors[0], tile_rows)
+    mix_right = _pick_rows(inverse_gram_factors[1], tile_rows)
+    mix_second = _pick_rows(inverse_gram_factors[2], tile_rows)
+    new_vector_momentum = 0.9 * vector_momentum + vector_summed / replicas
+    group_select = (
+        matrix_group[:, None] == jnp.arange(group_scale.shape[0], dtype=jnp.int32)[None, :]
+    ).astype(jnp.float32)
+    matrix_scale = jnp.dot(group_select, group_scale, precision=TOP_PRECISION)
+    tile_scale = jnp.dot(selector, matrix_scale, precision=TOP_PRECISION)
+    first_left, mix_right, mix_second, new_vector_momentum, tile_scale = lax.optimization_barrier(
+        (first_left, mix_right, mix_second, new_vector_momentum, tile_scale)
+    )
     first_ortho = jnp.einsum("tks,tsa->tka", first_left, mix_first, precision=TOP_PRECISION)
     first_parts = jnp.einsum("tkd,tks->tsd", combined, first_ortho, precision=WIDE_PRECISION)
     first_table = _scatter_rows(first_parts, tile_rows, matrix_count)
     first_rows = table_rows(first_table, tile_rows, replicas, n_own) / replicas
-    mix_right = _pick_rows(inverse_gram_factors[1], tile_rows)
     right_rows = jnp.einsum("tjw,tjd->twd", mix_right, first_rows, precision=TOP_PRECISION)
     second_local = jnp.einsum("tkd,tsd->tks", combined, right_rows, precision=WIDE_PRECISION)
     second_left = swap_sum(second_local, "rep") / replicas
-    mix_second = _pick_rows(inverse_gram_factors[2], tile_rows)
     second_ortho = jnp.einsum("tks,tsa->tka", second_left, mix_second, precision=TOP_PRECISION)
     second_parts = jnp.einsum("tkd,tks->tsd", combined, second_ortho, precision=WIDE_PRECISION)
     second_table = _scatter_rows(second_parts, tile_rows, matrix_count)
     back_rows = table_rows(second_table, tile_rows, replicas, n_own) / replicas
     approximation = jnp.einsum("tks,tsd->tkd", second_ortho, back_rows, precision=WIDE_PRECISION)
     new_feedback = (combined - approximation)[None]
-    group_select = (
-        matrix_group[:, None] == jnp.arange(group_scale.shape[0], dtype=jnp.int32)[None, :]
-    ).astype(jnp.float32)
-    matrix_scale = jnp.dot(group_select, group_scale, precision=TOP_PRECISION)
-    tile_scale = jnp.dot(selector, matrix_scale, precision=TOP_PRECISION)
     new_momentum = 0.9 * momentum + tile_scale[:, None, None] * approximation
-    new_vector_momentum = 0.9 * vector_momentum + vector_summed / replicas
     return (new_feedback, new_momentum, new_vector_momentum)
 
 

time: 117 us -> 117 us (level)
  waiting for transfers between devices: 64.8 us -> 67 us
  local copies, waits for them, and re-layouts: 4.61 us -> 2.91 us
    ppermute x6, waiting for transfers between devices: 21.8 us -> 23.5 us  [table_rows(): other = lax.ppermute(cur, axes, perm_of(p0, p1))]
    dynamic_slice x10 -> x5, local copies, waits for them, and re-layouts: 3.22 us -> 2.17 us  [_pick_rows(): lax.dynamic_index_in_dim(table, r, 0, keepdims=False)]
  transfers between devices with their start and end apart: 18 -> 18, of which waited for: 18 -> 18; matrix products, arithmetic and copies ran while one was open for 2% -> 0% of each run, Pallas kernels for 0% -> 0%
where the time goes in v13:
time: 117 us
  waiting for transfers between devices  67 us (57%)
  starting transfers between devices  31.9 us (27%)
  matrix products  6.88 us (6%)
  other arithmetic  4.16 us (4%)
  between operations  3.82 us (3%)
  local copies, waits for them, and re-layouts  2.91 us (2%)
    ppermute x6, waiting for transfers between devices, table_rows(): other = lax.ppermute(cur, axes, perm_of(p0, p1))  23.5 us
    ppermute x6, waiting for transfers between devices, table_rows(): cur = keep + lax.ppermute(send, axes, perm_of(p0, p1))  19.9 us
    ppermute x4, waiting for transfers between devices, table_rows(): cur = cur + lax.ppermute(cur, axes, perm_of(p0, p1))  19.6 us
    ppermute x4, starting transfers between devices, table_rows(): cur = cur + lax.ppermute(cur, axes, perm_of(p0, p1))  10.3 us
    ppermute x6, starting transfers between devices, table_rows(): cur = keep + lax.ppermute(send, axes, perm_of(p0, p1))  8.37 us
    ppermute x6, starting transfers between devices, table_rows(): other = lax.ppermute(cur, axes, perm_of(p0, p1))  8.35 us
    ppermute x2, starting transfers between devices, swap_sum(): x = x + lax.ppermute(x, axis, _pair_perm(n, j))  4.91 us
    ppermute x2, waiting for transfers between devices, swap_sum(): x = x + lax.ppermute(x, axis, _pair_perm(n, j))  4.02 us
  transfers between devices with their start and end apart: 18, of which 18 were waited for; matrix products, arithmetic and copies ran while one was open for 0% of the time, Pallas kernels for 0%

profile of v13, /device:TPU:0, one launch (start us, length us, event | category | flops | bytes accessed | tf_op | source)
XLA Modules:
  0.0 116.7 jit_solution(4050758728348877938)
XLA Ops:
  5.8 1.7 %fusion.6 = f32[4,64,32]{2,1,0:T(8,128)S(1)} fusion(f32[1,1024,32]{1,2,0:T(8,128)S(1)} %get-tuple-element.15, f32[1,1024,32]{1,2,0:T(8,128)S(1)} %get-tuple-element.16, f32[1,1024,32]{1,2,0:T(8,128)S(1)} %get-tuple-element.14, f32[1,1024,32]{1,2,0:T(8,128)S(1)} %get-tuple-element.13, f32[1,4,64,1024]{3,2,1,0:T(8,128)S(1)} %copy-done.1, ...), kind=kOutput, calls=%fused_computation.9 | convolution fusion | flops 51249152 | bytes 2129920 | tf_op jit(solution)/shard_map/tkd,tds->tks/dot_general | solution.py:133
  7.7 3.0 %collective-permute-start = (f32[13312]{0:T(1024)S(1)}, f32[13312]{0:T(1024)S(1)}, u32[]{:S(2)}, u32[]{:S(2)}) collective-permute-start(f32[13312]{0:T(1024)S(1)} %pad_maximum_fusion.10), channel_id=1, source_target_pairs={{0,16},{16,0},{1,17},{17,1},{2,18},{18,2},{3,19},{19,3},{4,20},{20... | collective-permute-start | bytes 159752 | tf_op jit(solution)/shard_map/ppermute | solution.py:21
  14.8 2.1 %collective-permute-done.1 = f32[9,32,512]{2,1,0:T(8,128)} collective-permute-done((f32[9,32,512]{2,1,0:T(8,128)S(1)}, f32[9,32,512]{2,1,0:T(8,128)}, u32[]{:S(2)}, u32[]{:S(2)}) %collective-permute-start.1) | collective-permute-done | bytes 589856 | tf_op jit(solution)/shard_map/ppermute | solution.py:94
  18.1 2.1 %collective-permute-start.2 = (f32[9,32,256]{2,1,0:T(8,128)S(1)}, f32[9,32,256]{2,1,0:T(8,128)S(1)}, u32[]{:S(2)}, u32[]{:S(2)}) collective-permute-start(f32[9,32,256]{2,1,0:T(8,128)S(1)} %constant_dynamic-slice_fusion.12), channel_id=1, source_target_pairs={{0,2},{1,5},{2,0},{3,7},{4,6},{5,1},{6,4},{7,3},{8,10},{9,13},{10,... | collective-permute-start | bytes 884744 | tf_op jit(solution)/shard_map/ppermute | solution.py:94
  20.2 4.7 %collective-permute-done.2 = f32[9,32,256]{2,1,0:T(8,128)S(1)} collective-permute-done((f32[9,32,256]{2,1,0:T(8,128)S(1)}, f32[9,32,256]{2,1,0:T(8,128)S(1)}, u32[]{:S(2)}, u32[]{:S(2)}) %collective-permute-start.2) | collective-permute-done | bytes 294944 | tf_op jit(solution)/shard_map/ppermute | solution.py:94
  25.0 2.1 %collective-permute-start.3 = (f32[9,32,128]{2,1,0:T(8,128)S(1)}, f32[9,32,128]{2,1,0:T(8,128)S(1)}, u32[]{:S(2)}, u32[]{:S(2)}) collective-permute-start(f32[9,32,128]{2,1,0:T(8,128)S(1)} %constant_dynamic-slice_fusion.11), channel_id=1, source_target_pairs={{0,4},{1,3},{2,6},{3,1},{4,0},{5,7},{6,2},{7,5},{8,12},{9,11},{10,... | collective-permute-start | bytes 442376 | tf_op jit(solution)/shard_map/ppermute | solution.py:94
  27.1 3.1 %collective-permute-done.3 = f32[9,32,128]{2,1,0:T(8,128)S(1)} collective-permute-done((f32[9,32,128]{2,1,0:T(8,128)S(1)}, f32[9,32,128]{2,1,0:T(8,128)S(1)}, u32[]{:S(2)}, u32[]{:S(2)}) %collective-permute-start.3) | collective-permute-done | bytes 147488 | tf_op jit(solution)/shard_map/ppermute | solution.py:94
  30.3 3.1 %collective-permute-start.4 = (f32[9,32,128]{2,1,0:T(8,128)S(1)}, f32[9,32,128]{2,1,0:T(8,128)S(1)}, u32[]{:S(2)}, u32[]{:S(2)}) collective-permute-start(f32[9,32,128]{2,1,0:T(8,128)S(1)} %dynamic-slice_add_fusion.5), channel_id=1, source_target_pairs={{0,8},{1,17},{2,10},{3,19},{4,12},{5,21},{6,14},{7,23},{8,0},{9,25... | collective-permute-start | bytes 442376 | tf_op jit(solution)/shard_map/ppermute | solution.py:97
  33.4 6.4 %collective-permute-done.4 = f32[9,32,128]{2,1,0:T(8,128)S(1)} collective-permute-done((f32[9,32,128]{2,1,0:T(8,128)S(1)}, f32[9,32,128]{2,1,0:T(8,128)S(1)}, u32[]{:S(2)}, u32[]{:S(2)}) %collective-permute-start.4) | collective-permute-done | bytes 147488 | tf_op jit(solution)/shard_map/ppermute | solution.py:97
  39.8 2.2 %collective-permute-start.5 = (f32[9,32,128]{2,1,0:T(8,128)S(1)}, f32[9,32,128]{2,1,0:T(8,128)S(1)}, u32[]{:S(2)}, u32[]{:S(2)}) collective-permute-start(f32[9,32,128]{2,1,0:T(8,128)S(1)} %add.178), channel_id=1, source_target_pairs={{0,16},{1,9},{2,18},{3,11},{4,20},{5,13},{6,22},{7,15},{8,24},{9,1... | collective-permute-start | bytes 442376 | tf_op jit(solution)/shard_map/ppermute | solution.py:97
  42.0 3.1 %collective-permute-done.5 = f32[9,32,128]{2,1,0:T(8,128)S(1)} collective-permute-done((f32[9,32,128]{2,1,0:T(8,128)S(1)}, f32[9,32,128]{2,1,0:T(8,128)S(1)}, u32[]{:S(2)}, u32[]{:S(2)}) %collective-permute-start.5) | collective-permute-done | bytes 147488 | tf_op jit(solution)/shard_map/ppermute | solution.py:97
  45.2 2.3 %collective-permute-start.6 = (f32[9,32,128]{2,1,0:T(8,128)S(1)}, f32[9,32,128]{2,1,0:T(8,128)S(1)}, u32[]{:S(2)}, u32[]{:S(2)}) collective-permute-start(f32[9,32,128]{2,1,0:T(8,128)S(1)} %add.179), channel_id=1, source_target_pairs={{0,4},{1,3},{2,6},{3,1},{4,0},{5,7},{6,2},{7,5},{8,12},{9,11},{10,... | collective-permute-start | bytes 442376 | tf_op jit(solution)/shard_map/ppermute | solution.py:100
  47.5 4.7 %collective-permute-done.6 = f32[9,32,128]{2,1,0:T(8,128)S(1)} collective-permute-done((f32[9,32,128]{2,1,0:T(8,128)S(1)}, f32[9,32,128]{2,1,0:T(8,128)S(1)}, u32[]{:S(2)}, u32[]{:S(2)}) %collective-permute-start.6) | collective-permute-done | bytes 147488 | tf_op jit(solution)/shard_map/ppermute | solution.py:100
  52.2 1.9 %collective-permute-start.7 = (f32[9,32,256]{2,1,0:T(8,128)S(1)}, f32[9,32,256]{2,1,0:T(8,128)S(1)}, u32[]{:S(2)}, u32[]{:S(2)}) collective-permute-start(f32[9,32,256]{2,1,0:T(8,128)S(1)} %pad_maximum_fusion.2), channel_id=1, source_target_pairs={{0,2},{1,5},{2,0},{3,7},{4,6},{5,1},{6,4},{7,3},{8,10},{9,13},{10,... | collective-permute-start | bytes 884744 | tf_op jit(solution)/shard_map/ppermute | solution.py:100
  54.2 4.9 %collective-permute-done.7 = f32[9,32,256]{2,1,0:T(8,128)S(1)} collective-permute-done((f32[9,32,256]{2,1,0:T(8,128)S(1)}, f32[9,32,256]{2,1,0:T(8,128)S(1)}, u32[]{:S(2)}, u32[]{:S(2)}) %collective-permute-start.7) | collective-permute-done | bytes 294944 | tf_op jit(solution)/shard_map/ppermute | solution.py:100
  59.3 2.1 %collective-permute-done.8 = f32[9,32,512]{2,1,0:T(8,128)} collective-permute-done((f32[9,32,512]{2,1,0:T(8,128)S(1)}, f32[9,32,512]{2,1,0:T(8,128)}, u32[]{:S(2)}, u32[]{:S(2)}) %collective-permute-start.8) | collective-permute-done | bytes 589856 | tf_op jit(solution)/shard_map/ppermute | solution.py:100
  63.6 1.9 %collective-permute-start.9 = (f32[4,64,32]{1,2,0:T(8,128)S(1)}, f32[4,64,32]{1,2,0:T(8,128)S(1)}, u32[]{:S(2)}, u32[]{:S(2)}) collective-permute-start(f32[4,64,32]{1,2,0:T(8,128)S(1)} %fusion.2), channel_id=1, source_target_pairs={{0,16},{16,0},{1,17},{17,1},{2,18},{18,2},{3,19},{19,3},{4,20},{20... | collective-permute-start | bytes 98312 | tf_op jit(solution)/shard_map/ppermute | solution.py:21
  65.5 2.4 %collective-permute-done.9 = f32[4,64,32]{1,2,0:T(8,128)S(1)} collective-permute-done((f32[4,64,32]{1,2,0:T(8,128)S(1)}, f32[4,64,32]{1,2,0:T(8,128)S(1)}, u32[]{:S(2)}, u32[]{:S(2)}) %collective-permute-start.9) | collective-permute-done | bytes 32800 | tf_op jit(solution)/shard_map/ppermute | solution.py:21
  69.0 2.0 %collective-permute-done.10 = f32[9,32,512]{2,1,0:T(8,128)S(1)} collective-permute-done((f32[9,32,512]{2,1,0:T(8,128)S(1)}, f32[9,32,512]{2,1,0:T(8,128)S(1)}, u32[]{:S(2)}, u32[]{:S(2)}) %collective-permute-start.10) | collective-permute-done | bytes 589856 | tf_op jit(solution)/shard_map/ppermute | solution.py:94
  71.2 1.9 %collective-permute-start.11 = (f32[9,32,256]{2,1,0:T(8,128)S(1)}, f32[9,32,256]{2,1,0:T(8,128)S(1)}, u32[]{:S(2)}, u32[]{:S(2)}) collective-permute-start(f32[9,32,256]{2,1,0:T(8,128)S(1)} %constant_dynamic-slice_fusion.1), channel_id=1, source_target_pairs={{0,2},{1,5},{2,0},{3,7},{4,6},{5,1},{6,4},{7,3},{8,10},{9,13},{10,... | collective-permute-start | bytes 884744 | tf_op jit(solution)/shard_map/ppermute | solution.py:94
  73.1 4.9 %collective-permute-done.11 = f32[9,32,256]{2,1,0:T(8,128)S(1)} collective-permute-done((f32[9,32,256]{2,1,0:T(8,128)S(1)}, f32[9,32,256]{2,1,0:T(8,128)S(1)}, u32[]{:S(2)}, u32[]{:S(2)}) %collective-permute-start.11) | collective-permute-done | bytes 294944 | tf_op jit(solution)/shard_map/ppermute | solution.py:94
  78.0 2.1 %collective-permute-start.12 = (f32[9,32,128]{2,1,0:T(8,128)S(1)}, f32[9,32,128]{2,1,0:T(8,128)S(1)}, u32[]{:S(2)}, u32[]{:S(2)}) collective-permute-start(f32[9,32,128]{2,1,0:T(8,128)S(1)} %constant_dynamic-slice_fusion), channel_id=1, source_target_pairs={{0,4},{1,3},{2,6},{3,1},{4,0},{5,7},{6,2},{7,5},{8,12},{9,11},{10,... | collective-permute-start | bytes 442376 | tf_op jit(solution)/shard_map/ppermute | solution.py:94
  80.1 3.1 %collective-permute-done.12 = f32[9,32,128]{2,1,0:T(8,128)S(1)} collective-permute-done((f32[9,32,128]{2,1,0:T(8,128)S(1)}, f32[9,32,128]{2,1,0:T(8,128)S(1)}, u32[]{:S(2)}, u32[]{:S(2)}) %collective-permute-start.12) | collective-permute-done | bytes 147488 | tf_op jit(solution)/shard_map/ppermute | solution.py:94
  83.3 3.4 %collective-permute-start.13 = (f32[9,32,128]{2,1,0:T(8,128)S(1)}, f32[9,32,128]{2,1,0:T(8,128)S(1)}, u32[]{:S(2)}, u32[]{:S(2)}) collective-permute-start(f32[9,32,128]{2,1,0:T(8,128)S(1)} %dynamic-slice_add_fusion.4), channel_id=1, source_target_pairs={{0,8},{1,17},{2,10},{3,19},{4,12},{5,21},{6,14},{7,23},{8,0},{9,25... | collective-permute-start | bytes 442376 | tf_op jit(solution)/shard_map/ppermute | solution.py:97
  86.7 6.4 %collective-permute-done.13 = f32[9,32,128]{2,1,0:T(8,128)S(1)} collective-permute-done((f32[9,32,128]{2,1,0:T(8,128)S(1)}, f32[9,32,128]{2,1,0:T(8,128)S(1)}, u32[]{:S(2)}, u32[]{:S(2)}) %collective-permute-start.13) | collective-permute-done | bytes 147488 | tf_op jit(solution)/shard_map/ppermute | solution.py:97
  94.7 3.6 %collective-permute-done.14 = f32[9,32,128]{2,1,0:T(8,128)S(1)} collective-permute-done((f32[9,32,128]{2,1,0:T(8,128)S(1)}, f32[9,32,128]{2,1,0:T(8,128)S(1)}, u32[]{:S(2)}, u32[]{:S(2)}) %collective-permute-start.14) | collective-permute-done | bytes 147488 | tf_op jit(solution)/shard_map/ppermute | solution.py:97
  98.3 2.4 %collective-permute-start.15 = (f32[9,32,128]{2,1,0:T(8,128)S(1)}, f32[9,32,128]{2,1,0:T(8,128)S(1)}, u32[]{:S(2)}, u32[]{:S(2)}) collective-permute-start(f32[9,32,128]{2,1,0:T(8,128)S(1)} %add.188), channel_id=1, source_target_pairs={{0,4},{1,3},{2,6},{3,1},{4,0},{5,7},{6,2},{7,5},{8,12},{9,11},{10,... | collective-permute-start | bytes 442376 | tf_op jit(solution)/shard_map/ppermute | solution.py:100
  100.7 4.7 %collective-permute-done.15 = f32[9,32,128]{2,1,0:T(8,128)S(1)} collective-permute-done((f32[9,32,128]{2,1,0:T(8,128)S(1)}, f32[9,32,128]{2,1,0:T(8,128)S(1)}, u32[]{:S(2)}, u32[]{:S(2)}) %collective-permute-start.15) | collective-permute-done | bytes 147488 | tf_op jit(solution)/shard_map/ppermute | solution.py:100
  105.5 1.6 %collective-permute-start.16 = (f32[9,32,256]{2,1,0:T(8,128)S(1)}, f32[9,32,256]{2,1,0:T(8,128)S(1)}, u32[]{:S(2)}, u32[]{:S(2)}) collective-permute-start(f32[9,32,256]{2,1,0:T(8,128)S(1)} %pad_maximum_fusion.3), channel_id=1, source_target_pairs={{0,2},{1,5},{2,0},{3,7},{4,6},{5,1},{6,4},{7,3},{8,10},{9,13},{10,... | collective-permute-start | bytes 884744 | tf_op jit(solution)/shard_map/ppermute | solution.py:100
  107.1 5.2 %collective-permute-done.16 = f32[9,32,256]{2,1,0:T(8,128)S(1)} collective-permute-done((f32[9,32,256]{2,1,0:T(8,128)S(1)}, f32[9,32,256]{2,1,0:T(8,128)S(1)}, u32[]{:S(2)}, u32[]{:S(2)}) %collective-permute-start.16) | collective-permute-done | bytes 294944 | tf_op jit(solution)/shard_map/ppermute | solution.py:100
  112.5 2.0 %collective-permute-done.17 = f32[9,32,512]{2,1,0:T(8,128)S(1)} collective-permute-done((f32[9,32,512]{2,1,0:T(8,128)S(1)}, f32[9,32,512]{2,1,0:T(8,128)S(1)}, u32[]{:S(2)}, u32[]{:S(2)}) %collective-permute-start.17) | collective-permute-done | bytes 589856 | tf_op jit(solution)/shard_map/ppermute | solution.py:100
  114.6 2.1 %multiply_add_fusion = (f32[4,64,1024]{2,1,0:T(8,128)}, f32[1,4,64,1024]{3,2,1,0:T(8,128)}) fusion(f32[4,64,1024]{2,1,0:T(8,128)S(1)} %copy-done.3, f32[4]{0:T(128)S(1)} %convolution_bitcast_fusion, f32[1,4,64,1024]{3,2,1,0:T(8,128)S(1)} %copy-done.1, bf16[1,4,64,1024]{3,2,1,0:T(8,128)(2,1)S(1)} %copy-done.2, f32[4,64,32]{1,2,0:T(8,128)S(1)} %fusion.50, ...), kind=kOutput, calls=%fused_computation.12 | convolution fusion | flops 52166656 | bytes 5275664 | tf_op jit(solution)/shard_map/tks,tsd->tkd/dot_general | solution.py:162
  (87 shorter events, 13.5 us)
Async XLA Ops:
  0.6 10.2 %copy-start = (f32[4]{0:T(128)S(1)}, f32[4]{0:T(128)}, u32[]{:S(2)}) copy-start(f32[4]{0:T(128)} %param.15) | copy-start | bytes 52
  0.6 5.1 %copy-start.1 = (f32[1,4,64,1024]{3,2,1,0:T(8,128)S(1)}, f32[1,4,64,1024]{3,2,1,0:T(8,128)}, u32[]{:S(2)}) copy-start(f32[1,4,64,1024]{3,2,1,0:T(8,128)} %param.11) | copy-start | bytes 3145732
  5.8 1.8 %copy-start.5 = (f32[1,5,1024]{2,0,1:T(1,128)S(1)}, f32[1,5,1024]{2,0,1:T(1,128)}, u32[]{:S(2)}) copy-start(f32[1,5,1024]{2,0,1:T(1,128)} %param.18) | copy-start | bytes 61444
  5.8 4.9 %copy-start.4 = (f32[3,9,32,32]{3,2,1,0:T(8,128)S(1)}, f32[3,9,32,32]{3,2,1,0:T(8,128)}, u32[]{:S(2)}) copy-start(f32[3,9,32,32]{3,2,1,0:T(8,128)} %param.17) | copy-start | bytes 331780
  7.5 3.3 %copy-start.7 = (s32[9]{0:T(128)S(1)}, s32[9]{0:T(128)}, u32[]{:S(2)}) copy-start(s32[9]{0:T(128)} %param.14) | copy-start | bytes 112
  7.5 3.5 %copy-start.8 = (s32[4]{0:T(128)S(1)}, s32[4]{0:T(128)}, u32[]{:S(2)}) copy-start(s32[4]{0:T(128)} %param.13) | copy-start | bytes 52
  7.6 5.3 %copy-start.6 = (f32[5,1024]{1,0:T(8,128)S(1)}, f32[5,1024]{1,0:T(8,128)}, u32[]{:S(2)}) copy-start(f32[5,1024]{1,0:T(8,128)} %param.19) | copy-start | bytes 61444
  7.6 6.3 %copy-start.2 = (bf16[1,4,64,1024]{3,2,1,0:T(8,128)(2,1)S(1)}, bf16[1,4,64,1024]{3,2,1,0:T(8,128)(2,1)}, u32[]{:S(2)}) copy-start(bf16[1,4,64,1024]{3,2,1,0:T(8,128)(2,1)} %param.10) | copy-start | bytes 1572868
  7.7 5.1 %collective-permute-start = (f32[13312]{0:T(1024)S(1)}, f32[13312]{0:T(1024)S(1)}, u32[]{:S(2)}, u32[]{:S(2)}) collective-permute-start(f32[13312]{0:T(1024)S(1)} %pad_maximum_fusion.10), channel_id=1, source_target_pairs={{0,16},{16,0},{1,17},{17,1},{2,18},{18,2},{3,19},{19,3},{4,20},{20... | collective-permute-start | bytes 159752 | tf_op jit(solution)/shard_map/ppermute | solution.py:21
  14.7 2.2 %collective-permute-start.1 = (f32[9,32,512]{2,1,0:T(8,128)S(1)}, f32[9,32,512]{2,1,0:T(8,128)}, u32[]{:S(2)}, u32[]{:S(2)}) collective-permute-start(f32[9,32,512]{2,1,0:T(8,128)S(1)} %constant_dynamic-slice_fusion.13), channel_id=1, source_target_pairs={{0,1},{1,0},{2,3},{3,2},{4,5},{5,4},{6,7},{7,6},{8,9},{9,8},{10,11... | collective-permute-start | bytes 1769480 | tf_op jit(solution)/shard_map/ppermute | solution.py:94
  18.1 6.8 %collective-permute-start.2 = (f32[9,32,256]{2,1,0:T(8,128)S(1)}, f32[9,32,256]{2,1,0:T(8,128)S(1)}, u32[]{:S(2)}, u32[]{:S(2)}) collective-permute-start(f32[9,32,256]{2,1,0:T(8,128)S(1)} %constant_dynamic-slice_fusion.12), channel_id=1, source_target_pairs={{0,2},{1,5},{2,0},{3,7},{4,6},{5,1},{6,4},{7,3},{8,10},{9,13},{10,... | collective-permute-start | bytes 884744 | tf_op jit(solution)/shard_map/ppermute | solution.py:94
  25.0 5.3 %collective-permute-start.3 = (f32[9,32,128]{2,1,0:T(8,128)S(1)}, f32[9,32,128]{2,1,0:T(8,128)S(1)}, u32[]{:S(2)}, u32[]{:S(2)}) collective-permute-start(f32[9,32,128]{2,1,0:T(8,128)S(1)} %constant_dynamic-slice_fusion.11), channel_id=1, source_target_pairs={{0,4},{1,3},{2,6},{3,1},{4,0},{5,7},{6,2},{7,5},{8,12},{9,11},{10,... | collective-permute-start | bytes 442376 | tf_op jit(solution)/shard_map/ppermute | solution.py:94
  30.3 9.5 %collective-permute-start.4 = (f32[9,32,128]{2,1,0:T(8,128)S(1)}, f32[9,32,128]{2,1,0:T(8,128)S(1)}, u32[]{:S(2)}, u32[]{:S(2)}) collective-permute-start(f32[9,32,128]{2,1,0:T(8,128)S(1)} %dynamic-slice_add_fusion.5), channel_id=1, source_target_pairs={{0,8},{1,17},{2,10},{3,19},{4,12},{5,21},{6,14},{7,23},{8,0},{9,25... | collective-permute-start | bytes 442376 | tf_op jit(solution)/shard_map/ppermute | solution.py:97
  39.8 5.3 %collective-permute-start.5 = (f32[9,32,128]{2,1,0:T(8,128)S(1)}, f32[9,32,128]{2,1,0:T(8,128)S(1)}, u32[]{:S(2)}, u32[]{:S(2)}) collective-permute-start(f32[9,32,128]{2,1,0:T(8,128)S(1)} %add.178), channel_id=1, source_target_pairs={{0,16},{1,9},{2,18},{3,11},{4,20},{5,13},{6,22},{7,15},{8,24},{9,1... | collective-permute-start | bytes 442376 | tf_op jit(solution)/shard_map/ppermute | solution.py:97
  45.2 7.0 %collective-permute-start.6 = (f32[9,32,128]{2,1,0:T(8,128)S(1)}, f32[9,32,128]{2,1,0:T(8,128)S(1)}, u32[]{:S(2)}, u32[]{:S(2)}) collective-permute-start(f32[9,32,128]{2,1,0:T(8,128)S(1)} %add.179), channel_id=1, source_target_pairs={{0,4},{1,3},{2,6},{3,1},{4,0},{5,7},{6,2},{7,5},{8,12},{9,11},{10,... | collective-permute-start | bytes 442376 | tf_op jit(solution)/shard_map/ppermute | solution.py:100
  52.2 6.8 %collective-permute-start.7 = (f32[9,32,256]{2,1,0:T(8,128)S(1)}, f32[9,32,256]{2,1,0:T(8,128)S(1)}, u32[]{:S(2)}, u32[]{:S(2)}) collective-permute-start(f32[9,32,256]{2,1,0:T(8,128)S(1)} %pad_maximum_fusion.2), channel_id=1, source_target_pairs={{0,2},{1,5},{2,0},{3,7},{4,6},{5,1},{6,4},{7,3},{8,10},{9,13},{10,... | collective-permute-start | bytes 884744 | tf_op jit(solution)/shard_map/ppermute | solution.py:100
  59.2 2.2 %collective-permute-start.8 = (f32[9,32,512]{2,1,0:T(8,128)S(1)}, f32[9,32,512]{2,1,0:T(8,128)}, u32[]{:S(2)}, u32[]{:S(2)}) collective-permute-start(f32[9,32,512]{2,1,0:T(8,128)S(1)} %pad_maximum_fusion), channel_id=1, source_target_pairs={{0,1},{1,0},{2,3},{3,2},{4,5},{5,4},{6,7},{7,6},{8,9},{9,8},{10,11... | collective-permute-start | bytes 1769480 | tf_op jit(solution)/shard_map/ppermute | solution.py:100
  63.6 4.3 %collective-permute-start.9 = (f32[4,64,32]{1,2,0:T(8,128)S(1)}, f32[4,64,32]{1,2,0:T(8,128)S(1)}, u32[]{:S(2)}, u32[]{:S(2)}) collective-permute-start(f32[4,64,32]{1,2,0:T(8,128)S(1)} %fusion.2), channel_id=1, source_target_pairs={{0,16},{16,0},{1,17},{17,1},{2,18},{18,2},{3,19},{19,3},{4,20},{20... | collective-permute-start | bytes 98312 | tf_op jit(solution)/shard_map/ppermute | solution.py:21
  69.0 2.1 %collective-permute-start.10 = (f32[9,32,512]{2,1,0:T(8,128)S(1)}, f32[9,32,512]{2,1,0:T(8,128)S(1)}, u32[]{:S(2)}, u32[]{:S(2)}) collective-permute-start(f32[9,32,512]{2,1,0:T(8,128)S(1)} %constant_dynamic-slice_fusion.2), channel_id=1, source_target_pairs={{0,1},{1,0},{2,3},{3,2},{4,5},{5,4},{6,7},{7,6},{8,9},{9,8},{10,11... | collective-permute-start | bytes 1769480 | tf_op jit(solution)/shard_map/ppermute | solution.py:94
  71.2 6.8 %collective-permute-start.11 = (f32[9,32,256]{2,1,0:T(8,128)S(1)}, f32[9,32,256]{2,1,0:T(8,128)S(1)}, u32[]{:S(2)}, u32[]{:S(2)}) collective-permute-start(f32[9,32,256]{2,1,0:T(8,128)S(1)} %constant_dynamic-slice_fusion.1), channel_id=1, source_target_pairs={{0,2},{1,5},{2,0},{3,7},{4,6},{5,1},{6,4},{7,3},{8,10},{9,13},{10,... | collective-permute-start | bytes 884744 | tf_op jit(solution)/shard_map/ppermute | solution.py:94
  78.0 5.2 %collective-permute-start.12 = (f32[9,32,128]{2,1,0:T(8,128)S(1)}, f32[9,32,128]{2,1,0:T(8,128)S(1)}, u32[]{:S(2)}, u32[]{:S(2)}) collective-permute-start(f32[9,32,128]{2,1,0:T(8,128)S(1)} %constant_dynamic-slice_fusion), channel_id=1, source_target_pairs={{0,4},{1,3},{2,6},{3,1},{4,0},{5,7},{6,2},{7,5},{8,12},{9,11},{10,... | collective-permute-start | bytes 442376 | tf_op jit(solution)/shard_map/ppermute | solution.py:94
  83.3 9.8 %collective-permute-start.13 = (f32[9,32,128]{2,1,0:T(8,128)S(1)}, f32[9,32,128]{2,1,0:T(8,128)S(1)}, u32[]{:S(2)}, u32[]{:S(2)}) collective-permute-start(f32[9,32,128]{2,1,0:T(8,128)S(1)} %dynamic-slice_add_fusion.4), channel_id=1, source_target_pairs={{0,8},{1,17},{2,10},{3,19},{4,12},{5,21},{6,14},{7,23},{8,0},{9,25... | collective-permute-start | bytes 442376 | tf_op jit(solution)/shard_map/ppermute | solution.py:97
  93.1 5.2 %collective-permute-start.14 = (f32[9,32,128]{2,1,0:T(8,128)S(1)}, f32[9,32,128]{2,1,0:T(8,128)S(1)}, u32[]{:S(2)}, u32[]{:S(2)}) collective-permute-start(f32[9,32,128]{2,1,0:T(8,128)S(1)} %add.187), channel_id=1, source_target_pairs={{0,16},{1,9},{2,18},{3,11},{4,20},{5,13},{6,22},{7,15},{8,24},{9,1... | collective-permute-start | bytes 442376 | tf_op jit(solution)/shard_map/ppermute | solution.py:97
  98.3 7.1 %collective-permute-start.15 = (f32[9,32,128]{2,1,0:T(8,128)S(1)}, f32[9,32,128]{2,1,0:T(8,128)S(1)}, u32[]{:S(2)}, u32[]{:S(2)}) collective-permute-start(f32[9,32,128]{2,1,0:T(8,128)S(1)} %add.188), channel_id=1, source_target_pairs={{0,4},{1,3},{2,6},{3,1},{4,0},{5,7},{6,2},{7,5},{8,12},{9,11},{10,... | collective-permute-start | bytes 442376 | tf_op jit(solution)/shard_map/ppermute | solution.py:100
  105.5 6.8 %collective-permute-start.16 = (f32[9,32,256]{2,1,0:T(8,128)S(1)}, f32[9,32,256]{2,1,0:T(8,128)S(1)}, u32[]{:S(2)}, u32[]{:S(2)}) collective-permute-start(f32[9,32,256]{2,1,0:T(8,128)S(1)} %pad_maximum_fusion.3), channel_id=1, source_target_pairs={{0,2},{1,5},{2,0},{3,7},{4,6},{5,1},{6,4},{7,3},{8,10},{9,13},{10,... | collective-permute-start | bytes 884744 | tf_op jit(solution)/shard_map/ppermute | solution.py:100
  112.4 2.2 %copy-start.3 = (f32[4,64,1024]{2,1,0:T(8,128)S(1)}, f32[4,64,1024]{2,1,0:T(8,128)}, u32[]{:S(2)}) copy-start(f32[4,64,1024]{2,1,0:T(8,128)} %param.12) | copy-start | bytes 3145732
  112.4 2.1 %collective-permute-start.17 = (f32[9,32,512]{2,1,0:T(8,128)S(1)}, f32[9,32,512]{2,1,0:T(8,128)S(1)}, u32[]{:S(2)}, u32[]{:S(2)}) collective-permute-start(f32[9,32,512]{2,1,0:T(8,128)S(1)} %pad_maximum_fusion.1), channel_id=1, source_target_pairs={{0,1},{1,0},{2,3},{3,2},{4,5},{5,4},{6,7},{7,6},{8,9},{9,8},{10,11... | collective-permute-start | bytes 1769480 | tf_op jit(solution)/shard_map/ppermute | solution.py:100

commit v14 on v13

--- a/solution.py
+++ b/solution.py
@@ -129,8 +129,9 @@
     )
     combined = gradient[0].astype(jnp.float32) + feedback[0]
     tile_rows = _scalar_rows(tile_matrix, matrix_count)
-    q_tiles = _pick_rows(start_basis, tile_rows)
-    first_local = jnp.einsum("tkd,tds->tks", combined, q_tiles, precision=WIDE_PRECISION)
+    every_basis = jnp.einsum("tkd,mds->tkms", combined, start_basis, precision=WIDE_PRECISION)
+    own_basis = tile_matrix[:, None, None] == jnp.arange(matrix_count, dtype=tile_matrix.dtype)[None, :, None]
+    first_local = jnp.sum(jnp.where(own_basis[:, None, :, :], every_basis, 0.0), axis=2)
     left_size = first_local.size
     carried = jnp.concatenate([first_local.reshape(-1), vector_grad[0].reshape(-1)])
     carried = swap_sum(carried, "rep")

time: 117 us -> 128 us (1.094)
  starting transfers between devices: 31.9 us -> 23.8 us
  other arithmetic: 4.16 us -> 11.6 us
  waiting for transfers between devices: 67 us -> 73.4 us
  local copies, waits for them, and re-layouts: 2.91 us -> 7.11 us
    ppermute x4, starting transfers between devices: 10.3 us -> 6.4 us  [table_rows(): cur = cur + lax.ppermute(cur, axes, perm_of(p0, p1))]
    ppermute x4, waiting for transfers between devices: 19.6 us -> 23.1 us  [table_rows(): cur = cur + lax.ppermute(cur, axes, perm_of(p0, p1))]
    unnamed x18 -> x28, local copies, waits for them, and re-layouts: 0.06 us -> 2.91 us
    add x6, other arithmetic: 1.38 us -> 3.45 us  [table_rows(): cur = keep + lax.ppermute(send, axes, perm_of(p0, p1))]
    ppermute x6, waiting for transfers between devices: 19.9 us -> 21.7 us  [table_rows(): cur = keep + lax.ppermute(send, axes, perm_of(p0, p1))]
    ppermute x2, starting transfers between devices: 4.91 us -> 3.2 us  [swap_sum(): x = x + lax.ppermute(x, axis, _pair_perm(n, j))]
    ppermute x6, starting transfers between devices: 8.37 us -> 6.77 us  [table_rows(): cur = keep + lax.ppermute(send, axes, perm_of(p0, p1))]
  transfers between devices with their start and end apart: 18 -> 18, of which waited for: 18 -> 17; matrix products, arithmetic and copies ran while one was open for 0% -> 3% of each run, Pallas kernels for 0% -> 0%
where the time goes in v14:
time: 128 us; the launch traced here: 127 us
  waiting for transfers between devices  73.4 us (57%)
  starting transfers between devices  23.8 us (19%)
  other arithmetic  11.6 us (9%)
  matrix products  7.63 us (6%)
  local copies, waits for them, and re-layouts  7.11 us (6%)
  between operations  3.76 us (3%)
    ppermute x6, waiting for transfers between devices, table_rows(): other = lax.ppermute(cur, axes, perm_of(p0, p1))  24.4 us
    ppermute x4, waiting for transfers between devices, table_rows(): cur = cur + lax.ppermute(cur, axes, perm_of(p0, p1))  23.1 us
    ppermute x6, waiting for transfers between devices, table_rows(): cur = keep + lax.ppermute(send, axes, perm_of(p0, p1))  21.7 us
    ppermute x6, starting transfers between devices, table_rows(): other = lax.ppermute(cur, axes, perm_of(p0, p1))  7.46 us
    ppermute x6, starting transfers between devices, table_rows(): cur = keep + lax.ppermute(send, axes, perm_of(p0, p1))  6.77 us
    ppermute x4, starting transfers between devices, table_rows(): cur = cur + lax.ppermute(cur, axes, perm_of(p0, p1))  6.4 us
    ppermute x2, waiting for transfers between devices, swap_sum(): x = x + lax.ppermute(x, axis, _pair_perm(n, j))  4.1 us
    add x6, other arithmetic, table_rows(): cur = keep + lax.ppermute(send, axes, perm_of(p0, p1))  3.45 us
  transfers between devices with their start and end apart: 18, of which 17 were waited for; matrix products, arithmetic and copies ran while one was open for 3% of the time, Pallas kernels for 0%

profile of v14, /device:TPU:0, one launch (start us, length us, event | category | flops | bytes accessed | tf_op | source)
XLA Modules:
  0.0 127.3 jit_solution(16298340259833902827)
XLA Ops:
  1.9 2.5 %fusion = f32[4,64,32]{1,2,0:T(8,128)S(1)} fusion(f32[9,1024,32]{1,2,0:T(8,128)S(1)} %copy-done, pred[4,9]{1,0:T(4,128)(4,1)S(1)} %iota_compare_fusion.2, f32[1,4,64,1024]{3,2,1,0:T(8,128)} %param.11, bf16[1,4,64,1024]{3,2,1,0:T(8,128)(2,1)} %param.10), kind=kOutput, calls=%fused_computation.1 | convolution fusion | flops 453648384 | bytes 2785316 | tf_op jit(solution)/shard_map/tkd,mds->tkms/dot_general | solution.py:132
  5.3 3.0 %collective-permute-start = (f32[13312]{0:T(1024)}, f32[13312]{0:T(1024)}, u32[]{:S(2)}, u32[]{:S(2)}) collective-permute-start(f32[13312]{0:T(1024)} %pad_maximum_fusion.10), channel_id=1, source_target_pairs={{0,16},{16,0},{1,17},{17,1},{2,18},{18,2},{3,19},{19,3},{4,20},{20... | collective-permute-start | bytes 159752 | tf_op jit(solution)/shard_map/ppermute | solution.py:21
  16.0 1.4 %multiply_add_fusion.1 = f32[5,1024]{1,0:T(8,128)} fusion(f32[5,1024]{1,0:T(8,128)S(1)} %div.26, f32[5,1024]{1,0:T(8,128)} %param.19), kind=kLoop, calls=%fused_computation.106 | loop fusion | flops 10240 | bytes 61440 | tf_op jit(solution)/shard_map/add | solution.py:143
  19.6 2.1 %collective-permute-done.1 = f32[9,32,512]{2,1,0:T(8,128)} collective-permute-done((f32[9,32,512]{2,1,0:T(8,128)S(1)}, f32[9,32,512]{2,1,0:T(8,128)}, u32[]{:S(2)}, u32[]{:S(2)}) %collective-permute-start.1) | collective-permute-done | bytes 589856 | tf_op jit(solution)/shard_map/ppermute | solution.py:94
  21.7 1.3 %dynamic-slice_add_fusion.1 = f32[9,32,512]{2,1,0:T(8,128)S(1)} fusion(f32[9,32,512]{2,1,0:T(8,128)} %collective-permute-done.1, f32[9,32,1024]{2,1,0:T(8,128)} %copy-done.3, s32[]{:T(128)S(6)} %select_n.165), kind=kLoop, calls=%fused_computation.35 | loop fusion | flops 147456 | bytes 1769476 | tf_op jit(solution)/shard_map/add | solution.py:94
  23.8 1.6 %collective-permute-start.2 = (f32[9,32,256]{2,1,0:T(8,128)}, f32[9,32,256]{2,1,0:T(8,128)}, u32[]{:S(2)}, u32[]{:S(2)}) collective-permute-start(f32[9,32,256]{2,1,0:T(8,128)} %constant_dynamic-slice_fusion.12), channel_id=1, source_target_pairs={{0,2},{1,5},{2,0},{3,7},{4,6},{5,1},{6,4},{7,3},{8,10},{9,13},{10,... | collective-permute-start | bytes 884744 | tf_op jit(solution)/shard_map/ppermute | solution.py:94
  25.3 5.5 %collective-permute-done.2 = f32[9,32,256]{2,1,0:T(8,128)} collective-permute-done((f32[9,32,256]{2,1,0:T(8,128)}, f32[9,32,256]{2,1,0:T(8,128)}, u32[]{:S(2)}, u32[]{:S(2)}) %collective-permute-start.2) | collective-permute-done | bytes 294944 | tf_op jit(solution)/shard_map/ppermute | solution.py:94
  32.6 1.6 %collective-permute-start.3 = (f32[9,32,128]{2,1,0:T(8,128)S(1)}, f32[9,32,128]{2,1,0:T(8,128)S(1)}, u32[]{:S(2)}, u32[]{:S(2)}) collective-permute-start(f32[9,32,128]{2,1,0:T(8,128)S(1)} %constant_dynamic-slice_fusion.11), channel_id=1, source_target_pairs={{0,4},{1,3},{2,6},{3,1},{4,0},{5,7},{6,2},{7,5},{8,12},{9,11},{10,... | collective-permute-start | bytes 442376 | tf_op jit(solution)/shard_map/ppermute | solution.py:94
  34.2 3.6 %collective-permute-done.3 = f32[9,32,128]{2,1,0:T(8,128)S(1)} collective-permute-done((f32[9,32,128]{2,1,0:T(8,128)S(1)}, f32[9,32,128]{2,1,0:T(8,128)S(1)}, u32[]{:S(2)}, u32[]{:S(2)}) %collective-permute-start.3) | collective-permute-done | bytes 147488 | tf_op jit(solution)/shard_map/ppermute | solution.py:94
  38.7 2.6 %collective-permute-start.4 = (f32[9,32,128]{2,1,0:T(8,128)S(1)}, f32[9,32,128]{2,1,0:T(8,128)S(1)}, u32[]{:S(2)}, u32[]{:S(2)}) collective-permute-start(f32[9,32,128]{2,1,0:T(8,128)S(1)} %dynamic-slice_add_fusion.5), channel_id=1, source_target_pairs={{0,8},{1,17},{2,10},{3,19},{4,12},{5,21},{6,14},{7,23},{8,0},{9,25... | collective-permute-start | bytes 442376 | tf_op jit(solution)/shard_map/ppermute | solution.py:97
  41.3 7.1 %collective-permute-done.4 = f32[9,32,128]{2,1,0:T(8,128)S(1)} collective-permute-done((f32[9,32,128]{2,1,0:T(8,128)S(1)}, f32[9,32,128]{2,1,0:T(8,128)S(1)}, u32[]{:S(2)}, u32[]{:S(2)}) %collective-permute-start.4) | collective-permute-done | bytes 147488 | tf_op jit(solution)/shard_map/ppermute | solution.py:97
  48.5 5.1 %collective-permute-done.5 = f32[9,32,128]{2,1,0:T(8,128)S(1)} collective-permute-done((f32[9,32,128]{2,1,0:T(8,128)S(1)}, f32[9,32,128]{2,1,0:T(8,128)S(1)}, u32[]{:S(2)}, u32[]{:S(2)}) %collective-permute-start.5) | collective-permute-done | bytes 147488 | tf_op jit(solution)/shard_map/ppermute | solution.py:97
  53.7 1.7 %collective-permute-start.6 = (f32[9,32,128]{2,1,0:T(8,128)S(1)}, f32[9,32,128]{2,1,0:T(8,128)S(1)}, u32[]{:S(2)}, u32[]{:S(2)}) collective-permute-start(f32[9,32,128]{2,1,0:T(8,128)S(1)} %add.174), channel_id=1, source_target_pairs={{0,4},{1,3},{2,6},{3,1},{4,0},{5,7},{6,2},{7,5},{8,12},{9,11},{10,... | collective-permute-start | bytes 442376 | tf_op jit(solution)/shard_map/ppermute | solution.py:100
  55.4 5.1 %collective-permute-done.6 = f32[9,32,128]{2,1,0:T(8,128)S(1)} collective-permute-done((f32[9,32,128]{2,1,0:T(8,128)S(1)}, f32[9,32,128]{2,1,0:T(8,128)S(1)}, u32[]{:S(2)}, u32[]{:S(2)}) %collective-permute-start.6) | collective-permute-done | bytes 147488 | tf_op jit(solution)/shard_map/ppermute | solution.py:100
  61.2 1.7 %collective-permute-start.7 = (f32[9,32,256]{2,1,0:T(8,128)S(1)}, f32[9,32,256]{2,1,0:T(8,128)}, u32[]{:S(2)}, u32[]{:S(2)}) collective-permute-start(f32[9,32,256]{2,1,0:T(8,128)S(1)} %pad_maximum_fusion.2), channel_id=1, source_target_pairs={{0,2},{1,5},{2,0},{3,7},{4,6},{5,1},{6,4},{7,3},{8,10},{9,13},{10,... | collective-permute-start | bytes 884744 | tf_op jit(solution)/shard_map/ppermute | solution.py:100
  62.9 5.2 %collective-permute-done.7 = f32[9,32,256]{2,1,0:T(8,128)} collective-permute-done((f32[9,32,256]{2,1,0:T(8,128)S(1)}, f32[9,32,256]{2,1,0:T(8,128)}, u32[]{:S(2)}, u32[]{:S(2)}) %collective-permute-start.7) | collective-permute-done | bytes 294944 | tf_op jit(solution)/shard_map/ppermute | solution.py:100
  70.1 2.3 %collective-permute-done.8 = f32[9,32,512]{2,1,0:T(8,128)} collective-permute-done((f32[9,32,512]{2,1,0:T(8,128)}, f32[9,32,512]{2,1,0:T(8,128)}, u32[]{:S(2)}, u32[]{:S(2)}) %collective-permute-start.8) | collective-permute-done | bytes 589856 | tf_op jit(solution)/shard_map/ppermute | solution.py:100
  74.8 4.1 %collective-permute-done.9 = f32[4,64,32]{1,2,0:T(8,128)S(1)} collective-permute-done((f32[4,64,32]{1,2,0:T(8,128)S(1)}, f32[4,64,32]{1,2,0:T(8,128)S(1)}, u32[]{:S(2)}, u32[]{:S(2)}) %collective-permute-start.9) | collective-permute-done | bytes 32800 | tf_op jit(solution)/shard_map/ppermute | solution.py:21
  80.1 2.0 %collective-permute-done.10 = f32[9,32,512]{2,1,0:T(8,128)S(1)} collective-permute-done((f32[9,32,512]{2,1,0:T(8,128)S(1)}, f32[9,32,512]{2,1,0:T(8,128)S(1)}, u32[]{:S(2)}, u32[]{:S(2)}) %collective-permute-start.10) | collective-permute-done | bytes 589856 | tf_op jit(solution)/shard_map/ppermute | solution.py:94
  82.2 1.7 %collective-permute-start.11 = (f32[9,32,256]{2,1,0:T(8,128)S(1)}, f32[9,32,256]{2,1,0:T(8,128)S(1)}, u32[]{:S(2)}, u32[]{:S(2)}) collective-permute-start(f32[9,32,256]{2,1,0:T(8,128)S(1)} %constant_dynamic-slice_fusion.1), channel_id=1, source_target_pairs={{0,2},{1,5},{2,0},{3,7},{4,6},{5,1},{6,4},{7,3},{8,10},{9,13},{10,... | collective-permute-start | bytes 884744 | tf_op jit(solution)/shard_map/ppermute | solution.py:94
  83.9 5.1 %collective-permute-done.11 = f32[9,32,256]{2,1,0:T(8,128)S(1)} collective-permute-done((f32[9,32,256]{2,1,0:T(8,128)S(1)}, f32[9,32,256]{2,1,0:T(8,128)S(1)}, u32[]{:S(2)}, u32[]{:S(2)}) %collective-permute-start.11) | collective-permute-done | bytes 294944 | tf_op jit(solution)/shard_map/ppermute | solution.py:94
  89.1 1.7 %collective-permute-start.12 = (f32[9,32,128]{2,1,0:T(8,128)S(1)}, f32[9,32,128]{2,1,0:T(8,128)S(1)}, u32[]{:S(2)}, u32[]{:S(2)}) collective-permute-start(f32[9,32,128]{2,1,0:T(8,128)S(1)} %constant_dynamic-slice_fusion), channel_id=1, source_target_pairs={{0,4},{1,3},{2,6},{3,1},{4,0},{5,7},{6,2},{7,5},{8,12},{9,11},{10,... | collective-permute-start | bytes 442376 | tf_op jit(solution)/shard_map/ppermute | solution.py:94
  90.8 3.5 %collective-permute-done.12 = f32[9,32,128]{2,1,0:T(8,128)S(1)} collective-permute-done((f32[9,32,128]{2,1,0:T(8,128)S(1)}, f32[9,32,128]{2,1,0:T(8,128)S(1)}, u32[]{:S(2)}, u32[]{:S(2)}) %collective-permute-start.12) | collective-permute-done | bytes 147488 | tf_op jit(solution)/shard_map/ppermute | solution.py:94
  94.3 3.1 %collective-permute-start.13 = (f32[9,32,128]{2,1,0:T(8,128)S(1)}, f32[9,32,128]{2,1,0:T(8,128)S(1)}, u32[]{:S(2)}, u32[]{:S(2)}) collective-permute-start(f32[9,32,128]{2,1,0:T(8,128)S(1)} %dynamic-slice_add_fusion.4), channel_id=1, source_target_pairs={{0,8},{1,17},{2,10},{3,19},{4,12},{5,21},{6,14},{7,23},{8,0},{9,25... | collective-permute-start | bytes 442376 | tf_op jit(solution)/shard_map/ppermute | solution.py:97
  97.4 6.3 %collective-permute-done.13 = f32[9,32,128]{2,1,0:T(8,128)S(1)} collective-permute-done((f32[9,32,128]{2,1,0:T(8,128)S(1)}, f32[9,32,128]{2,1,0:T(8,128)S(1)}, u32[]{:S(2)}, u32[]{:S(2)}) %collective-permute-start.13) | collective-permute-done | bytes 147488 | tf_op jit(solution)/shard_map/ppermute | solution.py:97
  104.3 4.6 %collective-permute-done.14 = f32[9,32,128]{2,1,0:T(8,128)S(1)} collective-permute-done((f32[9,32,128]{2,1,0:T(8,128)S(1)}, f32[9,32,128]{2,1,0:T(8,128)S(1)}, u32[]{:S(2)}, u32[]{:S(2)}) %collective-permute-start.14) | collective-permute-done | bytes 147488 | tf_op jit(solution)/shard_map/ppermute | solution.py:97
  109.0 2.4 %collective-permute-start.15 = (f32[9,32,128]{2,1,0:T(8,128)S(1)}, f32[9,32,128]{2,1,0:T(8,128)S(1)}, u32[]{:S(2)}, u32[]{:S(2)}) collective-permute-start(f32[9,32,128]{2,1,0:T(8,128)S(1)} %add.183), channel_id=1, source_target_pairs={{0,4},{1,3},{2,6},{3,1},{4,0},{5,7},{6,2},{7,5},{8,12},{9,11},{10,... | collective-permute-start | bytes 442376 | tf_op jit(solution)/shard_map/ppermute | solution.py:100
  111.4 4.7 %collective-permute-done.15 = f32[9,32,128]{2,1,0:T(8,128)S(1)} collective-permute-done((f32[9,32,128]{2,1,0:T(8,128)S(1)}, f32[9,32,128]{2,1,0:T(8,128)S(1)}, u32[]{:S(2)}, u32[]{:S(2)}) %collective-permute-start.15) | collective-permute-done | bytes 147488 | tf_op jit(solution)/shard_map/ppermute | solution.py:100
  116.1 1.6 %collective-permute-start.16 = (f32[9,32,256]{2,1,0:T(8,128)S(1)}, f32[9,32,256]{2,1,0:T(8,128)S(1)}, u32[]{:S(2)}, u32[]{:S(2)}) collective-permute-start(f32[9,32,256]{2,1,0:T(8,128)S(1)} %pad_maximum_fusion.3), channel_id=1, source_target_pairs={{0,2},{1,5},{2,0},{3,7},{4,6},{5,1},{6,4},{7,3},{8,10},{9,13},{10,... | collective-permute-start | bytes 884744 | tf_op jit(solution)/shard_map/ppermute | solution.py:100
  117.7 5.2 %collective-permute-done.16 = f32[9,32,256]{2,1,0:T(8,128)S(1)} collective-permute-done((f32[9,32,256]{2,1,0:T(8,128)S(1)}, f32[9,32,256]{2,1,0:T(8,128)S(1)}, u32[]{:S(2)}, u32[]{:S(2)}) %collective-permute-start.16) | collective-permute-done | bytes 294944 | tf_op jit(solution)/shard_map/ppermute | solution.py:100
  123.2 2.0 %collective-permute-done.17 = f32[9,32,512]{2,1,0:T(8,128)S(1)} collective-permute-done((f32[9,32,512]{2,1,0:T(8,128)S(1)}, f32[9,32,512]{2,1,0:T(8,128)S(1)}, u32[]{:S(2)}, u32[]{:S(2)}) %collective-permute-start.17) | collective-permute-done | bytes 589856 | tf_op jit(solution)/shard_map/ppermute | solution.py:100
  125.2 2.1 %multiply_add_fusion = (f32[4,64,1024]{2,1,0:T(8,128)}, f32[1,4,64,1024]{3,2,1,0:T(8,128)}) fusion(f32[4,64,1024]{2,1,0:T(8,128)S(1)} %copy-done.6, f32[4]{0:T(128)S(1)} %convolution_bitcast_fusion, f32[1,4,64,1024]{3,2,1,0:T(8,128)S(1)} %copy-done.1, bf16[1,4,64,1024]{3,2,1,0:T(8,128)(2,1)S(1)} %copy-done.2, f32[4,64,32]{1,2,0:T(8,128)S(1)} %fusion.44, ...), kind=kOutput, calls=%fused_computation.14 | convolution fusion | flops 52166656 | bytes 5275664 | tf_op jit(solution)/shard_map/tks,tsd->tkd/dot_general | solution.py:163
  (102 shorter events, 20.1 us)
Async XLA Ops:
  0.6 1.3 %copy-start = (f32[9,1024,32]{1,2,0:T(8,128)S(1)}, f32[9,1024,32]{1,2,0:T(8,128)}, u32[]{:S(2)}) copy-start(f32[9,1024,32]{1,2,0:T(8,128)} %param.16) | copy-start | bytes 3538948
  1.9 2.8 %copy-start.10 = (f32[1,5,1024]{2,0,1:T(1,128)S(1)}, f32[1,5,1024]{2,0,1:T(1,128)}, u32[]{:S(2)}) copy-start(f32[1,5,1024]{2,0,1:T(1,128)} %param.18) | copy-start | bytes 61444
  1.9 6.4 %copy-start.13 = (s32[4]{0:T(128)S(1)}, s32[4]{0:T(128)}, u32[]{:S(2)}) copy-start(s32[4]{0:T(128)} %param.13) | copy-start | bytes 52
  1.9 9.6 %copy-start.7 = (f32[3,9,32,32]{3,2,1,0:T(8,128)S(1)}, f32[3,9,32,32]{3,2,1,0:T(8,128)}, u32[]{:S(2)}) copy-start(f32[3,9,32,32]{3,2,1,0:T(8,128)} %param.17) | copy-start | bytes 331780
  4.5 8.6 %copy-start.11 = (s32[9]{0:T(128)S(1)}, s32[9]{0:T(128)}, u32[]{:S(2)}) copy-start(s32[9]{0:T(128)} %param.14) | copy-start | bytes 112
  4.5 8.6 %copy-start.12 = (f32[4]{0:T(128)S(1)}, f32[4]{0:T(128)}, u32[]{:S(2)}) copy-start(f32[4]{0:T(128)} %param.15) | copy-start | bytes 52
  5.3 9.7 %collective-permute-start = (f32[13312]{0:T(1024)}, f32[13312]{0:T(1024)}, u32[]{:S(2)}, u32[]{:S(2)}) collective-permute-start(f32[13312]{0:T(1024)} %pad_maximum_fusion.10), channel_id=1, source_target_pairs={{0,16},{16,0},{1,17},{17,1},{2,18},{18,2},{3,19},{19,3},{4,20},{20... | collective-permute-start | bytes 159752 | tf_op jit(solution)/shard_map/ppermute | solution.py:21
  11.5 6.2 %copy-start.1 = (f32[1,4,64,1024]{3,2,1,0:T(8,128)S(1)}, f32[1,4,64,1024]{3,2,1,0:T(8,128)}, u32[]{:S(2)}) copy-start(f32[1,4,64,1024]{3,2,1,0:T(8,128)} %param.11) | copy-start | bytes 3145732
  11.5 6.2 %copy-start.2 = (bf16[1,4,64,1024]{3,2,1,0:T(8,128)(2,1)S(1)}, bf16[1,4,64,1024]{3,2,1,0:T(8,128)(2,1)}, u32[]{:S(2)}) copy-start(bf16[1,4,64,1024]{3,2,1,0:T(8,128)(2,1)} %param.10) | copy-start | bytes 1572868
  18.4 1.0 copy-start.3
  19.5 2.2 %collective-permute-start.1 = (f32[9,32,512]{2,1,0:T(8,128)S(1)}, f32[9,32,512]{2,1,0:T(8,128)}, u32[]{:S(2)}, u32[]{:S(2)}) collective-permute-start(f32[9,32,512]{2,1,0:T(8,128)S(1)} %constant_dynamic-slice_fusion.13), channel_id=1, source_target_pairs={{0,1},{1,0},{2,3},{3,2},{4,5},{5,4},{6,7},{7,6},{8,9},{9,8},{10,11... | collective-permute-start | bytes 1769480 | tf_op jit(solution)/shard_map/ppermute | solution.py:94
  23.8 7.0 %collective-permute-start.2 = (f32[9,32,256]{2,1,0:T(8,128)}, f32[9,32,256]{2,1,0:T(8,128)}, u32[]{:S(2)}, u32[]{:S(2)}) collective-permute-start(f32[9,32,256]{2,1,0:T(8,128)} %constant_dynamic-slice_fusion.12), channel_id=1, source_target_pairs={{0,2},{1,5},{2,0},{3,7},{4,6},{5,1},{6,4},{7,3},{8,10},{9,13},{10,... | collective-permute-start | bytes 884744 | tf_op jit(solution)/shard_map/ppermute | solution.py:94
  31.8 0.7 copy-start.5
  32.6 5.2 %collective-permute-start.3 = (f32[9,32,128]{2,1,0:T(8,128)S(1)}, f32[9,32,128]{2,1,0:T(8,128)S(1)}, u32[]{:S(2)}, u32[]{:S(2)}) collective-permute-start(f32[9,32,128]{2,1,0:T(8,128)S(1)} %constant_dynamic-slice_fusion.11), channel_id=1, source_target_pairs={{0,4},{1,3},{2,6},{3,1},{4,0},{5,7},{6,2},{7,5},{8,12},{9,11},{10,... | collective-permute-start | bytes 442376 | tf_op jit(solution)/shard_map/ppermute | solution.py:94
  38.7 9.7 %collective-permute-start.4 = (f32[9,32,128]{2,1,0:T(8,128)S(1)}, f32[9,32,128]{2,1,0:T(8,128)S(1)}, u32[]{:S(2)}, u32[]{:S(2)}) collective-permute-start(f32[9,32,128]{2,1,0:T(8,128)S(1)} %dynamic-slice_add_fusion.5), channel_id=1, source_target_pairs={{0,8},{1,17},{2,10},{3,19},{4,12},{5,21},{6,14},{7,23},{8,0},{9,25... | collective-permute-start | bytes 442376 | tf_op jit(solution)/shard_map/ppermute | solution.py:97
  48.5 5.2 %collective-permute-start.5 = (f32[9,32,128]{2,1,0:T(8,128)S(1)}, f32[9,32,128]{2,1,0:T(8,128)S(1)}, u32[]{:S(2)}, u32[]{:S(2)}) collective-permute-start(f32[9,32,128]{2,1,0:T(8,128)S(1)} %add.173), channel_id=1, source_target_pairs={{0,16},{1,9},{2,18},{3,11},{4,20},{5,13},{6,22},{7,15},{8,24},{9,1... | collective-permute-start | bytes 442376 | tf_op jit(solution)/shard_map/ppermute | solution.py:97
  53.7 6.8 %collective-permute-start.6 = (f32[9,32,128]{2,1,0:T(8,128)S(1)}, f32[9,32,128]{2,1,0:T(8,128)S(1)}, u32[]{:S(2)}, u32[]{:S(2)}) collective-permute-start(f32[9,32,128]{2,1,0:T(8,128)S(1)} %add.174), channel_id=1, source_target_pairs={{0,4},{1,3},{2,6},{3,1},{4,0},{5,7},{6,2},{7,5},{8,12},{9,11},{10,... | collective-permute-start | bytes 442376 | tf_op jit(solution)/shard_map/ppermute | solution.py:100
  60.5 0.7 copy-start.4
  61.2 6.9 %collective-permute-start.7 = (f32[9,32,256]{2,1,0:T(8,128)S(1)}, f32[9,32,256]{2,1,0:T(8,128)}, u32[]{:S(2)}, u32[]{:S(2)}) collective-permute-start(f32[9,32,256]{2,1,0:T(8,128)S(1)} %pad_maximum_fusion.2), channel_id=1, source_target_pairs={{0,2},{1,5},{2,0},{3,7},{4,6},{5,1},{6,4},{7,3},{8,10},{9,13},{10,... | collective-permute-start | bytes 884744 | tf_op jit(solution)/shard_map/ppermute | solution.py:100
  70.0 2.3 %collective-permute-start.8 = (f32[9,32,512]{2,1,0:T(8,128)}, f32[9,32,512]{2,1,0:T(8,128)}, u32[]{:S(2)}, u32[]{:S(2)}) collective-permute-start(f32[9,32,512]{2,1,0:T(8,128)} %pad_maximum_fusion), channel_id=1, source_target_pairs={{0,1},{1,0},{2,3},{3,2},{4,5},{5,4},{6,7},{7,6},{8,9},{9,8},{10,11... | collective-permute-start | bytes 1769480 | tf_op jit(solution)/shard_map/ppermute | solution.py:100
  70.0 3.4 %copy-start.8 = (f32[4,32,32]{2,1,0:T(8,128)S(1)}, f32[4,32,32]{2,1,0:T(8,128)}, u32[]{:S(2)}) copy-start(f32[4,32,32]{2,1,0:T(8,128)} %pad_maximum_fusion.8) | copy-start | bytes 49156
  74.1 4.9 %copy-start.9 = (f32[4,32,32]{2,1,0:T(8,128)S(1)}, f32[4,32,32]{2,1,0:T(8,128)}, u32[]{:S(2)}) copy-start(f32[4,32,32]{2,1,0:T(8,128)} %pad_maximum_fusion.9) | copy-start | bytes 49156
  74.6 4.3 %collective-permute-start.9 = (f32[4,64,32]{1,2,0:T(8,128)S(1)}, f32[4,64,32]{1,2,0:T(8,128)S(1)}, u32[]{:S(2)}, u32[]{:S(2)}) collective-permute-start(f32[4,64,32]{1,2,0:T(8,128)S(1)} %fusion.5), channel_id=1, source_target_pairs={{0,16},{16,0},{1,17},{17,1},{2,18},{18,2},{3,19},{19,3},{4,20},{20... | collective-permute-start | bytes 98312 | tf_op jit(solution)/shard_map/ppermute | solution.py:21
  80.0 2.1 %collective-permute-start.10 = (f32[9,32,512]{2,1,0:T(8,128)S(1)}, f32[9,32,512]{2,1,0:T(8,128)S(1)}, u32[]{:S(2)}, u32[]{:S(2)}) collective-permute-start(f32[9,32,512]{2,1,0:T(8,128)S(1)} %constant_dynamic-slice_fusion.2), channel_id=1, source_target_pairs={{0,1},{1,0},{2,3},{3,2},{4,5},{5,4},{6,7},{7,6},{8,9},{9,8},{10,11... | collective-permute-start | bytes 1769480 | tf_op jit(solution)/shard_map/ppermute | solution.py:94
  82.2 6.8 %collective-permute-start.11 = (f32[9,32,256]{2,1,0:T(8,128)S(1)}, f32[9,32,256]{2,1,0:T(8,128)S(1)}, u32[]{:S(2)}, u32[]{:S(2)}) collective-permute-start(f32[9,32,256]{2,1,0:T(8,128)S(1)} %constant_dynamic-slice_fusion.1), channel_id=1, source_target_pairs={{0,2},{1,5},{2,0},{3,7},{4,6},{5,1},{6,4},{7,3},{8,10},{9,13},{10,... | collective-permute-start | bytes 884744 | tf_op jit(solution)/shard_map/ppermute | solution.py:94
  89.1 5.2 %collective-permute-start.12 = (f32[9,32,128]{2,1,0:T(8,128)S(1)}, f32[9,32,128]{2,1,0:T(8,128)S(1)}, u32[]{:S(2)}, u32[]{:S(2)}) collective-permute-start(f32[9,32,128]{2,1,0:T(8,128)S(1)} %constant_dynamic-slice_fusion), channel_id=1, source_target_pairs={{0,4},{1,3},{2,6},{3,1},{4,0},{5,7},{6,2},{7,5},{8,12},{9,11},{10,... | collective-permute-start | bytes 442376 | tf_op jit(solution)/shard_map/ppermute | solution.py:94
  94.3 9.4 %collective-permute-start.13 = (f32[9,32,128]{2,1,0:T(8,128)S(1)}, f32[9,32,128]{2,1,0:T(8,128)S(1)}, u32[]{:S(2)}, u32[]{:S(2)}) collective-permute-start(f32[9,32,128]{2,1,0:T(8,128)S(1)} %dynamic-slice_add_fusion.4), channel_id=1, source_target_pairs={{0,8},{1,17},{2,10},{3,19},{4,12},{5,21},{6,14},{7,23},{8,0},{9,25... | collective-permute-start | bytes 442376 | tf_op jit(solution)/shard_map/ppermute | solution.py:97
  103.7 5.2 %collective-permute-start.14 = (f32[9,32,128]{2,1,0:T(8,128)S(1)}, f32[9,32,128]{2,1,0:T(8,128)S(1)}, u32[]{:S(2)}, u32[]{:S(2)}) collective-permute-start(f32[9,32,128]{2,1,0:T(8,128)S(1)} %add.182), channel_id=1, source_target_pairs={{0,16},{1,9},{2,18},{3,11},{4,20},{5,13},{6,22},{7,15},{8,24},{9,1... | collective-permute-start | bytes 442376 | tf_op jit(solution)/shard_map/ppermute | solution.py:97
  109.0 7.1 %collective-permute-start.15 = (f32[9,32,128]{2,1,0:T(8,128)S(1)}, f32[9,32,128]{2,1,0:T(8,128)S(1)}, u32[]{:S(2)}, u32[]{:S(2)}) collective-permute-start(f32[9,32,128]{2,1,0:T(8,128)S(1)} %add.183), channel_id=1, source_target_pairs={{0,4},{1,3},{2,6},{3,1},{4,0},{5,7},{6,2},{7,5},{8,12},{9,11},{10,... | collective-permute-start | bytes 442376 | tf_op jit(solution)/shard_map/ppermute | solution.py:100
  116.1 6.8 %collective-permute-start.16 = (f32[9,32,256]{2,1,0:T(8,128)S(1)}, f32[9,32,256]{2,1,0:T(8,128)S(1)}, u32[]{:S(2)}, u32[]{:S(2)}) collective-permute-start(f32[9,32,256]{2,1,0:T(8,128)S(1)} %pad_maximum_fusion.3), channel_id=1, source_target_pairs={{0,2},{1,5},{2,0},{3,7},{4,6},{5,1},{6,4},{7,3},{8,10},{9,13},{10,... | collective-permute-start | bytes 884744 | tf_op jit(solution)/shard_map/ppermute | solution.py:100
  123.0 2.2 %copy-start.6 = (f32[4,64,1024]{2,1,0:T(8,128)S(1)}, f32[4,64,1024]{2,1,0:T(8,128)}, u32[]{:S(2)}) copy-start(f32[4,64,1024]{2,1,0:T(8,128)} %param.12) | copy-start | bytes 3145732
  123.1 2.1 %collective-permute-start.17 = (f32[9,32,512]{2,1,0:T(8,128)S(1)}, f32[9,32,512]{2,1,0:T(8,128)S(1)}, u32[]{:S(2)}, u32[]{:S(2)}) collective-permute-start(f32[9,32,512]{2,1,0:T(8,128)S(1)} %pad_maximum_fusion.1), channel_id=1, source_target_pairs={{0,1},{1,0},{2,3},{3,2},{4,5},{5,4},{6,7},{7,6},{8,9},{9,8},{10,11... | collective-permute-start | bytes 1769480 | tf_op jit(solution)/shard_map/ppermute | solution.py:100

commit v15 on v13

--- a/solution.py
+++ b/solution.py
@@ -93,8 +93,26 @@
         send = lax.dynamic_slice_in_dim(cur, (1 - bit) * half, half, axis)
         cur = keep + lax.ppermute(send, axes, perm_of(p0, p1))
         bits.append(bit)
-    for p0, p1 in pairing:
-        cur = cur + lax.ppermute(cur, axes, perm_of(p0, p1))
+    if len(pairing) == 2:
+        (a0, a1), (b0, b1) = pairing
+
+        def group_perm(k):
+            pairs = []
+            for i in range(count):
+                pa, pb = (a0, b0) if i % 2 == 0 else (a1, b1)
+                pairs.append((i, i ^ (((k & 1) << pa) | ((k >> 1) << pb))))
+            return pairs
+
+        place = bit_of(a0, a1) + 2 * bit_of(b0, b1)
+        held = [cur] + [lax.ppermute(cur, axes, group_perm(k)) for k in (1, 2, 3)]
+        total = None
+        for member in range(4):
+            term = lax.select_n(place ^ member, *held)
+            total = term if total is None else total + term
+        cur = total
+    else:
+        for p0, p1 in pairing:
+            cur = cur + lax.ppermute(cur, axes, perm_of(p0, p1))
     steps_back = list(reversed(list(zip(halving, plan, bits))))
     for index_step, ((p0, p1), axis, bit) in enumerate(steps_back):
         other = lax.ppermute(cur, axes, perm_of(p0, p1))

time: 117 us -> 115 us (0.983)
  starting transfers between devices: 31.9 us -> 24.4 us
  waiting for transfers between devices: 67 us -> 72.6 us
    ppermute x6, starting transfers between devices: 8.35 us -> 4.35 us  [table_rows(): other = lax.ppermute(cur, axes, perm_of(p0, p1))]
    ppermute x4 -> x6, waiting for transfers between devices: 19.6 us -> 22.5 us  [table_rows(): held = [cur] + [lax.ppermute(cur, axes, group_perm(k)) for k in (1, 2, 3)]]
    ppermute x6, starting transfers between devices: 8.37 us -> 6.49 us  [table_rows(): cur = keep + lax.ppermute(send, axes, perm_of(p0, p1))]
    ppermute x6, waiting for transfers between devices: 19.9 us -> 21.8 us  [table_rows(): cur = keep + lax.ppermute(send, axes, perm_of(p0, p1))]
    ppermute x4 -> x6, starting transfers between devices: 10.3 us -> 9.09 us  [table_rows(): held = [cur] + [lax.ppermute(cur, axes, group_perm(k)) for k in (1, 2, 3)]]
  transfers between devices with their start and end apart: 18 -> 20, of which waited for: 18 -> 18; matrix products, arithmetic and copies ran while one was open for 0% -> 0% of each run, Pallas kernels for 0% -> 0%
where the time goes in v15:
time: 115 us
  waiting for transfers between devices  72.6 us (63%)
  starting transfers between devices  24.4 us (21%)
  matrix products  6.88 us (6%)
  other arithmetic  4.24 us (4%)
  between operations  3.81 us (3%)
  local copies, waits for them, and re-layouts  2.89 us (3%)
    ppermute x6, waiting for transfers between devices, table_rows(): other = lax.ppermute(cur, axes, perm_of(p0, p1))  23.8 us
    ppermute x6, waiting for transfers between devices, table_rows(): held = [cur] + [lax.ppermute(cur, axes, group_perm(k)) for k in (1, 2, 3)]  22.5 us
    ppermute x6, waiting for transfers between devices, table_rows(): cur = keep + lax.ppermute(send, axes, perm_of(p0, p1))  21.8 us
    ppermute x6, starting transfers between devices, table_rows(): held = [cur] + [lax.ppermute(cur, axes, group_perm(k)) for k in (1, 2, 3)]  9.09 us
    ppermute x6, starting transfers between devices, table_rows(): cur = keep + lax.ppermute(send, axes, perm_of(p0, p1))  6.49 us
    ppermute x2, waiting for transfers between devices, swap_sum(): x = x + lax.ppermute(x, axis, _pair_perm(n, j))  4.48 us
    ppermute x2, starting transfers between devices, swap_sum(): x = x + lax.ppermute(x, axis, _pair_perm(n, j))  4.45 us
    ppermute x6, starting transfers between devices, table_rows(): other = lax.ppermute(cur, axes, perm_of(p0, p1))  4.35 us
  transfers between devices with their start and end apart: 20, of which 18 were waited for; matrix products, arithmetic and copies ran while one was open for 0% of the time, Pallas kernels for 0%

profile of v15, /device:TPU:0, one launch (start us, length us, event | category | flops | bytes accessed | tf_op | source)
XLA Modules:
  0.0 114.8 jit_solution(221112011161294084)
XLA Ops:
  0.7 1.4 %shift-left_reduce_fusion = s32[]{:T(128)} fusion(s32[4]{0:T(128)} %param.13), kind=kLoop, calls=%fused_computation.161 | loop fusion | flops 11 | bytes 20 | tf_op jit(solution)/shard_map/reduce_sum | solution.py:49
  5.8 1.7 %fusion.6 = f32[4,64,32]{2,1,0:T(8,128)S(1)} fusion(f32[1,1024,32]{1,2,0:T(8,128)S(1)} %get-tuple-element.15, f32[1,1024,32]{1,2,0:T(8,128)S(1)} %get-tuple-element.16, f32[1,1024,32]{1,2,0:T(8,128)S(1)} %get-tuple-element.14, f32[1,1024,32]{1,2,0:T(8,128)S(1)} %get-tuple-element.13, f32[1,4,64,1024]{3,2,1,0:T(8,128)S(1)} %copy-done.1, ...), kind=kOutput, calls=%fused_computation.9 | convolution fusion | flops 51249152 | bytes 2129920 | tf_op jit(solution)/shard_map/tkd,tds->tks/dot_general | solution.py:151
  7.7 3.0 %collective-permute-start = (f32[13312]{0:T(1024)S(1)}, f32[13312]{0:T(1024)S(1)}, u32[]{:S(2)}, u32[]{:S(2)}) collective-permute-start(f32[13312]{0:T(1024)S(1)} %pad_maximum_fusion.10), channel_id=1, source_target_pairs={{0,16},{16,0},{1,17},{17,1},{2,18},{18,2},{3,19},{19,3},{4,20},{20... | collective-permute-start | bytes 159752 | tf_op jit(solution)/shard_map/ppermute | solution.py:21
  11.2 1.6 %collective-permute-done = f32[13312]{0:T(1024)S(1)} collective-permute-done((f32[13312]{0:T(1024)S(1)}, f32[13312]{0:T(1024)S(1)}, u32[]{:S(2)}, u32[]{:S(2)}) %collective-permute-start) | collective-permute-done | bytes 53280 | tf_op jit(solution)/shard_map/ppermute | solution.py:21
  14.8 2.1 %collective-permute-done.1 = f32[9,32,512]{2,1,0:T(8,128)} collective-permute-done((f32[9,32,512]{2,1,0:T(8,128)S(1)}, f32[9,32,512]{2,1,0:T(8,128)}, u32[]{:S(2)}, u32[]{:S(2)}) %collective-permute-start.1) | collective-permute-done | bytes 589856 | tf_op jit(solution)/shard_map/ppermute | solution.py:94
  18.1 2.1 %collective-permute-start.2 = (f32[9,32,256]{2,1,0:T(8,128)S(1)}, f32[9,32,256]{2,1,0:T(8,128)S(1)}, u32[]{:S(2)}, u32[]{:S(2)}) collective-permute-start(f32[9,32,256]{2,1,0:T(8,128)S(1)} %constant_dynamic-slice_fusion.12), channel_id=1, source_target_pairs={{0,2},{1,5},{2,0},{3,7},{4,6},{5,1},{6,4},{7,3},{8,10},{9,13},{10,... | collective-permute-start | bytes 884744 | tf_op jit(solution)/shard_map/ppermute | solution.py:94
  20.2 4.7 %collective-permute-done.2 = f32[9,32,256]{2,1,0:T(8,128)S(1)} collective-permute-done((f32[9,32,256]{2,1,0:T(8,128)S(1)}, f32[9,32,256]{2,1,0:T(8,128)S(1)}, u32[]{:S(2)}, u32[]{:S(2)}) %collective-permute-start.2) | collective-permute-done | bytes 294944 | tf_op jit(solution)/shard_map/ppermute | solution.py:94
  25.0 2.1 %collective-permute-start.3 = (f32[9,32,128]{2,1,0:T(8,128)S(1)}, f32[9,32,128]{2,1,0:T(8,128)S(1)}, u32[]{:S(2)}, u32[]{:S(2)}) collective-permute-start(f32[9,32,128]{2,1,0:T(8,128)S(1)} %constant_dynamic-slice_fusion.11), channel_id=1, source_target_pairs={{0,4},{1,3},{2,6},{3,1},{4,0},{5,7},{6,2},{7,5},{8,12},{9,11},{10,... | collective-permute-start | bytes 442376 | tf_op jit(solution)/shard_map/ppermute | solution.py:94
  27.1 3.1 %collective-permute-done.3 = f32[9,32,128]{2,1,0:T(8,128)S(1)} collective-permute-done((f32[9,32,128]{2,1,0:T(8,128)S(1)}, f32[9,32,128]{2,1,0:T(8,128)S(1)}, u32[]{:S(2)}, u32[]{:S(2)}) %collective-permute-start.3) | collective-permute-done | bytes 147488 | tf_op jit(solution)/shard_map/ppermute | solution.py:94
  30.3 3.1 %collective-permute-start.4 = (f32[9,32,128]{2,1,0:T(8,128)S(1)}, f32[9,32,128]{2,1,0:T(8,128)S(1)}, u32[]{:S(2)}, u32[]{:S(2)}) collective-permute-start(f32[9,32,128]{2,1,0:T(8,128)S(1)} %dynamic-slice_add_fusion.5), channel_id=1, source_target_pairs={{0,8},{1,17},{2,10},{3,19},{4,12},{5,21},{6,14},{7,23},{8,0},{9,25... | collective-permute-start | bytes 442376 | tf_op jit(solution)/shard_map/ppermute | solution.py:107
  33.4 1.5 %collective-permute-start.5 = (f32[9,32,128]{2,1,0:T(8,128)S(1)}, f32[9,32,128]{2,1,0:T(8,128)S(1)}, u32[]{:S(2)}, u32[]{:S(2)}) collective-permute-start(f32[9,32,128]{2,1,0:T(8,128)S(1)} %dynamic-slice_add_fusion.5), channel_id=1, source_target_pairs={{0,16},{1,9},{2,18},{3,11},{4,20},{5,13},{6,22},{7,15},{8,24},{9,1... | collective-permute-start | bytes 442376 | tf_op jit(solution)/shard_map/ppermute | solution.py:107
  34.9 9.3 %collective-permute-done.4 = f32[9,32,128]{2,1,0:T(8,128)S(1)} collective-permute-done((f32[9,32,128]{2,1,0:T(8,128)S(1)}, f32[9,32,128]{2,1,0:T(8,128)S(1)}, u32[]{:S(2)}, u32[]{:S(2)}) %collective-permute-start.4) | collective-permute-done | bytes 147488 | tf_op jit(solution)/shard_map/ppermute | solution.py:107
  44.2 2.1 %collective-permute-done.6 = f32[9,32,128]{2,1,0:T(8,128)S(1)} collective-permute-done((f32[9,32,128]{2,1,0:T(8,128)S(1)}, f32[9,32,128]{2,1,0:T(8,128)S(1)}, u32[]{:S(2)}, u32[]{:S(2)}) %collective-permute-start.6) | collective-permute-done | bytes 147488 | tf_op jit(solution)/shard_map/ppermute | solution.py:107
  47.1 4.6 %collective-permute-done.7 = f32[9,32,128]{2,1,0:T(8,128)S(1)} collective-permute-done((f32[9,32,128]{2,1,0:T(8,128)S(1)}, f32[9,32,128]{2,1,0:T(8,128)S(1)}, u32[]{:S(2)}, u32[]{:S(2)}) %collective-permute-start.7) | collective-permute-done | bytes 147488 | tf_op jit(solution)/shard_map/ppermute | solution.py:118
  51.7 1.5 %collective-permute-start.8 = (f32[9,32,256]{2,1,0:T(8,128)S(1)}, f32[9,32,256]{2,1,0:T(8,128)S(1)}, u32[]{:S(2)}, u32[]{:S(2)}) collective-permute-start(f32[9,32,256]{2,1,0:T(8,128)S(1)} %pad_maximum_fusion.2), channel_id=1, source_target_pairs={{0,2},{1,5},{2,0},{3,7},{4,6},{5,1},{6,4},{7,3},{8,10},{9,13},{10,... | collective-permute-start | bytes 884744 | tf_op jit(solution)/shard_map/ppermute | solution.py:118
  53.2 5.3 %collective-permute-done.8 = f32[9,32,256]{2,1,0:T(8,128)S(1)} collective-permute-done((f32[9,32,256]{2,1,0:T(8,128)S(1)}, f32[9,32,256]{2,1,0:T(8,128)S(1)}, u32[]{:S(2)}, u32[]{:S(2)}) %collective-permute-start.8) | collective-permute-done | bytes 294944 | tf_op jit(solution)/shard_map/ppermute | solution.py:118
  58.8 2.1 %collective-permute-done.9 = f32[9,32,512]{2,1,0:T(8,128)} collective-permute-done((f32[9,32,512]{2,1,0:T(8,128)S(1)}, f32[9,32,512]{2,1,0:T(8,128)}, u32[]{:S(2)}, u32[]{:S(2)}) %collective-permute-start.9) | collective-permute-done | bytes 589856 | tf_op jit(solution)/shard_map/ppermute | solution.py:118
  63.1 1.4 %collective-permute-start.10 = (f32[4,64,32]{1,2,0:T(8,128)S(1)}, f32[4,64,32]{1,2,0:T(8,128)S(1)}, u32[]{:S(2)}, u32[]{:S(2)}) collective-permute-start(f32[4,64,32]{1,2,0:T(8,128)S(1)} %fusion.2), channel_id=1, source_target_pairs={{0,16},{16,0},{1,17},{17,1},{2,18},{18,2},{3,19},{19,3},{4,20},{20... | collective-permute-start | bytes 98312 | tf_op jit(solution)/shard_map/ppermute | solution.py:21
  64.5 2.9 %collective-permute-done.10 = f32[4,64,32]{1,2,0:T(8,128)S(1)} collective-permute-done((f32[4,64,32]{1,2,0:T(8,128)S(1)}, f32[4,64,32]{1,2,0:T(8,128)S(1)}, u32[]{:S(2)}, u32[]{:S(2)}) %collective-permute-start.10) | collective-permute-done | bytes 32800 | tf_op jit(solution)/shard_map/ppermute | solution.py:21
  68.5 2.0 %collective-permute-done.11 = f32[9,32,512]{2,1,0:T(8,128)S(1)} collective-permute-done((f32[9,32,512]{2,1,0:T(8,128)S(1)}, f32[9,32,512]{2,1,0:T(8,128)S(1)}, u32[]{:S(2)}, u32[]{:S(2)}) %collective-permute-start.11) | collective-permute-done | bytes 589856 | tf_op jit(solution)/shard_map/ppermute | solution.py:94
  70.6 1.5 %collective-permute-start.12 = (f32[9,32,256]{2,1,0:T(8,128)S(1)}, f32[9,32,256]{2,1,0:T(8,128)S(1)}, u32[]{:S(2)}, u32[]{:S(2)}) collective-permute-start(f32[9,32,256]{2,1,0:T(8,128)S(1)} %constant_dynamic-slice_fusion.1), channel_id=1, source_target_pairs={{0,2},{1,5},{2,0},{3,7},{4,6},{5,1},{6,4},{7,3},{8,10},{9,13},{10,... | collective-permute-start | bytes 884744 | tf_op jit(solution)/shard_map/ppermute | solution.py:94
  72.1 5.3 %collective-permute-done.12 = f32[9,32,256]{2,1,0:T(8,128)S(1)} collective-permute-done((f32[9,32,256]{2,1,0:T(8,128)S(1)}, f32[9,32,256]{2,1,0:T(8,128)S(1)}, u32[]{:S(2)}, u32[]{:S(2)}) %collective-permute-start.12) | collective-permute-done | bytes 294944 | tf_op jit(solution)/shard_map/ppermute | solution.py:94
  78.1 4.6 %collective-permute-done.13 = f32[9,32,128]{2,1,0:T(8,128)S(1)} collective-permute-done((f32[9,32,128]{2,1,0:T(8,128)S(1)}, f32[9,32,128]{2,1,0:T(8,128)S(1)}, u32[]{:S(2)}, u32[]{:S(2)}) %collective-permute-start.13) | collective-permute-done | bytes 147488 | tf_op jit(solution)/shard_map/ppermute | solution.py:94
  82.7 2.0 %collective-permute-start.14 = (f32[9,32,128]{2,1,0:T(8,128)S(1)}, f32[9,32,128]{2,1,0:T(8,128)S(1)}, u32[]{:S(2)}, u32[]{:S(2)}) collective-permute-start(f32[9,32,128]{2,1,0:T(8,128)S(1)} %dynamic-slice_add_fusion.4), channel_id=1, source_target_pairs={{0,8},{1,17},{2,10},{3,19},{4,12},{5,21},{6,14},{7,23},{8,0},{9,25... | collective-permute-start | bytes 442376 | tf_op jit(solution)/shard_map/ppermute | solution.py:107
  84.7 1.5 %collective-permute-start.15 = (f32[9,32,128]{2,1,0:T(8,128)S(1)}, f32[9,32,128]{2,1,0:T(8,128)S(1)}, u32[]{:S(2)}, u32[]{:S(2)}) collective-permute-start(f32[9,32,128]{2,1,0:T(8,128)S(1)} %dynamic-slice_add_fusion.4), channel_id=1, source_target_pairs={{0,16},{1,9},{2,18},{3,11},{4,20},{5,13},{6,22},{7,15},{8,24},{9,1... | collective-permute-start | bytes 442376 | tf_op jit(solution)/shard_map/ppermute | solution.py:107
  87.2 8.7 %collective-permute-done.14 = f32[9,32,128]{2,1,0:T(8,128)S(1)} collective-permute-done((f32[9,32,128]{2,1,0:T(8,128)S(1)}, f32[9,32,128]{2,1,0:T(8,128)S(1)}, u32[]{:S(2)}, u32[]{:S(2)}) %collective-permute-start.14) | collective-permute-done | bytes 147488 | tf_op jit(solution)/shard_map/ppermute | solution.py:107
  95.9 2.3 %collective-permute-done.16 = f32[9,32,128]{2,1,0:T(8,128)S(1)} collective-permute-done((f32[9,32,128]{2,1,0:T(8,128)S(1)}, f32[9,32,128]{2,1,0:T(8,128)S(1)}, u32[]{:S(2)}, u32[]{:S(2)}) %collective-permute-start.16) | collective-permute-done | bytes 147488 | tf_op jit(solution)/shard_map/ppermute | solution.py:107
  99.0 4.6 %collective-permute-done.17 = f32[9,32,128]{2,1,0:T(8,128)S(1)} collective-permute-done((f32[9,32,128]{2,1,0:T(8,128)S(1)}, f32[9,32,128]{2,1,0:T(8,128)S(1)}, u32[]{:S(2)}, u32[]{:S(2)}) %collective-permute-start.17) | collective-permute-done | bytes 147488 | tf_op jit(solution)/shard_map/ppermute | solution.py:118
  103.6 1.5 %collective-permute-start.18 = (f32[9,32,256]{2,1,0:T(8,128)S(1)}, f32[9,32,256]{2,1,0:T(8,128)S(1)}, u32[]{:S(2)}, u32[]{:S(2)}) collective-permute-start(f32[9,32,256]{2,1,0:T(8,128)S(1)} %pad_maximum_fusion.3), channel_id=1, source_target_pairs={{0,2},{1,5},{2,0},{3,7},{4,6},{5,1},{6,4},{7,3},{8,10},{9,13},{10,... | collective-permute-start | bytes 884744 | tf_op jit(solution)/shard_map/ppermute | solution.py:118
  105.1 5.3 %collective-permute-done.18 = f32[9,32,256]{2,1,0:T(8,128)S(1)} collective-permute-done((f32[9,32,256]{2,1,0:T(8,128)S(1)}, f32[9,32,256]{2,1,0:T(8,128)S(1)}, u32[]{:S(2)}, u32[]{:S(2)}) %collective-permute-start.18) | collective-permute-done | bytes 294944 | tf_op jit(solution)/shard_map/ppermute | solution.py:118
  110.6 2.0 %collective-permute-done.19 = f32[9,32,512]{2,1,0:T(8,128)S(1)} collective-permute-done((f32[9,32,512]{2,1,0:T(8,128)S(1)}, f32[9,32,512]{2,1,0:T(8,128)S(1)}, u32[]{:S(2)}, u32[]{:S(2)}) %collective-permute-start.19) | collective-permute-done | bytes 589856 | tf_op jit(solution)/shard_map/ppermute | solution.py:118
  112.7 2.2 %multiply_add_fusion = (f32[4,64,1024]{2,1,0:T(8,128)}, f32[1,4,64,1024]{3,2,1,0:T(8,128)}) fusion(f32[4,64,1024]{2,1,0:T(8,128)S(1)} %copy-done.3, f32[4]{0:T(128)S(1)} %convolution_bitcast_fusion, f32[1,4,64,1024]{3,2,1,0:T(8,128)S(1)} %copy-done.1, bf16[1,4,64,1024]{3,2,1,0:T(8,128)(2,1)S(1)} %copy-done.2, f32[4,64,32]{1,2,0:T(8,128)S(1)} %fusion.50, ...), kind=kOutput, calls=%fused_computation.12 | convolution fusion | flops 52166656 | bytes 5275664 | tf_op jit(solution)/shard_map/tks,tsd->tkd/dot_general | solution.py:180
  (89 shorter events, 12.0 us)
Async XLA Ops:
  0.6 10.2 %copy-start = (f32[4]{0:T(128)S(1)}, f32[4]{0:T(128)}, u32[]{:S(2)}) copy-start(f32[4]{0:T(128)} %param.15) | copy-start | bytes 52
  0.6 5.1 %copy-start.1 = (f32[1,4,64,1024]{3,2,1,0:T(8,128)S(1)}, f32[1,4,64,1024]{3,2,1,0:T(8,128)}, u32[]{:S(2)}) copy-start(f32[1,4,64,1024]{3,2,1,0:T(8,128)} %param.11) | copy-start | bytes 3145732
  5.8 1.8 %copy-start.5 = (f32[1,5,1024]{2,0,1:T(1,128)S(1)}, f32[1,5,1024]{2,0,1:T(1,128)}, u32[]{:S(2)}) copy-start(f32[1,5,1024]{2,0,1:T(1,128)} %param.18) | copy-start | bytes 61444
  5.8 4.9 %copy-start.4 = (f32[3,9,32,32]{3,2,1,0:T(8,128)S(1)}, f32[3,9,32,32]{3,2,1,0:T(8,128)}, u32[]{:S(2)}) copy-start(f32[3,9,32,32]{3,2,1,0:T(8,128)} %param.17) | copy-start | bytes 331780
  7.5 3.3 %copy-start.7 = (s32[9]{0:T(128)S(1)}, s32[9]{0:T(128)}, u32[]{:S(2)}) copy-start(s32[9]{0:T(128)} %param.14) | copy-start | bytes 112
  7.5 3.5 %copy-start.8 = (s32[4]{0:T(128)S(1)}, s32[4]{0:T(128)}, u32[]{:S(2)}) copy-start(s32[4]{0:T(128)} %param.13) | copy-start | bytes 52
  7.6 5.3 %copy-start.6 = (f32[5,1024]{1,0:T(8,128)S(1)}, f32[5,1024]{1,0:T(8,128)}, u32[]{:S(2)}) copy-start(f32[5,1024]{1,0:T(8,128)} %param.19) | copy-start | bytes 61444
  7.6 6.3 %copy-start.2 = (bf16[1,4,64,1024]{3,2,1,0:T(8,128)(2,1)S(1)}, bf16[1,4,64,1024]{3,2,1,0:T(8,128)(2,1)}, u32[]{:S(2)}) copy-start(bf16[1,4,64,1024]{3,2,1,0:T(8,128)(2,1)} %param.10) | copy-start | bytes 1572868
  7.7 5.1 %collective-permute-start = (f32[13312]{0:T(1024)S(1)}, f32[13312]{0:T(1024)S(1)}, u32[]{:S(2)}, u32[]{:S(2)}) collective-permute-start(f32[13312]{0:T(1024)S(1)} %pad_maximum_fusion.10), channel_id=1, source_target_pairs={{0,16},{16,0},{1,17},{17,1},{2,18},{18,2},{3,19},{19,3},{4,20},{20... | collective-permute-start | bytes 159752 | tf_op jit(solution)/shard_map/ppermute | solution.py:21
  14.7 2.2 %collective-permute-start.1 = (f32[9,32,512]{2,1,0:T(8,128)S(1)}, f32[9,32,512]{2,1,0:T(8,128)}, u32[]{:S(2)}, u32[]{:S(2)}) collective-permute-start(f32[9,32,512]{2,1,0:T(8,128)S(1)} %constant_dynamic-slice_fusion.13), channel_id=1, source_target_pairs={{0,1},{1,0},{2,3},{3,2},{4,5},{5,4},{6,7},{7,6},{8,9},{9,8},{10,11... | collective-permute-start | bytes 1769480 | tf_op jit(solution)/shard_map/ppermute | solution.py:94
  18.1 6.8 %collective-permute-start.2 = (f32[9,32,256]{2,1,0:T(8,128)S(1)}, f32[9,32,256]{2,1,0:T(8,128)S(1)}, u32[]{:S(2)}, u32[]{:S(2)}) collective-permute-start(f32[9,32,256]{2,1,0:T(8,128)S(1)} %constant_dynamic-slice_fusion.12), channel_id=1, source_target_pairs={{0,2},{1,5},{2,0},{3,7},{4,6},{5,1},{6,4},{7,3},{8,10},{9,13},{10,... | collective-permute-start | bytes 884744 | tf_op jit(solution)/shard_map/ppermute | solution.py:94
  25.0 5.3 %collective-permute-start.3 = (f32[9,32,128]{2,1,0:T(8,128)S(1)}, f32[9,32,128]{2,1,0:T(8,128)S(1)}, u32[]{:S(2)}, u32[]{:S(2)}) collective-permute-start(f32[9,32,128]{2,1,0:T(8,128)S(1)} %constant_dynamic-slice_fusion.11), channel_id=1, source_target_pairs={{0,4},{1,3},{2,6},{3,1},{4,0},{5,7},{6,2},{7,5},{8,12},{9,11},{10,... | collective-permute-start | bytes 442376 | tf_op jit(solution)/shard_map/ppermute | solution.py:94
  30.3 13.9 %collective-permute-start.4 = (f32[9,32,128]{2,1,0:T(8,128)S(1)}, f32[9,32,128]{2,1,0:T(8,128)S(1)}, u32[]{:S(2)}, u32[]{:S(2)}) collective-permute-start(f32[9,32,128]{2,1,0:T(8,128)S(1)} %dynamic-slice_add_fusion.5), channel_id=1, source_target_pairs={{0,8},{1,17},{2,10},{3,19},{4,12},{5,21},{6,14},{7,23},{8,0},{9,25... | collective-permute-start | bytes 442376 | tf_op jit(solution)/shard_map/ppermute | solution.py:107
  33.4 10.9 %collective-permute-start.5 = (f32[9,32,128]{2,1,0:T(8,128)S(1)}, f32[9,32,128]{2,1,0:T(8,128)S(1)}, u32[]{:S(2)}, u32[]{:S(2)}) collective-permute-start(f32[9,32,128]{2,1,0:T(8,128)S(1)} %dynamic-slice_add_fusion.5), channel_id=1, source_target_pairs={{0,16},{1,9},{2,18},{3,11},{4,20},{5,13},{6,22},{7,15},{8,24},{9,1... | collective-permute-start | bytes 442376 | tf_op jit(solution)/shard_map/ppermute | solution.py:107
  34.9 11.5 %collective-permute-start.6 = (f32[9,32,128]{2,1,0:T(8,128)S(1)}, f32[9,32,128]{2,1,0:T(8,128)S(1)}, u32[]{:S(2)}, u32[]{:S(2)}) collective-permute-start(f32[9,32,128]{2,1,0:T(8,128)S(1)} %dynamic-slice_add_fusion.5), channel_id=1, source_target_pairs={{0,24},{1,25},{2,26},{3,27},{4,28},{5,29},{6,30},{7,31},{8,16},{9,... | collective-permute-start | bytes 442376 | tf_op jit(solution)/shard_map/ppermute | solution.py:107
  46.5 5.2 %collective-permute-start.7 = (f32[9,32,128]{2,1,0:T(8,128)S(1)}, f32[9,32,128]{2,1,0:T(8,128)S(1)}, u32[]{:S(2)}, u32[]{:S(2)}) collective-permute-start(f32[9,32,128]{2,1,0:T(8,128)S(1)} %select_add_fusion.1), channel_id=1, source_target_pairs={{0,4},{1,3},{2,6},{3,1},{4,0},{5,7},{6,2},{7,5},{8,12},{9,11},{10,... | collective-permute-start | bytes 442376 | tf_op jit(solution)/shard_map/ppermute | solution.py:118
  51.7 6.8 %collective-permute-start.8 = (f32[9,32,256]{2,1,0:T(8,128)S(1)}, f32[9,32,256]{2,1,0:T(8,128)S(1)}, u32[]{:S(2)}, u32[]{:S(2)}) collective-permute-start(f32[9,32,256]{2,1,0:T(8,128)S(1)} %pad_maximum_fusion.2), channel_id=1, source_target_pairs={{0,2},{1,5},{2,0},{3,7},{4,6},{5,1},{6,4},{7,3},{8,10},{9,13},{10,... | collective-permute-start | bytes 884744 | tf_op jit(solution)/shard_map/ppermute | solution.py:118
  58.6 2.2 %collective-permute-start.9 = (f32[9,32,512]{2,1,0:T(8,128)S(1)}, f32[9,32,512]{2,1,0:T(8,128)}, u32[]{:S(2)}, u32[]{:S(2)}) collective-permute-start(f32[9,32,512]{2,1,0:T(8,128)S(1)} %pad_maximum_fusion), channel_id=1, source_target_pairs={{0,1},{1,0},{2,3},{3,2},{4,5},{5,4},{6,7},{7,6},{8,9},{9,8},{10,11... | collective-permute-start | bytes 1769480 | tf_op jit(solution)/shard_map/ppermute | solution.py:118
  63.1 4.3 %collective-permute-start.10 = (f32[4,64,32]{1,2,0:T(8,128)S(1)}, f32[4,64,32]{1,2,0:T(8,128)S(1)}, u32[]{:S(2)}, u32[]{:S(2)}) collective-permute-start(f32[4,64,32]{1,2,0:T(8,128)S(1)} %fusion.2), channel_id=1, source_target_pairs={{0,16},{16,0},{1,17},{17,1},{2,18},{18,2},{3,19},{19,3},{4,20},{20... | collective-permute-start | bytes 98312 | tf_op jit(solution)/shard_map/ppermute | solution.py:21
  68.4 2.1 %collective-permute-start.11 = (f32[9,32,512]{2,1,0:T(8,128)S(1)}, f32[9,32,512]{2,1,0:T(8,128)S(1)}, u32[]{:S(2)}, u32[]{:S(2)}) collective-permute-start(f32[9,32,512]{2,1,0:T(8,128)S(1)} %constant_dynamic-slice_fusion.2), channel_id=1, source_target_pairs={{0,1},{1,0},{2,3},{3,2},{4,5},{5,4},{6,7},{7,6},{8,9},{9,8},{10,11... | collective-permute-start | bytes 1769480 | tf_op jit(solution)/shard_map/ppermute | solution.py:94
  70.6 6.8 %collective-permute-start.12 = (f32[9,32,256]{2,1,0:T(8,128)S(1)}, f32[9,32,256]{2,1,0:T(8,128)S(1)}, u32[]{:S(2)}, u32[]{:S(2)}) collective-permute-start(f32[9,32,256]{2,1,0:T(8,128)S(1)} %constant_dynamic-slice_fusion.1), channel_id=1, source_target_pairs={{0,2},{1,5},{2,0},{3,7},{4,6},{5,1},{6,4},{7,3},{8,10},{9,13},{10,... | collective-permute-start | bytes 884744 | tf_op jit(solution)/shard_map/ppermute | solution.py:94
  77.5 5.2 %collective-permute-start.13 = (f32[9,32,128]{2,1,0:T(8,128)S(1)}, f32[9,32,128]{2,1,0:T(8,128)S(1)}, u32[]{:S(2)}, u32[]{:S(2)}) collective-permute-start(f32[9,32,128]{2,1,0:T(8,128)S(1)} %constant_dynamic-slice_fusion), channel_id=1, source_target_pairs={{0,4},{1,3},{2,6},{3,1},{4,0},{5,7},{6,2},{7,5},{8,12},{9,11},{10,... | collective-permute-start | bytes 442376 | tf_op jit(solution)/shard_map/ppermute | solution.py:94
  82.7 13.2 %collective-permute-start.14 = (f32[9,32,128]{2,1,0:T(8,128)S(1)}, f32[9,32,128]{2,1,0:T(8,128)S(1)}, u32[]{:S(2)}, u32[]{:S(2)}) collective-permute-start(f32[9,32,128]{2,1,0:T(8,128)S(1)} %dynamic-slice_add_fusion.4), channel_id=1, source_target_pairs={{0,8},{1,17},{2,10},{3,19},{4,12},{5,21},{6,14},{7,23},{8,0},{9,25... | collective-permute-start | bytes 442376 | tf_op jit(solution)/shard_map/ppermute | solution.py:107
  84.7 11.2 %collective-permute-start.15 = (f32[9,32,128]{2,1,0:T(8,128)S(1)}, f32[9,32,128]{2,1,0:T(8,128)S(1)}, u32[]{:S(2)}, u32[]{:S(2)}) collective-permute-start(f32[9,32,128]{2,1,0:T(8,128)S(1)} %dynamic-slice_add_fusion.4), channel_id=1, source_target_pairs={{0,16},{1,9},{2,18},{3,11},{4,20},{5,13},{6,22},{7,15},{8,24},{9,1... | collective-permute-start | bytes 442376 | tf_op jit(solution)/shard_map/ppermute | solution.py:107
  86.2 12.1 %collective-permute-start.16 = (f32[9,32,128]{2,1,0:T(8,128)S(1)}, f32[9,32,128]{2,1,0:T(8,128)S(1)}, u32[]{:S(2)}, u32[]{:S(2)}) collective-permute-start(f32[9,32,128]{2,1,0:T(8,128)S(1)} %dynamic-slice_add_fusion.4), channel_id=1, source_target_pairs={{0,24},{1,25},{2,26},{3,27},{4,28},{5,29},{6,30},{7,31},{8,16},{9,... | collective-permute-start | bytes 442376 | tf_op jit(solution)/shard_map/ppermute | solution.py:107
  98.3 5.2 %collective-permute-start.17 = (f32[9,32,128]{2,1,0:T(8,128)S(1)}, f32[9,32,128]{2,1,0:T(8,128)S(1)}, u32[]{:S(2)}, u32[]{:S(2)}) collective-permute-start(f32[9,32,128]{2,1,0:T(8,128)S(1)} %select_add_fusion), channel_id=1, source_target_pairs={{0,4},{1,3},{2,6},{3,1},{4,0},{5,7},{6,2},{7,5},{8,12},{9,11},{10,... | collective-permute-start | bytes 442376 | tf_op jit(solution)/shard_map/ppermute | solution.py:118
  103.6 6.8 %collective-permute-start.18 = (f32[9,32,256]{2,1,0:T(8,128)S(1)}, f32[9,32,256]{2,1,0:T(8,128)S(1)}, u32[]{:S(2)}, u32[]{:S(2)}) collective-permute-start(f32[9,32,256]{2,1,0:T(8,128)S(1)} %pad_maximum_fusion.3), channel_id=1, source_target_pairs={{0,2},{1,5},{2,0},{3,7},{4,6},{5,1},{6,4},{7,3},{8,10},{9,13},{10,... | collective-permute-start | bytes 884744 | tf_op jit(solution)/shard_map/ppermute | solution.py:118
  110.5 2.2 %copy-start.3 = (f32[4,64,1024]{2,1,0:T(8,128)S(1)}, f32[4,64,1024]{2,1,0:T(8,128)}, u32[]{:S(2)}) copy-start(f32[4,64,1024]{2,1,0:T(8,128)} %param.12) | copy-start | bytes 3145732
  110.5 2.1 %collective-permute-start.19 = (f32[9,32,512]{2,1,0:T(8,128)S(1)}, f32[9,32,512]{2,1,0:T(8,128)S(1)}, u32[]{:S(2)}, u32[]{:S(2)}) collective-permute-start(f32[9,32,512]{2,1,0:T(8,128)S(1)} %pad_maximum_fusion.1), channel_id=1, source_target_pairs={{0,1},{1,0},{2,3},{3,2},{4,5},{5,4},{6,7},{7,6},{8,9},{9,8},{10,11... | collective-permute-start | bytes 1769480 | tf_op jit(solution)/shard_map/ppermute | solution.py:118

commit v16 on v15

--- a/solution.py
+++ b/solution.py
@@ -4,7 +4,6 @@
 from jax.sharding import PartitionSpec as P
 
 TOP_PRECISION = lax.Precision.HIGHEST
-WIDE_PRECISION = lax.Precision.HIGH
 
 
 def _bits(n):
@@ -148,7 +147,7 @@
     combined = gradient[0].astype(jnp.float32) + feedback[0]
     tile_rows = _scalar_rows(tile_matrix, matrix_count)
     q_tiles = _pick_rows(start_basis, tile_rows)
-    first_local = jnp.einsum("tkd,tds->tks", combined, q_tiles, precision=WIDE_PRECISION)
+    first_local = jnp.einsum("tkd,tds->tks", combined, q_tiles, precision=TOP_PRECISION)
     left_size = first_local.size
     carried = jnp.concatenate([first_local.reshape(-1), vector_grad[0].reshape(-1)])
     carried = swap_sum(carried, "rep")
@@ -167,17 +166,17 @@
         (first_left, mix_right, mix_second, new_vector_momentum, tile_scale)
     )
     first_ortho = jnp.einsum("tks,tsa->tka", first_left, mix_first, precision=TOP_PRECISION)
-    first_parts = jnp.einsum("tkd,tks->tsd", combined, first_ortho, precision=WIDE_PRECISION)
+    first_parts = jnp.einsum("tkd,tks->tsd", combined, first_ortho, precision=TOP_PRECISION)
     first_table = _scatter_rows(first_parts, tile_rows, matrix_count)
     first_rows = table_rows(first_table, tile_rows, replicas, n_own) / replicas
     right_rows = jnp.einsum("tjw,tjd->twd", mix_right, first_rows, precision=TOP_PRECISION)
-    second_local = jnp.einsum("tkd,tsd->tks", combined, right_rows, precision=WIDE_PRECISION)
+    second_local = jnp.einsum("tkd,tsd->tks", combined, right_rows, precision=TOP_PRECISION)
     second_left = swap_sum(second_local, "rep") / replicas
     second_ortho = jnp.einsum("tks,tsa->tka", second_left, mix_second, precision=TOP_PRECISION)
-    second_parts = jnp.einsum("tkd,tks->tsd", combined, second_ortho, precision=WIDE_PRECISION)
+    second_parts = jnp.einsum("tkd,tks->tsd", combined, second_ortho, precision=TOP_PRECISION)
     second_table = _scatter_rows(second_parts, tile_rows, matrix_count)
     back_rows = table_rows(second_table, tile_rows, replicas, n_own) / replicas
-    approximation = jnp.einsum("tks,tsd->tkd", second_ortho, back_rows, precision=WIDE_PRECISION)
+    approximation = jnp.einsum("tks,tsd->tkd", second_ortho, back_rows, precision=TOP_PRECISION)
     new_feedback = (combined - approximation)[None]
     new_momentum = 0.9 * momentum + tile_scale[:, None, None] * approximation
     return (new_feedback, new_momentum, new_vector_momentum)

time: 115 us -> 117 us (1.017)
  matrix products: 6.88 us -> 8.87 us
    dot_general x5, matrix products: 5.24 us -> 7.23 us  [the longest x1 2.57 us: local(): jnp.einsum('tks,tsd->tkd', second_ortho, back_rows, precision=TOP_PRECISION)]
where the time goes in v16:
time: 117 us
  waiting for transfers between devices  72.6 us (62%)
  starting transfers between devices  24.4 us (21%)
  matrix products  8.87 us (8%)
  other arithmetic  4.24 us (4%)
  between operations  3.82 us (3%)
  local copies, waits for them, and re-layouts  2.89 us (2%)
    ppermute x6, waiting for transfers between devices, table_rows(): other = lax.ppermute(cur, axes, perm_of(p0, p1))  23.8 us
    ppermute x6, waiting for transfers between devices, table_rows(): held = [cur] + [lax.ppermute(cur, axes, group_perm(k)) for k in (1, 2, 3)]  22.5 us
    ppermute x6, waiting for transfers between devices, table_rows(): cur = keep + lax.ppermute(send, axes, perm_of(p0, p1))  21.8 us
    ppermute x6, starting transfers between devices, table_rows(): held = [cur] + [lax.ppermute(cur, axes, group_perm(k)) for k in (1, 2, 3)]  9.09 us
    ppermute x6, starting transfers between devices, table_rows(): cur = keep + lax.ppermute(send, axes, perm_of(p0, p1))  6.51 us
    ppermute x2, waiting for transfers between devices, swap_sum(): x = x + lax.ppermute(x, axis, _pair_perm(n, j))  4.48 us
    ppermute x2, starting transfers between devices, swap_sum(): x = x + lax.ppermute(x, axis, _pair_perm(n, j))  4.46 us
    ppermute x6, starting transfers between devices, table_rows(): other = lax.ppermute(cur, axes, perm_of(p0, p1))  4.35 us
  transfers between devices with their start and end apart: 20, of which 18 were waited for; matrix products, arithmetic and copies ran while one was open for 0% of the time, Pallas kernels for 0%

profile of v16, /device:TPU:0, one launch (start us, length us, event | category | flops | bytes accessed | tf_op | source)
XLA Modules:
  0.0 116.8 jit_solution(18352118990194064502)
XLA Ops:
  0.7 1.4 %shift-left_reduce_fusion = s32[]{:T(128)} fusion(s32[4]{0:T(128)} %param.13), kind=kLoop, calls=%fused_computation.161 | loop fusion | flops 11 | bytes 20 | tf_op jit(solution)/shard_map/reduce_sum | solution.py:48
  5.8 2.2 %fusion.6 = f32[4,64,32]{2,1,0:T(8,128)S(1)} fusion(f32[1,1024,32]{1,2,0:T(8,128)S(1)} %get-tuple-element.15, f32[1,1024,32]{1,2,0:T(8,128)S(1)} %get-tuple-element.16, f32[1,1024,32]{1,2,0:T(8,128)S(1)} %get-tuple-element.14, f32[1,1024,32]{1,2,0:T(8,128)S(1)} %get-tuple-element.13, f32[1,4,64,1024]{3,2,1,0:T(8,128)S(1)} %copy-done.1, ...), kind=kOutput, calls=%fused_computation.9 | convolution fusion | flops 101580800 | bytes 2129920 | tf_op jit(solution)/shard_map/tkd,tds->tks/dot_general | solution.py:150
  8.2 3.0 %collective-permute-start = (f32[13312]{0:T(1024)S(1)}, f32[13312]{0:T(1024)S(1)}, u32[]{:S(2)}, u32[]{:S(2)}) collective-permute-start(f32[13312]{0:T(1024)S(1)} %pad_maximum_fusion.10), channel_id=1, source_target_pairs={{0,16},{16,0},{1,17},{17,1},{2,18},{18,2},{3,19},{19,3},{4,20},{20... | collective-permute-start | bytes 159752 | tf_op jit(solution)/shard_map/ppermute | solution.py:20
  11.8 1.6 %collective-permute-done = f32[13312]{0:T(1024)S(1)} collective-permute-done((f32[13312]{0:T(1024)S(1)}, f32[13312]{0:T(1024)S(1)}, u32[]{:S(2)}, u32[]{:S(2)}) %collective-permute-start) | collective-permute-done | bytes 53280 | tf_op jit(solution)/shard_map/ppermute | solution.py:20
  15.6 2.1 %collective-permute-done.1 = f32[9,32,512]{2,1,0:T(8,128)} collective-permute-done((f32[9,32,512]{2,1,0:T(8,128)S(1)}, f32[9,32,512]{2,1,0:T(8,128)}, u32[]{:S(2)}, u32[]{:S(2)}) %collective-permute-start.1) | collective-permute-done | bytes 589856 | tf_op jit(solution)/shard_map/ppermute | solution.py:93
  18.9 2.1 %collective-permute-start.2 = (f32[9,32,256]{2,1,0:T(8,128)S(1)}, f32[9,32,256]{2,1,0:T(8,128)S(1)}, u32[]{:S(2)}, u32[]{:S(2)}) collective-permute-start(f32[9,32,256]{2,1,0:T(8,128)S(1)} %constant_dynamic-slice_fusion.12), channel_id=1, source_target_pairs={{0,2},{1,5},{2,0},{3,7},{4,6},{5,1},{6,4},{7,3},{8,10},{9,13},{10,... | collective-permute-start | bytes 884744 | tf_op jit(solution)/shard_map/ppermute | solution.py:93
  21.0 4.7 %collective-permute-done.2 = f32[9,32,256]{2,1,0:T(8,128)S(1)} collective-permute-done((f32[9,32,256]{2,1,0:T(8,128)S(1)}, f32[9,32,256]{2,1,0:T(8,128)S(1)}, u32[]{:S(2)}, u32[]{:S(2)}) %collective-permute-start.2) | collective-permute-done | bytes 294944 | tf_op jit(solution)/shard_map/ppermute | solution.py:93
  25.8 2.1 %collective-permute-start.3 = (f32[9,32,128]{2,1,0:T(8,128)S(1)}, f32[9,32,128]{2,1,0:T(8,128)S(1)}, u32[]{:S(2)}, u32[]{:S(2)}) collective-permute-start(f32[9,32,128]{2,1,0:T(8,128)S(1)} %constant_dynamic-slice_fusion.11), channel_id=1, source_target_pairs={{0,4},{1,3},{2,6},{3,1},{4,0},{5,7},{6,2},{7,5},{8,12},{9,11},{10,... | collective-permute-start | bytes 442376 | tf_op jit(solution)/shard_map/ppermute | solution.py:93
  27.9 3.1 %collective-permute-done.3 = f32[9,32,128]{2,1,0:T(8,128)S(1)} collective-permute-done((f32[9,32,128]{2,1,0:T(8,128)S(1)}, f32[9,32,128]{2,1,0:T(8,128)S(1)}, u32[]{:S(2)}, u32[]{:S(2)}) %collective-permute-start.3) | collective-permute-done | bytes 147488 | tf_op jit(solution)/shard_map/ppermute | solution.py:93
  31.1 3.1 %collective-permute-start.4 = (f32[9,32,128]{2,1,0:T(8,128)S(1)}, f32[9,32,128]{2,1,0:T(8,128)S(1)}, u32[]{:S(2)}, u32[]{:S(2)}) collective-permute-start(f32[9,32,128]{2,1,0:T(8,128)S(1)} %dynamic-slice_add_fusion.5), channel_id=1, source_target_pairs={{0,8},{1,17},{2,10},{3,19},{4,12},{5,21},{6,14},{7,23},{8,0},{9,25... | collective-permute-start | bytes 442376 | tf_op jit(solution)/shard_map/ppermute | solution.py:106
  34.2 1.5 %collective-permute-start.5 = (f32[9,32,128]{2,1,0:T(8,128)S(1)}, f32[9,32,128]{2,1,0:T(8,128)S(1)}, u32[]{:S(2)}, u32[]{:S(2)}) collective-permute-start(f32[9,32,128]{2,1,0:T(8,128)S(1)} %dynamic-slice_add_fusion.5), channel_id=1, source_target_pairs={{0,16},{1,9},{2,18},{3,11},{4,20},{5,13},{6,22},{7,15},{8,24},{9,1... | collective-permute-start | bytes 442376 | tf_op jit(solution)/shard_map/ppermute | solution.py:106
  35.7 9.3 %collective-permute-done.4 = f32[9,32,128]{2,1,0:T(8,128)S(1)} collective-permute-done((f32[9,32,128]{2,1,0:T(8,128)S(1)}, f32[9,32,128]{2,1,0:T(8,128)S(1)}, u32[]{:S(2)}, u32[]{:S(2)}) %collective-permute-start.4) | collective-permute-done | bytes 147488 | tf_op jit(solution)/shard_map/ppermute | solution.py:106
  45.0 2.1 %collective-permute-done.6 = f32[9,32,128]{2,1,0:T(8,128)S(1)} collective-permute-done((f32[9,32,128]{2,1,0:T(8,128)S(1)}, f32[9,32,128]{2,1,0:T(8,128)S(1)}, u32[]{:S(2)}, u32[]{:S(2)}) %collective-permute-start.6) | collective-permute-done | bytes 147488 | tf_op jit(solution)/shard_map/ppermute | solution.py:106
  47.9 4.6 %collective-permute-done.7 = f32[9,32,128]{2,1,0:T(8,128)S(1)} collective-permute-done((f32[9,32,128]{2,1,0:T(8,128)S(1)}, f32[9,32,128]{2,1,0:T(8,128)S(1)}, u32[]{:S(2)}, u32[]{:S(2)}) %collective-permute-start.7) | collective-permute-done | bytes 147488 | tf_op jit(solution)/shard_map/ppermute | solution.py:117
  52.5 1.5 %collective-permute-start.8 = (f32[9,32,256]{2,1,0:T(8,128)S(1)}, f32[9,32,256]{2,1,0:T(8,128)S(1)}, u32[]{:S(2)}, u32[]{:S(2)}) collective-permute-start(f32[9,32,256]{2,1,0:T(8,128)S(1)} %pad_maximum_fusion.2), channel_id=1, source_target_pairs={{0,2},{1,5},{2,0},{3,7},{4,6},{5,1},{6,4},{7,3},{8,10},{9,13},{10,... | collective-permute-start | bytes 884744 | tf_op jit(solution)/shard_map/ppermute | solution.py:117
  54.0 5.3 %collective-permute-done.8 = f32[9,32,256]{2,1,0:T(8,128)S(1)} collective-permute-done((f32[9,32,256]{2,1,0:T(8,128)S(1)}, f32[9,32,256]{2,1,0:T(8,128)S(1)}, u32[]{:S(2)}, u32[]{:S(2)}) %collective-permute-start.8) | collective-permute-done | bytes 294944 | tf_op jit(solution)/shard_map/ppermute | solution.py:117
  59.6 2.1 %collective-permute-done.9 = f32[9,32,512]{2,1,0:T(8,128)} collective-permute-done((f32[9,32,512]{2,1,0:T(8,128)S(1)}, f32[9,32,512]{2,1,0:T(8,128)}, u32[]{:S(2)}, u32[]{:S(2)}) %collective-permute-start.9) | collective-permute-done | bytes 589856 | tf_op jit(solution)/shard_map/ppermute | solution.py:117
  64.4 1.4 %collective-permute-start.10 = (f32[4,64,32]{1,2,0:T(8,128)S(1)}, f32[4,64,32]{1,2,0:T(8,128)S(1)}, u32[]{:S(2)}, u32[]{:S(2)}) collective-permute-start(f32[4,64,32]{1,2,0:T(8,128)S(1)} %fusion.2), channel_id=1, source_target_pairs={{0,16},{16,0},{1,17},{17,1},{2,18},{18,2},{3,19},{19,3},{4,20},{20... | collective-permute-start | bytes 98312 | tf_op jit(solution)/shard_map/ppermute | solution.py:20
  65.8 2.9 %collective-permute-done.10 = f32[4,64,32]{1,2,0:T(8,128)S(1)} collective-permute-done((f32[4,64,32]{1,2,0:T(8,128)S(1)}, f32[4,64,32]{1,2,0:T(8,128)S(1)}, u32[]{:S(2)}, u32[]{:S(2)}) %collective-permute-start.10) | collective-permute-done | bytes 32800 | tf_op jit(solution)/shard_map/ppermute | solution.py:20
  70.1 2.0 %collective-permute-done.11 = f32[9,32,512]{2,1,0:T(8,128)S(1)} collective-permute-done((f32[9,32,512]{2,1,0:T(8,128)S(1)}, f32[9,32,512]{2,1,0:T(8,128)S(1)}, u32[]{:S(2)}, u32[]{:S(2)}) %collective-permute-start.11) | collective-permute-done | bytes 589856 | tf_op jit(solution)/shard_map/ppermute | solution.py:93
  72.2 1.5 %collective-permute-start.12 = (f32[9,32,256]{2,1,0:T(8,128)S(1)}, f32[9,32,256]{2,1,0:T(8,128)S(1)}, u32[]{:S(2)}, u32[]{:S(2)}) collective-permute-start(f32[9,32,256]{2,1,0:T(8,128)S(1)} %constant_dynamic-slice_fusion.1), channel_id=1, source_target_pairs={{0,2},{1,5},{2,0},{3,7},{4,6},{5,1},{6,4},{7,3},{8,10},{9,13},{10,... | collective-permute-start | bytes 884744 | tf_op jit(solution)/shard_map/ppermute | solution.py:93
  73.7 5.3 %collective-permute-done.12 = f32[9,32,256]{2,1,0:T(8,128)S(1)} collective-permute-done((f32[9,32,256]{2,1,0:T(8,128)S(1)}, f32[9,32,256]{2,1,0:T(8,128)S(1)}, u32[]{:S(2)}, u32[]{:S(2)}) %collective-permute-start.12) | collective-permute-done | bytes 294944 | tf_op jit(solution)/shard_map/ppermute | solution.py:93
  79.7 4.6 %collective-permute-done.13 = f32[9,32,128]{2,1,0:T(8,128)S(1)} collective-permute-done((f32[9,32,128]{2,1,0:T(8,128)S(1)}, f32[9,32,128]{2,1,0:T(8,128)S(1)}, u32[]{:S(2)}, u32[]{:S(2)}) %collective-permute-start.13) | collective-permute-done | bytes 147488 | tf_op jit(solution)/shard_map/ppermute | solution.py:93
  84.3 2.0 %collective-permute-start.14 = (f32[9,32,128]{2,1,0:T(8,128)S(1)}, f32[9,32,128]{2,1,0:T(8,128)S(1)}, u32[]{:S(2)}, u32[]{:S(2)}) collective-permute-start(f32[9,32,128]{2,1,0:T(8,128)S(1)} %dynamic-slice_add_fusion.4), channel_id=1, source_target_pairs={{0,8},{1,17},{2,10},{3,19},{4,12},{5,21},{6,14},{7,23},{8,0},{9,25... | collective-permute-start | bytes 442376 | tf_op jit(solution)/shard_map/ppermute | solution.py:106
  86.3 1.5 %collective-permute-start.15 = (f32[9,32,128]{2,1,0:T(8,128)S(1)}, f32[9,32,128]{2,1,0:T(8,128)S(1)}, u32[]{:S(2)}, u32[]{:S(2)}) collective-permute-start(f32[9,32,128]{2,1,0:T(8,128)S(1)} %dynamic-slice_add_fusion.4), channel_id=1, source_target_pairs={{0,16},{1,9},{2,18},{3,11},{4,20},{5,13},{6,22},{7,15},{8,24},{9,1... | collective-permute-start | bytes 442376 | tf_op jit(solution)/shard_map/ppermute | solution.py:106
  88.8 8.8 %collective-permute-done.14 = f32[9,32,128]{2,1,0:T(8,128)S(1)} collective-permute-done((f32[9,32,128]{2,1,0:T(8,128)S(1)}, f32[9,32,128]{2,1,0:T(8,128)S(1)}, u32[]{:S(2)}, u32[]{:S(2)}) %collective-permute-start.14) | collective-permute-done | bytes 147488 | tf_op jit(solution)/shard_map/ppermute | solution.py:106
  97.5 2.3 %collective-permute-done.16 = f32[9,32,128]{2,1,0:T(8,128)S(1)} collective-permute-done((f32[9,32,128]{2,1,0:T(8,128)S(1)}, f32[9,32,128]{2,1,0:T(8,128)S(1)}, u32[]{:S(2)}, u32[]{:S(2)}) %collective-permute-start.16) | collective-permute-done | bytes 147488 | tf_op jit(solution)/shard_map/ppermute | solution.py:106
  100.6 4.5 %collective-permute-done.17 = f32[9,32,128]{2,1,0:T(8,128)S(1)} collective-permute-done((f32[9,32,128]{2,1,0:T(8,128)S(1)}, f32[9,32,128]{2,1,0:T(8,128)S(1)}, u32[]{:S(2)}, u32[]{:S(2)}) %collective-permute-start.17) | collective-permute-done | bytes 147488 | tf_op jit(solution)/shard_map/ppermute | solution.py:117
  105.2 1.5 %collective-permute-start.18 = (f32[9,32,256]{2,1,0:T(8,128)S(1)}, f32[9,32,256]{2,1,0:T(8,128)S(1)}, u32[]{:S(2)}, u32[]{:S(2)}) collective-permute-start(f32[9,32,256]{2,1,0:T(8,128)S(1)} %pad_maximum_fusion.3), channel_id=1, source_target_pairs={{0,2},{1,5},{2,0},{3,7},{4,6},{5,1},{6,4},{7,3},{8,10},{9,13},{10,... | collective-permute-start | bytes 884744 | tf_op jit(solution)/shard_map/ppermute | solution.py:117
  106.6 5.3 %collective-permute-done.18 = f32[9,32,256]{2,1,0:T(8,128)S(1)} collective-permute-done((f32[9,32,256]{2,1,0:T(8,128)S(1)}, f32[9,32,256]{2,1,0:T(8,128)S(1)}, u32[]{:S(2)}, u32[]{:S(2)}) %collective-permute-start.18) | collective-permute-done | bytes 294944 | tf_op jit(solution)/shard_map/ppermute | solution.py:117
  112.2 2.0 %collective-permute-done.19 = f32[9,32,512]{2,1,0:T(8,128)S(1)} collective-permute-done((f32[9,32,512]{2,1,0:T(8,128)S(1)}, f32[9,32,512]{2,1,0:T(8,128)S(1)}, u32[]{:S(2)}, u32[]{:S(2)}) %collective-permute-start.19) | collective-permute-done | bytes 589856 | tf_op jit(solution)/shard_map/ppermute | solution.py:117
  114.3 2.6 %multiply_add_fusion = (f32[4,64,1024]{2,1,0:T(8,128)}, f32[1,4,64,1024]{3,2,1,0:T(8,128)}) fusion(f32[4,64,1024]{2,1,0:T(8,128)S(1)} %copy-done.3, f32[4]{0:T(128)S(1)} %convolution_bitcast_fusion, f32[1,4,64,1024]{3,2,1,0:T(8,128)S(1)} %copy-done.1, bf16[1,4,64,1024]{3,2,1,0:T(8,128)(2,1)S(1)} %copy-done.2, f32[4,64,32]{1,2,0:T(8,128)S(1)} %fusion.50, ...), kind=kOutput, calls=%fused_computation.12 | convolution fusion | flops 102498304 | bytes 5275664 | tf_op jit(solution)/shard_map/tks,tsd->tkd/dot_general | solution.py:179
  (89 shorter events, 13.1 us)
Async XLA Ops:
  0.6 10.7 %copy-start = (f32[4]{0:T(128)S(1)}, f32[4]{0:T(128)}, u32[]{:S(2)}) copy-start(f32[4]{0:T(128)} %param.15) | copy-start | bytes 52
  0.6 5.1 %copy-start.1 = (f32[1,4,64,1024]{3,2,1,0:T(8,128)S(1)}, f32[1,4,64,1024]{3,2,1,0:T(8,128)}, u32[]{:S(2)}) copy-start(f32[1,4,64,1024]{3,2,1,0:T(8,128)} %param.11) | copy-start | bytes 3145732
  5.8 2.4 %copy-start.5 = (f32[1,5,1024]{2,0,1:T(1,128)S(1)}, f32[1,5,1024]{2,0,1:T(1,128)}, u32[]{:S(2)}) copy-start(f32[1,5,1024]{2,0,1:T(1,128)} %param.18) | copy-start | bytes 61444
  5.8 5.4 %copy-start.4 = (f32[3,9,32,32]{3,2,1,0:T(8,128)S(1)}, f32[3,9,32,32]{3,2,1,0:T(8,128)}, u32[]{:S(2)}) copy-start(f32[3,9,32,32]{3,2,1,0:T(8,128)} %param.17) | copy-start | bytes 331780
  8.0 3.3 %copy-start.7 = (s32[9]{0:T(128)S(1)}, s32[9]{0:T(128)}, u32[]{:S(2)}) copy-start(s32[9]{0:T(128)} %param.14) | copy-start | bytes 112
  8.0 3.5 %copy-start.8 = (s32[4]{0:T(128)S(1)}, s32[4]{0:T(128)}, u32[]{:S(2)}) copy-start(s32[4]{0:T(128)} %param.13) | copy-start | bytes 52
  8.1 5.3 %copy-start.6 = (f32[5,1024]{1,0:T(8,128)S(1)}, f32[5,1024]{1,0:T(8,128)}, u32[]{:S(2)}) copy-start(f32[5,1024]{1,0:T(8,128)} %param.19) | copy-start | bytes 61444
  8.2 6.3 %copy-start.2 = (bf16[1,4,64,1024]{3,2,1,0:T(8,128)(2,1)S(1)}, bf16[1,4,64,1024]{3,2,1,0:T(8,128)(2,1)}, u32[]{:S(2)}) copy-start(bf16[1,4,64,1024]{3,2,1,0:T(8,128)(2,1)} %param.10) | copy-start | bytes 1572868
  8.2 5.1 %collective-permute-start = (f32[13312]{0:T(1024)S(1)}, f32[13312]{0:T(1024)S(1)}, u32[]{:S(2)}, u32[]{:S(2)}) collective-permute-start(f32[13312]{0:T(1024)S(1)} %pad_maximum_fusion.10), channel_id=1, source_target_pairs={{0,16},{16,0},{1,17},{17,1},{2,18},{18,2},{3,19},{19,3},{4,20},{20... | collective-permute-start | bytes 159752 | tf_op jit(solution)/shard_map/ppermute | solution.py:20
  15.5 2.2 %collective-permute-start.1 = (f32[9,32,512]{2,1,0:T(8,128)S(1)}, f32[9,32,512]{2,1,0:T(8,128)}, u32[]{:S(2)}, u32[]{:S(2)}) collective-permute-start(f32[9,32,512]{2,1,0:T(8,128)S(1)} %constant_dynamic-slice_fusion.13), channel_id=1, source_target_pairs={{0,1},{1,0},{2,3},{3,2},{4,5},{5,4},{6,7},{7,6},{8,9},{9,8},{10,11... | collective-permute-start | bytes 1769480 | tf_op jit(solution)/shard_map/ppermute | solution.py:93
  18.9 6.8 %collective-permute-start.2 = (f32[9,32,256]{2,1,0:T(8,128)S(1)}, f32[9,32,256]{2,1,0:T(8,128)S(1)}, u32[]{:S(2)}, u32[]{:S(2)}) collective-permute-start(f32[9,32,256]{2,1,0:T(8,128)S(1)} %constant_dynamic-slice_fusion.12), channel_id=1, source_target_pairs={{0,2},{1,5},{2,0},{3,7},{4,6},{5,1},{6,4},{7,3},{8,10},{9,13},{10,... | collective-permute-start | bytes 884744 | tf_op jit(solution)/shard_map/ppermute | solution.py:93
  25.8 5.3 %collective-permute-start.3 = (f32[9,32,128]{2,1,0:T(8,128)S(1)}, f32[9,32,128]{2,1,0:T(8,128)S(1)}, u32[]{:S(2)}, u32[]{:S(2)}) collective-permute-start(f32[9,32,128]{2,1,0:T(8,128)S(1)} %constant_dynamic-slice_fusion.11), channel_id=1, source_target_pairs={{0,4},{1,3},{2,6},{3,1},{4,0},{5,7},{6,2},{7,5},{8,12},{9,11},{10,... | collective-permute-start | bytes 442376 | tf_op jit(solution)/shard_map/ppermute | solution.py:93
  31.1 13.9 %collective-permute-start.4 = (f32[9,32,128]{2,1,0:T(8,128)S(1)}, f32[9,32,128]{2,1,0:T(8,128)S(1)}, u32[]{:S(2)}, u32[]{:S(2)}) collective-permute-start(f32[9,32,128]{2,1,0:T(8,128)S(1)} %dynamic-slice_add_fusion.5), channel_id=1, source_target_pairs={{0,8},{1,17},{2,10},{3,19},{4,12},{5,21},{6,14},{7,23},{8,0},{9,25... | collective-permute-start | bytes 442376 | tf_op jit(solution)/shard_map/ppermute | solution.py:106
  34.2 10.9 %collective-permute-start.5 = (f32[9,32,128]{2,1,0:T(8,128)S(1)}, f32[9,32,128]{2,1,0:T(8,128)S(1)}, u32[]{:S(2)}, u32[]{:S(2)}) collective-permute-start(f32[9,32,128]{2,1,0:T(8,128)S(1)} %dynamic-slice_add_fusion.5), channel_id=1, source_target_pairs={{0,16},{1,9},{2,18},{3,11},{4,20},{5,13},{6,22},{7,15},{8,24},{9,1... | collective-permute-start | bytes 442376 | tf_op jit(solution)/shard_map/ppermute | solution.py:106
  35.7 11.5 %collective-permute-start.6 = (f32[9,32,128]{2,1,0:T(8,128)S(1)}, f32[9,32,128]{2,1,0:T(8,128)S(1)}, u32[]{:S(2)}, u32[]{:S(2)}) collective-permute-start(f32[9,32,128]{2,1,0:T(8,128)S(1)} %dynamic-slice_add_fusion.5), channel_id=1, source_target_pairs={{0,24},{1,25},{2,26},{3,27},{4,28},{5,29},{6,30},{7,31},{8,16},{9,... | collective-permute-start | bytes 442376 | tf_op jit(solution)/shard_map/ppermute | solution.py:106
  47.2 5.2 %collective-permute-start.7 = (f32[9,32,128]{2,1,0:T(8,128)S(1)}, f32[9,32,128]{2,1,0:T(8,128)S(1)}, u32[]{:S(2)}, u32[]{:S(2)}) collective-permute-start(f32[9,32,128]{2,1,0:T(8,128)S(1)} %select_add_fusion.1), channel_id=1, source_target_pairs={{0,4},{1,3},{2,6},{3,1},{4,0},{5,7},{6,2},{7,5},{8,12},{9,11},{10,... | collective-permute-start | bytes 442376 | tf_op jit(solution)/shard_map/ppermute | solution.py:117
  52.5 6.8 %collective-permute-start.8 = (f32[9,32,256]{2,1,0:T(8,128)S(1)}, f32[9,32,256]{2,1,0:T(8,128)S(1)}, u32[]{:S(2)}, u32[]{:S(2)}) collective-permute-start(f32[9,32,256]{2,1,0:T(8,128)S(1)} %pad_maximum_fusion.2), channel_id=1, source_target_pairs={{0,2},{1,5},{2,0},{3,7},{4,6},{5,1},{6,4},{7,3},{8,10},{9,13},{10,... | collective-permute-start | bytes 884744 | tf_op jit(solution)/shard_map/ppermute | solution.py:117
  59.4 2.2 %collective-permute-start.9 = (f32[9,32,512]{2,1,0:T(8,128)S(1)}, f32[9,32,512]{2,1,0:T(8,128)}, u32[]{:S(2)}, u32[]{:S(2)}) collective-permute-start(f32[9,32,512]{2,1,0:T(8,128)S(1)} %pad_maximum_fusion), channel_id=1, source_target_pairs={{0,1},{1,0},{2,3},{3,2},{4,5},{5,4},{6,7},{7,6},{8,9},{9,8},{10,11... | collective-permute-start | bytes 1769480 | tf_op jit(solution)/shard_map/ppermute | solution.py:117
  64.4 4.3 %collective-permute-start.10 = (f32[4,64,32]{1,2,0:T(8,128)S(1)}, f32[4,64,32]{1,2,0:T(8,128)S(1)}, u32[]{:S(2)}, u32[]{:S(2)}) collective-permute-start(f32[4,64,32]{1,2,0:T(8,128)S(1)} %fusion.2), channel_id=1, source_target_pairs={{0,16},{16,0},{1,17},{17,1},{2,18},{18,2},{3,19},{19,3},{4,20},{20... | collective-permute-start | bytes 98312 | tf_op jit(solution)/shard_map/ppermute | solution.py:20
  70.0 2.1 %collective-permute-start.11 = (f32[9,32,512]{2,1,0:T(8,128)S(1)}, f32[9,32,512]{2,1,0:T(8,128)S(1)}, u32[]{:S(2)}, u32[]{:S(2)}) collective-permute-start(f32[9,32,512]{2,1,0:T(8,128)S(1)} %constant_dynamic-slice_fusion.2), channel_id=1, source_target_pairs={{0,1},{1,0},{2,3},{3,2},{4,5},{5,4},{6,7},{7,6},{8,9},{9,8},{10,11... | collective-permute-start | bytes 1769480 | tf_op jit(solution)/shard_map/ppermute | solution.py:93
  72.2 6.8 %collective-permute-start.12 = (f32[9,32,256]{2,1,0:T(8,128)S(1)}, f32[9,32,256]{2,1,0:T(8,128)S(1)}, u32[]{:S(2)}, u32[]{:S(2)}) collective-permute-start(f32[9,32,256]{2,1,0:T(8,128)S(1)} %constant_dynamic-slice_fusion.1), channel_id=1, source_target_pairs={{0,2},{1,5},{2,0},{3,7},{4,6},{5,1},{6,4},{7,3},{8,10},{9,13},{10,... | collective-permute-start | bytes 884744 | tf_op jit(solution)/shard_map/ppermute | solution.py:93
  79.1 5.2 %collective-permute-start.13 = (f32[9,32,128]{2,1,0:T(8,128)S(1)}, f32[9,32,128]{2,1,0:T(8,128)S(1)}, u32[]{:S(2)}, u32[]{:S(2)}) collective-permute-start(f32[9,32,128]{2,1,0:T(8,128)S(1)} %constant_dynamic-slice_fusion), channel_id=1, source_target_pairs={{0,4},{1,3},{2,6},{3,1},{4,0},{5,7},{6,2},{7,5},{8,12},{9,11},{10,... | collective-permute-start | bytes 442376 | tf_op jit(solution)/shard_map/ppermute | solution.py:93
  84.3 13.2 %collective-permute-start.14 = (f32[9,32,128]{2,1,0:T(8,128)S(1)}, f32[9,32,128]{2,1,0:T(8,128)S(1)}, u32[]{:S(2)}, u32[]{:S(2)}) collective-permute-start(f32[9,32,128]{2,1,0:T(8,128)S(1)} %dynamic-slice_add_fusion.4), channel_id=1, source_target_pairs={{0,8},{1,17},{2,10},{3,19},{4,12},{5,21},{6,14},{7,23},{8,0},{9,25... | collective-permute-start | bytes 442376 | tf_op jit(solution)/shard_map/ppermute | solution.py:106
  86.3 11.2 %collective-permute-start.15 = (f32[9,32,128]{2,1,0:T(8,128)S(1)}, f32[9,32,128]{2,1,0:T(8,128)S(1)}, u32[]{:S(2)}, u32[]{:S(2)}) collective-permute-start(f32[9,32,128]{2,1,0:T(8,128)S(1)} %dynamic-slice_add_fusion.4), channel_id=1, source_target_pairs={{0,16},{1,9},{2,18},{3,11},{4,20},{5,13},{6,22},{7,15},{8,24},{9,1... | collective-permute-start | bytes 442376 | tf_op jit(solution)/shard_map/ppermute | solution.py:106
  87.8 12.0 %collective-permute-start.16 = (f32[9,32,128]{2,1,0:T(8,128)S(1)}, f32[9,32,128]{2,1,0:T(8,128)S(1)}, u32[]{:S(2)}, u32[]{:S(2)}) collective-permute-start(f32[9,32,128]{2,1,0:T(8,128)S(1)} %dynamic-slice_add_fusion.4), channel_id=1, source_target_pairs={{0,24},{1,25},{2,26},{3,27},{4,28},{5,29},{6,30},{7,31},{8,16},{9,... | collective-permute-start | bytes 442376 | tf_op jit(solution)/shard_map/ppermute | solution.py:106
  99.9 5.2 %collective-permute-start.17 = (f32[9,32,128]{2,1,0:T(8,128)S(1)}, f32[9,32,128]{2,1,0:T(8,128)S(1)}, u32[]{:S(2)}, u32[]{:S(2)}) collective-permute-start(f32[9,32,128]{2,1,0:T(8,128)S(1)} %select_add_fusion), channel_id=1, source_target_pairs={{0,4},{1,3},{2,6},{3,1},{4,0},{5,7},{6,2},{7,5},{8,12},{9,11},{10,... | collective-permute-start | bytes 442376 | tf_op jit(solution)/shard_map/ppermute | solution.py:117
  105.2 6.8 %collective-permute-start.18 = (f32[9,32,256]{2,1,0:T(8,128)S(1)}, f32[9,32,256]{2,1,0:T(8,128)S(1)}, u32[]{:S(2)}, u32[]{:S(2)}) collective-permute-start(f32[9,32,256]{2,1,0:T(8,128)S(1)} %pad_maximum_fusion.3), channel_id=1, source_target_pairs={{0,2},{1,5},{2,0},{3,7},{4,6},{5,1},{6,4},{7,3},{8,10},{9,13},{10,... | collective-permute-start | bytes 884744 | tf_op jit(solution)/shard_map/ppermute | solution.py:117
  112.1 2.2 %copy-start.3 = (f32[4,64,1024]{2,1,0:T(8,128)S(1)}, f32[4,64,1024]{2,1,0:T(8,128)}, u32[]{:S(2)}) copy-start(f32[4,64,1024]{2,1,0:T(8,128)} %param.12) | copy-start | bytes 3145732
  112.1 2.1 %collective-permute-start.19 = (f32[9,32,512]{2,1,0:T(8,128)S(1)}, f32[9,32,512]{2,1,0:T(8,128)S(1)}, u32[]{:S(2)}, u32[]{:S(2)}) collective-permute-start(f32[9,32,512]{2,1,0:T(8,128)S(1)} %pad_maximum_fusion.1), channel_id=1, source_target_pairs={{0,1},{1,0},{2,3},{3,2},{4,5},{5,4},{6,7},{7,6},{8,9},{9,8},{10,11... | collective-permute-start | bytes 1769480 | tf_op jit(solution)/shard_map/ppermute | solution.py:117

commit v17 on v15

--- a/solution.py
+++ b/solution.py
@@ -1,6 +1,8 @@
 import jax
 import jax.numpy as jnp
 from jax import lax
+from jax.experimental import pallas as pl
+from jax.experimental.pallas import tpu as pltpu
 from jax.sharding import PartitionSpec as P
 
 TOP_PRECISION = lax.Precision.HIGHEST
@@ -38,6 +40,42 @@
         dims[axis] //= 2
         plan.append(axis)
     return plan
+
+
+def _first_kernel(rows_ref, grad_ref, feed_ref, basis_ref, out_ref):
+    summed = grad_ref[0, 0].astype(jnp.float32) + feed_ref[0, 0]
+    out_ref[0] = lax.dot_general(
+        summed,
+        basis_ref[0],
+        (((1,), (1,)), ((), ())),
+        precision=TOP_PRECISION,
+        preferred_element_type=jnp.float32,
+    )
+
+
+def first_products(tile_matrix, gradient, feedback, basis_rows):
+    tiles, rows, width = gradient.shape[1:]
+    rank = basis_rows.shape[1]
+    grid_spec = pltpu.PrefetchScalarGridSpec(
+        num_scalar_prefetch=1,
+        grid=(tiles,),
+        in_specs=[
+            pl.BlockSpec((1, 1, rows, width), lambda t, idx: (0, t, 0, 0)),
+            pl.BlockSpec((1, 1, rows, width), lambda t, idx: (0, t, 0, 0)),
+            pl.BlockSpec((1, rank, width), lambda t, idx: (idx[t], 0, 0)),
+        ],
+        out_specs=pl.BlockSpec((1, rows, rank), lambda t, idx: (t, 0, 0)),
+    )
+    return pl.pallas_call(
+        _first_kernel,
+        grid_spec=grid_spec,
+        out_shape=jax.ShapeDtypeStruct((tiles, rows, rank), jnp.float32),
+        cost_estimate=pl.CostEstimate(
+            flops=2 * tiles * rows * width * rank,
+            transcendentals=0,
+            bytes_accessed=tiles * (rows * width * 6 + rank * width * 4 + rows * rank * 4),
+        ),
+    )(tile_matrix, gradient, feedback, basis_rows)
 
 
 def _scalar_rows(rows, count):
@@ -147,8 +185,7 @@
     )
     combined = gradient[0].astype(jnp.float32) + feedback[0]
     tile_rows = _scalar_rows(tile_matrix, matrix_count)
-    q_tiles = _pick_rows(start_basis, tile_rows)
-    first_local = jnp.einsum("tkd,tds->tks", combined, q_tiles, precision=WIDE_PRECISION)
+    first_local = first_products(tile_matrix, gradient, feedback, jnp.swapaxes(start_basis, 1, 2))
     left_size = first_local.size
     carried = jnp.concatenate([first_local.reshape(-1), vector_grad[0].reshape(-1)])
     carried = swap_sum(carried, "rep")

time: 115 us -> 115 us (level)
  Pallas kernels: 0 us -> 4.87 us
  starting transfers between devices: 24.4 us -> 20.8 us
  matrix products: 6.88 us -> 5.19 us
  waiting for transfers between devices: 72.6 us -> 74 us
    pallas_call x0 -> x1, Pallas kernels: none -> 4.87 us  [first_products(): pl.pallas_call(_first_kernel, grid_spec=grid_spec, out_shape=jax.ShapeDty...]
    dot_general x1 -> x0, matrix products: 1.68 us -> none  [local(): jnp.einsum('tkd,tds->tks', combined, q_tiles, precision=WIDE_PRECISION)]
    ppermute x6, starting transfers between devices: 6.49 us -> 4.92 us  [table_rows(): cur = keep + lax.ppermute(send, axes, perm_of(p0, p1))]
    ppermute x6, waiting for transfers between devices: 21.8 us -> 23.3 us  [table_rows(): cur = keep + lax.ppermute(send, axes, perm_of(p0, p1))]
  transfers between devices with their start and end apart: 20 -> 20, of which waited for: 18 -> 17; matrix products, arithmetic and copies ran while one was open for 0% -> 1% of each run, Pallas kernels for 0% -> 0%
where the time goes in v17:
time: 115 us
  waiting for transfers between devices  74 us (64%)
  starting transfers between devices  20.8 us (18%)
  matrix products  5.19 us (5%)
  Pallas kernels  4.87 us (4%)
  between operations  3.83 us (3%)
  other arithmetic  3.53 us (3%)
  local copies, waits for them, and re-layouts  2.72 us (2%)
    ppermute x6, waiting for transfers between devices, table_rows(): other = lax.ppermute(cur, axes, perm_of(p0, p1))  24.8 us
    ppermute x6, waiting for transfers between devices, table_rows(): cur = keep + lax.ppermute(send, axes, perm_of(p0, p1))  23.3 us
    ppermute x6, waiting for transfers between devices, table_rows(): held = [cur] + [lax.ppermute(cur, axes, group_perm(k)) for k in (1, 2, 3)]  22.1 us
    ppermute x6, starting transfers between devices, table_rows(): held = [cur] + [lax.ppermute(cur, axes, group_perm(k)) for k in (1, 2, 3)]  8.9 us
    ppermute x6, starting transfers between devices, table_rows(): cur = keep + lax.ppermute(send, axes, perm_of(p0, p1))  4.92 us
    pallas_call x1, Pallas kernels, first_products(): pl.pallas_call(_first_kernel, grid_spec=grid_spec, out_shape=jax.ShapeDty...  4.87 us
    ppermute x2, waiting for transfers between devices, swap_sum(): x = x + lax.ppermute(x, axis, _pair_perm(n, j))  3.78 us
    ppermute x2, starting transfers between devices, swap_sum(): x = x + lax.ppermute(x, axis, _pair_perm(n, j))  3.57 us
  transfers between devices with their start and end apart: 20, of which 17 were waited for; matrix products, arithmetic and copies ran while one was open for 1% of the time, Pallas kernels for 0%

profile of v17, /device:TPU:0, one launch (start us, length us, event | category | flops | bytes accessed | tf_op | source)
XLA Modules:
  0.0 114.9 jit_solution(9380200124371221830)
XLA Ops:
  0.7 4.9 %shard_map.121 = f32[4,64,32]{2,1,0:T(8,128)} custom-call(s32[4]{0:T(128)} %rows_ref.1, bf16[1,4,64,1024]{3,2,1,0:T(8,128)(2,1)} %grad_ref.1, f32[1,4,64,1024]{3,2,1,0:T(8,128)} %feed_ref.1, f32[9,32,1024]{2,1,0:T(8,128)} %bitcast.54), custom_call_target="tpu_custom_call" | custom-call | flops 16777216 | bytes 2129920 | tf_op jit(solution)/shard_map/pallas_call | solution.py:69
  5.5 1.0 reshape.40
  6.6 3.0 %collective-permute-start = (f32[13312]{0:T(1024)S(1)}, f32[13312]{0:T(1024)S(1)}, u32[]{:S(2)}, u32[]{:S(2)}) collective-permute-start(f32[13312]{0:T(1024)S(1)} %pad_maximum_fusion.10), channel_id=1, source_target_pairs={{0,16},{16,0},{1,17},{17,1},{2,18},{18,2},{3,19},{19,3},{4,20},{20... | collective-permute-start | bytes 159752 | tf_op jit(solution)/shard_map/ppermute | solution.py:23
  15.4 2.1 %collective-permute-done.1 = f32[9,32,512]{2,1,0:T(8,128)} collective-permute-done((f32[9,32,512]{2,1,0:T(8,128)S(1)}, f32[9,32,512]{2,1,0:T(8,128)}, u32[]{:S(2)}, u32[]{:S(2)}) %collective-permute-start.1) | collective-permute-done | bytes 589856 | tf_op jit(solution)/shard_map/ppermute | solution.py:132
  17.5 1.2 %dynamic-slice_add_fusion.1 = f32[9,32,512]{2,1,0:T(8,128)S(1)} fusion(f32[9,32,512]{2,1,0:T(8,128)} %collective-permute-done.1, f32[9,32,1024]{2,1,0:T(8,128)S(1)} %fusion.22, s32[]{:T(128)S(6)} %select_n.342), kind=kLoop, calls=%fused_computation.31 | loop fusion | flops 147456 | bytes 1769476 | tf_op jit(solution)/shard_map/add | solution.py:132
  18.8 1.5 %collective-permute-start.2 = (f32[9,32,256]{2,1,0:T(8,128)S(1)}, f32[9,32,256]{2,1,0:T(8,128)S(1)}, u32[]{:S(2)}, u32[]{:S(2)}) collective-permute-start(f32[9,32,256]{2,1,0:T(8,128)S(1)} %constant_dynamic-slice_fusion.12), channel_id=1, source_target_pairs={{0,2},{1,5},{2,0},{3,7},{4,6},{5,1},{6,4},{7,3},{8,10},{9,13},{10,... | collective-permute-start | bytes 884744 | tf_op jit(solution)/shard_map/ppermute | solution.py:132
  20.3 5.3 %collective-permute-done.2 = f32[9,32,256]{2,1,0:T(8,128)S(1)} collective-permute-done((f32[9,32,256]{2,1,0:T(8,128)S(1)}, f32[9,32,256]{2,1,0:T(8,128)S(1)}, u32[]{:S(2)}, u32[]{:S(2)}) %collective-permute-start.2) | collective-permute-done | bytes 294944 | tf_op jit(solution)/shard_map/ppermute | solution.py:132
  25.6 1.6 %collective-permute-start.3 = (f32[9,32,128]{2,1,0:T(8,128)S(1)}, f32[9,32,128]{2,1,0:T(8,128)S(1)}, u32[]{:S(2)}, u32[]{:S(2)}) collective-permute-start(f32[9,32,128]{2,1,0:T(8,128)S(1)} %constant_dynamic-slice_fusion.11), channel_id=1, source_target_pairs={{0,4},{1,3},{2,6},{3,1},{4,0},{5,7},{6,2},{7,5},{8,12},{9,11},{10,... | collective-permute-start | bytes 442376 | tf_op jit(solution)/shard_map/ppermute | solution.py:132
  27.3 3.6 %collective-permute-done.3 = f32[9,32,128]{2,1,0:T(8,128)S(1)} collective-permute-done((f32[9,32,128]{2,1,0:T(8,128)S(1)}, f32[9,32,128]{2,1,0:T(8,128)S(1)}, u32[]{:S(2)}, u32[]{:S(2)}) %collective-permute-start.3) | collective-permute-done | bytes 147488 | tf_op jit(solution)/shard_map/ppermute | solution.py:132
  30.9 2.7 %collective-permute-start.4 = (f32[9,32,128]{2,1,0:T(8,128)S(1)}, f32[9,32,128]{2,1,0:T(8,128)S(1)}, u32[]{:S(2)}, u32[]{:S(2)}) collective-permute-start(f32[9,32,128]{2,1,0:T(8,128)S(1)} %dynamic-slice_add_fusion.5), channel_id=1, source_target_pairs={{0,8},{1,17},{2,10},{3,19},{4,12},{5,21},{6,14},{7,23},{8,0},{9,25... | collective-permute-start | bytes 442376 | tf_op jit(solution)/shard_map/ppermute | solution.py:145
  34.0 1.3 %collective-permute-start.6 = (f32[9,32,128]{2,1,0:T(8,128)S(1)}, f32[9,32,128]{2,1,0:T(8,128)S(1)}, u32[]{:S(2)}, u32[]{:S(2)}) collective-permute-start(f32[9,32,128]{2,1,0:T(8,128)S(1)} %dynamic-slice_add_fusion.5), channel_id=1, source_target_pairs={{0,24},{1,25},{2,26},{3,27},{4,28},{5,29},{6,30},{7,31},{8,16},{9,... | collective-permute-start | bytes 442376 | tf_op jit(solution)/shard_map/ppermute | solution.py:145
  35.3 8.1 %collective-permute-done.4 = f32[9,32,128]{2,1,0:T(8,128)S(1)} collective-permute-done((f32[9,32,128]{2,1,0:T(8,128)S(1)}, f32[9,32,128]{2,1,0:T(8,128)S(1)}, u32[]{:S(2)}, u32[]{:S(2)}) %collective-permute-start.4) | collective-permute-done | bytes 147488 | tf_op jit(solution)/shard_map/ppermute | solution.py:145
  43.4 3.0 %collective-permute-done.6 = f32[9,32,128]{2,1,0:T(8,128)S(1)} collective-permute-done((f32[9,32,128]{2,1,0:T(8,128)S(1)}, f32[9,32,128]{2,1,0:T(8,128)S(1)}, u32[]{:S(2)}, u32[]{:S(2)}) %collective-permute-start.6) | collective-permute-done | bytes 147488 | tf_op jit(solution)/shard_map/ppermute | solution.py:145
  46.5 5.1 %collective-permute-done.7 = f32[9,32,128]{2,1,0:T(8,128)S(1)} collective-permute-done((f32[9,32,128]{2,1,0:T(8,128)S(1)}, f32[9,32,128]{2,1,0:T(8,128)S(1)}, u32[]{:S(2)}, u32[]{:S(2)}) %collective-permute-start.7) | collective-permute-done | bytes 147488 | tf_op jit(solution)/shard_map/ppermute | solution.py:156
  51.7 1.5 %collective-permute-start.8 = (f32[9,32,256]{2,1,0:T(8,128)S(1)}, f32[9,32,256]{2,1,0:T(8,128)S(1)}, u32[]{:S(2)}, u32[]{:S(2)}) collective-permute-start(f32[9,32,256]{2,1,0:T(8,128)S(1)} %pad_maximum_fusion.2), channel_id=1, source_target_pairs={{0,2},{1,5},{2,0},{3,7},{4,6},{5,1},{6,4},{7,3},{8,10},{9,13},{10,... | collective-permute-start | bytes 884744 | tf_op jit(solution)/shard_map/ppermute | solution.py:156
  53.2 5.3 %collective-permute-done.8 = f32[9,32,256]{2,1,0:T(8,128)S(1)} collective-permute-done((f32[9,32,256]{2,1,0:T(8,128)S(1)}, f32[9,32,256]{2,1,0:T(8,128)S(1)}, u32[]{:S(2)}, u32[]{:S(2)}) %collective-permute-start.8) | collective-permute-done | bytes 294944 | tf_op jit(solution)/shard_map/ppermute | solution.py:156
  58.8 2.1 %collective-permute-done.9 = f32[9,32,512]{2,1,0:T(8,128)} collective-permute-done((f32[9,32,512]{2,1,0:T(8,128)S(1)}, f32[9,32,512]{2,1,0:T(8,128)}, u32[]{:S(2)}, u32[]{:S(2)}) %collective-permute-start.9) | collective-permute-done | bytes 589856 | tf_op jit(solution)/shard_map/ppermute | solution.py:156
  60.8 1.0 constant_dynamic-slice_fusion.6
  63.7 3.8 %collective-permute-done.10 = f32[4,64,32]{1,2,0:T(8,128)S(1)} collective-permute-done((f32[4,64,32]{1,2,0:T(8,128)S(1)}, f32[4,64,32]{1,2,0:T(8,128)S(1)}, u32[]{:S(2)}, u32[]{:S(2)}) %collective-permute-start.10) | collective-permute-done | bytes 32800 | tf_op jit(solution)/shard_map/ppermute | solution.py:23
  68.6 2.0 %collective-permute-done.11 = f32[9,32,512]{2,1,0:T(8,128)S(1)} collective-permute-done((f32[9,32,512]{2,1,0:T(8,128)S(1)}, f32[9,32,512]{2,1,0:T(8,128)S(1)}, u32[]{:S(2)}, u32[]{:S(2)}) %collective-permute-start.11) | collective-permute-done | bytes 589856 | tf_op jit(solution)/shard_map/ppermute | solution.py:132
  70.7 1.5 %collective-permute-start.12 = (f32[9,32,256]{2,1,0:T(8,128)S(1)}, f32[9,32,256]{2,1,0:T(8,128)S(1)}, u32[]{:S(2)}, u32[]{:S(2)}) collective-permute-start(f32[9,32,256]{2,1,0:T(8,128)S(1)} %constant_dynamic-slice_fusion.1), channel_id=1, source_target_pairs={{0,2},{1,5},{2,0},{3,7},{4,6},{5,1},{6,4},{7,3},{8,10},{9,13},{10,... | collective-permute-start | bytes 884744 | tf_op jit(solution)/shard_map/ppermute | solution.py:132
  72.2 5.3 %collective-permute-done.12 = f32[9,32,256]{2,1,0:T(8,128)S(1)} collective-permute-done((f32[9,32,256]{2,1,0:T(8,128)S(1)}, f32[9,32,256]{2,1,0:T(8,128)S(1)}, u32[]{:S(2)}, u32[]{:S(2)}) %collective-permute-start.12) | collective-permute-done | bytes 294944 | tf_op jit(solution)/shard_map/ppermute | solution.py:132
  77.6 5.1 %collective-permute-done.13 = f32[9,32,128]{2,1,0:T(8,128)S(1)} collective-permute-done((f32[9,32,128]{2,1,0:T(8,128)S(1)}, f32[9,32,128]{2,1,0:T(8,128)S(1)}, u32[]{:S(2)}, u32[]{:S(2)}) %collective-permute-start.13) | collective-permute-done | bytes 147488 | tf_op jit(solution)/shard_map/ppermute | solution.py:132
  82.8 2.1 %collective-permute-start.14 = (f32[9,32,128]{2,1,0:T(8,128)S(1)}, f32[9,32,128]{2,1,0:T(8,128)S(1)}, u32[]{:S(2)}, u32[]{:S(2)}) collective-permute-start(f32[9,32,128]{2,1,0:T(8,128)S(1)} %dynamic-slice_add_fusion.4), channel_id=1, source_target_pairs={{0,8},{1,17},{2,10},{3,19},{4,12},{5,21},{6,14},{7,23},{8,0},{9,25... | collective-permute-start | bytes 442376 | tf_op jit(solution)/shard_map/ppermute | solution.py:145
  85.4 1.8 %collective-permute-start.16 = (f32[9,32,128]{2,1,0:T(8,128)S(1)}, f32[9,32,128]{2,1,0:T(8,128)S(1)}, u32[]{:S(2)}, u32[]{:S(2)}) collective-permute-start(f32[9,32,128]{2,1,0:T(8,128)S(1)} %dynamic-slice_add_fusion.4), channel_id=1, source_target_pairs={{0,24},{1,25},{2,26},{3,27},{4,28},{5,29},{6,30},{7,31},{8,16},{9,... | collective-permute-start | bytes 442376 | tf_op jit(solution)/shard_map/ppermute | solution.py:145
  87.2 8.0 %collective-permute-done.14 = f32[9,32,128]{2,1,0:T(8,128)S(1)} collective-permute-done((f32[9,32,128]{2,1,0:T(8,128)S(1)}, f32[9,32,128]{2,1,0:T(8,128)S(1)}, u32[]{:S(2)}, u32[]{:S(2)}) %collective-permute-start.14) | collective-permute-done | bytes 147488 | tf_op jit(solution)/shard_map/ppermute | solution.py:145
  95.2 3.1 %collective-permute-done.16 = f32[9,32,128]{2,1,0:T(8,128)S(1)} collective-permute-done((f32[9,32,128]{2,1,0:T(8,128)S(1)}, f32[9,32,128]{2,1,0:T(8,128)S(1)}, u32[]{:S(2)}, u32[]{:S(2)}) %collective-permute-start.16) | collective-permute-done | bytes 147488 | tf_op jit(solution)/shard_map/ppermute | solution.py:145
  98.5 5.1 %collective-permute-done.17 = f32[9,32,128]{2,1,0:T(8,128)S(1)} collective-permute-done((f32[9,32,128]{2,1,0:T(8,128)S(1)}, f32[9,32,128]{2,1,0:T(8,128)S(1)}, u32[]{:S(2)}, u32[]{:S(2)}) %collective-permute-start.17) | collective-permute-done | bytes 147488 | tf_op jit(solution)/shard_map/ppermute | solution.py:156
  103.6 1.5 %collective-permute-start.18 = (f32[9,32,256]{2,1,0:T(8,128)S(1)}, f32[9,32,256]{2,1,0:T(8,128)S(1)}, u32[]{:S(2)}, u32[]{:S(2)}) collective-permute-start(f32[9,32,256]{2,1,0:T(8,128)S(1)} %pad_maximum_fusion.3), channel_id=1, source_target_pairs={{0,2},{1,5},{2,0},{3,7},{4,6},{5,1},{6,4},{7,3},{8,10},{9,13},{10,... | collective-permute-start | bytes 884744 | tf_op jit(solution)/shard_map/ppermute | solution.py:156
  105.2 5.3 %collective-permute-done.18 = f32[9,32,256]{2,1,0:T(8,128)S(1)} collective-permute-done((f32[9,32,256]{2,1,0:T(8,128)S(1)}, f32[9,32,256]{2,1,0:T(8,128)S(1)}, u32[]{:S(2)}, u32[]{:S(2)}) %collective-permute-start.18) | collective-permute-done | bytes 294944 | tf_op jit(solution)/shard_map/ppermute | solution.py:156
  110.7 2.0 %collective-permute-done.19 = f32[9,32,512]{2,1,0:T(8,128)S(1)} collective-permute-done((f32[9,32,512]{2,1,0:T(8,128)S(1)}, f32[9,32,512]{2,1,0:T(8,128)S(1)}, u32[]{:S(2)}, u32[]{:S(2)}) %collective-permute-start.19) | collective-permute-done | bytes 589856 | tf_op jit(solution)/shard_map/ppermute | solution.py:156
  112.7 2.1 %multiply_add_fusion = (f32[4,64,1024]{2,1,0:T(8,128)}, f32[1,4,64,1024]{3,2,1,0:T(8,128)}) fusion(f32[4,64,1024]{2,1,0:T(8,128)S(1)} %copy-done.3, f32[4]{0:T(128)S(1)} %convolution_bitcast_fusion, f32[1,4,64,1024]{3,2,1,0:T(8,128)S(1)} %copy-done.1, bf16[1,4,64,1024]{3,2,1,0:T(8,128)(2,1)S(1)} %copy-done.2, f32[4,64,32]{1,2,0:T(8,128)S(1)} %fusion.41, ...), kind=kOutput, calls=%fused_computation.10 | convolution fusion | flops 52166656 | bytes 5275664 | tf_op jit(solution)/shard_map/tks,tsd->tkd/dot_general | solution.py:217
  (88 shorter events, 8.2 us)
Async XLA Ops:
  0.6 12.4 %copy-start = (f32[4]{0:T(128)S(1)}, f32[4]{0:T(128)}, u32[]{:S(2)}) copy-start(f32[4]{0:T(128)} %param.15) | copy-start | bytes 52
  0.6 5.9 %copy-start.5 = (f32[1,5,1024]{2,0,1:T(1,128)S(1)}, f32[1,5,1024]{2,0,1:T(1,128)}, u32[]{:S(2)}) copy-start(f32[1,5,1024]{2,0,1:T(1,128)} %param.18) | copy-start | bytes 61444
  0.7 9.0 %copy-start.7 = (s32[4]{0:T(128)S(1)}, s32[4]{0:T(128)}, u32[]{:S(2)}) copy-start(s32[4]{0:T(128)} %rows_ref.1) | copy-start | bytes 52
  0.7 12.2 %copy-start.4 = (f32[3,9,32,32]{3,2,1,0:T(8,128)S(1)}, f32[3,9,32,32]{3,2,1,0:T(8,128)}, u32[]{:S(2)}) copy-start(f32[3,9,32,32]{3,2,1,0:T(8,128)} %param.17) | copy-start | bytes 331780
  5.5 7.4 %copy-start.8 = (s32[9]{0:T(128)S(1)}, s32[9]{0:T(128)}, u32[]{:S(2)}) copy-start(s32[9]{0:T(128)} %param.14) | copy-start | bytes 112
  6.6 7.0 %copy-start.6 = (f32[5,1024]{1,0:T(8,128)S(1)}, f32[5,1024]{1,0:T(8,128)}, u32[]{:S(2)}) copy-start(f32[5,1024]{1,0:T(8,128)} %param.19) | copy-start | bytes 61444
  6.6 6.8 %collective-permute-start = (f32[13312]{0:T(1024)S(1)}, f32[13312]{0:T(1024)S(1)}, u32[]{:S(2)}, u32[]{:S(2)}) collective-permute-start(f32[13312]{0:T(1024)S(1)} %pad_maximum_fusion.10), channel_id=1, source_target_pairs={{0,16},{16,0},{1,17},{17,1},{2,18},{18,2},{3,19},{19,3},{4,20},{20... | collective-permute-start | bytes 159752 | tf_op jit(solution)/shard_map/ppermute | solution.py:23
  12.9 1.7 %copy-start.1 = (f32[1,4,64,1024]{3,2,1,0:T(8,128)S(1)}, f32[1,4,64,1024]{3,2,1,0:T(8,128)}, u32[]{:S(2)}) copy-start(f32[1,4,64,1024]{3,2,1,0:T(8,128)} %feed_ref.1) | copy-start | bytes 3145732
  12.9 1.7 %copy-start.2 = (bf16[1,4,64,1024]{3,2,1,0:T(8,128)(2,1)S(1)}, bf16[1,4,64,1024]{3,2,1,0:T(8,128)(2,1)}, u32[]{:S(2)}) copy-start(bf16[1,4,64,1024]{3,2,1,0:T(8,128)(2,1)} %grad_ref.1) | copy-start | bytes 1572868
  15.3 2.2 %collective-permute-start.1 = (f32[9,32,512]{2,1,0:T(8,128)S(1)}, f32[9,32,512]{2,1,0:T(8,128)}, u32[]{:S(2)}, u32[]{:S(2)}) collective-permute-start(f32[9,32,512]{2,1,0:T(8,128)S(1)} %constant_dynamic-slice_fusion.13), channel_id=1, source_target_pairs={{0,1},{1,0},{2,3},{3,2},{4,5},{5,4},{6,7},{7,6},{8,9},{9,8},{10,11... | collective-permute-start | bytes 1769480 | tf_op jit(solution)/shard_map/ppermute | solution.py:132
  18.8 6.8 %collective-permute-start.2 = (f32[9,32,256]{2,1,0:T(8,128)S(1)}, f32[9,32,256]{2,1,0:T(8,128)S(1)}, u32[]{:S(2)}, u32[]{:S(2)}) collective-permute-start(f32[9,32,256]{2,1,0:T(8,128)S(1)} %constant_dynamic-slice_fusion.12), channel_id=1, source_target_pairs={{0,2},{1,5},{2,0},{3,7},{4,6},{5,1},{6,4},{7,3},{8,10},{9,13},{10,... | collective-permute-start | bytes 884744 | tf_op jit(solution)/shard_map/ppermute | solution.py:132
  25.6 5.2 %collective-permute-start.3 = (f32[9,32,128]{2,1,0:T(8,128)S(1)}, f32[9,32,128]{2,1,0:T(8,128)S(1)}, u32[]{:S(2)}, u32[]{:S(2)}) collective-permute-start(f32[9,32,128]{2,1,0:T(8,128)S(1)} %constant_dynamic-slice_fusion.11), channel_id=1, source_target_pairs={{0,4},{1,3},{2,6},{3,1},{4,0},{5,7},{6,2},{7,5},{8,12},{9,11},{10,... | collective-permute-start | bytes 442376 | tf_op jit(solution)/shard_map/ppermute | solution.py:132
  30.9 12.5 %collective-permute-start.4 = (f32[9,32,128]{2,1,0:T(8,128)S(1)}, f32[9,32,128]{2,1,0:T(8,128)S(1)}, u32[]{:S(2)}, u32[]{:S(2)}) collective-permute-start(f32[9,32,128]{2,1,0:T(8,128)S(1)} %dynamic-slice_add_fusion.5), channel_id=1, source_target_pairs={{0,8},{1,17},{2,10},{3,19},{4,12},{5,21},{6,14},{7,23},{8,0},{9,25... | collective-permute-start | bytes 442376 | tf_op jit(solution)/shard_map/ppermute | solution.py:145
  33.5 9.9 %collective-permute-start.5 = (f32[9,32,128]{2,1,0:T(8,128)S(1)}, f32[9,32,128]{2,1,0:T(8,128)S(1)}, u32[]{:S(2)}, u32[]{:S(2)}) collective-permute-start(f32[9,32,128]{2,1,0:T(8,128)S(1)} %dynamic-slice_add_fusion.5), channel_id=1, source_target_pairs={{0,16},{1,9},{2,18},{3,11},{4,20},{5,13},{6,22},{7,15},{8,24},{9,1... | collective-permute-start | bytes 442376 | tf_op jit(solution)/shard_map/ppermute | solution.py:145
  34.0 12.3 %collective-permute-start.6 = (f32[9,32,128]{2,1,0:T(8,128)S(1)}, f32[9,32,128]{2,1,0:T(8,128)S(1)}, u32[]{:S(2)}, u32[]{:S(2)}) collective-permute-start(f32[9,32,128]{2,1,0:T(8,128)S(1)} %dynamic-slice_add_fusion.5), channel_id=1, source_target_pairs={{0,24},{1,25},{2,26},{3,27},{4,28},{5,29},{6,30},{7,31},{8,16},{9,... | collective-permute-start | bytes 442376 | tf_op jit(solution)/shard_map/ppermute | solution.py:145
  46.4 5.2 %collective-permute-start.7 = (f32[9,32,128]{2,1,0:T(8,128)S(1)}, f32[9,32,128]{2,1,0:T(8,128)S(1)}, u32[]{:S(2)}, u32[]{:S(2)}) collective-permute-start(f32[9,32,128]{2,1,0:T(8,128)S(1)} %select_add_fusion.1), channel_id=1, source_target_pairs={{0,4},{1,3},{2,6},{3,1},{4,0},{5,7},{6,2},{7,5},{8,12},{9,11},{10,... | collective-permute-start | bytes 442376 | tf_op jit(solution)/shard_map/ppermute | solution.py:156
  51.7 6.8 %collective-permute-start.8 = (f32[9,32,256]{2,1,0:T(8,128)S(1)}, f32[9,32,256]{2,1,0:T(8,128)S(1)}, u32[]{:S(2)}, u32[]{:S(2)}) collective-permute-start(f32[9,32,256]{2,1,0:T(8,128)S(1)} %pad_maximum_fusion.2), channel_id=1, source_target_pairs={{0,2},{1,5},{2,0},{3,7},{4,6},{5,1},{6,4},{7,3},{8,10},{9,13},{10,... | collective-permute-start | bytes 884744 | tf_op jit(solution)/shard_map/ppermute | solution.py:156
  58.6 2.2 %collective-permute-start.9 = (f32[9,32,512]{2,1,0:T(8,128)S(1)}, f32[9,32,512]{2,1,0:T(8,128)}, u32[]{:S(2)}, u32[]{:S(2)}) collective-permute-start(f32[9,32,512]{2,1,0:T(8,128)S(1)} %pad_maximum_fusion), channel_id=1, source_target_pairs={{0,1},{1,0},{2,3},{3,2},{4,5},{5,4},{6,7},{7,6},{8,9},{9,8},{10,11... | collective-permute-start | bytes 1769480 | tf_op jit(solution)/shard_map/ppermute | solution.py:156
  63.1 4.3 %collective-permute-start.10 = (f32[4,64,32]{1,2,0:T(8,128)S(1)}, f32[4,64,32]{1,2,0:T(8,128)S(1)}, u32[]{:S(2)}, u32[]{:S(2)}) collective-permute-start(f32[4,64,32]{1,2,0:T(8,128)S(1)} %fusion.2), channel_id=1, source_target_pairs={{0,16},{16,0},{1,17},{17,1},{2,18},{18,2},{3,19},{19,3},{4,20},{20... | collective-permute-start | bytes 98312 | tf_op jit(solution)/shard_map/ppermute | solution.py:23
  68.5 2.1 %collective-permute-start.11 = (f32[9,32,512]{2,1,0:T(8,128)S(1)}, f32[9,32,512]{2,1,0:T(8,128)S(1)}, u32[]{:S(2)}, u32[]{:S(2)}) collective-permute-start(f32[9,32,512]{2,1,0:T(8,128)S(1)} %constant_dynamic-slice_fusion.2), channel_id=1, source_target_pairs={{0,1},{1,0},{2,3},{3,2},{4,5},{5,4},{6,7},{7,6},{8,9},{9,8},{10,11... | collective-permute-start | bytes 1769480 | tf_op jit(solution)/shard_map/ppermute | solution.py:132
  70.7 6.8 %collective-permute-start.12 = (f32[9,32,256]{2,1,0:T(8,128)S(1)}, f32[9,32,256]{2,1,0:T(8,128)S(1)}, u32[]{:S(2)}, u32[]{:S(2)}) collective-permute-start(f32[9,32,256]{2,1,0:T(8,128)S(1)} %constant_dynamic-slice_fusion.1), channel_id=1, source_target_pairs={{0,2},{1,5},{2,0},{3,7},{4,6},{5,1},{6,4},{7,3},{8,10},{9,13},{10,... | collective-permute-start | bytes 884744 | tf_op jit(solution)/shard_map/ppermute | solution.py:132
  77.6 5.2 %collective-permute-start.13 = (f32[9,32,128]{2,1,0:T(8,128)S(1)}, f32[9,32,128]{2,1,0:T(8,128)S(1)}, u32[]{:S(2)}, u32[]{:S(2)}) collective-permute-start(f32[9,32,128]{2,1,0:T(8,128)S(1)} %constant_dynamic-slice_fusion), channel_id=1, source_target_pairs={{0,4},{1,3},{2,6},{3,1},{4,0},{5,7},{6,2},{7,5},{8,12},{9,11},{10,... | collective-permute-start | bytes 442376 | tf_op jit(solution)/shard_map/ppermute | solution.py:132
  82.8 12.4 %collective-permute-start.14 = (f32[9,32,128]{2,1,0:T(8,128)S(1)}, f32[9,32,128]{2,1,0:T(8,128)S(1)}, u32[]{:S(2)}, u32[]{:S(2)}) collective-permute-start(f32[9,32,128]{2,1,0:T(8,128)S(1)} %dynamic-slice_add_fusion.4), channel_id=1, source_target_pairs={{0,8},{1,17},{2,10},{3,19},{4,12},{5,21},{6,14},{7,23},{8,0},{9,25... | collective-permute-start | bytes 442376 | tf_op jit(solution)/shard_map/ppermute | solution.py:145
  84.9 10.3 %collective-permute-start.15 = (f32[9,32,128]{2,1,0:T(8,128)S(1)}, f32[9,32,128]{2,1,0:T(8,128)S(1)}, u32[]{:S(2)}, u32[]{:S(2)}) collective-permute-start(f32[9,32,128]{2,1,0:T(8,128)S(1)} %dynamic-slice_add_fusion.4), channel_id=1, source_target_pairs={{0,16},{1,9},{2,18},{3,11},{4,20},{5,13},{6,22},{7,15},{8,24},{9,1... | collective-permute-start | bytes 442376 | tf_op jit(solution)/shard_map/ppermute | solution.py:145
  85.4 12.9 %collective-permute-start.16 = (f32[9,32,128]{2,1,0:T(8,128)S(1)}, f32[9,32,128]{2,1,0:T(8,128)S(1)}, u32[]{:S(2)}, u32[]{:S(2)}) collective-permute-start(f32[9,32,128]{2,1,0:T(8,128)S(1)} %dynamic-slice_add_fusion.4), channel_id=1, source_target_pairs={{0,24},{1,25},{2,26},{3,27},{4,28},{5,29},{6,30},{7,31},{8,16},{9,... | collective-permute-start | bytes 442376 | tf_op jit(solution)/shard_map/ppermute | solution.py:145
  98.4 5.2 %collective-permute-start.17 = (f32[9,32,128]{2,1,0:T(8,128)S(1)}, f32[9,32,128]{2,1,0:T(8,128)S(1)}, u32[]{:S(2)}, u32[]{:S(2)}) collective-permute-start(f32[9,32,128]{2,1,0:T(8,128)S(1)} %select_add_fusion), channel_id=1, source_target_pairs={{0,4},{1,3},{2,6},{3,1},{4,0},{5,7},{6,2},{7,5},{8,12},{9,11},{10,... | collective-permute-start | bytes 442376 | tf_op jit(solution)/shard_map/ppermute | solution.py:156
  103.6 6.8 %collective-permute-start.18 = (f32[9,32,256]{2,1,0:T(8,128)S(1)}, f32[9,32,256]{2,1,0:T(8,128)S(1)}, u32[]{:S(2)}, u32[]{:S(2)}) collective-permute-start(f32[9,32,256]{2,1,0:T(8,128)S(1)} %pad_maximum_fusion.3), channel_id=1, source_target_pairs={{0,2},{1,5},{2,0},{3,7},{4,6},{5,1},{6,4},{7,3},{8,10},{9,13},{10,... | collective-permute-start | bytes 884744 | tf_op jit(solution)/shard_map/ppermute | solution.py:156
  110.6 2.2 %copy-start.3 = (f32[4,64,1024]{2,1,0:T(8,128)S(1)}, f32[4,64,1024]{2,1,0:T(8,128)}, u32[]{:S(2)}) copy-start(f32[4,64,1024]{2,1,0:T(8,128)} %param.12) | copy-start | bytes 3145732
  110.6 2.1 %collective-permute-start.19 = (f32[9,32,512]{2,1,0:T(8,128)S(1)}, f32[9,32,512]{2,1,0:T(8,128)S(1)}, u32[]{:S(2)}, u32[]{:S(2)}) collective-permute-start(f32[9,32,512]{2,1,0:T(8,128)S(1)} %pad_maximum_fusion.1), channel_id=1, source_target_pairs={{0,1},{1,0},{2,3},{3,2},{4,5},{5,4},{6,7},{7,6},{8,9},{9,8},{10,11... | collective-permute-start | bytes 1769480 | tf_op jit(solution)/shard_map/ppermute | solution.py:156

commit v18 on v17

--- a/solution.py
+++ b/solution.py
@@ -44,13 +44,16 @@
 
 def _first_kernel(rows_ref, grad_ref, feed_ref, basis_ref, out_ref):
     summed = grad_ref[0, 0].astype(jnp.float32) + feed_ref[0, 0]
-    out_ref[0] = lax.dot_general(
-        summed,
-        basis_ref[0],
-        (((1,), (1,)), ((), ())),
-        precision=TOP_PRECISION,
-        preferred_element_type=jnp.float32,
-    )
+    basis = basis_ref[0]
+    summed_hi = summed.astype(jnp.bfloat16)
+    summed_lo = (summed - summed_hi.astype(jnp.float32)).astype(jnp.bfloat16)
+    basis_hi = basis.astype(jnp.bfloat16)
+    basis_lo = (basis - basis_hi.astype(jnp.float32)).astype(jnp.bfloat16)
+
+    def product(a, b):
+        return lax.dot_general(a, b, (((1,), (1,)), ((), ())), preferred_element_type=jnp.float32)
+
+    out_ref[0] = product(summed_hi, basis_hi) + (product(summed_hi, basis_lo) + product(summed_lo, basis_hi))
 
 
 def first_products(tile_matrix, gradient, feedback, basis_rows):

time: 115 us -> 115 us (level)
  no operation moved by 1% of the time
where the time goes in v18:
time: 115 us
  waiting for transfers between devices  73.8 us (64%)
  starting transfers between devices  21 us (18%)
  matrix products  5.19 us (5%)
  Pallas kernels  4.67 us (4%)
  between operations  3.83 us (3%)
  other arithmetic  3.53 us (3%)
  local copies, waits for them, and re-layouts  2.67 us (2%)
    ppermute x6, waiting for transfers between devices, table_rows(): other = lax.ppermute(cur, axes, perm_of(p0, p1))  24.7 us
    ppermute x6, waiting for transfers between devices, table_rows(): cur = keep + lax.ppermute(send, axes, perm_of(p0, p1))  23.2 us
    ppermute x6, waiting for transfers between devices, table_rows(): held = [cur] + [lax.ppermute(cur, axes, group_perm(k)) for k in (1, 2, 3)]  22.1 us
    ppermute x6, starting transfers between devices, table_rows(): held = [cur] + [lax.ppermute(cur, axes, group_perm(k)) for k in (1, 2, 3)]  8.9 us
    ppermute x6, starting transfers between devices, table_rows(): cur = keep + lax.ppermute(send, axes, perm_of(p0, p1))  5.03 us
    pallas_call x1, Pallas kernels, first_products(): pl.pallas_call(_first_kernel, grid_spec=grid_spec, out_shape=jax.ShapeDty...  4.67 us
    ppermute x2, waiting for transfers between devices, swap_sum(): x = x + lax.ppermute(x, axis, _pair_perm(n, j))  3.79 us
    ppermute x2, starting transfers between devices, swap_sum(): x = x + lax.ppermute(x, axis, _pair_perm(n, j))  3.57 us
  transfers between devices with their start and end apart: 20, of which 17 were waited for; matrix products, arithmetic and copies ran while one was open for 1% of the time, Pallas kernels for 0%

profile of v18, /device:TPU:0, one launch (start us, length us, event | category | flops | bytes accessed | tf_op | source)
XLA Modules:
  0.0 114.6 jit_solution(15842529586963821747)
XLA Ops:
  0.7 4.7 %shard_map.121 = f32[4,64,32]{2,1,0:T(8,128)} custom-call(s32[4]{0:T(128)} %rows_ref.1, bf16[1,4,64,1024]{3,2,1,0:T(8,128)(2,1)} %grad_ref.1, f32[1,4,64,1024]{3,2,1,0:T(8,128)} %feed_ref.1, f32[9,32,1024]{2,1,0:T(8,128)} %bitcast.54), custom_call_target="tpu_custom_call" | custom-call | flops 16777216 | bytes 2129920 | tf_op jit(solution)/shard_map/pallas_call | solution.py:72
  5.3 1.0 reshape.40
  6.4 3.0 %collective-permute-start = (f32[13312]{0:T(1024)S(1)}, f32[13312]{0:T(1024)S(1)}, u32[]{:S(2)}, u32[]{:S(2)}) collective-permute-start(f32[13312]{0:T(1024)S(1)} %pad_maximum_fusion.10), channel_id=1, source_target_pairs={{0,16},{16,0},{1,17},{17,1},{2,18},{18,2},{3,19},{19,3},{4,20},{20... | collective-permute-start | bytes 159752 | tf_op jit(solution)/shard_map/ppermute | solution.py:23
  15.2 2.1 %collective-permute-done.1 = f32[9,32,512]{2,1,0:T(8,128)} collective-permute-done((f32[9,32,512]{2,1,0:T(8,128)S(1)}, f32[9,32,512]{2,1,0:T(8,128)}, u32[]{:S(2)}, u32[]{:S(2)}) %collective-permute-start.1) | collective-permute-done | bytes 589856 | tf_op jit(solution)/shard_map/ppermute | solution.py:135
  17.3 1.2 %dynamic-slice_add_fusion.1 = f32[9,32,512]{2,1,0:T(8,128)S(1)} fusion(f32[9,32,512]{2,1,0:T(8,128)} %collective-permute-done.1, f32[9,32,1024]{2,1,0:T(8,128)S(1)} %fusion.22, s32[]{:T(128)S(6)} %select_n.342), kind=kLoop, calls=%fused_computation.31 | loop fusion | flops 147456 | bytes 1769476 | tf_op jit(solution)/shard_map/add | solution.py:135
  18.6 1.6 %collective-permute-start.2 = (f32[9,32,256]{2,1,0:T(8,128)S(1)}, f32[9,32,256]{2,1,0:T(8,128)S(1)}, u32[]{:S(2)}, u32[]{:S(2)}) collective-permute-start(f32[9,32,256]{2,1,0:T(8,128)S(1)} %constant_dynamic-slice_fusion.12), channel_id=1, source_target_pairs={{0,2},{1,5},{2,0},{3,7},{4,6},{5,1},{6,4},{7,3},{8,10},{9,13},{10,... | collective-permute-start | bytes 884744 | tf_op jit(solution)/shard_map/ppermute | solution.py:135
  20.1 5.2 %collective-permute-done.2 = f32[9,32,256]{2,1,0:T(8,128)S(1)} collective-permute-done((f32[9,32,256]{2,1,0:T(8,128)S(1)}, f32[9,32,256]{2,1,0:T(8,128)S(1)}, u32[]{:S(2)}, u32[]{:S(2)}) %collective-permute-start.2) | collective-permute-done | bytes 294944 | tf_op jit(solution)/shard_map/ppermute | solution.py:135
  25.4 1.6 %collective-permute-start.3 = (f32[9,32,128]{2,1,0:T(8,128)S(1)}, f32[9,32,128]{2,1,0:T(8,128)S(1)}, u32[]{:S(2)}, u32[]{:S(2)}) collective-permute-start(f32[9,32,128]{2,1,0:T(8,128)S(1)} %constant_dynamic-slice_fusion.11), channel_id=1, source_target_pairs={{0,4},{1,3},{2,6},{3,1},{4,0},{5,7},{6,2},{7,5},{8,12},{9,11},{10,... | collective-permute-start | bytes 442376 | tf_op jit(solution)/shard_map/ppermute | solution.py:135
  27.1 3.6 %collective-permute-done.3 = f32[9,32,128]{2,1,0:T(8,128)S(1)} collective-permute-done((f32[9,32,128]{2,1,0:T(8,128)S(1)}, f32[9,32,128]{2,1,0:T(8,128)S(1)}, u32[]{:S(2)}, u32[]{:S(2)}) %collective-permute-start.3) | collective-permute-done | bytes 147488 | tf_op jit(solution)/shard_map/ppermute | solution.py:135
  30.7 2.7 %collective-permute-start.4 = (f32[9,32,128]{2,1,0:T(8,128)S(1)}, f32[9,32,128]{2,1,0:T(8,128)S(1)}, u32[]{:S(2)}, u32[]{:S(2)}) collective-permute-start(f32[9,32,128]{2,1,0:T(8,128)S(1)} %dynamic-slice_add_fusion.5), channel_id=1, source_target_pairs={{0,8},{1,17},{2,10},{3,19},{4,12},{5,21},{6,14},{7,23},{8,0},{9,25... | collective-permute-start | bytes 442376 | tf_op jit(solution)/shard_map/ppermute | solution.py:148
  33.9 1.3 %collective-permute-start.6 = (f32[9,32,128]{2,1,0:T(8,128)S(1)}, f32[9,32,128]{2,1,0:T(8,128)S(1)}, u32[]{:S(2)}, u32[]{:S(2)}) collective-permute-start(f32[9,32,128]{2,1,0:T(8,128)S(1)} %dynamic-slice_add_fusion.5), channel_id=1, source_target_pairs={{0,24},{1,25},{2,26},{3,27},{4,28},{5,29},{6,30},{7,31},{8,16},{9,... | collective-permute-start | bytes 442376 | tf_op jit(solution)/shard_map/ppermute | solution.py:148
  35.1 8.1 %collective-permute-done.4 = f32[9,32,128]{2,1,0:T(8,128)S(1)} collective-permute-done((f32[9,32,128]{2,1,0:T(8,128)S(1)}, f32[9,32,128]{2,1,0:T(8,128)S(1)}, u32[]{:S(2)}, u32[]{:S(2)}) %collective-permute-start.4) | collective-permute-done | bytes 147488 | tf_op jit(solution)/shard_map/ppermute | solution.py:148
  43.2 3.0 %collective-permute-done.6 = f32[9,32,128]{2,1,0:T(8,128)S(1)} collective-permute-done((f32[9,32,128]{2,1,0:T(8,128)S(1)}, f32[9,32,128]{2,1,0:T(8,128)S(1)}, u32[]{:S(2)}, u32[]{:S(2)}) %collective-permute-start.6) | collective-permute-done | bytes 147488 | tf_op jit(solution)/shard_map/ppermute | solution.py:148
  46.3 5.1 %collective-permute-done.7 = f32[9,32,128]{2,1,0:T(8,128)S(1)} collective-permute-done((f32[9,32,128]{2,1,0:T(8,128)S(1)}, f32[9,32,128]{2,1,0:T(8,128)S(1)}, u32[]{:S(2)}, u32[]{:S(2)}) %collective-permute-start.7) | collective-permute-done | bytes 147488 | tf_op jit(solution)/shard_map/ppermute | solution.py:159
  51.5 1.6 %collective-permute-start.8 = (f32[9,32,256]{2,1,0:T(8,128)S(1)}, f32[9,32,256]{2,1,0:T(8,128)S(1)}, u32[]{:S(2)}, u32[]{:S(2)}) collective-permute-start(f32[9,32,256]{2,1,0:T(8,128)S(1)} %pad_maximum_fusion.2), channel_id=1, source_target_pairs={{0,2},{1,5},{2,0},{3,7},{4,6},{5,1},{6,4},{7,3},{8,10},{9,13},{10,... | collective-permute-start | bytes 884744 | tf_op jit(solution)/shard_map/ppermute | solution.py:159
  53.1 5.2 %collective-permute-done.8 = f32[9,32,256]{2,1,0:T(8,128)S(1)} collective-permute-done((f32[9,32,256]{2,1,0:T(8,128)S(1)}, f32[9,32,256]{2,1,0:T(8,128)S(1)}, u32[]{:S(2)}, u32[]{:S(2)}) %collective-permute-start.8) | collective-permute-done | bytes 294944 | tf_op jit(solution)/shard_map/ppermute | solution.py:159
  58.6 2.1 %collective-permute-done.9 = f32[9,32,512]{2,1,0:T(8,128)} collective-permute-done((f32[9,32,512]{2,1,0:T(8,128)S(1)}, f32[9,32,512]{2,1,0:T(8,128)}, u32[]{:S(2)}, u32[]{:S(2)}) %collective-permute-start.9) | collective-permute-done | bytes 589856 | tf_op jit(solution)/shard_map/ppermute | solution.py:159
  60.6 1.0 constant_dynamic-slice_fusion.6
  63.4 3.8 %collective-permute-done.10 = f32[4,64,32]{1,2,0:T(8,128)S(1)} collective-permute-done((f32[4,64,32]{1,2,0:T(8,128)S(1)}, f32[4,64,32]{1,2,0:T(8,128)S(1)}, u32[]{:S(2)}, u32[]{:S(2)}) %collective-permute-start.10) | collective-permute-done | bytes 32800 | tf_op jit(solution)/shard_map/ppermute | solution.py:23
  68.3 2.0 %collective-permute-done.11 = f32[9,32,512]{2,1,0:T(8,128)S(1)} collective-permute-done((f32[9,32,512]{2,1,0:T(8,128)S(1)}, f32[9,32,512]{2,1,0:T(8,128)S(1)}, u32[]{:S(2)}, u32[]{:S(2)}) %collective-permute-start.11) | collective-permute-done | bytes 589856 | tf_op jit(solution)/shard_map/ppermute | solution.py:135
  70.4 1.6 %collective-permute-start.12 = (f32[9,32,256]{2,1,0:T(8,128)S(1)}, f32[9,32,256]{2,1,0:T(8,128)S(1)}, u32[]{:S(2)}, u32[]{:S(2)}) collective-permute-start(f32[9,32,256]{2,1,0:T(8,128)S(1)} %constant_dynamic-slice_fusion.1), channel_id=1, source_target_pairs={{0,2},{1,5},{2,0},{3,7},{4,6},{5,1},{6,4},{7,3},{8,10},{9,13},{10,... | collective-permute-start | bytes 884744 | tf_op jit(solution)/shard_map/ppermute | solution.py:135
  72.0 5.2 %collective-permute-done.12 = f32[9,32,256]{2,1,0:T(8,128)S(1)} collective-permute-done((f32[9,32,256]{2,1,0:T(8,128)S(1)}, f32[9,32,256]{2,1,0:T(8,128)S(1)}, u32[]{:S(2)}, u32[]{:S(2)}) %collective-permute-start.12) | collective-permute-done | bytes 294944 | tf_op jit(solution)/shard_map/ppermute | solution.py:135
  77.4 5.1 %collective-permute-done.13 = f32[9,32,128]{2,1,0:T(8,128)S(1)} collective-permute-done((f32[9,32,128]{2,1,0:T(8,128)S(1)}, f32[9,32,128]{2,1,0:T(8,128)S(1)}, u32[]{:S(2)}, u32[]{:S(2)}) %collective-permute-start.13) | collective-permute-done | bytes 147488 | tf_op jit(solution)/shard_map/ppermute | solution.py:135
  82.5 2.1 %collective-permute-start.14 = (f32[9,32,128]{2,1,0:T(8,128)S(1)}, f32[9,32,128]{2,1,0:T(8,128)S(1)}, u32[]{:S(2)}, u32[]{:S(2)}) collective-permute-start(f32[9,32,128]{2,1,0:T(8,128)S(1)} %dynamic-slice_add_fusion.4), channel_id=1, source_target_pairs={{0,8},{1,17},{2,10},{3,19},{4,12},{5,21},{6,14},{7,23},{8,0},{9,25... | collective-permute-start | bytes 442376 | tf_op jit(solution)/shard_map/ppermute | solution.py:148
  85.2 1.8 %collective-permute-start.16 = (f32[9,32,128]{2,1,0:T(8,128)S(1)}, f32[9,32,128]{2,1,0:T(8,128)S(1)}, u32[]{:S(2)}, u32[]{:S(2)}) collective-permute-start(f32[9,32,128]{2,1,0:T(8,128)S(1)} %dynamic-slice_add_fusion.4), channel_id=1, source_target_pairs={{0,24},{1,25},{2,26},{3,27},{4,28},{5,29},{6,30},{7,31},{8,16},{9,... | collective-permute-start | bytes 442376 | tf_op jit(solution)/shard_map/ppermute | solution.py:148
  87.0 8.0 %collective-permute-done.14 = f32[9,32,128]{2,1,0:T(8,128)S(1)} collective-permute-done((f32[9,32,128]{2,1,0:T(8,128)S(1)}, f32[9,32,128]{2,1,0:T(8,128)S(1)}, u32[]{:S(2)}, u32[]{:S(2)}) %collective-permute-start.14) | collective-permute-done | bytes 147488 | tf_op jit(solution)/shard_map/ppermute | solution.py:148
  95.0 3.1 %collective-permute-done.16 = f32[9,32,128]{2,1,0:T(8,128)S(1)} collective-permute-done((f32[9,32,128]{2,1,0:T(8,128)S(1)}, f32[9,32,128]{2,1,0:T(8,128)S(1)}, u32[]{:S(2)}, u32[]{:S(2)}) %collective-permute-start.16) | collective-permute-done | bytes 147488 | tf_op jit(solution)/shard_map/ppermute | solution.py:148
  98.2 5.1 %collective-permute-done.17 = f32[9,32,128]{2,1,0:T(8,128)S(1)} collective-permute-done((f32[9,32,128]{2,1,0:T(8,128)S(1)}, f32[9,32,128]{2,1,0:T(8,128)S(1)}, u32[]{:S(2)}, u32[]{:S(2)}) %collective-permute-start.17) | collective-permute-done | bytes 147488 | tf_op jit(solution)/shard_map/ppermute | solution.py:159
  103.4 1.6 %collective-permute-start.18 = (f32[9,32,256]{2,1,0:T(8,128)S(1)}, f32[9,32,256]{2,1,0:T(8,128)S(1)}, u32[]{:S(2)}, u32[]{:S(2)}) collective-permute-start(f32[9,32,256]{2,1,0:T(8,128)S(1)} %pad_maximum_fusion.3), channel_id=1, source_target_pairs={{0,2},{1,5},{2,0},{3,7},{4,6},{5,1},{6,4},{7,3},{8,10},{9,13},{10,... | collective-permute-start | bytes 884744 | tf_op jit(solution)/shard_map/ppermute | solution.py:159
  105.0 5.2 %collective-permute-done.18 = f32[9,32,256]{2,1,0:T(8,128)S(1)} collective-permute-done((f32[9,32,256]{2,1,0:T(8,128)S(1)}, f32[9,32,256]{2,1,0:T(8,128)S(1)}, u32[]{:S(2)}, u32[]{:S(2)}) %collective-permute-start.18) | collective-permute-done | bytes 294944 | tf_op jit(solution)/shard_map/ppermute | solution.py:159
  110.4 2.0 %collective-permute-done.19 = f32[9,32,512]{2,1,0:T(8,128)S(1)} collective-permute-done((f32[9,32,512]{2,1,0:T(8,128)S(1)}, f32[9,32,512]{2,1,0:T(8,128)S(1)}, u32[]{:S(2)}, u32[]{:S(2)}) %collective-permute-start.19) | collective-permute-done | bytes 589856 | tf_op jit(solution)/shard_map/ppermute | solution.py:159
  112.5 2.1 %multiply_add_fusion = (f32[4,64,1024]{2,1,0:T(8,128)}, f32[1,4,64,1024]{3,2,1,0:T(8,128)}) fusion(f32[4,64,1024]{2,1,0:T(8,128)S(1)} %copy-done.3, f32[4]{0:T(128)S(1)} %convolution_bitcast_fusion, f32[1,4,64,1024]{3,2,1,0:T(8,128)S(1)} %copy-done.1, bf16[1,4,64,1024]{3,2,1,0:T(8,128)(2,1)S(1)} %copy-done.2, f32[4,64,32]{1,2,0:T(8,128)S(1)} %fusion.41, ...), kind=kOutput, calls=%fused_computation.10 | convolution fusion | flops 52166656 | bytes 5275664 | tf_op jit(solution)/shard_map/tks,tsd->tkd/dot_general | solution.py:220
  (88 shorter events, 8.2 us)
Async XLA Ops:
  0.6 12.2 %copy-start = (f32[4]{0:T(128)S(1)}, f32[4]{0:T(128)}, u32[]{:S(2)}) copy-start(f32[4]{0:T(128)} %param.15) | copy-start | bytes 52
  0.6 5.7 %copy-start.5 = (f32[1,5,1024]{2,0,1:T(1,128)S(1)}, f32[1,5,1024]{2,0,1:T(1,128)}, u32[]{:S(2)}) copy-start(f32[1,5,1024]{2,0,1:T(1,128)} %param.18) | copy-start | bytes 61444
  0.7 8.8 %copy-start.7 = (s32[4]{0:T(128)S(1)}, s32[4]{0:T(128)}, u32[]{:S(2)}) copy-start(s32[4]{0:T(128)} %rows_ref.1) | copy-start | bytes 52
  0.7 12.0 %copy-start.4 = (f32[3,9,32,32]{3,2,1,0:T(8,128)S(1)}, f32[3,9,32,32]{3,2,1,0:T(8,128)}, u32[]{:S(2)}) copy-start(f32[3,9,32,32]{3,2,1,0:T(8,128)} %param.17) | copy-start | bytes 331780
  5.3 7.4 %copy-start.8 = (s32[9]{0:T(128)S(1)}, s32[9]{0:T(128)}, u32[]{:S(2)}) copy-start(s32[9]{0:T(128)} %param.14) | copy-start | bytes 112
  6.4 7.0 %copy-start.6 = (f32[5,1024]{1,0:T(8,128)S(1)}, f32[5,1024]{1,0:T(8,128)}, u32[]{:S(2)}) copy-start(f32[5,1024]{1,0:T(8,128)} %param.19) | copy-start | bytes 61444
  6.4 6.8 %collective-permute-start = (f32[13312]{0:T(1024)S(1)}, f32[13312]{0:T(1024)S(1)}, u32[]{:S(2)}, u32[]{:S(2)}) collective-permute-start(f32[13312]{0:T(1024)S(1)} %pad_maximum_fusion.10), channel_id=1, source_target_pairs={{0,16},{16,0},{1,17},{17,1},{2,18},{18,2},{3,19},{19,3},{4,20},{20... | collective-permute-start | bytes 159752 | tf_op jit(solution)/shard_map/ppermute | solution.py:23
  12.7 1.7 %copy-start.1 = (f32[1,4,64,1024]{3,2,1,0:T(8,128)S(1)}, f32[1,4,64,1024]{3,2,1,0:T(8,128)}, u32[]{:S(2)}) copy-start(f32[1,4,64,1024]{3,2,1,0:T(8,128)} %feed_ref.1) | copy-start | bytes 3145732
  12.7 1.7 %copy-start.2 = (bf16[1,4,64,1024]{3,2,1,0:T(8,128)(2,1)S(1)}, bf16[1,4,64,1024]{3,2,1,0:T(8,128)(2,1)}, u32[]{:S(2)}) copy-start(bf16[1,4,64,1024]{3,2,1,0:T(8,128)(2,1)} %grad_ref.1) | copy-start | bytes 1572868
  15.1 2.2 %collective-permute-start.1 = (f32[9,32,512]{2,1,0:T(8,128)S(1)}, f32[9,32,512]{2,1,0:T(8,128)}, u32[]{:S(2)}, u32[]{:S(2)}) collective-permute-start(f32[9,32,512]{2,1,0:T(8,128)S(1)} %constant_dynamic-slice_fusion.13), channel_id=1, source_target_pairs={{0,1},{1,0},{2,3},{3,2},{4,5},{5,4},{6,7},{7,6},{8,9},{9,8},{10,11... | collective-permute-start | bytes 1769480 | tf_op jit(solution)/shard_map/ppermute | solution.py:135
  18.6 6.8 %collective-permute-start.2 = (f32[9,32,256]{2,1,0:T(8,128)S(1)}, f32[9,32,256]{2,1,0:T(8,128)S(1)}, u32[]{:S(2)}, u32[]{:S(2)}) collective-permute-start(f32[9,32,256]{2,1,0:T(8,128)S(1)} %constant_dynamic-slice_fusion.12), channel_id=1, source_target_pairs={{0,2},{1,5},{2,0},{3,7},{4,6},{5,1},{6,4},{7,3},{8,10},{9,13},{10,... | collective-permute-start | bytes 884744 | tf_op jit(solution)/shard_map/ppermute | solution.py:135
  25.4 5.2 %collective-permute-start.3 = (f32[9,32,128]{2,1,0:T(8,128)S(1)}, f32[9,32,128]{2,1,0:T(8,128)S(1)}, u32[]{:S(2)}, u32[]{:S(2)}) collective-permute-start(f32[9,32,128]{2,1,0:T(8,128)S(1)} %constant_dynamic-slice_fusion.11), channel_id=1, source_target_pairs={{0,4},{1,3},{2,6},{3,1},{4,0},{5,7},{6,2},{7,5},{8,12},{9,11},{10,... | collective-permute-start | bytes 442376 | tf_op jit(solution)/shard_map/ppermute | solution.py:135
  30.7 12.5 %collective-permute-start.4 = (f32[9,32,128]{2,1,0:T(8,128)S(1)}, f32[9,32,128]{2,1,0:T(8,128)S(1)}, u32[]{:S(2)}, u32[]{:S(2)}) collective-permute-start(f32[9,32,128]{2,1,0:T(8,128)S(1)} %dynamic-slice_add_fusion.5), channel_id=1, source_target_pairs={{0,8},{1,17},{2,10},{3,19},{4,12},{5,21},{6,14},{7,23},{8,0},{9,25... | collective-permute-start | bytes 442376 | tf_op jit(solution)/shard_map/ppermute | solution.py:148
  33.3 9.9 %collective-permute-start.5 = (f32[9,32,128]{2,1,0:T(8,128)S(1)}, f32[9,32,128]{2,1,0:T(8,128)S(1)}, u32[]{:S(2)}, u32[]{:S(2)}) collective-permute-start(f32[9,32,128]{2,1,0:T(8,128)S(1)} %dynamic-slice_add_fusion.5), channel_id=1, source_target_pairs={{0,16},{1,9},{2,18},{3,11},{4,20},{5,13},{6,22},{7,15},{8,24},{9,1... | collective-permute-start | bytes 442376 | tf_op jit(solution)/shard_map/ppermute | solution.py:148
  33.9 12.3 %collective-permute-start.6 = (f32[9,32,128]{2,1,0:T(8,128)S(1)}, f32[9,32,128]{2,1,0:T(8,128)S(1)}, u32[]{:S(2)}, u32[]{:S(2)}) collective-permute-start(f32[9,32,128]{2,1,0:T(8,128)S(1)} %dynamic-slice_add_fusion.5), channel_id=1, source_target_pairs={{0,24},{1,25},{2,26},{3,27},{4,28},{5,29},{6,30},{7,31},{8,16},{9,... | collective-permute-start | bytes 442376 | tf_op jit(solution)/shard_map/ppermute | solution.py:148
  46.2 5.2 %collective-permute-start.7 = (f32[9,32,128]{2,1,0:T(8,128)S(1)}, f32[9,32,128]{2,1,0:T(8,128)S(1)}, u32[]{:S(2)}, u32[]{:S(2)}) collective-permute-start(f32[9,32,128]{2,1,0:T(8,128)S(1)} %select_add_fusion.1), channel_id=1, source_target_pairs={{0,4},{1,3},{2,6},{3,1},{4,0},{5,7},{6,2},{7,5},{8,12},{9,11},{10,... | collective-permute-start | bytes 442376 | tf_op jit(solution)/shard_map/ppermute | solution.py:159
  51.5 6.8 %collective-permute-start.8 = (f32[9,32,256]{2,1,0:T(8,128)S(1)}, f32[9,32,256]{2,1,0:T(8,128)S(1)}, u32[]{:S(2)}, u32[]{:S(2)}) collective-permute-start(f32[9,32,256]{2,1,0:T(8,128)S(1)} %pad_maximum_fusion.2), channel_id=1, source_target_pairs={{0,2},{1,5},{2,0},{3,7},{4,6},{5,1},{6,4},{7,3},{8,10},{9,13},{10,... | collective-permute-start | bytes 884744 | tf_op jit(solution)/shard_map/ppermute | solution.py:159
  58.4 2.2 %collective-permute-start.9 = (f32[9,32,512]{2,1,0:T(8,128)S(1)}, f32[9,32,512]{2,1,0:T(8,128)}, u32[]{:S(2)}, u32[]{:S(2)}) collective-permute-start(f32[9,32,512]{2,1,0:T(8,128)S(1)} %pad_maximum_fusion), channel_id=1, source_target_pairs={{0,1},{1,0},{2,3},{3,2},{4,5},{5,4},{6,7},{7,6},{8,9},{9,8},{10,11... | collective-permute-start | bytes 1769480 | tf_op jit(solution)/shard_map/ppermute | solution.py:159
  62.9 4.3 %collective-permute-start.10 = (f32[4,64,32]{1,2,0:T(8,128)S(1)}, f32[4,64,32]{1,2,0:T(8,128)S(1)}, u32[]{:S(2)}, u32[]{:S(2)}) collective-permute-start(f32[4,64,32]{1,2,0:T(8,128)S(1)} %fusion.2), channel_id=1, source_target_pairs={{0,16},{16,0},{1,17},{17,1},{2,18},{18,2},{3,19},{19,3},{4,20},{20... | collective-permute-start | bytes 98312 | tf_op jit(solution)/shard_map/ppermute | solution.py:23
  68.2 2.1 %collective-permute-start.11 = (f32[9,32,512]{2,1,0:T(8,128)S(1)}, f32[9,32,512]{2,1,0:T(8,128)S(1)}, u32[]{:S(2)}, u32[]{:S(2)}) collective-permute-start(f32[9,32,512]{2,1,0:T(8,128)S(1)} %constant_dynamic-slice_fusion.2), channel_id=1, source_target_pairs={{0,1},{1,0},{2,3},{3,2},{4,5},{5,4},{6,7},{7,6},{8,9},{9,8},{10,11... | collective-permute-start | bytes 1769480 | tf_op jit(solution)/shard_map/ppermute | solution.py:135
  70.4 6.8 %collective-permute-start.12 = (f32[9,32,256]{2,1,0:T(8,128)S(1)}, f32[9,32,256]{2,1,0:T(8,128)S(1)}, u32[]{:S(2)}, u32[]{:S(2)}) collective-permute-start(f32[9,32,256]{2,1,0:T(8,128)S(1)} %constant_dynamic-slice_fusion.1), channel_id=1, source_target_pairs={{0,2},{1,5},{2,0},{3,7},{4,6},{5,1},{6,4},{7,3},{8,10},{9,13},{10,... | collective-permute-start | bytes 884744 | tf_op jit(solution)/shard_map/ppermute | solution.py:135
  77.3 5.2 %collective-permute-start.13 = (f32[9,32,128]{2,1,0:T(8,128)S(1)}, f32[9,32,128]{2,1,0:T(8,128)S(1)}, u32[]{:S(2)}, u32[]{:S(2)}) collective-permute-start(f32[9,32,128]{2,1,0:T(8,128)S(1)} %constant_dynamic-slice_fusion), channel_id=1, source_target_pairs={{0,4},{1,3},{2,6},{3,1},{4,0},{5,7},{6,2},{7,5},{8,12},{9,11},{10,... | collective-permute-start | bytes 442376 | tf_op jit(solution)/shard_map/ppermute | solution.py:135
  82.5 12.4 %collective-permute-start.14 = (f32[9,32,128]{2,1,0:T(8,128)S(1)}, f32[9,32,128]{2,1,0:T(8,128)S(1)}, u32[]{:S(2)}, u32[]{:S(2)}) collective-permute-start(f32[9,32,128]{2,1,0:T(8,128)S(1)} %dynamic-slice_add_fusion.4), channel_id=1, source_target_pairs={{0,8},{1,17},{2,10},{3,19},{4,12},{5,21},{6,14},{7,23},{8,0},{9,25... | collective-permute-start | bytes 442376 | tf_op jit(solution)/shard_map/ppermute | solution.py:148
  84.6 10.3 %collective-permute-start.15 = (f32[9,32,128]{2,1,0:T(8,128)S(1)}, f32[9,32,128]{2,1,0:T(8,128)S(1)}, u32[]{:S(2)}, u32[]{:S(2)}) collective-permute-start(f32[9,32,128]{2,1,0:T(8,128)S(1)} %dynamic-slice_add_fusion.4), channel_id=1, source_target_pairs={{0,16},{1,9},{2,18},{3,11},{4,20},{5,13},{6,22},{7,15},{8,24},{9,1... | collective-permute-start | bytes 442376 | tf_op jit(solution)/shard_map/ppermute | solution.py:148
  85.2 12.9 %collective-permute-start.16 = (f32[9,32,128]{2,1,0:T(8,128)S(1)}, f32[9,32,128]{2,1,0:T(8,128)S(1)}, u32[]{:S(2)}, u32[]{:S(2)}) collective-permute-start(f32[9,32,128]{2,1,0:T(8,128)S(1)} %dynamic-slice_add_fusion.4), channel_id=1, source_target_pairs={{0,24},{1,25},{2,26},{3,27},{4,28},{5,29},{6,30},{7,31},{8,16},{9,... | collective-permute-start | bytes 442376 | tf_op jit(solution)/shard_map/ppermute | solution.py:148
  98.1 5.2 %collective-permute-start.17 = (f32[9,32,128]{2,1,0:T(8,128)S(1)}, f32[9,32,128]{2,1,0:T(8,128)S(1)}, u32[]{:S(2)}, u32[]{:S(2)}) collective-permute-start(f32[9,32,128]{2,1,0:T(8,128)S(1)} %select_add_fusion), channel_id=1, source_target_pairs={{0,4},{1,3},{2,6},{3,1},{4,0},{5,7},{6,2},{7,5},{8,12},{9,11},{10,... | collective-permute-start | bytes 442376 | tf_op jit(solution)/shard_map/ppermute | solution.py:159
  103.4 6.8 %collective-permute-start.18 = (f32[9,32,256]{2,1,0:T(8,128)S(1)}, f32[9,32,256]{2,1,0:T(8,128)S(1)}, u32[]{:S(2)}, u32[]{:S(2)}) collective-permute-start(f32[9,32,256]{2,1,0:T(8,128)S(1)} %pad_maximum_fusion.3), channel_id=1, source_target_pairs={{0,2},{1,5},{2,0},{3,7},{4,6},{5,1},{6,4},{7,3},{8,10},{9,13},{10,... | collective-permute-start | bytes 884744 | tf_op jit(solution)/shard_map/ppermute | solution.py:159
  110.3 2.2 %copy-start.3 = (f32[4,64,1024]{2,1,0:T(8,128)S(1)}, f32[4,64,1024]{2,1,0:T(8,128)}, u32[]{:S(2)}) copy-start(f32[4,64,1024]{2,1,0:T(8,128)} %param.12) | copy-start | bytes 3145732
  110.3 2.1 %collective-permute-start.19 = (f32[9,32,512]{2,1,0:T(8,128)S(1)}, f32[9,32,512]{2,1,0:T(8,128)S(1)}, u32[]{:S(2)}, u32[]{:S(2)}) collective-permute-start(f32[9,32,512]{2,1,0:T(8,128)S(1)} %pad_maximum_fusion.1), channel_id=1, source_target_pairs={{0,1},{1,0},{2,3},{3,2},{4,5},{5,4},{6,7},{7,6},{8,9},{9,8},{10,11... | collective-permute-start | bytes 1769480 | tf_op jit(solution)/shard_map/ppermute | solution.py:159

commit v19 on v15

--- a/solution.py
+++ b/solution.py
@@ -104,7 +104,9 @@
             return pairs
 
         place = bit_of(a0, a1) + 2 * bit_of(b0, b1)
-        held = [cur] + [lax.ppermute(cur, axes, group_perm(k)) for k in (1, 2, 3)]
+        diagonal = lax.ppermute(cur, axes, group_perm(3))
+        sides = [lax.ppermute(cur, axes, group_perm(k)) for k in (1, 2)]
+        held = [cur] + sides + [diagonal]
         total = None
         for member in range(4):
             term = lax.select_n(place ^ member, *held)
@@ -149,11 +151,8 @@
     tile_rows = _scalar_rows(tile_matrix, matrix_count)
     q_tiles = _pick_rows(start_basis, tile_rows)
     first_local = jnp.einsum("tkd,tds->tks", combined, q_tiles, precision=WIDE_PRECISION)
-    left_size = first_local.size
-    carried = jnp.concatenate([first_local.reshape(-1), vector_grad[0].reshape(-1)])
-    carried = swap_sum(carried, "rep")
-    first_left = carried[:left_size].reshape(first_local.shape) / replicas
-    vector_summed = carried[left_size:].reshape(vector_grad.shape[1:])
+    vector_summed = swap_sum(vector_grad[0], "rep")
+    first_left = swap_sum(first_local, "rep") / replicas
     mix_first = _pick_rows(inverse_gram_factors[0], tile_rows)
     mix_right = _pick_rows(inverse_gram_factors[1], tile_rows)
     mix_second = _pick_rows(inverse_gram_factors[2], tile_rows)

time: 115 us -> 116 us (level)
  waiting for transfers between devices: 72.6 us -> 77 us
  starting transfers between devices: 24.4 us -> 21.2 us
    ppermute x2 -> x3, waiting for transfers between devices: 4.48 us -> 7 us  [swap_sum(): x = x + lax.ppermute(x, axis, _pair_perm(n, j))]
    ppermute x6, starting transfers between devices: 6.49 us -> 5.02 us  [table_rows(): cur = keep + lax.ppermute(send, axes, perm_of(p0, p1))]
    ppermute x6, waiting for transfers between devices: 21.8 us -> 23.2 us  [table_rows(): cur = keep + lax.ppermute(send, axes, perm_of(p0, p1))]
    ppermute x2 -> x3, starting transfers between devices: 4.45 us -> 3.8 us  [swap_sum(): x = x + lax.ppermute(x, axis, _pair_perm(n, j))]
  transfers between devices with their start and end apart: 20 -> 21, of which waited for: 18 -> 18; matrix products, arithmetic and copies ran while one was open for 0% -> 1% of each run, Pallas kernels for 0% -> 0%
where the time goes in v19:
time: 116 us
  waiting for transfers between devices  77 us (66%)
  starting transfers between devices  21.2 us (18%)
  matrix products  6.81 us (6%)
  other arithmetic  4.23 us (4%)
  between operations  3.78 us (3%)
  local copies, waits for them, and re-layouts  2.73 us (2%)
    ppermute x6, waiting for transfers between devices, table_rows(): other = lax.ppermute(cur, axes, perm_of(p0, p1))  24.7 us
    ppermute x6, waiting for transfers between devices, table_rows(): cur = keep + lax.ppermute(send, axes, perm_of(p0, p1))  23.2 us
    ppermute x4, waiting for transfers between devices, table_rows(): sides = [lax.ppermute(cur, axes, group_perm(k)) for k in (1, 2)]  16.2 us
    ppermute x3, waiting for transfers between devices, swap_sum(): x = x + lax.ppermute(x, axis, _pair_perm(n, j))  7 us
    ppermute x4, starting transfers between devices, table_rows(): sides = [lax.ppermute(cur, axes, group_perm(k)) for k in (1, 2)]  6 us
    ppermute x2, waiting for transfers between devices, table_rows(): diagonal = lax.ppermute(cur, axes, group_perm(3))  5.92 us
    ppermute x6, starting transfers between devices, table_rows(): cur = keep + lax.ppermute(send, axes, perm_of(p0, p1))  5.02 us
    ppermute x3, starting transfers between devices, swap_sum(): x = x + lax.ppermute(x, axis, _pair_perm(n, j))  3.8 us
  transfers between devices with their start and end apart: 21, of which 18 were waited for; matrix products, arithmetic and copies ran while one was open for 1% of the time, Pallas kernels for 0%

profile of v19, /device:TPU:0, one launch (start us, length us, event | category | flops | bytes accessed | tf_op | source)
XLA Modules:
  0.0 115.7 jit_solution(8877596280400617390)
XLA Ops:
  0.7 1.4 %shift-left_reduce_fusion = s32[]{:T(128)} fusion(s32[4]{0:T(128)} %param.13), kind=kLoop, calls=%fused_computation.160 | loop fusion | flops 11 | bytes 20 | tf_op jit(solution)/shard_map/reduce_sum | solution.py:49
  5.8 1.7 %fusion.6 = f32[4,64,32]{1,2,0:T(8,128)S(1)} fusion(f32[1,1024,32]{1,2,0:T(8,128)S(1)} %get-tuple-element.15, f32[1,1024,32]{1,2,0:T(8,128)S(1)} %get-tuple-element.16, f32[1,1024,32]{1,2,0:T(8,128)S(1)} %get-tuple-element.14, f32[1,1024,32]{1,2,0:T(8,128)S(1)} %get-tuple-element.13, f32[1,4,64,1024]{3,2,1,0:T(8,128)S(1)} %copy-done.1, ...), kind=kOutput, calls=%fused_computation.9 | convolution fusion | flops 51249152 | bytes 2129920 | tf_op jit(solution)/shard_map/tkd,tds->tks/dot_general | solution.py:153
  7.5 3.0 %collective-permute-start = (f32[4,64,32]{1,2,0:T(8,128)S(1)}, f32[4,64,32]{1,2,0:T(8,128)S(1)}, u32[]{:S(2)}, u32[]{:S(2)}) collective-permute-start(f32[4,64,32]{1,2,0:T(8,128)S(1)} %fusion.6), channel_id=1, source_target_pairs={{0,16},{16,0},{1,17},{17,1},{2,18},{18,2},{3,19},{19,3},{4,20},{20... | collective-permute-start | bytes 98312 | tf_op jit(solution)/shard_map/ppermute | solution.py:21
  11.2 3.4 %collective-permute-done.1 = f32[5,1024]{1,0:T(8,128)S(1)} collective-permute-done((f32[5,1024]{1,0:T(8,128)S(1)}, f32[5,1024]{1,0:T(8,128)S(1)}, u32[]{:S(2)}, u32[]{:S(2)}) %collective-permute-start.1) | collective-permute-done | bytes 20512 | tf_op jit(solution)/shard_map/ppermute | solution.py:21
  16.4 2.1 %collective-permute-done.2 = f32[9,32,512]{2,1,0:T(8,128)} collective-permute-done((f32[9,32,512]{2,1,0:T(8,128)S(1)}, f32[9,32,512]{2,1,0:T(8,128)}, u32[]{:S(2)}, u32[]{:S(2)}) %collective-permute-start.2) | collective-permute-done | bytes 589856 | tf_op jit(solution)/shard_map/ppermute | solution.py:94
  18.5 1.2 %dynamic-slice_add_fusion.1 = f32[9,32,512]{2,1,0:T(8,128)S(1)} fusion(f32[9,32,512]{2,1,0:T(8,128)} %collective-permute-done.2, f32[9,32,1024]{2,1,0:T(8,128)S(1)} %fusion.31, s32[]{:T(128)S(6)} %select_n.347), kind=kLoop, calls=%fused_computation.33 | loop fusion | flops 147456 | bytes 1769476 | tf_op jit(solution)/shard_map/add | solution.py:94
  19.7 1.6 %collective-permute-start.3 = (f32[9,32,256]{2,1,0:T(8,128)S(1)}, f32[9,32,256]{2,1,0:T(8,128)S(1)}, u32[]{:S(2)}, u32[]{:S(2)}) collective-permute-start(f32[9,32,256]{2,1,0:T(8,128)S(1)} %constant_dynamic-slice_fusion.12), channel_id=1, source_target_pairs={{0,2},{1,5},{2,0},{3,7},{4,6},{5,1},{6,4},{7,3},{8,10},{9,13},{10,... | collective-permute-start | bytes 884744 | tf_op jit(solution)/shard_map/ppermute | solution.py:94
  21.3 5.2 %collective-permute-done.3 = f32[9,32,256]{2,1,0:T(8,128)S(1)} collective-permute-done((f32[9,32,256]{2,1,0:T(8,128)S(1)}, f32[9,32,256]{2,1,0:T(8,128)S(1)}, u32[]{:S(2)}, u32[]{:S(2)}) %collective-permute-start.3) | collective-permute-done | bytes 294944 | tf_op jit(solution)/shard_map/ppermute | solution.py:94
  26.5 1.6 %collective-permute-start.4 = (f32[9,32,128]{2,1,0:T(8,128)S(1)}, f32[9,32,128]{2,1,0:T(8,128)S(1)}, u32[]{:S(2)}, u32[]{:S(2)}) collective-permute-start(f32[9,32,128]{2,1,0:T(8,128)S(1)} %constant_dynamic-slice_fusion.11), channel_id=1, source_target_pairs={{0,4},{1,3},{2,6},{3,1},{4,0},{5,7},{6,2},{7,5},{8,12},{9,11},{10,... | collective-permute-start | bytes 442376 | tf_op jit(solution)/shard_map/ppermute | solution.py:94
  28.2 3.6 %collective-permute-done.4 = f32[9,32,128]{2,1,0:T(8,128)S(1)} collective-permute-done((f32[9,32,128]{2,1,0:T(8,128)S(1)}, f32[9,32,128]{2,1,0:T(8,128)S(1)}, u32[]{:S(2)}, u32[]{:S(2)}) %collective-permute-start.4) | collective-permute-done | bytes 147488 | tf_op jit(solution)/shard_map/ppermute | solution.py:94
  31.8 2.7 %collective-permute-start.5 = (f32[9,32,128]{2,1,0:T(8,128)S(1)}, f32[9,32,128]{2,1,0:T(8,128)S(1)}, u32[]{:S(2)}, u32[]{:S(2)}) collective-permute-start(f32[9,32,128]{2,1,0:T(8,128)S(1)} %dynamic-slice_add_fusion.5), channel_id=1, source_target_pairs={{0,8},{1,17},{2,10},{3,19},{4,12},{5,21},{6,14},{7,23},{8,0},{9,25... | collective-permute-start | bytes 442376 | tf_op jit(solution)/shard_map/ppermute | solution.py:108
  35.0 1.2 %collective-permute-start.7 = (f32[9,32,128]{2,1,0:T(8,128)S(1)}, f32[9,32,128]{2,1,0:T(8,128)S(1)}, u32[]{:S(2)}, u32[]{:S(2)}) collective-permute-start(f32[9,32,128]{2,1,0:T(8,128)S(1)} %dynamic-slice_add_fusion.5), channel_id=1, source_target_pairs={{0,24},{1,25},{2,26},{3,27},{4,28},{5,29},{6,30},{7,31},{8,16},{9,... | collective-permute-start | bytes 442376 | tf_op jit(solution)/shard_map/ppermute | solution.py:107
  36.2 8.2 %collective-permute-done.5 = f32[9,32,128]{2,1,0:T(8,128)S(1)} collective-permute-done((f32[9,32,128]{2,1,0:T(8,128)S(1)}, f32[9,32,128]{2,1,0:T(8,128)S(1)}, u32[]{:S(2)}, u32[]{:S(2)}) %collective-permute-start.5) | collective-permute-done | bytes 147488 | tf_op jit(solution)/shard_map/ppermute | solution.py:108
  44.4 2.9 %collective-permute-done.7 = f32[9,32,128]{2,1,0:T(8,128)S(1)} collective-permute-done((f32[9,32,128]{2,1,0:T(8,128)S(1)}, f32[9,32,128]{2,1,0:T(8,128)S(1)}, u32[]{:S(2)}, u32[]{:S(2)}) %collective-permute-start.7) | collective-permute-done | bytes 147488 | tf_op jit(solution)/shard_map/ppermute | solution.py:107
  47.4 5.1 %collective-permute-done.8 = f32[9,32,128]{2,1,0:T(8,128)S(1)} collective-permute-done((f32[9,32,128]{2,1,0:T(8,128)S(1)}, f32[9,32,128]{2,1,0:T(8,128)S(1)}, u32[]{:S(2)}, u32[]{:S(2)}) %collective-permute-start.8) | collective-permute-done | bytes 147488 | tf_op jit(solution)/shard_map/ppermute | solution.py:120
  52.6 1.6 %collective-permute-start.9 = (f32[9,32,256]{2,1,0:T(8,128)S(1)}, f32[9,32,256]{2,1,0:T(8,128)S(1)}, u32[]{:S(2)}, u32[]{:S(2)}) collective-permute-start(f32[9,32,256]{2,1,0:T(8,128)S(1)} %pad_maximum_fusion.2), channel_id=1, source_target_pairs={{0,2},{1,5},{2,0},{3,7},{4,6},{5,1},{6,4},{7,3},{8,10},{9,13},{10,... | collective-permute-start | bytes 884744 | tf_op jit(solution)/shard_map/ppermute | solution.py:120
  54.2 5.2 %collective-permute-done.9 = f32[9,32,256]{2,1,0:T(8,128)S(1)} collective-permute-done((f32[9,32,256]{2,1,0:T(8,128)S(1)}, f32[9,32,256]{2,1,0:T(8,128)S(1)}, u32[]{:S(2)}, u32[]{:S(2)}) %collective-permute-start.9) | collective-permute-done | bytes 294944 | tf_op jit(solution)/shard_map/ppermute | solution.py:120
  59.7 2.1 %collective-permute-done.10 = f32[9,32,512]{2,1,0:T(8,128)} collective-permute-done((f32[9,32,512]{2,1,0:T(8,128)S(1)}, f32[9,32,512]{2,1,0:T(8,128)}, u32[]{:S(2)}, u32[]{:S(2)}) %collective-permute-start.10) | collective-permute-done | bytes 589856 | tf_op jit(solution)/shard_map/ppermute | solution.py:120
  64.6 3.6 %collective-permute-done.11 = f32[4,64,32]{1,2,0:T(8,128)S(1)} collective-permute-done((f32[4,64,32]{1,2,0:T(8,128)S(1)}, f32[4,64,32]{1,2,0:T(8,128)S(1)}, u32[]{:S(2)}, u32[]{:S(2)}) %collective-permute-start.11) | collective-permute-done | bytes 32800 | tf_op jit(solution)/shard_map/ppermute | solution.py:21
  69.4 2.0 %collective-permute-done.12 = f32[9,32,512]{2,1,0:T(8,128)S(1)} collective-permute-done((f32[9,32,512]{2,1,0:T(8,128)S(1)}, f32[9,32,512]{2,1,0:T(8,128)S(1)}, u32[]{:S(2)}, u32[]{:S(2)}) %collective-permute-start.12) | collective-permute-done | bytes 589856 | tf_op jit(solution)/shard_map/ppermute | solution.py:94
  71.5 1.6 %collective-permute-start.13 = (f32[9,32,256]{2,1,0:T(8,128)S(1)}, f32[9,32,256]{2,1,0:T(8,128)S(1)}, u32[]{:S(2)}, u32[]{:S(2)}) collective-permute-start(f32[9,32,256]{2,1,0:T(8,128)S(1)} %constant_dynamic-slice_fusion.1), channel_id=1, source_target_pairs={{0,2},{1,5},{2,0},{3,7},{4,6},{5,1},{6,4},{7,3},{8,10},{9,13},{10,... | collective-permute-start | bytes 884744 | tf_op jit(solution)/shard_map/ppermute | solution.py:94
  73.1 5.2 %collective-permute-done.13 = f32[9,32,256]{2,1,0:T(8,128)S(1)} collective-permute-done((f32[9,32,256]{2,1,0:T(8,128)S(1)}, f32[9,32,256]{2,1,0:T(8,128)S(1)}, u32[]{:S(2)}, u32[]{:S(2)}) %collective-permute-start.13) | collective-permute-done | bytes 294944 | tf_op jit(solution)/shard_map/ppermute | solution.py:94
  78.5 5.1 %collective-permute-done.14 = f32[9,32,128]{2,1,0:T(8,128)S(1)} collective-permute-done((f32[9,32,128]{2,1,0:T(8,128)S(1)}, f32[9,32,128]{2,1,0:T(8,128)S(1)}, u32[]{:S(2)}, u32[]{:S(2)}) %collective-permute-start.14) | collective-permute-done | bytes 147488 | tf_op jit(solution)/shard_map/ppermute | solution.py:94
  83.6 2.1 %collective-permute-start.15 = (f32[9,32,128]{2,1,0:T(8,128)S(1)}, f32[9,32,128]{2,1,0:T(8,128)S(1)}, u32[]{:S(2)}, u32[]{:S(2)}) collective-permute-start(f32[9,32,128]{2,1,0:T(8,128)S(1)} %dynamic-slice_add_fusion.4), channel_id=1, source_target_pairs={{0,8},{1,17},{2,10},{3,19},{4,12},{5,21},{6,14},{7,23},{8,0},{9,25... | collective-permute-start | bytes 442376 | tf_op jit(solution)/shard_map/ppermute | solution.py:108
  86.4 1.7 %collective-permute-start.17 = (f32[9,32,128]{2,1,0:T(8,128)S(1)}, f32[9,32,128]{2,1,0:T(8,128)S(1)}, u32[]{:S(2)}, u32[]{:S(2)}) collective-permute-start(f32[9,32,128]{2,1,0:T(8,128)S(1)} %dynamic-slice_add_fusion.4), channel_id=1, source_target_pairs={{0,24},{1,25},{2,26},{3,27},{4,28},{5,29},{6,30},{7,31},{8,16},{9,... | collective-permute-start | bytes 442376 | tf_op jit(solution)/shard_map/ppermute | solution.py:107
  88.1 8.0 %collective-permute-done.15 = f32[9,32,128]{2,1,0:T(8,128)S(1)} collective-permute-done((f32[9,32,128]{2,1,0:T(8,128)S(1)}, f32[9,32,128]{2,1,0:T(8,128)S(1)}, u32[]{:S(2)}, u32[]{:S(2)}) %collective-permute-start.15) | collective-permute-done | bytes 147488 | tf_op jit(solution)/shard_map/ppermute | solution.py:108
  96.1 3.0 %collective-permute-done.17 = f32[9,32,128]{2,1,0:T(8,128)S(1)} collective-permute-done((f32[9,32,128]{2,1,0:T(8,128)S(1)}, f32[9,32,128]{2,1,0:T(8,128)S(1)}, u32[]{:S(2)}, u32[]{:S(2)}) %collective-permute-start.17) | collective-permute-done | bytes 147488 | tf_op jit(solution)/shard_map/ppermute | solution.py:107
  99.3 5.1 %collective-permute-done.18 = f32[9,32,128]{2,1,0:T(8,128)S(1)} collective-permute-done((f32[9,32,128]{2,1,0:T(8,128)S(1)}, f32[9,32,128]{2,1,0:T(8,128)S(1)}, u32[]{:S(2)}, u32[]{:S(2)}) %collective-permute-start.18) | collective-permute-done | bytes 147488 | tf_op jit(solution)/shard_map/ppermute | solution.py:120
  104.5 1.6 %collective-permute-start.19 = (f32[9,32,256]{2,1,0:T(8,128)S(1)}, f32[9,32,256]{2,1,0:T(8,128)S(1)}, u32[]{:S(2)}, u32[]{:S(2)}) collective-permute-start(f32[9,32,256]{2,1,0:T(8,128)S(1)} %pad_maximum_fusion.3), channel_id=1, source_target_pairs={{0,2},{1,5},{2,0},{3,7},{4,6},{5,1},{6,4},{7,3},{8,10},{9,13},{10,... | collective-permute-start | bytes 884744 | tf_op jit(solution)/shard_map/ppermute | solution.py:120
  106.1 5.2 %collective-permute-done.19 = f32[9,32,256]{2,1,0:T(8,128)S(1)} collective-permute-done((f32[9,32,256]{2,1,0:T(8,128)S(1)}, f32[9,32,256]{2,1,0:T(8,128)S(1)}, u32[]{:S(2)}, u32[]{:S(2)}) %collective-permute-start.19) | collective-permute-done | bytes 294944 | tf_op jit(solution)/shard_map/ppermute | solution.py:120
  111.5 2.0 %collective-permute-done.20 = f32[9,32,512]{2,1,0:T(8,128)S(1)} collective-permute-done((f32[9,32,512]{2,1,0:T(8,128)S(1)}, f32[9,32,512]{2,1,0:T(8,128)S(1)}, u32[]{:S(2)}, u32[]{:S(2)}) %collective-permute-start.20) | collective-permute-done | bytes 589856 | tf_op jit(solution)/shard_map/ppermute | solution.py:120
  113.6 2.1 %multiply_add_fusion = (f32[4,64,1024]{2,1,0:T(8,128)}, f32[1,4,64,1024]{3,2,1,0:T(8,128)}) fusion(f32[4,64,1024]{2,1,0:T(8,128)S(1)} %copy-done.3, f32[4]{0:T(128)S(1)} %convolution_bitcast_fusion, f32[1,4,64,1024]{3,2,1,0:T(8,128)S(1)} %copy-done.1, bf16[1,4,64,1024]{3,2,1,0:T(8,128)(2,1)S(1)} %copy-done.2, f32[4,64,32]{1,2,0:T(8,128)S(1)} %fusion.50, ...), kind=kOutput, calls=%fused_computation.12 | convolution fusion | flops 52166656 | bytes 5275664 | tf_op jit(solution)/shard_map/tks,tsd->tkd/dot_general | solution.py:179
  (86 shorter events, 9.9 us)
Async XLA Ops:
  0.6 10.1 %copy-start = (f32[4]{0:T(128)S(1)}, f32[4]{0:T(128)}, u32[]{:S(2)}) copy-start(f32[4]{0:T(128)} %param.15) | copy-start | bytes 52
  0.6 5.2 %copy-start.1 = (f32[1,4,64,1024]{3,2,1,0:T(8,128)S(1)}, f32[1,4,64,1024]{3,2,1,0:T(8,128)}, u32[]{:S(2)}) copy-start(f32[1,4,64,1024]{3,2,1,0:T(8,128)} %param.11) | copy-start | bytes 3145732
  5.8 4.8 %copy-start.5 = (f32[1,5,1024]{2,0,1:T(1,128)S(1)}, f32[1,5,1024]{2,0,1:T(1,128)}, u32[]{:S(2)}) copy-start(f32[1,5,1024]{2,0,1:T(1,128)} %param.18) | copy-start | bytes 61444
  5.8 4.9 %copy-start.4 = (f32[3,9,32,32]{3,2,1,0:T(8,128)S(1)}, f32[3,9,32,32]{3,2,1,0:T(8,128)}, u32[]{:S(2)}) copy-start(f32[3,9,32,32]{3,2,1,0:T(8,128)} %param.17) | copy-start | bytes 331780
  7.5 3.3 %copy-start.7 = (s32[9]{0:T(128)S(1)}, s32[9]{0:T(128)}, u32[]{:S(2)}) copy-start(s32[9]{0:T(128)} %param.14) | copy-start | bytes 112
  7.5 3.5 %copy-start.8 = (s32[4]{0:T(128)S(1)}, s32[4]{0:T(128)}, u32[]{:S(2)}) copy-start(s32[4]{0:T(128)} %param.13) | copy-start | bytes 52
  7.5 7.1 %copy-start.6 = (f32[5,1024]{1,0:T(8,128)S(1)}, f32[5,1024]{1,0:T(8,128)}, u32[]{:S(2)}) copy-start(f32[5,1024]{1,0:T(8,128)} %param.19) | copy-start | bytes 61444
  7.5 8.0 %copy-start.2 = (bf16[1,4,64,1024]{3,2,1,0:T(8,128)(2,1)S(1)}, bf16[1,4,64,1024]{3,2,1,0:T(8,128)(2,1)}, u32[]{:S(2)}) copy-start(bf16[1,4,64,1024]{3,2,1,0:T(8,128)(2,1)} %param.10) | copy-start | bytes 1572868
  7.5 7.7 %collective-permute-start = (f32[4,64,32]{1,2,0:T(8,128)S(1)}, f32[4,64,32]{1,2,0:T(8,128)S(1)}, u32[]{:S(2)}, u32[]{:S(2)}) collective-permute-start(f32[4,64,32]{1,2,0:T(8,128)S(1)} %fusion.6), channel_id=1, source_target_pairs={{0,16},{16,0},{1,17},{17,1},{2,18},{18,2},{3,19},{19,3},{4,20},{20... | collective-permute-start | bytes 98312 | tf_op jit(solution)/shard_map/ppermute | solution.py:21
  10.6 4.0 %collective-permute-start.1 = (f32[5,1024]{1,0:T(8,128)S(1)}, f32[5,1024]{1,0:T(8,128)S(1)}, u32[]{:S(2)}, u32[]{:S(2)}) collective-permute-start(f32[5,1024]{1,0:T(8,128)S(1)} %bitcast.59), channel_id=1, source_target_pairs={{0,16},{16,0},{1,17},{17,1},{2,18},{18,2},{3,19},{19,3},{4,20},{20... | collective-permute-start | bytes 61448 | tf_op jit(solution)/shard_map/ppermute | solution.py:21
  16.3 2.2 %collective-permute-start.2 = (f32[9,32,512]{2,1,0:T(8,128)S(1)}, f32[9,32,512]{2,1,0:T(8,128)}, u32[]{:S(2)}, u32[]{:S(2)}) collective-permute-start(f32[9,32,512]{2,1,0:T(8,128)S(1)} %constant_dynamic-slice_fusion.13), channel_id=1, source_target_pairs={{0,1},{1,0},{2,3},{3,2},{4,5},{5,4},{6,7},{7,6},{8,9},{9,8},{10,11... | collective-permute-start | bytes 1769480 | tf_op jit(solution)/shard_map/ppermute | solution.py:94
  19.7 6.8 %collective-permute-start.3 = (f32[9,32,256]{2,1,0:T(8,128)S(1)}, f32[9,32,256]{2,1,0:T(8,128)S(1)}, u32[]{:S(2)}, u32[]{:S(2)}) collective-permute-start(f32[9,32,256]{2,1,0:T(8,128)S(1)} %constant_dynamic-slice_fusion.12), channel_id=1, source_target_pairs={{0,2},{1,5},{2,0},{3,7},{4,6},{5,1},{6,4},{7,3},{8,10},{9,13},{10,... | collective-permute-start | bytes 884744 | tf_op jit(solution)/shard_map/ppermute | solution.py:94
  26.5 5.2 %collective-permute-start.4 = (f32[9,32,128]{2,1,0:T(8,128)S(1)}, f32[9,32,128]{2,1,0:T(8,128)S(1)}, u32[]{:S(2)}, u32[]{:S(2)}) collective-permute-start(f32[9,32,128]{2,1,0:T(8,128)S(1)} %constant_dynamic-slice_fusion.11), channel_id=1, source_target_pairs={{0,4},{1,3},{2,6},{3,1},{4,0},{5,7},{6,2},{7,5},{8,12},{9,11},{10,... | collective-permute-start | bytes 442376 | tf_op jit(solution)/shard_map/ppermute | solution.py:94
  31.8 12.6 %collective-permute-start.5 = (f32[9,32,128]{2,1,0:T(8,128)S(1)}, f32[9,32,128]{2,1,0:T(8,128)S(1)}, u32[]{:S(2)}, u32[]{:S(2)}) collective-permute-start(f32[9,32,128]{2,1,0:T(8,128)S(1)} %dynamic-slice_add_fusion.5), channel_id=1, source_target_pairs={{0,8},{1,17},{2,10},{3,19},{4,12},{5,21},{6,14},{7,23},{8,0},{9,25... | collective-permute-start | bytes 442376 | tf_op jit(solution)/shard_map/ppermute | solution.py:108
  34.4 10.0 %collective-permute-start.6 = (f32[9,32,128]{2,1,0:T(8,128)S(1)}, f32[9,32,128]{2,1,0:T(8,128)S(1)}, u32[]{:S(2)}, u32[]{:S(2)}) collective-permute-start(f32[9,32,128]{2,1,0:T(8,128)S(1)} %dynamic-slice_add_fusion.5), channel_id=1, source_target_pairs={{0,16},{1,9},{2,18},{3,11},{4,20},{5,13},{6,22},{7,15},{8,24},{9,1... | collective-permute-start | bytes 442376 | tf_op jit(solution)/shard_map/ppermute | solution.py:108
  35.0 12.2 %collective-permute-start.7 = (f32[9,32,128]{2,1,0:T(8,128)S(1)}, f32[9,32,128]{2,1,0:T(8,128)S(1)}, u32[]{:S(2)}, u32[]{:S(2)}) collective-permute-start(f32[9,32,128]{2,1,0:T(8,128)S(1)} %dynamic-slice_add_fusion.5), channel_id=1, source_target_pairs={{0,24},{1,25},{2,26},{3,27},{4,28},{5,29},{6,30},{7,31},{8,16},{9,... | collective-permute-start | bytes 442376 | tf_op jit(solution)/shard_map/ppermute | solution.py:107
  47.4 5.2 %collective-permute-start.8 = (f32[9,32,128]{2,1,0:T(8,128)S(1)}, f32[9,32,128]{2,1,0:T(8,128)S(1)}, u32[]{:S(2)}, u32[]{:S(2)}) collective-permute-start(f32[9,32,128]{2,1,0:T(8,128)S(1)} %select_add_fusion.1), channel_id=1, source_target_pairs={{0,4},{1,3},{2,6},{3,1},{4,0},{5,7},{6,2},{7,5},{8,12},{9,11},{10,... | collective-permute-start | bytes 442376 | tf_op jit(solution)/shard_map/ppermute | solution.py:120
  52.6 6.8 %collective-permute-start.9 = (f32[9,32,256]{2,1,0:T(8,128)S(1)}, f32[9,32,256]{2,1,0:T(8,128)S(1)}, u32[]{:S(2)}, u32[]{:S(2)}) collective-permute-start(f32[9,32,256]{2,1,0:T(8,128)S(1)} %pad_maximum_fusion.2), channel_id=1, source_target_pairs={{0,2},{1,5},{2,0},{3,7},{4,6},{5,1},{6,4},{7,3},{8,10},{9,13},{10,... | collective-permute-start | bytes 884744 | tf_op jit(solution)/shard_map/ppermute | solution.py:120
  59.5 2.2 %collective-permute-start.10 = (f32[9,32,512]{2,1,0:T(8,128)S(1)}, f32[9,32,512]{2,1,0:T(8,128)}, u32[]{:S(2)}, u32[]{:S(2)}) collective-permute-start(f32[9,32,512]{2,1,0:T(8,128)S(1)} %pad_maximum_fusion), channel_id=1, source_target_pairs={{0,1},{1,0},{2,3},{3,2},{4,5},{5,4},{6,7},{7,6},{8,9},{9,8},{10,11... | collective-permute-start | bytes 1769480 | tf_op jit(solution)/shard_map/ppermute | solution.py:120
  64.0 4.3 %collective-permute-start.11 = (f32[4,64,32]{1,2,0:T(8,128)S(1)}, f32[4,64,32]{1,2,0:T(8,128)S(1)}, u32[]{:S(2)}, u32[]{:S(2)}) collective-permute-start(f32[4,64,32]{1,2,0:T(8,128)S(1)} %fusion.2), channel_id=1, source_target_pairs={{0,16},{16,0},{1,17},{17,1},{2,18},{18,2},{3,19},{19,3},{4,20},{20... | collective-permute-start | bytes 98312 | tf_op jit(solution)/shard_map/ppermute | solution.py:21
  69.3 2.1 %collective-permute-start.12 = (f32[9,32,512]{2,1,0:T(8,128)S(1)}, f32[9,32,512]{2,1,0:T(8,128)S(1)}, u32[]{:S(2)}, u32[]{:S(2)}) collective-permute-start(f32[9,32,512]{2,1,0:T(8,128)S(1)} %constant_dynamic-slice_fusion.2), channel_id=1, source_target_pairs={{0,1},{1,0},{2,3},{3,2},{4,5},{5,4},{6,7},{7,6},{8,9},{9,8},{10,11... | collective-permute-start | bytes 1769480 | tf_op jit(solution)/shard_map/ppermute | solution.py:94
  71.5 6.8 %collective-permute-start.13 = (f32[9,32,256]{2,1,0:T(8,128)S(1)}, f32[9,32,256]{2,1,0:T(8,128)S(1)}, u32[]{:S(2)}, u32[]{:S(2)}) collective-permute-start(f32[9,32,256]{2,1,0:T(8,128)S(1)} %constant_dynamic-slice_fusion.1), channel_id=1, source_target_pairs={{0,2},{1,5},{2,0},{3,7},{4,6},{5,1},{6,4},{7,3},{8,10},{9,13},{10,... | collective-permute-start | bytes 884744 | tf_op jit(solution)/shard_map/ppermute | solution.py:94
  78.4 5.2 %collective-permute-start.14 = (f32[9,32,128]{2,1,0:T(8,128)S(1)}, f32[9,32,128]{2,1,0:T(8,128)S(1)}, u32[]{:S(2)}, u32[]{:S(2)}) collective-permute-start(f32[9,32,128]{2,1,0:T(8,128)S(1)} %constant_dynamic-slice_fusion), channel_id=1, source_target_pairs={{0,4},{1,3},{2,6},{3,1},{4,0},{5,7},{6,2},{7,5},{8,12},{9,11},{10,... | collective-permute-start | bytes 442376 | tf_op jit(solution)/shard_map/ppermute | solution.py:94
  83.6 12.5 %collective-permute-start.15 = (f32[9,32,128]{2,1,0:T(8,128)S(1)}, f32[9,32,128]{2,1,0:T(8,128)S(1)}, u32[]{:S(2)}, u32[]{:S(2)}) collective-permute-start(f32[9,32,128]{2,1,0:T(8,128)S(1)} %dynamic-slice_add_fusion.4), channel_id=1, source_target_pairs={{0,8},{1,17},{2,10},{3,19},{4,12},{5,21},{6,14},{7,23},{8,0},{9,25... | collective-permute-start | bytes 442376 | tf_op jit(solution)/shard_map/ppermute | solution.py:108
  85.7 10.4 %collective-permute-start.16 = (f32[9,32,128]{2,1,0:T(8,128)S(1)}, f32[9,32,128]{2,1,0:T(8,128)S(1)}, u32[]{:S(2)}, u32[]{:S(2)}) collective-permute-start(f32[9,32,128]{2,1,0:T(8,128)S(1)} %dynamic-slice_add_fusion.4), channel_id=1, source_target_pairs={{0,16},{1,9},{2,18},{3,11},{4,20},{5,13},{6,22},{7,15},{8,24},{9,1... | collective-permute-start | bytes 442376 | tf_op jit(solution)/shard_map/ppermute | solution.py:108
  86.4 12.8 %collective-permute-start.17 = (f32[9,32,128]{2,1,0:T(8,128)S(1)}, f32[9,32,128]{2,1,0:T(8,128)S(1)}, u32[]{:S(2)}, u32[]{:S(2)}) collective-permute-start(f32[9,32,128]{2,1,0:T(8,128)S(1)} %dynamic-slice_add_fusion.4), channel_id=1, source_target_pairs={{0,24},{1,25},{2,26},{3,27},{4,28},{5,29},{6,30},{7,31},{8,16},{9,... | collective-permute-start | bytes 442376 | tf_op jit(solution)/shard_map/ppermute | solution.py:107
  99.2 5.2 %collective-permute-start.18 = (f32[9,32,128]{2,1,0:T(8,128)S(1)}, f32[9,32,128]{2,1,0:T(8,128)S(1)}, u32[]{:S(2)}, u32[]{:S(2)}) collective-permute-start(f32[9,32,128]{2,1,0:T(8,128)S(1)} %select_add_fusion), channel_id=1, source_target_pairs={{0,4},{1,3},{2,6},{3,1},{4,0},{5,7},{6,2},{7,5},{8,12},{9,11},{10,... | collective-permute-start | bytes 442376 | tf_op jit(solution)/shard_map/ppermute | solution.py:120
  104.5 6.8 %collective-permute-start.19 = (f32[9,32,256]{2,1,0:T(8,128)S(1)}, f32[9,32,256]{2,1,0:T(8,128)S(1)}, u32[]{:S(2)}, u32[]{:S(2)}) collective-permute-start(f32[9,32,256]{2,1,0:T(8,128)S(1)} %pad_maximum_fusion.3), channel_id=1, source_target_pairs={{0,2},{1,5},{2,0},{3,7},{4,6},{5,1},{6,4},{7,3},{8,10},{9,13},{10,... | collective-permute-start | bytes 884744 | tf_op jit(solution)/shard_map/ppermute | solution.py:120
  111.4 2.2 %copy-start.3 = (f32[4,64,1024]{2,1,0:T(8,128)S(1)}, f32[4,64,1024]{2,1,0:T(8,128)}, u32[]{:S(2)}) copy-start(f32[4,64,1024]{2,1,0:T(8,128)} %param.12) | copy-start | bytes 3145732
  111.4 2.1 %collective-permute-start.20 = (f32[9,32,512]{2,1,0:T(8,128)S(1)}, f32[9,32,512]{2,1,0:T(8,128)S(1)}, u32[]{:S(2)}, u32[]{:S(2)}) collective-permute-start(f32[9,32,512]{2,1,0:T(8,128)S(1)} %pad_maximum_fusion.1), channel_id=1, source_target_pairs={{0,1},{1,0},{2,3},{3,2},{4,5},{5,4},{6,7},{7,6},{8,9},{9,8},{10,11... | collective-permute-start | bytes 1769480 | tf_op jit(solution)/shard_map/ppermute | solution.py:120

commit v20 on v15

--- a/solution.py
+++ b/solution.py
@@ -104,7 +104,11 @@
             return pairs
 
         place = bit_of(a0, a1) + 2 * bit_of(b0, b1)
-        held = [cur] + [lax.ppermute(cur, axes, group_perm(k)) for k in (1, 2, 3)]
+        diagonal = lax.ppermute(cur, axes, group_perm(3))
+        near = lax.ppermute(cur, axes, group_perm(2))
+        far = lax.ppermute(cur, axes, group_perm(1))
+        sides = [far, near]
+        held = [cur] + sides + [diagonal]
         total = None
         for member in range(4):
             term = lax.select_n(place ^ member, *held)

time: 115 us -> 115 us (level)
  no operation moved by 1% of the time
where the time goes in v20:
time: 115 us
  waiting for transfers between devices  72.7 us (63%)
  starting transfers between devices  24.4 us (21%)
  matrix products  6.88 us (6%)
  other arithmetic  4.24 us (4%)
  between operations  3.81 us (3%)
  local copies, waits for them, and re-layouts  2.89 us (3%)
    ppermute x6, waiting for transfers between devices, table_rows(): other = lax.ppermute(cur, axes, perm_of(p0, p1))  23.8 us
    ppermute x6, waiting for transfers between devices, table_rows(): cur = keep + lax.ppermute(send, axes, perm_of(p0, p1))  21.8 us
    ppermute x2, waiting for transfers between devices, table_rows(): far = lax.ppermute(cur, axes, group_perm(1))  18.1 us
    ppermute x6, starting transfers between devices, table_rows(): cur = keep + lax.ppermute(send, axes, perm_of(p0, p1))  6.49 us
    ppermute x2, starting transfers between devices, table_rows(): far = lax.ppermute(cur, axes, group_perm(1))  5.06 us
    ppermute x2, waiting for transfers between devices, swap_sum(): x = x + lax.ppermute(x, axis, _pair_perm(n, j))  4.48 us
    ppermute x2, starting transfers between devices, swap_sum(): x = x + lax.ppermute(x, axis, _pair_perm(n, j))  4.45 us
    ppermute x2, waiting for transfers between devices, table_rows(): diagonal = lax.ppermute(cur, axes, group_perm(3))  4.45 us
  transfers between devices with their start and end apart: 20, of which 18 were waited for; matrix products, arithmetic and copies ran while one was open for 0% of the time, Pallas kernels for 0%

profile of v20, /device:TPU:0, one launch (start us, length us, event | category | flops | bytes accessed | tf_op | source)
XLA Modules:
  0.0 114.8 jit_solution(221112011161294084)
XLA Ops:
  0.7 1.4 %shift-left_reduce_fusion = s32[]{:T(128)} fusion(s32[4]{0:T(128)} %param.13), kind=kLoop, calls=%fused_computation.161 | loop fusion | flops 11 | bytes 20 | tf_op jit(solution)/shard_map/reduce_sum | solution.py:49
  5.8 1.7 %fusion.6 = f32[4,64,32]{2,1,0:T(8,128)S(1)} fusion(f32[1,1024,32]{1,2,0:T(8,128)S(1)} %get-tuple-element.15, f32[1,1024,32]{1,2,0:T(8,128)S(1)} %get-tuple-element.16, f32[1,1024,32]{1,2,0:T(8,128)S(1)} %get-tuple-element.14, f32[1,1024,32]{1,2,0:T(8,128)S(1)} %get-tuple-element.13, f32[1,4,64,1024]{3,2,1,0:T(8,128)S(1)} %copy-done.1, ...), kind=kOutput, calls=%fused_computation.9 | convolution fusion | flops 51249152 | bytes 2129920 | tf_op jit(solution)/shard_map/tkd,tds->tks/dot_general | solution.py:155
  7.7 3.0 %collective-permute-start = (f32[13312]{0:T(1024)S(1)}, f32[13312]{0:T(1024)S(1)}, u32[]{:S(2)}, u32[]{:S(2)}) collective-permute-start(f32[13312]{0:T(1024)S(1)} %pad_maximum_fusion.10), channel_id=1, source_target_pairs={{0,16},{16,0},{1,17},{17,1},{2,18},{18,2},{3,19},{19,3},{4,20},{20... | collective-permute-start | bytes 159752 | tf_op jit(solution)/shard_map/ppermute | solution.py:21
  11.2 1.6 %collective-permute-done = f32[13312]{0:T(1024)S(1)} collective-permute-done((f32[13312]{0:T(1024)S(1)}, f32[13312]{0:T(1024)S(1)}, u32[]{:S(2)}, u32[]{:S(2)}) %collective-permute-start) | collective-permute-done | bytes 53280 | tf_op jit(solution)/shard_map/ppermute | solution.py:21
  14.8 2.1 %collective-permute-done.1 = f32[9,32,512]{2,1,0:T(8,128)} collective-permute-done((f32[9,32,512]{2,1,0:T(8,128)S(1)}, f32[9,32,512]{2,1,0:T(8,128)}, u32[]{:S(2)}, u32[]{:S(2)}) %collective-permute-start.1) | collective-permute-done | bytes 589856 | tf_op jit(solution)/shard_map/ppermute | solution.py:94
  18.1 2.1 %collective-permute-start.2 = (f32[9,32,256]{2,1,0:T(8,128)S(1)}, f32[9,32,256]{2,1,0:T(8,128)S(1)}, u32[]{:S(2)}, u32[]{:S(2)}) collective-permute-start(f32[9,32,256]{2,1,0:T(8,128)S(1)} %constant_dynamic-slice_fusion.12), channel_id=1, source_target_pairs={{0,2},{1,5},{2,0},{3,7},{4,6},{5,1},{6,4},{7,3},{8,10},{9,13},{10,... | collective-permute-start | bytes 884744 | tf_op jit(solution)/shard_map/ppermute | solution.py:94
  20.2 4.7 %collective-permute-done.2 = f32[9,32,256]{2,1,0:T(8,128)S(1)} collective-permute-done((f32[9,32,256]{2,1,0:T(8,128)S(1)}, f32[9,32,256]{2,1,0:T(8,128)S(1)}, u32[]{:S(2)}, u32[]{:S(2)}) %collective-permute-start.2) | collective-permute-done | bytes 294944 | tf_op jit(solution)/shard_map/ppermute | solution.py:94
  25.0 2.1 %collective-permute-start.3 = (f32[9,32,128]{2,1,0:T(8,128)S(1)}, f32[9,32,128]{2,1,0:T(8,128)S(1)}, u32[]{:S(2)}, u32[]{:S(2)}) collective-permute-start(f32[9,32,128]{2,1,0:T(8,128)S(1)} %constant_dynamic-slice_fusion.11), channel_id=1, source_target_pairs={{0,4},{1,3},{2,6},{3,1},{4,0},{5,7},{6,2},{7,5},{8,12},{9,11},{10,... | collective-permute-start | bytes 442376 | tf_op jit(solution)/shard_map/ppermute | solution.py:94
  27.1 3.1 %collective-permute-done.3 = f32[9,32,128]{2,1,0:T(8,128)S(1)} collective-permute-done((f32[9,32,128]{2,1,0:T(8,128)S(1)}, f32[9,32,128]{2,1,0:T(8,128)S(1)}, u32[]{:S(2)}, u32[]{:S(2)}) %collective-permute-start.3) | collective-permute-done | bytes 147488 | tf_op jit(solution)/shard_map/ppermute | solution.py:94
  30.3 3.1 %collective-permute-start.4 = (f32[9,32,128]{2,1,0:T(8,128)S(1)}, f32[9,32,128]{2,1,0:T(8,128)S(1)}, u32[]{:S(2)}, u32[]{:S(2)}) collective-permute-start(f32[9,32,128]{2,1,0:T(8,128)S(1)} %dynamic-slice_add_fusion.5), channel_id=1, source_target_pairs={{0,8},{1,17},{2,10},{3,19},{4,12},{5,21},{6,14},{7,23},{8,0},{9,25... | collective-permute-start | bytes 442376 | tf_op jit(solution)/shard_map/ppermute | solution.py:109
  33.4 1.5 %collective-permute-start.5 = (f32[9,32,128]{2,1,0:T(8,128)S(1)}, f32[9,32,128]{2,1,0:T(8,128)S(1)}, u32[]{:S(2)}, u32[]{:S(2)}) collective-permute-start(f32[9,32,128]{2,1,0:T(8,128)S(1)} %dynamic-slice_add_fusion.5), channel_id=1, source_target_pairs={{0,16},{1,9},{2,18},{3,11},{4,20},{5,13},{6,22},{7,15},{8,24},{9,1... | collective-permute-start | bytes 442376 | tf_op jit(solution)/shard_map/ppermute | solution.py:108
  34.9 9.3 %collective-permute-done.4 = f32[9,32,128]{2,1,0:T(8,128)S(1)} collective-permute-done((f32[9,32,128]{2,1,0:T(8,128)S(1)}, f32[9,32,128]{2,1,0:T(8,128)S(1)}, u32[]{:S(2)}, u32[]{:S(2)}) %collective-permute-start.4) | collective-permute-done | bytes 147488 | tf_op jit(solution)/shard_map/ppermute | solution.py:109
  44.2 2.1 %collective-permute-done.6 = f32[9,32,128]{2,1,0:T(8,128)S(1)} collective-permute-done((f32[9,32,128]{2,1,0:T(8,128)S(1)}, f32[9,32,128]{2,1,0:T(8,128)S(1)}, u32[]{:S(2)}, u32[]{:S(2)}) %collective-permute-start.6) | collective-permute-done | bytes 147488 | tf_op jit(solution)/shard_map/ppermute | solution.py:107
  47.1 4.6 %collective-permute-done.7 = f32[9,32,128]{2,1,0:T(8,128)S(1)} collective-permute-done((f32[9,32,128]{2,1,0:T(8,128)S(1)}, f32[9,32,128]{2,1,0:T(8,128)S(1)}, u32[]{:S(2)}, u32[]{:S(2)}) %collective-permute-start.7) | collective-permute-done | bytes 147488 | tf_op jit(solution)/shard_map/ppermute | solution.py:122
  51.7 1.5 %collective-permute-start.8 = (f32[9,32,256]{2,1,0:T(8,128)S(1)}, f32[9,32,256]{2,1,0:T(8,128)S(1)}, u32[]{:S(2)}, u32[]{:S(2)}) collective-permute-start(f32[9,32,256]{2,1,0:T(8,128)S(1)} %pad_maximum_fusion.2), channel_id=1, source_target_pairs={{0,2},{1,5},{2,0},{3,7},{4,6},{5,1},{6,4},{7,3},{8,10},{9,13},{10,... | collective-permute-start | bytes 884744 | tf_op jit(solution)/shard_map/ppermute | solution.py:122
  53.2 5.3 %collective-permute-done.8 = f32[9,32,256]{2,1,0:T(8,128)S(1)} collective-permute-done((f32[9,32,256]{2,1,0:T(8,128)S(1)}, f32[9,32,256]{2,1,0:T(8,128)S(1)}, u32[]{:S(2)}, u32[]{:S(2)}) %collective-permute-start.8) | collective-permute-done | bytes 294944 | tf_op jit(solution)/shard_map/ppermute | solution.py:122
  58.8 2.1 %collective-permute-done.9 = f32[9,32,512]{2,1,0:T(8,128)} collective-permute-done((f32[9,32,512]{2,1,0:T(8,128)S(1)}, f32[9,32,512]{2,1,0:T(8,128)}, u32[]{:S(2)}, u32[]{:S(2)}) %collective-permute-start.9) | collective-permute-done | bytes 589856 | tf_op jit(solution)/shard_map/ppermute | solution.py:122
  63.1 1.4 %collective-permute-start.10 = (f32[4,64,32]{1,2,0:T(8,128)S(1)}, f32[4,64,32]{1,2,0:T(8,128)S(1)}, u32[]{:S(2)}, u32[]{:S(2)}) collective-permute-start(f32[4,64,32]{1,2,0:T(8,128)S(1)} %fusion.2), channel_id=1, source_target_pairs={{0,16},{16,0},{1,17},{17,1},{2,18},{18,2},{3,19},{19,3},{4,20},{20... | collective-permute-start | bytes 98312 | tf_op jit(solution)/shard_map/ppermute | solution.py:21
  64.5 2.9 %collective-permute-done.10 = f32[4,64,32]{1,2,0:T(8,128)S(1)} collective-permute-done((f32[4,64,32]{1,2,0:T(8,128)S(1)}, f32[4,64,32]{1,2,0:T(8,128)S(1)}, u32[]{:S(2)}, u32[]{:S(2)}) %collective-permute-start.10) | collective-permute-done | bytes 32800 | tf_op jit(solution)/shard_map/ppermute | solution.py:21
  68.5 2.0 %collective-permute-done.11 = f32[9,32,512]{2,1,0:T(8,128)S(1)} collective-permute-done((f32[9,32,512]{2,1,0:T(8,128)S(1)}, f32[9,32,512]{2,1,0:T(8,128)S(1)}, u32[]{:S(2)}, u32[]{:S(2)}) %collective-permute-start.11) | collective-permute-done | bytes 589856 | tf_op jit(solution)/shard_map/ppermute | solution.py:94
  70.6 1.5 %collective-permute-start.12 = (f32[9,32,256]{2,1,0:T(8,128)S(1)}, f32[9,32,256]{2,1,0:T(8,128)S(1)}, u32[]{:S(2)}, u32[]{:S(2)}) collective-permute-start(f32[9,32,256]{2,1,0:T(8,128)S(1)} %constant_dynamic-slice_fusion.1), channel_id=1, source_target_pairs={{0,2},{1,5},{2,0},{3,7},{4,6},{5,1},{6,4},{7,3},{8,10},{9,13},{10,... | collective-permute-start | bytes 884744 | tf_op jit(solution)/shard_map/ppermute | solution.py:94
  72.1 5.3 %collective-permute-done.12 = f32[9,32,256]{2,1,0:T(8,128)S(1)} collective-permute-done((f32[9,32,256]{2,1,0:T(8,128)S(1)}, f32[9,32,256]{2,1,0:T(8,128)S(1)}, u32[]{:S(2)}, u32[]{:S(2)}) %collective-permute-start.12) | collective-permute-done | bytes 294944 | tf_op jit(solution)/shard_map/ppermute | solution.py:94
  78.1 4.6 %collective-permute-done.13 = f32[9,32,128]{2,1,0:T(8,128)S(1)} collective-permute-done((f32[9,32,128]{2,1,0:T(8,128)S(1)}, f32[9,32,128]{2,1,0:T(8,128)S(1)}, u32[]{:S(2)}, u32[]{:S(2)}) %collective-permute-start.13) | collective-permute-done | bytes 147488 | tf_op jit(solution)/shard_map/ppermute | solution.py:94
  82.7 2.0 %collective-permute-start.14 = (f32[9,32,128]{2,1,0:T(8,128)S(1)}, f32[9,32,128]{2,1,0:T(8,128)S(1)}, u32[]{:S(2)}, u32[]{:S(2)}) collective-permute-start(f32[9,32,128]{2,1,0:T(8,128)S(1)} %dynamic-slice_add_fusion.4), channel_id=1, source_target_pairs={{0,8},{1,17},{2,10},{3,19},{4,12},{5,21},{6,14},{7,23},{8,0},{9,25... | collective-permute-start | bytes 442376 | tf_op jit(solution)/shard_map/ppermute | solution.py:109
  84.7 1.5 %collective-permute-start.15 = (f32[9,32,128]{2,1,0:T(8,128)S(1)}, f32[9,32,128]{2,1,0:T(8,128)S(1)}, u32[]{:S(2)}, u32[]{:S(2)}) collective-permute-start(f32[9,32,128]{2,1,0:T(8,128)S(1)} %dynamic-slice_add_fusion.4), channel_id=1, source_target_pairs={{0,16},{1,9},{2,18},{3,11},{4,20},{5,13},{6,22},{7,15},{8,24},{9,1... | collective-permute-start | bytes 442376 | tf_op jit(solution)/shard_map/ppermute | solution.py:108
  87.2 8.7 %collective-permute-done.14 = f32[9,32,128]{2,1,0:T(8,128)S(1)} collective-permute-done((f32[9,32,128]{2,1,0:T(8,128)S(1)}, f32[9,32,128]{2,1,0:T(8,128)S(1)}, u32[]{:S(2)}, u32[]{:S(2)}) %collective-permute-start.14) | collective-permute-done | bytes 147488 | tf_op jit(solution)/shard_map/ppermute | solution.py:109
  95.9 2.3 %collective-permute-done.16 = f32[9,32,128]{2,1,0:T(8,128)S(1)} collective-permute-done((f32[9,32,128]{2,1,0:T(8,128)S(1)}, f32[9,32,128]{2,1,0:T(8,128)S(1)}, u32[]{:S(2)}, u32[]{:S(2)}) %collective-permute-start.16) | collective-permute-done | bytes 147488 | tf_op jit(solution)/shard_map/ppermute | solution.py:107
  99.0 4.6 %collective-permute-done.17 = f32[9,32,128]{2,1,0:T(8,128)S(1)} collective-permute-done((f32[9,32,128]{2,1,0:T(8,128)S(1)}, f32[9,32,128]{2,1,0:T(8,128)S(1)}, u32[]{:S(2)}, u32[]{:S(2)}) %collective-permute-start.17) | collective-permute-done | bytes 147488 | tf_op jit(solution)/shard_map/ppermute | solution.py:122
  103.6 1.5 %collective-permute-start.18 = (f32[9,32,256]{2,1,0:T(8,128)S(1)}, f32[9,32,256]{2,1,0:T(8,128)S(1)}, u32[]{:S(2)}, u32[]{:S(2)}) collective-permute-start(f32[9,32,256]{2,1,0:T(8,128)S(1)} %pad_maximum_fusion.3), channel_id=1, source_target_pairs={{0,2},{1,5},{2,0},{3,7},{4,6},{5,1},{6,4},{7,3},{8,10},{9,13},{10,... | collective-permute-start | bytes 884744 | tf_op jit(solution)/shard_map/ppermute | solution.py:122
  105.0 5.3 %collective-permute-done.18 = f32[9,32,256]{2,1,0:T(8,128)S(1)} collective-permute-done((f32[9,32,256]{2,1,0:T(8,128)S(1)}, f32[9,32,256]{2,1,0:T(8,128)S(1)}, u32[]{:S(2)}, u32[]{:S(2)}) %collective-permute-start.18) | collective-permute-done | bytes 294944 | tf_op jit(solution)/shard_map/ppermute | solution.py:122
  110.6 2.0 %collective-permute-done.19 = f32[9,32,512]{2,1,0:T(8,128)S(1)} collective-permute-done((f32[9,32,512]{2,1,0:T(8,128)S(1)}, f32[9,32,512]{2,1,0:T(8,128)S(1)}, u32[]{:S(2)}, u32[]{:S(2)}) %collective-permute-start.19) | collective-permute-done | bytes 589856 | tf_op jit(solution)/shard_map/ppermute | solution.py:122
  112.7 2.2 %multiply_add_fusion = (f32[4,64,1024]{2,1,0:T(8,128)}, f32[1,4,64,1024]{3,2,1,0:T(8,128)}) fusion(f32[4,64,1024]{2,1,0:T(8,128)S(1)} %copy-done.3, f32[4]{0:T(128)S(1)} %convolution_bitcast_fusion, f32[1,4,64,1024]{3,2,1,0:T(8,128)S(1)} %copy-done.1, bf16[1,4,64,1024]{3,2,1,0:T(8,128)(2,1)S(1)} %copy-done.2, f32[4,64,32]{1,2,0:T(8,128)S(1)} %fusion.50, ...), kind=kOutput, calls=%fused_computation.12 | convolution fusion | flops 52166656 | bytes 5275664 | tf_op jit(solution)/shard_map/tks,tsd->tkd/dot_general | solution.py:184
  (89 shorter events, 12.0 us)
Async XLA Ops:
  0.6 10.2 %copy-start = (f32[4]{0:T(128)S(1)}, f32[4]{0:T(128)}, u32[]{:S(2)}) copy-start(f32[4]{0:T(128)} %param.15) | copy-start | bytes 52
  0.6 5.1 %copy-start.1 = (f32[1,4,64,1024]{3,2,1,0:T(8,128)S(1)}, f32[1,4,64,1024]{3,2,1,0:T(8,128)}, u32[]{:S(2)}) copy-start(f32[1,4,64,1024]{3,2,1,0:T(8,128)} %param.11) | copy-start | bytes 3145732
  5.8 1.8 %copy-start.5 = (f32[1,5,1024]{2,0,1:T(1,128)S(1)}, f32[1,5,1024]{2,0,1:T(1,128)}, u32[]{:S(2)}) copy-start(f32[1,5,1024]{2,0,1:T(1,128)} %param.18) | copy-start | bytes 61444
  5.8 4.9 %copy-start.4 = (f32[3,9,32,32]{3,2,1,0:T(8,128)S(1)}, f32[3,9,32,32]{3,2,1,0:T(8,128)}, u32[]{:S(2)}) copy-start(f32[3,9,32,32]{3,2,1,0:T(8,128)} %param.17) | copy-start | bytes 331780
  7.5 3.3 %copy-start.7 = (s32[9]{0:T(128)S(1)}, s32[9]{0:T(128)}, u32[]{:S(2)}) copy-start(s32[9]{0:T(128)} %param.14) | copy-start | bytes 112
  7.5 3.5 %copy-start.8 = (s32[4]{0:T(128)S(1)}, s32[4]{0:T(128)}, u32[]{:S(2)}) copy-start(s32[4]{0:T(128)} %param.13) | copy-start | bytes 52
  7.6 5.3 %copy-start.6 = (f32[5,1024]{1,0:T(8,128)S(1)}, f32[5,1024]{1,0:T(8,128)}, u32[]{:S(2)}) copy-start(f32[5,1024]{1,0:T(8,128)} %param.19) | copy-start | bytes 61444
  7.6 6.3 %copy-start.2 = (bf16[1,4,64,1024]{3,2,1,0:T(8,128)(2,1)S(1)}, bf16[1,4,64,1024]{3,2,1,0:T(8,128)(2,1)}, u32[]{:S(2)}) copy-start(bf16[1,4,64,1024]{3,2,1,0:T(8,128)(2,1)} %param.10) | copy-start | bytes 1572868
  7.7 5.1 %collective-permute-start = (f32[13312]{0:T(1024)S(1)}, f32[13312]{0:T(1024)S(1)}, u32[]{:S(2)}, u32[]{:S(2)}) collective-permute-start(f32[13312]{0:T(1024)S(1)} %pad_maximum_fusion.10), channel_id=1, source_target_pairs={{0,16},{16,0},{1,17},{17,1},{2,18},{18,2},{3,19},{19,3},{4,20},{20... | collective-permute-start | bytes 159752 | tf_op jit(solution)/shard_map/ppermute | solution.py:21
  14.7 2.2 %collective-permute-start.1 = (f32[9,32,512]{2,1,0:T(8,128)S(1)}, f32[9,32,512]{2,1,0:T(8,128)}, u32[]{:S(2)}, u32[]{:S(2)}) collective-permute-start(f32[9,32,512]{2,1,0:T(8,128)S(1)} %constant_dynamic-slice_fusion.13), channel_id=1, source_target_pairs={{0,1},{1,0},{2,3},{3,2},{4,5},{5,4},{6,7},{7,6},{8,9},{9,8},{10,11... | collective-permute-start | bytes 1769480 | tf_op jit(solution)/shard_map/ppermute | solution.py:94
  18.1 6.8 %collective-permute-start.2 = (f32[9,32,256]{2,1,0:T(8,128)S(1)}, f32[9,32,256]{2,1,0:T(8,128)S(1)}, u32[]{:S(2)}, u32[]{:S(2)}) collective-permute-start(f32[9,32,256]{2,1,0:T(8,128)S(1)} %constant_dynamic-slice_fusion.12), channel_id=1, source_target_pairs={{0,2},{1,5},{2,0},{3,7},{4,6},{5,1},{6,4},{7,3},{8,10},{9,13},{10,... | collective-permute-start | bytes 884744 | tf_op jit(solution)/shard_map/ppermute | solution.py:94
  25.0 5.3 %collective-permute-start.3 = (f32[9,32,128]{2,1,0:T(8,128)S(1)}, f32[9,32,128]{2,1,0:T(8,128)S(1)}, u32[]{:S(2)}, u32[]{:S(2)}) collective-permute-start(f32[9,32,128]{2,1,0:T(8,128)S(1)} %constant_dynamic-slice_fusion.11), channel_id=1, source_target_pairs={{0,4},{1,3},{2,6},{3,1},{4,0},{5,7},{6,2},{7,5},{8,12},{9,11},{10,... | collective-permute-start | bytes 442376 | tf_op jit(solution)/shard_map/ppermute | solution.py:94
  30.3 13.9 %collective-permute-start.4 = (f32[9,32,128]{2,1,0:T(8,128)S(1)}, f32[9,32,128]{2,1,0:T(8,128)S(1)}, u32[]{:S(2)}, u32[]{:S(2)}) collective-permute-start(f32[9,32,128]{2,1,0:T(8,128)S(1)} %dynamic-slice_add_fusion.5), channel_id=1, source_target_pairs={{0,8},{1,17},{2,10},{3,19},{4,12},{5,21},{6,14},{7,23},{8,0},{9,25... | collective-permute-start | bytes 442376 | tf_op jit(solution)/shard_map/ppermute | solution.py:109
  33.4 10.9 %collective-permute-start.5 = (f32[9,32,128]{2,1,0:T(8,128)S(1)}, f32[9,32,128]{2,1,0:T(8,128)S(1)}, u32[]{:S(2)}, u32[]{:S(2)}) collective-permute-start(f32[9,32,128]{2,1,0:T(8,128)S(1)} %dynamic-slice_add_fusion.5), channel_id=1, source_target_pairs={{0,16},{1,9},{2,18},{3,11},{4,20},{5,13},{6,22},{7,15},{8,24},{9,1... | collective-permute-start | bytes 442376 | tf_op jit(solution)/shard_map/ppermute | solution.py:108
  34.9 11.5 %collective-permute-start.6 = (f32[9,32,128]{2,1,0:T(8,128)S(1)}, f32[9,32,128]{2,1,0:T(8,128)S(1)}, u32[]{:S(2)}, u32[]{:S(2)}) collective-permute-start(f32[9,32,128]{2,1,0:T(8,128)S(1)} %dynamic-slice_add_fusion.5), channel_id=1, source_target_pairs={{0,24},{1,25},{2,26},{3,27},{4,28},{5,29},{6,30},{7,31},{8,16},{9,... | collective-permute-start | bytes 442376 | tf_op jit(solution)/shard_map/ppermute | solution.py:107
  46.5 5.2 %collective-permute-start.7 = (f32[9,32,128]{2,1,0:T(8,128)S(1)}, f32[9,32,128]{2,1,0:T(8,128)S(1)}, u32[]{:S(2)}, u32[]{:S(2)}) collective-permute-start(f32[9,32,128]{2,1,0:T(8,128)S(1)} %select_add_fusion.1), channel_id=1, source_target_pairs={{0,4},{1,3},{2,6},{3,1},{4,0},{5,7},{6,2},{7,5},{8,12},{9,11},{10,... | collective-permute-start | bytes 442376 | tf_op jit(solution)/shard_map/ppermute | solution.py:122
  51.7 6.8 %collective-permute-start.8 = (f32[9,32,256]{2,1,0:T(8,128)S(1)}, f32[9,32,256]{2,1,0:T(8,128)S(1)}, u32[]{:S(2)}, u32[]{:S(2)}) collective-permute-start(f32[9,32,256]{2,1,0:T(8,128)S(1)} %pad_maximum_fusion.2), channel_id=1, source_target_pairs={{0,2},{1,5},{2,0},{3,7},{4,6},{5,1},{6,4},{7,3},{8,10},{9,13},{10,... | collective-permute-start | bytes 884744 | tf_op jit(solution)/shard_map/ppermute | solution.py:122
  58.6 2.2 %collective-permute-start.9 = (f32[9,32,512]{2,1,0:T(8,128)S(1)}, f32[9,32,512]{2,1,0:T(8,128)}, u32[]{:S(2)}, u32[]{:S(2)}) collective-permute-start(f32[9,32,512]{2,1,0:T(8,128)S(1)} %pad_maximum_fusion), channel_id=1, source_target_pairs={{0,1},{1,0},{2,3},{3,2},{4,5},{5,4},{6,7},{7,6},{8,9},{9,8},{10,11... | collective-permute-start | bytes 1769480 | tf_op jit(solution)/shard_map/ppermute | solution.py:122
  63.1 4.3 %collective-permute-start.10 = (f32[4,64,32]{1,2,0:T(8,128)S(1)}, f32[4,64,32]{1,2,0:T(8,128)S(1)}, u32[]{:S(2)}, u32[]{:S(2)}) collective-permute-start(f32[4,64,32]{1,2,0:T(8,128)S(1)} %fusion.2), channel_id=1, source_target_pairs={{0,16},{16,0},{1,17},{17,1},{2,18},{18,2},{3,19},{19,3},{4,20},{20... | collective-permute-start | bytes 98312 | tf_op jit(solution)/shard_map/ppermute | solution.py:21
  68.4 2.1 %collective-permute-start.11 = (f32[9,32,512]{2,1,0:T(8,128)S(1)}, f32[9,32,512]{2,1,0:T(8,128)S(1)}, u32[]{:S(2)}, u32[]{:S(2)}) collective-permute-start(f32[9,32,512]{2,1,0:T(8,128)S(1)} %constant_dynamic-slice_fusion.2), channel_id=1, source_target_pairs={{0,1},{1,0},{2,3},{3,2},{4,5},{5,4},{6,7},{7,6},{8,9},{9,8},{10,11... | collective-permute-start | bytes 1769480 | tf_op jit(solution)/shard_map/ppermute | solution.py:94
  70.6 6.8 %collective-permute-start.12 = (f32[9,32,256]{2,1,0:T(8,128)S(1)}, f32[9,32,256]{2,1,0:T(8,128)S(1)}, u32[]{:S(2)}, u32[]{:S(2)}) collective-permute-start(f32[9,32,256]{2,1,0:T(8,128)S(1)} %constant_dynamic-slice_fusion.1), channel_id=1, source_target_pairs={{0,2},{1,5},{2,0},{3,7},{4,6},{5,1},{6,4},{7,3},{8,10},{9,13},{10,... | collective-permute-start | bytes 884744 | tf_op jit(solution)/shard_map/ppermute | solution.py:94
  77.5 5.2 %collective-permute-start.13 = (f32[9,32,128]{2,1,0:T(8,128)S(1)}, f32[9,32,128]{2,1,0:T(8,128)S(1)}, u32[]{:S(2)}, u32[]{:S(2)}) collective-permute-start(f32[9,32,128]{2,1,0:T(8,128)S(1)} %constant_dynamic-slice_fusion), channel_id=1, source_target_pairs={{0,4},{1,3},{2,6},{3,1},{4,0},{5,7},{6,2},{7,5},{8,12},{9,11},{10,... | collective-permute-start | bytes 442376 | tf_op jit(solution)/shard_map/ppermute | solution.py:94
  82.7 13.2 %collective-permute-start.14 = (f32[9,32,128]{2,1,0:T(8,128)S(1)}, f32[9,32,128]{2,1,0:T(8,128)S(1)}, u32[]{:S(2)}, u32[]{:S(2)}) collective-permute-start(f32[9,32,128]{2,1,0:T(8,128)S(1)} %dynamic-slice_add_fusion.4), channel_id=1, source_target_pairs={{0,8},{1,17},{2,10},{3,19},{4,12},{5,21},{6,14},{7,23},{8,0},{9,25... | collective-permute-start | bytes 442376 | tf_op jit(solution)/shard_map/ppermute | solution.py:109
  84.7 11.2 %collective-permute-start.15 = (f32[9,32,128]{2,1,0:T(8,128)S(1)}, f32[9,32,128]{2,1,0:T(8,128)S(1)}, u32[]{:S(2)}, u32[]{:S(2)}) collective-permute-start(f32[9,32,128]{2,1,0:T(8,128)S(1)} %dynamic-slice_add_fusion.4), channel_id=1, source_target_pairs={{0,16},{1,9},{2,18},{3,11},{4,20},{5,13},{6,22},{7,15},{8,24},{9,1... | collective-permute-start | bytes 442376 | tf_op jit(solution)/shard_map/ppermute | solution.py:108
  86.2 12.1 %collective-permute-start.16 = (f32[9,32,128]{2,1,0:T(8,128)S(1)}, f32[9,32,128]{2,1,0:T(8,128)S(1)}, u32[]{:S(2)}, u32[]{:S(2)}) collective-permute-start(f32[9,32,128]{2,1,0:T(8,128)S(1)} %dynamic-slice_add_fusion.4), channel_id=1, source_target_pairs={{0,24},{1,25},{2,26},{3,27},{4,28},{5,29},{6,30},{7,31},{8,16},{9,... | collective-permute-start | bytes 442376 | tf_op jit(solution)/shard_map/ppermute | solution.py:107
  98.3 5.2 %collective-permute-start.17 = (f32[9,32,128]{2,1,0:T(8,128)S(1)}, f32[9,32,128]{2,1,0:T(8,128)S(1)}, u32[]{:S(2)}, u32[]{:S(2)}) collective-permute-start(f32[9,32,128]{2,1,0:T(8,128)S(1)} %select_add_fusion), channel_id=1, source_target_pairs={{0,4},{1,3},{2,6},{3,1},{4,0},{5,7},{6,2},{7,5},{8,12},{9,11},{10,... | collective-permute-start | bytes 442376 | tf_op jit(solution)/shard_map/ppermute | solution.py:122
  103.6 6.8 %collective-permute-start.18 = (f32[9,32,256]{2,1,0:T(8,128)S(1)}, f32[9,32,256]{2,1,0:T(8,128)S(1)}, u32[]{:S(2)}, u32[]{:S(2)}) collective-permute-start(f32[9,32,256]{2,1,0:T(8,128)S(1)} %pad_maximum_fusion.3), channel_id=1, source_target_pairs={{0,2},{1,5},{2,0},{3,7},{4,6},{5,1},{6,4},{7,3},{8,10},{9,13},{10,... | collective-permute-start | bytes 884744 | tf_op jit(solution)/shard_map/ppermute | solution.py:122
  110.5 2.2 %copy-start.3 = (f32[4,64,1024]{2,1,0:T(8,128)S(1)}, f32[4,64,1024]{2,1,0:T(8,128)}, u32[]{:S(2)}) copy-start(f32[4,64,1024]{2,1,0:T(8,128)} %param.12) | copy-start | bytes 3145732
  110.5 2.1 %collective-permute-start.19 = (f32[9,32,512]{2,1,0:T(8,128)S(1)}, f32[9,32,512]{2,1,0:T(8,128)S(1)}, u32[]{:S(2)}, u32[]{:S(2)}) collective-permute-start(f32[9,32,512]{2,1,0:T(8,128)S(1)} %pad_maximum_fusion.1), channel_id=1, source_target_pairs={{0,1},{1,0},{2,3},{3,2},{4,5},{5,4},{6,7},{7,6},{8,9},{9,8},{10,11... | collective-permute-start | bytes 1769480 | tf_op jit(solution)/shard_map/ppermute | solution.py:122
